TPU v7x, 32 devices: a whole 2x2x4 slice. The times are simulated.
32 devices in a mesh: groups: 2 (over y), seq: 8 (over z, x), hid: 2 (over core).
Axes of the slice: x: 2, y: 2, z: 4, core: 2. Of those that a mesh axis runs over, the one named last changes fastest.
Arguments:
- tokens: bfloat16 [2048, 2048], P(('groups', 'seq'), 'hid'), parts along dimension 0, may hold values from -6 to 6
- cotangent: bfloat16 [2048, 2048], P(('groups', 'seq'), 'hid'), parts along dimension 0, may hold values from -6 to 6
- blocks: bfloat16 [8, 128, 128], P('seq'), may hold values from -0.5 to 0.5
- coef_self: float32 [3, 1024], P(None, 'seq'), may hold values from 0.7 to 1
- coef_cross: float32 [3, 1024], P(None, 'seq'), may hold values from -0.5 to 0.5
- norm_gain: float32 [2048], P('hid'), may hold values from 0.5 to 1.5
- w_gate: bfloat16 [16, 128, 512], P('hid'), may hold values from -0.5 to 0.5
- w_up: bfloat16 [16, 128, 512], P('hid'), may hold values from -0.5 to 0.5
- w_down: bfloat16 [16, 512, 128], P('hid'), may hold values from -0.25 to 0.25
Outputs:
- grad_x: bfloat16 [2048, 2048], P(('groups', 'seq'), 'hid'), parts along dimension 0
- grad_self: float32 [3, 2048], P(None, ('groups', 'seq')), parts along dimension 1
- grad_cross: float32 [3, 2048], P(None, ('groups', 'seq')), parts along dimension 1
- grad_blocks: float32 [16, 128, 128], P(('groups', 'seq')), parts along dimension 0
There are 2 independent parts, one for each index of `groups`. A program takes and returns all parts, laid end to end along the dimension named above; an argument that names none is the same for every part. Nothing has to cross between parts.
All inputs are finite; a program needn't handle non-finite values.
Results may differ from a plain program's by a relative error of at most 0.0097.
Values may be sent and summed in bfloat16 or wider, within the bound.
No kernel may reach another device: no remote copies, remote signals or barrier semaphores. Data moves between devices by JAX's collectives and lax.ppermute only.
A program may use at most 64 MiB of HBM per device.

v0:
```python
import jax
import jax.numpy as jnp
from jax import lax
from jax.sharding import PartitionSpec as P

D = 2048


def from_partner(value, axis, distance):
    mask = 2**distance
    pairs = [(source, source ^ mask) for source in range(lax.axis_size(axis))]
    return lax.ppermute(value, axis, pairs)


def body(tokens, cotangent, blocks, coef_self, coef_cross, norm_gain, w_gate, w_up, w_down):
    tok, width = tokens.shape
    sections = lax.axis_size("seq").bit_length() - 1
    nblk = blocks.shape[0]
    blen = blocks.shape[1]
    groups_here = w_gate.shape[0]
    cblock = w_gate.shape[1]
    tok_blocks = tokens.reshape(nblk, blen, width)
    local = jnp.einsum("kij,kjd->kid", blocks, tok_blocks, preferred_element_type=jnp.float32)
    local = local.astype(jnp.bfloat16).reshape(tok, width)
    states = []
    mates = []
    current = local
    for section in range(sections):
        mate = from_partner(current, "seq", section)
        states.append(current)
        mates.append(mate)
        current = (
            coef_self[section][:, None] * current.astype(jnp.float32)
            + coef_cross[section][:, None] * mate.astype(jnp.float32)
        ).astype(jnp.bfloat16)
    tok_f = tokens.astype(jnp.float32)
    mixed_f = current.astype(jnp.float32)
    resid = tok_f + tok_f * mixed_f
    square = lax.psum(jnp.sum(resid * resid, axis=-1), "hid")
    inv = lax.rsqrt(square / D + 1e-06)
    normed = (
        (resid * inv[:, None] * norm_gain).astype(jnp.bfloat16).reshape(tok, groups_here, cblock)
    )
    gate_pre = jnp.einsum("tgc,gce->tge", normed, w_gate, preferred_element_type=jnp.float32)
    up_val = jnp.einsum("tgc,gce->tge", normed, w_up, preferred_element_type=jnp.float32)
    d_hidden = jnp.einsum(
        "tgc,gec->tge",
        cotangent.reshape(tok, groups_here, cblock),
        w_down,
        preferred_element_type=jnp.float32,
    )
    sig = jax.nn.sigmoid(gate_pre)
    d_up = (d_hidden * gate_pre * sig).astype(jnp.bfloat16)
    d_gate = (d_hidden * up_val * sig * (1.0 + gate_pre * (1.0 - sig))).astype(jnp.bfloat16)
    d_normed = jnp.einsum("tge,gce->tgc", d_gate, w_gate, preferred_element_type=jnp.float32)
    d_normed = d_normed + jnp.einsum("tge,gce->tgc", d_up, w_up, preferred_element_type=jnp.float32)
    scaled = norm_gain * d_normed.reshape(tok, width)
    inner = lax.psum(jnp.sum(resid * scaled, axis=-1), "hid")
    d_resid = (
        cotangent.astype(jnp.float32)
        + inv[:, None] * scaled
        - resid * (inv**3 * inner / D)[:, None]
    )
    d_mixed = (d_resid * tok_f).astype(jnp.bfloat16)
    grads_self = [None] * sections
    grads_cross = [None] * sections
    back = d_mixed
    for section in range(sections - 1, -1, -1):
        back_f = back.astype(jnp.float32)
        grads_self[section] = jnp.sum(back_f * states[section].astype(jnp.float32), axis=-1)
        grads_cross[section] = jnp.sum(back_f * mates[section].astype(jnp.float32), axis=-1)
        sent = (coef_cross[section][:, None] * back_f).astype(jnp.bfloat16)
        received = from_partner(sent, "seq", section)
        back = (coef_self[section][:, None] * back_f + received.astype(jnp.float32)).astype(
            jnp.bfloat16
        )
    part_self = jnp.stack(grads_self)
    part_cross = jnp.stack(grads_cross)
    back_blocks = back.reshape(nblk, blen, width)
    part_blocks = jnp.einsum(
        "kid,kjd->kij", back_blocks, tok_blocks, preferred_element_type=jnp.float32
    )
    from_blocks = jnp.einsum(
        "kij,kid->kjd", blocks, back_blocks, preferred_element_type=jnp.float32
    ).reshape(tok, width)
    grad_self, grad_cross, grad_blocks = lax.psum((part_self, part_cross, part_blocks), "hid")
    grad_x = (d_resid * (1.0 + mixed_f) + from_blocks).astype(jnp.bfloat16)
    return (grad_x, grad_self, grad_cross, grad_blocks)


def solution(mesh):
    return jax.shard_map(
        body,
        mesh=mesh,
        in_specs=(
            P(("groups", "seq"), "hid"),
            P(("groups", "seq"), "hid"),
            P("seq", None, None),
            P(None, "seq"),
            P(None, "seq"),
            P("hid"),
            P("hid", None, None),
            P("hid", None, None),
            P("hid", None, None),
        ),
        out_specs=(
            P(("groups", "seq"), "hid"),
            P(None, ("groups", "seq")),
            P(None, ("groups", "seq")),
            P(("groups", "seq"), None, None),
        ),
        check_vma=False,
    )
```

profile of v0, /device:TPU:0, one launch (start us, length us, event | category | flops | bytes accessed | tf_op | source)
XLA Modules:
  0.0 115.2 jit_solution(9888987271807249206)
XLA Ops:
  7.2 1.3 %convolution_convert_fusion = bf16[128,1024]{1,0:T(8,128)(2,1)S(1)} fusion(bf16[128,1024]{1,0:T(8,128)(2,1)} %param.9, bf16[1,128,128]{2,1,0:T(8,128)(2,1)} %param.11), kind=kOutput, calls=%fused_computation.18 | convolution fusion | flops 33685504 | bytes 557056 | tf_op jit(solution)/shard_map/kij,kjd->kid/dot_general | solution.py:23
  8.6 3.0 %collective-permute-start = (bf16[128,1024]{1,0:T(8,128)(2,1)S(1)}, bf16[128,1024]{1,0:T(8,128)(2,1)S(1)}, u32[]{:S(2)}, u32[]{:S(2)}) collective-permute-start(bf16[128,1024]{1,0:T(8,128)(2,1)S(1)} %convolution_convert_fusion), channel_id=1, source_target_pairs={{0,2},{2,0},{4,6},{6,4},{8,10},{10,8},{12,14},{14,12},{1,3},{3,1},... | collective-permute-start | bytes 786440 | tf_op jit(solution)/shard_map/ppermute | solution.py:12
  11.6 0.8 slice_bitcast_fusion
  12.4 5.5 %collective-permute-done = bf16[128,1024]{1,0:T(8,128)(2,1)S(1)} collective-permute-done((bf16[128,1024]{1,0:T(8,128)(2,1)S(1)}, bf16[128,1024]{1,0:T(8,128)(2,1)S(1)}, u32[]{:S(2)}, u32[]{:S(2)}) %collective-permute-start) | collective-permute-done | bytes 262176 | tf_op jit(solution)/shard_map/ppermute | solution.py:12
  17.9 0.2 fusion.16
  18.1 1.9 %collective-permute-start.1 = (bf16[128,1024]{1,0:T(8,128)(2,1)S(1)}, bf16[128,1024]{1,0:T(8,128)(2,1)S(1)}, u32[]{:S(2)}, u32[]{:S(2)}) collective-permute-start(bf16[128,1024]{1,0:T(8,128)(2,1)S(1)} %fusion.16), channel_id=1, source_target_pairs={{0,4},{2,6},{4,0},{6,2},{8,12},{10,14},{12,8},{14,10},{1,5},{3,7},... | collective-permute-start | bytes 786440 | tf_op jit(solution)/shard_map/ppermute | solution.py:12
  20.0 5.7 %collective-permute-done.1 = bf16[128,1024]{1,0:T(8,128)(2,1)S(1)} collective-permute-done((bf16[128,1024]{1,0:T(8,128)(2,1)S(1)}, bf16[128,1024]{1,0:T(8,128)(2,1)S(1)}, u32[]{:S(2)}, u32[]{:S(2)}) %collective-permute-start.1) | collective-permute-done | bytes 262176 | tf_op jit(solution)/shard_map/ppermute | solution.py:12
  25.6 0.7 copy-done.3
  26.3 0.2 fusion.18
  26.5 2.6 %collective-permute-start.2 = (bf16[128,1024]{1,0:T(8,128)(2,1)S(1)}, bf16[128,1024]{1,0:T(8,128)(2,1)S(1)}, u32[]{:S(2)}, u32[]{:S(2)}) collective-permute-start(bf16[128,1024]{1,0:T(8,128)(2,1)S(1)} %fusion.18), channel_id=1, source_target_pairs={{0,8},{2,10},{4,12},{6,14},{8,0},{10,2},{12,4},{14,6},{1,9},{3,11}... | collective-permute-start | bytes 786440 | tf_op jit(solution)/shard_map/ppermute | solution.py:12
  29.1 1.7 %fusion.42 = f32[8,512,128]{2,1,0:T(8,128)} fusion(bf16[8,512,128]{2,1,0:T(8,128)(2,1)S(1)} %copy-done.2, bf16[128,1024]{1,0:T(8,128)(2,1)S(1)} %copy-done.5), kind=kOutput, calls=%fused_computation.73 | convolution fusion | flops 134217728 | bytes 3407872 | tf_op jit(solution)/shard_map/tgc,gec->tge/dot_general | solution.py:46
  30.8 8.8 %collective-permute-done.2 = bf16[128,1024]{1,0:T(8,128)(2,1)S(1)} collective-permute-done((bf16[128,1024]{1,0:T(8,128)(2,1)S(1)}, bf16[128,1024]{1,0:T(8,128)(2,1)S(1)}, u32[]{:S(2)}, u32[]{:S(2)}) %collective-permute-start.2) | collective-permute-done | bytes 262176 | tf_op jit(solution)/shard_map/ppermute | solution.py:12
  39.7 0.4 multiply_reduce_fusion.1
  40.0 2.5 %psum.35 = f32[128]{0:T(128)S(1)} all-reduce(f32[128]{0:T(128)S(1)} %get-tuple-element.15), channel_id=1, replica_groups=mesh['groups'=2,'seq'=8,'hid'=2] {'hid'}, use_global_device_ids=true, to_apply=%region_1.0 | all-reduce | flops 128 | bytes 1024 | tf_op jit(solution)/shard_map/psum | solution.py:39
  42.5 1.9 %fusion.40 = f32[8,128,512]{1,2,0:T(8,128)} fusion(bf16[8,128,512]{2,1,0:T(8,128)(2,1)S(1)} %copy-done, bf16[128,1024]{1,0:T(8,128)(2,1)S(1)} %get-tuple-element.16, bf16[128,1024]{1,0:T(8,128)(2,1)S(1)} %copy-done.1, f32[1024]{0:T(1024)S(1)} %copy-done.7, f32[128]{0:T(128)S(1)} %add_rsqrt_fusion), kind=kOutput, calls=%fused_computation.71 | convolution fusion | flops 135135232 | bytes 3674624 | tf_op jit(solution)/shard_map/tgc,gce->tge/dot_general | solution.py:44
  44.4 3.9 %fusion.10 = f32[8,128,128]{1,2,0:T(8,128)S(1)} fusion(bf16[8,128,512]{2,1,0:T(8,128)(2,1)S(1)} %copy-done, f32[8,128,512]{1,2,0:T(8,128)} %fusion.40, f32[8,512,128]{2,1,0:T(8,128)} %fusion.42, bf16[8,128,512]{2,1,0:T(8,128)(2,1)} %param.16, bf16[128,1024]{1,0:T(8,128)(2,1)S(1)} %get-tuple-element.16, bf16[128,1024]{1,0:T(8,128)(2,1)S(1)} %copy-done.1, ...), kind=kOutput, calls=%fused_computation.16 | convolution fusion | flops 274595840 | bytes 7344640 | tf_op jit(solution)/shard_map/tge,gce->tgc/dot_general | solution.py:55
  48.3 4.2 %convolution_add_fusion = f32[8,128,128]{1,2,0:T(8,128)} fusion(f32[8,128,128]{1,2,0:T(8,128)S(1)} %fusion.10, bf16[8,128,512]{2,1,0:T(8,128)(2,1)} %param.16, f32[8,128,512]{1,2,0:T(8,128)} %fusion.40, f32[8,512,128]{2,1,0:T(8,128)} %fusion.42), kind=kOutput, calls=%fused_computation.13 | convolution fusion | flops 137494528 | bytes 6291456 | tf_op jit(solution)/shard_map/tge,gce->tgc/dot_general | solution.py:56
  52.5 1.2 %copy.24 = f32[128,1024]{1,0:T(8,128)S(1)} copy(f32[128,1024]{0,1:T(8,128)} %bitcast.102) | data formatting | bytes 1048576 | tf_op jit(solution)/shard_map/reshape | solution.py:57
  53.7 0.2 multiply_reduce_fusion
  53.9 2.5 %psum.36 = f32[128]{0:T(128)S(1)} all-reduce(f32[128]{0:T(128)S(1)} %multiply_reduce_fusion), channel_id=1, replica_groups=mesh['groups'=2,'seq'=8,'hid'=2] {'hid'}, use_global_device_ids=true, to_apply=%region_3.0 | all-reduce | flops 128 | bytes 1024 | tf_op jit(solution)/shard_map/psum | solution.py:58
  56.4 1.4 %fusion.26 = (f32[128]{0:T(128)S(1)}, f32[128]{0:T(128)S(1)}, bf16[128,1024]{1,0:T(8,128)(2,1)S(1)}) fusion(bf16[128,1024]{1,0:T(8,128)(2,1)S(1)} %collective-permute-done.2, bf16[128,1024]{1,0:T(8,128)(2,1)S(1)} %fusion.18, f32[128]{0:T(128)S(1)} %fusion.51, bf16[128,1024]{1,0:T(8,128)(2,1)S(1)} %get-tuple-element.16, bf16[128,1024]{1,0:T(8,128)(2,1)S(1)} %copy-done.1, ...), kind=kLoop, calls=%fused_computation.54 | loop fusion | flops 2490112 | bytes 2103296 | tf_op jit(solution)/shard_map/reduce_sum | solution.py:71
  58.1 14.9 %collective-permute-done.3 = bf16[128,1024]{1,0:T(8,128)(2,1)S(1)} collective-permute-done((bf16[128,1024]{1,0:T(8,128)(2,1)S(1)}, bf16[128,1024]{1,0:T(8,128)(2,1)S(1)}, u32[]{:S(2)}, u32[]{:S(2)}) %collective-permute-start.3) | collective-permute-done | bytes 262176 | tf_op jit(solution)/shard_map/ppermute | solution.py:12
  72.9 0.3 fusion.31
  73.5 7.8 %collective-permute-done.4 = bf16[128,1024]{1,0:T(8,128)(2,1)S(1)} collective-permute-done((bf16[128,1024]{1,0:T(8,128)(2,1)S(1)}, bf16[128,1024]{1,0:T(8,128)(2,1)S(1)}, u32[]{:S(2)}, u32[]{:S(2)}) %collective-permute-start.4) | collective-permute-done | bytes 262176 | tf_op jit(solution)/shard_map/ppermute | solution.py:12
  81.3 0.3 fusion.36
  81.7 0.9 collective-permute-start.5
  82.7 3.0 %all-reduce = (f32[3,128]{1,0:T(4,128)}, f32[3,128]{1,0:T(4,128)}) all-reduce(f32[3,128]{1,0:T(4,128)S(1)} %pad_maximum_fusion, f32[3,128]{1,0:T(4,128)S(1)} %pad_maximum_fusion.1), channel_id=1, replica_groups=mesh['groups'=2,'seq'=8,'hid'=2] {'hid'}, use_global_device_ids=true, to_apply=%region_7.0 | all-reduce | flops 768 | bytes 6144 | tf_op jit(solution)/shard_map/psum | solution.py:86
  85.7 2.9 %collective-permute-done.5 = bf16[128,1024]{1,0:T(8,128)(2,1)S(1)} collective-permute-done((bf16[128,1024]{1,0:T(8,128)(2,1)S(1)}, bf16[128,1024]{1,0:T(8,128)(2,1)S(1)}, u32[]{:S(2)}, u32[]{:S(2)}) %collective-permute-start.5) | collective-permute-done | bytes 262176 | tf_op jit(solution)/shard_map/ppermute | solution.py:12
  88.7 0.9 convolution_bitcast_fusion.1
  89.6 1.1 fusion.11
  90.8 16.1 %all-reduce.3.cloned.1.call-done = f32[1,128,128]{2,1,0:T(8,128)} async-done(((f32[1,128,128]{2,1,0:T(8,128)}), f32[1,128,128]{2,1,0:T(8,128)}) %all-reduce.3.cloned.1.call-update) | async-done | bytes 65552 | tf_op jit(solution)/shard_map/psum | solution.py:86
  106.9 1.5 %copy.41 = f32[1,128,128]{2,1,0:T(8,128)} copy(f32[1,128,128]{2,1,0:T(8,128)} %all-reduce.3.cloned.1.call-done) | data formatting | bytes 131072
  (28 shorter events, 0.6 us)
Async XLA Ops:
  7.2 35.3 %copy-start = (bf16[8,128,512]{2,1,0:T(8,128)(2,1)S(1)}, bf16[8,128,512]{2,1,0:T(8,128)(2,1)}, u32[]{:S(2)}) copy-start(bf16[8,128,512]{2,1,0:T(8,128)(2,1)} %param.15) | copy-start | bytes 3145732
  7.2 21.9 %copy-start.5 = (bf16[128,1024]{1,0:T(8,128)(2,1)S(1)}, bf16[128,1024]{1,0:T(8,128)(2,1)}, u32[]{:S(2)}) copy-start(bf16[128,1024]{1,0:T(8,128)(2,1)} %param.10) | copy-start | bytes 786436
  7.2 99.7 %all-reduce.3.cloned.1.call-start = ((), (), s32[]{:S(2)}) async-start(), calls=%async_computation | async-start | bytes 131072 | tf_op jit(solution)/shard_map/psum | solution.py:86
  7.2 21.9 %copy-start.2 = (bf16[8,512,128]{2,1,0:T(8,128)(2,1)S(1)}, bf16[8,512,128]{2,1,0:T(8,128)(2,1)}, u32[]{:S(2)}) copy-start(bf16[8,512,128]{2,1,0:T(8,128)(2,1)} %param.17) | copy-start | bytes 3145732
  8.6 9.3 %collective-permute-start = (bf16[128,1024]{1,0:T(8,128)(2,1)S(1)}, bf16[128,1024]{1,0:T(8,128)(2,1)S(1)}, u32[]{:S(2)}, u32[]{:S(2)}) collective-permute-start(bf16[128,1024]{1,0:T(8,128)(2,1)S(1)} %convolution_convert_fusion), channel_id=1, source_target_pairs={{0,2},{2,0},{4,6},{6,4},{8,10},{10,8},{12,14},{14,12},{1,3},{3,1},... | collective-permute-start | bytes 786440 | tf_op jit(solution)/shard_map/ppermute | solution.py:12
  18.1 7.6 %collective-permute-start.1 = (bf16[128,1024]{1,0:T(8,128)(2,1)S(1)}, bf16[128,1024]{1,0:T(8,128)(2,1)S(1)}, u32[]{:S(2)}, u32[]{:S(2)}) collective-permute-start(bf16[128,1024]{1,0:T(8,128)(2,1)S(1)} %fusion.16), channel_id=1, source_target_pairs={{0,4},{2,6},{4,0},{6,2},{8,12},{10,14},{12,8},{14,10},{1,5},{3,7},... | collective-permute-start | bytes 786440 | tf_op jit(solution)/shard_map/ppermute | solution.py:12
  25.6 0.7 copy-start.3
  26.3 13.3 %copy-start.1 = (bf16[128,1024]{1,0:T(8,128)(2,1)S(1)}, bf16[128,1024]{1,0:T(8,128)(2,1)}, u32[]{:S(2)}) copy-start(bf16[128,1024]{1,0:T(8,128)(2,1)} %param.9) | copy-start | bytes 786436
  26.5 16.0 %copy-start.7 = (f32[1024]{0:T(1024)S(1)}, f32[1024]{0:T(1024)}, u32[]{:S(2)}) copy-start(f32[1024]{0:T(1024)} %param.14) | copy-start | bytes 12292
  26.5 13.2 %collective-permute-start.2 = (bf16[128,1024]{1,0:T(8,128)(2,1)S(1)}, bf16[128,1024]{1,0:T(8,128)(2,1)S(1)}, u32[]{:S(2)}, u32[]{:S(2)}) collective-permute-start(bf16[128,1024]{1,0:T(8,128)(2,1)S(1)} %fusion.18), channel_id=1, source_target_pairs={{0,8},{2,10},{4,12},{6,14},{8,0},{10,2},{12,4},{14,6},{1,9},{3,11}... | collective-permute-start | bytes 786440 | tf_op jit(solution)/shard_map/ppermute | solution.py:12
  56.4 16.6 %copy-start.4 = (bf16[128,1024]{1,0:T(8,128)(2,1)S(1)}, bf16[128,1024]{1,0:T(8,128)(2,1)}, u32[]{:S(2)}) copy-start(bf16[128,1024]{1,0:T(8,128)(2,1)} %copy-done.3) | copy-start | bytes 786436
  58.0 31.7 %copy-start.6 = (bf16[128,1024]{1,0:T(8,128)(2,1)S(1)}, bf16[128,1024]{1,0:T(8,128)(2,1)}, u32[]{:S(2)}) copy-start(bf16[128,1024]{1,0:T(8,128)(2,1)} %param.10) | copy-start | bytes 786436
  58.0 31.6 %copy-start.8 = (bf16[1,128,128]{2,1,0:T(8,128)(2,1)S(1)}, bf16[1,128,128]{2,1,0:T(8,128)(2,1)}, u32[]{:S(2)}) copy-start(bf16[1,128,128]{2,1,0:T(8,128)(2,1)} %param.11) | copy-start | bytes 98308
  58.0 15.0 %collective-permute-start.3 = (bf16[128,1024]{1,0:T(8,128)(2,1)S(1)}, bf16[128,1024]{1,0:T(8,128)(2,1)S(1)}, u32[]{:S(2)}, u32[]{:S(2)}) collective-permute-start(bf16[128,1024]{1,0:T(8,128)(2,1)S(1)} %fusion.24), channel_id=1, source_target_pairs={{0,8},{2,10},{4,12},{6,14},{8,0},{10,2},{12,4},{14,6},{1,9},{3,11}... | collective-permute-start | bytes 786440 | tf_op jit(solution)/shard_map/ppermute | solution.py:12
  73.4 7.9 %collective-permute-start.4 = (bf16[128,1024]{1,0:T(8,128)(2,1)S(1)}, bf16[128,1024]{1,0:T(8,128)(2,1)S(1)}, u32[]{:S(2)}, u32[]{:S(2)}) collective-permute-start(bf16[128,1024]{1,0:T(8,128)(2,1)S(1)} %fusion.29), channel_id=1, source_target_pairs={{0,4},{2,6},{4,0},{6,2},{8,12},{10,14},{12,8},{14,10},{1,5},{3,7},... | collective-permute-start | bytes 786440 | tf_op jit(solution)/shard_map/ppermute | solution.py:12
  81.7 7.0 %collective-permute-start.5 = (bf16[128,1024]{1,0:T(8,128)(2,1)S(1)}, bf16[128,1024]{1,0:T(8,128)(2,1)S(1)}, u32[]{:S(2)}, u32[]{:S(2)}) collective-permute-start(bf16[128,1024]{1,0:T(8,128)(2,1)S(1)} %fusion.34), channel_id=1, source_target_pairs={{0,2},{2,0},{4,6},{6,4},{8,10},{10,8},{12,14},{14,12},{1,3},{3,1},... | collective-permute-start | bytes 786440 | tf_op jit(solution)/shard_map/ppermute | solution.py:12
Sparse Core Ops, SparseCore 0:
  89.7 17.1 all-reduce.2
where the time goes:
time: 116 us; the launch traced here: 115 us
  waiting for transfers between devices  61.8 us (53%)
  matrix products  15.1 us (13%)
  between operations  14.2 us (12%)
  starting transfers between devices  8.6 us (7%)
  blocking collectives  7.97 us (7%)
  local copies, waits for them, and re-layouts  4.26 us (4%)
  other arithmetic  3.34 us (3%)
    ppermute x6, waiting for transfers between devices, from_partner(): return lax.ppermute(value, axis, pairs)  45.6 us
    psum x1, waiting for transfers between devices, body(): lax.psum((part_self, part_cross, part_blocks), 'hid')  16.1 us
    ppermute x6, starting transfers between devices, from_partner(): return lax.ppermute(value, axis, pairs)  8.57 us
    dot_general x1, matrix products, body(): jnp.einsum('tge,gce->tgc', d_up, w_up, preferred_element_type=jnp.float32)  4.16 us
    dot_general x1, matrix products, body(): jnp.einsum('tge,gce->tgc', d_gate, w_gate, preferred_element_type=jnp.flo...  3.9 us
    psum x1, blocking collectives, body(): lax.psum((part_self, part_cross, part_blocks), 'hid')  3.04 us
    psum x1, blocking collectives, body(): square = lax.psum(jnp.sum(resid * resid, axis=-1), 'hid')  2.47 us
    psum x1, blocking collectives, body(): inner = lax.psum(jnp.sum(resid * scaled, axis=-1), 'hid')  2.46 us
  transfers between devices with their start and end apart: 7, of which 7 were waited for; matrix products, arithmetic and copies ran while one was open for 3% of the time, Pallas kernels for 0%

commit v1 on v0

--- a/solution.py
+++ b/solution.py
@@ -10,6 +10,15 @@
     mask = 2**distance
     pairs = [(source, source ^ mask) for source in range(lax.axis_size(axis))]
     return lax.ppermute(value, axis, pairs)
+
+
+def hid_sum(value):
+    size = lax.axis_size("hid")
+    total = value
+    for shift in range(1, size):
+        pairs = [(source, (source + shift) % size) for source in range(size)]
+        total = total + lax.ppermute(value, "hid", pairs)
+    return total
 
 
 def body(tokens, cotangent, blocks, coef_self, coef_cross, norm_gain, w_gate, w_up, w_down):
@@ -36,7 +45,7 @@
     tok_f = tokens.astype(jnp.float32)
     mixed_f = current.astype(jnp.float32)
     resid = tok_f + tok_f * mixed_f
-    square = lax.psum(jnp.sum(resid * resid, axis=-1), "hid")
+    square = hid_sum(jnp.sum(resid * resid, axis=-1))
     inv = lax.rsqrt(square / D + 1e-06)
     normed = (
         (resid * inv[:, None] * norm_gain).astype(jnp.bfloat16).reshape(tok, groups_here, cblock)
@@ -55,7 +64,7 @@
     d_normed = jnp.einsum("tge,gce->tgc", d_gate, w_gate, preferred_element_type=jnp.float32)
     d_normed = d_normed + jnp.einsum("tge,gce->tgc", d_up, w_up, preferred_element_type=jnp.float32)
     scaled = norm_gain * d_normed.reshape(tok, width)
-    inner = lax.psum(jnp.sum(resid * scaled, axis=-1), "hid")
+    inner = hid_sum(jnp.sum(resid * scaled, axis=-1))
     d_resid = (
         cotangent.astype(jnp.float32)
         + inv[:, None] * scaled
@@ -83,7 +92,7 @@
     from_blocks = jnp.einsum(
         "kij,kid->kjd", blocks, back_blocks, preferred_element_type=jnp.float32
     ).reshape(tok, width)
-    grad_self, grad_cross, grad_blocks = lax.psum((part_self, part_cross, part_blocks), "hid")
+    grad_self, grad_cross, grad_blocks = jax.tree.map(hid_sum, (part_self, part_cross, part_blocks))
     grad_x = (d_resid * (1.0 + mixed_f) + from_blocks).astype(jnp.bfloat16)
     return (grad_x, grad_self, grad_cross, grad_blocks)
 

time: 116 us -> 85 us (0.73)
  between operations: 14.2 us -> 0.86 us
  waiting for transfers between devices: 61.8 us -> 51.6 us
  blocking collectives: 7.97 us -> 0 us
  other arithmetic: 3.34 us -> 5.11 us
  local copies, waits for them, and re-layouts: 4.26 us -> 2.79 us
  starting transfers between devices: 8.6 us -> 9.97 us
    psum x1 -> x0, waiting for transfers between devices: 16.1 us -> none  [body(): lax.psum((part_self, part_cross, part_blocks), 'hid')]
    psum x3 -> x0, blocking collectives: 7.97 us -> none  [the longest x1 3.04 us: body(): lax.psum((part_self, part_cross, part_blocks), 'hid')]
    ppermute x6, waiting for transfers between devices: 45.6 us -> 50.6 us  [from_partner(): return lax.ppermute(value, axis, pairs)]
    add x0 -> x3, other arithmetic: none -> 1.81 us  [hid_sum(): total = total + lax.ppermute(value, 'hid', pairs)]
    unnamed x19 -> x18, local copies, waits for them, and re-layouts: 2.22 us -> 0.75 us
    ppermute x0 -> x5, starting transfers between devices: none -> 1.3 us  [hid_sum(): total = total + lax.ppermute(value, 'hid', pairs)]
  transfers between devices with their start and end apart: 7 -> 11, of which waited for: 7 -> 8; matrix products, arithmetic and copies ran while one was open for 3% -> 6% of each run, Pallas kernels for 0% -> 0%
where the time goes in v1:
time: 85 us; the launch traced here: 84.7 us
  waiting for transfers between devices  51.6 us (61%)
  matrix products  14.4 us (17%)
  starting transfers between devices  9.97 us (12%)
  other arithmetic  5.11 us (6%)
  local copies, waits for them, and re-layouts  2.79 us (3%)
  between operations  0.86 us (1%)
    ppermute x6, waiting for transfers between devices, from_partner(): return lax.ppermute(value, axis, pairs)  50.6 us
    ppermute x6, starting transfers between devices, from_partner(): return lax.ppermute(value, axis, pairs)  8.67 us
    dot_general x1, matrix products, body(): jnp.einsum('tge,gce->tgc', d_up, w_up, preferred_element_type=jnp.float32)  4.17 us
    dot_general x1, matrix products, body(): jnp.einsum('tge,gce->tgc', d_gate, w_gate, preferred_element_type=jnp.flo...  3.9 us
    reduce_sum x3, other arithmetic, body(): jnp.sum(back_f * mates[section].astype(jnp.float32), axis=-1)  2.05 us
    dot_general x1, matrix products, body(): jnp.einsum('tgc,gce->tge', normed, w_gate, preferred_element_type=jnp.flo...  1.89 us
    add x3, other arithmetic, hid_sum(): total = total + lax.ppermute(value, 'hid', pairs)  1.81 us
    dot_general x1, matrix products, body(): jnp.einsum('tgc,gec->tge', cotangent.reshape(tok, groups_here, cblock), w...  1.74 us
  transfers between devices with their start and end apart: 11, of which 8 were waited for; matrix products, arithmetic and copies ran while one was open for 6% of the time, Pallas kernels for 0%

profile of v1, /device:TPU:0, one launch (start us, length us, event | category | flops | bytes accessed | tf_op | source)
XLA Modules:
  0.0 84.7 jit_solution(14390448984519494138)
XLA Ops:
  0.7 1.3 %convolution_convert_fusion = bf16[128,1024]{1,0:T(8,128)(2,1)S(1)} fusion(bf16[128,1024]{1,0:T(8,128)(2,1)} %param.9, bf16[1,128,128]{2,1,0:T(8,128)(2,1)} %param.11), kind=kOutput, calls=%fused_computation.18 | convolution fusion | flops 33685504 | bytes 557056 | tf_op jit(solution)/shard_map/kij,kjd->kid/dot_general | solution.py:32
  2.0 3.0 %collective-permute-start = (bf16[128,1024]{1,0:T(8,128)(2,1)S(1)}, bf16[128,1024]{1,0:T(8,128)(2,1)S(1)}, u32[]{:S(2)}, u32[]{:S(2)}) collective-permute-start(bf16[128,1024]{1,0:T(8,128)(2,1)S(1)} %convolution_convert_fusion), channel_id=1, source_target_pairs={{0,2},{2,0},{4,6},{6,4},{8,10},{10,8},{12,14},{14,12},{1,3},{3,1},... | collective-permute-start | bytes 786440 | tf_op jit(solution)/shard_map/ppermute | solution.py:12
  5.0 0.8 slice_bitcast_fusion
  5.8 5.5 %collective-permute-done = bf16[128,1024]{1,0:T(8,128)(2,1)S(1)} collective-permute-done((bf16[128,1024]{1,0:T(8,128)(2,1)S(1)}, bf16[128,1024]{1,0:T(8,128)(2,1)S(1)}, u32[]{:S(2)}, u32[]{:S(2)}) %collective-permute-start) | collective-permute-done | bytes 262176 | tf_op jit(solution)/shard_map/ppermute | solution.py:12
  11.3 0.2 fusion.16
  11.5 1.9 %collective-permute-start.1 = (bf16[128,1024]{1,0:T(8,128)(2,1)S(1)}, bf16[128,1024]{1,0:T(8,128)(2,1)S(1)}, u32[]{:S(2)}, u32[]{:S(2)}) collective-permute-start(bf16[128,1024]{1,0:T(8,128)(2,1)S(1)} %fusion.16), channel_id=1, source_target_pairs={{0,4},{2,6},{4,0},{6,2},{8,12},{10,14},{12,8},{14,10},{1,5},{3,7},... | collective-permute-start | bytes 786440 | tf_op jit(solution)/shard_map/ppermute | solution.py:12
  13.4 5.7 %collective-permute-done.1 = bf16[128,1024]{1,0:T(8,128)(2,1)S(1)} collective-permute-done((bf16[128,1024]{1,0:T(8,128)(2,1)S(1)}, bf16[128,1024]{1,0:T(8,128)(2,1)S(1)}, u32[]{:S(2)}, u32[]{:S(2)}) %collective-permute-start.1) | collective-permute-done | bytes 262176 | tf_op jit(solution)/shard_map/ppermute | solution.py:12
  19.1 0.7 copy-done.3
  19.9 2.6 %collective-permute-start.2 = (bf16[128,1024]{1,0:T(8,128)(2,1)S(1)}, bf16[128,1024]{1,0:T(8,128)(2,1)S(1)}, u32[]{:S(2)}, u32[]{:S(2)}) collective-permute-start(bf16[128,1024]{1,0:T(8,128)(2,1)S(1)} %fusion.18), channel_id=1, source_target_pairs={{0,8},{2,10},{4,12},{6,14},{8,0},{10,2},{12,4},{14,6},{1,9},{3,11}... | collective-permute-start | bytes 786440 | tf_op jit(solution)/shard_map/ppermute | solution.py:12
  22.5 10.6 %collective-permute-done.2 = bf16[128,1024]{1,0:T(8,128)(2,1)S(1)} collective-permute-done((bf16[128,1024]{1,0:T(8,128)(2,1)S(1)}, bf16[128,1024]{1,0:T(8,128)(2,1)S(1)}, u32[]{:S(2)}, u32[]{:S(2)}) %collective-permute-start.2) | collective-permute-done | bytes 262176 | tf_op jit(solution)/shard_map/ppermute | solution.py:12
  33.1 0.4 multiply_reduce_fusion.1
  33.5 1.7 %fusion.42 = f32[8,512,128]{2,1,0:T(8,128)} fusion(bf16[8,512,128]{2,1,0:T(8,128)(2,1)S(1)} %copy-done.2, bf16[128,1024]{1,0:T(8,128)(2,1)S(1)} %copy-done.5), kind=kOutput, calls=%fused_computation.73 | convolution fusion | flops 134217728 | bytes 3407872 | tf_op jit(solution)/shard_map/tgc,gec->tge/dot_general | solution.py:55
  35.3 1.9 %fusion.40 = f32[8,128,512]{1,2,0:T(8,128)} fusion(bf16[8,128,512]{2,1,0:T(8,128)(2,1)S(1)} %copy-done, bf16[128,1024]{1,0:T(8,128)(2,1)S(1)} %get-tuple-element.14, bf16[128,1024]{1,0:T(8,128)(2,1)S(1)} %copy-done.1, f32[1024]{0:T(1024)S(1)} %copy-done.7, f32[128]{0:T(128)S(1)} %add_rsqrt_fusion), kind=kOutput, calls=%fused_computation.71 | convolution fusion | flops 135135232 | bytes 3674624 | tf_op jit(solution)/shard_map/tgc,gce->tge/dot_general | solution.py:53
  37.2 3.9 %fusion.10 = f32[8,128,128]{1,2,0:T(8,128)S(1)} fusion(bf16[8,128,512]{2,1,0:T(8,128)(2,1)S(1)} %copy-done, f32[8,128,512]{1,2,0:T(8,128)} %fusion.40, f32[8,512,128]{2,1,0:T(8,128)} %fusion.42, bf16[8,128,512]{2,1,0:T(8,128)(2,1)} %param.16, bf16[128,1024]{1,0:T(8,128)(2,1)S(1)} %get-tuple-element.14, bf16[128,1024]{1,0:T(8,128)(2,1)S(1)} %copy-done.1, ...), kind=kOutput, calls=%fused_computation.16 | convolution fusion | flops 274595840 | bytes 7344640 | tf_op jit(solution)/shard_map/tge,gce->tgc/dot_general | solution.py:64
  41.1 4.2 %convolution_add_fusion = f32[8,128,128]{1,2,0:T(8,128)} fusion(f32[8,128,128]{1,2,0:T(8,128)S(1)} %fusion.10, bf16[8,128,512]{2,1,0:T(8,128)(2,1)} %param.16, f32[8,128,512]{1,2,0:T(8,128)} %fusion.40, f32[8,512,128]{2,1,0:T(8,128)} %fusion.42), kind=kOutput, calls=%fused_computation.13 | convolution fusion | flops 137494528 | bytes 6291456 | tf_op jit(solution)/shard_map/tge,gce->tgc/dot_general | solution.py:65
  45.3 1.2 %copy.24 = f32[128,1024]{1,0:T(8,128)S(1)} copy(f32[128,1024]{0,1:T(8,128)} %bitcast.102) | data formatting | bytes 1048576 | tf_op jit(solution)/shard_map/reshape | solution.py:66
  46.5 0.2 multiply_reduce_fusion
  46.7 0.5 collective-permute-start.4
  47.3 0.8 collective-permute-done.4
  48.1 1.4 %fusion.26 = (f32[128]{0:T(128)S(1)}, f32[128]{0:T(128)S(1)}, bf16[128,1024]{1,0:T(8,128)(2,1)S(1)}) fusion(bf16[128,1024]{1,0:T(8,128)(2,1)S(1)} %collective-permute-done.2, bf16[128,1024]{1,0:T(8,128)(2,1)S(1)} %fusion.18, f32[128]{0:T(128)S(1)} %fusion.51, bf16[128,1024]{1,0:T(8,128)(2,1)S(1)} %get-tuple-element.14, bf16[128,1024]{1,0:T(8,128)(2,1)S(1)} %copy-done.1, ...), kind=kLoop, calls=%fused_computation.54 | loop fusion | flops 2490112 | bytes 2103296 | tf_op jit(solution)/shard_map/reduce_sum | solution.py:80
  49.7 15.0 %collective-permute-done.5 = bf16[128,1024]{1,0:T(8,128)(2,1)S(1)} collective-permute-done((bf16[128,1024]{1,0:T(8,128)(2,1)S(1)}, bf16[128,1024]{1,0:T(8,128)(2,1)S(1)}, u32[]{:S(2)}, u32[]{:S(2)}) %collective-permute-start.5) | collective-permute-done | bytes 262176 | tf_op jit(solution)/shard_map/ppermute | solution.py:12
  64.7 0.3 fusion.31
  65.2 7.8 %collective-permute-done.6 = bf16[128,1024]{1,0:T(8,128)(2,1)S(1)} collective-permute-done((bf16[128,1024]{1,0:T(8,128)(2,1)S(1)}, bf16[128,1024]{1,0:T(8,128)(2,1)S(1)}, u32[]{:S(2)}, u32[]{:S(2)}) %collective-permute-start.6) | collective-permute-done | bytes 262176 | tf_op jit(solution)/shard_map/ppermute | solution.py:12
  73.1 0.3 fusion.36
  73.5 0.5 collective-permute-start.8
  74.2 1.1 %collective-permute-start.7 = (bf16[128,1024]{1,0:T(8,128)(2,1)S(1)}, bf16[128,1024]{1,0:T(8,128)(2,1)S(1)}, u32[]{:S(2)}, u32[]{:S(2)}) collective-permute-start(bf16[128,1024]{1,0:T(8,128)(2,1)S(1)} %fusion.34), channel_id=1, source_target_pairs={{0,2},{2,0},{4,6},{6,4},{8,10},{10,8},{12,14},{14,12},{1,3},{3,1},... | collective-permute-start | bytes 786440 | tf_op jit(solution)/shard_map/ppermute | solution.py:12
  75.2 0.6 fusion.54
  75.8 0.6 fusion.55
  76.4 6.1 %collective-permute-done.7 = bf16[128,1024]{1,0:T(8,128)(2,1)S(1)} collective-permute-done((bf16[128,1024]{1,0:T(8,128)(2,1)S(1)}, bf16[128,1024]{1,0:T(8,128)(2,1)S(1)}, u32[]{:S(2)}, u32[]{:S(2)}) %collective-permute-start.7) | collective-permute-done | bytes 262176 | tf_op jit(solution)/shard_map/ppermute | solution.py:12
  82.5 0.3 convolution_bitcast_fusion.1
  82.9 1.1 %fusion.11 = bf16[128,1024]{1,0:T(8,128)(2,1)} fusion(bf16[128,1024]{1,0:T(8,128)(2,1)S(1)} %get-tuple-element.14, bf16[1,128,128]{2,1,0:T(8,128)(2,1)S(1)} %copy-done.8, bf16[128,1024]{1,0:T(8,128)(2,1)S(1)} %get-tuple-element.10, bf16[128,1024]{1,0:T(8,128)(2,1)S(1)} %collective-permute-done.7, f32[128]{0:T(128)S(1)} %get-tuple-element.22, ...), kind=kOutput, calls=%fused_computation.17 | convolution fusion | flops 36044800 | bytes 2135552 | tf_op jit(solution)/shard_map/kij,kid->kjd/dot_general | solution.py:92
  84.1 0.6 add.87
  (34 shorter events, 1.0 us)
Async XLA Ops:
  0.6 34.6 %copy-start = (bf16[8,128,512]{2,1,0:T(8,128)(2,1)S(1)}, bf16[8,128,512]{2,1,0:T(8,128)(2,1)}, u32[]{:S(2)}) copy-start(bf16[8,128,512]{2,1,0:T(8,128)(2,1)} %param.15) | copy-start | bytes 3145732
  0.6 32.4 %copy-start.1 = (bf16[128,1024]{1,0:T(8,128)(2,1)S(1)}, bf16[128,1024]{1,0:T(8,128)(2,1)}, u32[]{:S(2)}) copy-start(bf16[128,1024]{1,0:T(8,128)(2,1)} %param.9) | copy-start | bytes 786436
  0.7 32.9 %copy-start.5 = (bf16[128,1024]{1,0:T(8,128)(2,1)S(1)}, bf16[128,1024]{1,0:T(8,128)(2,1)}, u32[]{:S(2)}) copy-start(bf16[128,1024]{1,0:T(8,128)(2,1)} %param.10) | copy-start | bytes 786436
  0.7 32.9 %copy-start.2 = (bf16[8,512,128]{2,1,0:T(8,128)(2,1)S(1)}, bf16[8,512,128]{2,1,0:T(8,128)(2,1)}, u32[]{:S(2)}) copy-start(bf16[8,512,128]{2,1,0:T(8,128)(2,1)} %param.17) | copy-start | bytes 3145732
  2.0 9.3 %collective-permute-start = (bf16[128,1024]{1,0:T(8,128)(2,1)S(1)}, bf16[128,1024]{1,0:T(8,128)(2,1)S(1)}, u32[]{:S(2)}, u32[]{:S(2)}) collective-permute-start(bf16[128,1024]{1,0:T(8,128)(2,1)S(1)} %convolution_convert_fusion), channel_id=1, source_target_pairs={{0,2},{2,0},{4,6},{6,4},{8,10},{10,8},{12,14},{14,12},{1,3},{3,1},... | collective-permute-start | bytes 786440 | tf_op jit(solution)/shard_map/ppermute | solution.py:12
  11.5 7.6 %collective-permute-start.1 = (bf16[128,1024]{1,0:T(8,128)(2,1)S(1)}, bf16[128,1024]{1,0:T(8,128)(2,1)S(1)}, u32[]{:S(2)}, u32[]{:S(2)}) collective-permute-start(bf16[128,1024]{1,0:T(8,128)(2,1)S(1)} %fusion.16), channel_id=1, source_target_pairs={{0,4},{2,6},{4,0},{6,2},{8,12},{10,14},{12,8},{14,10},{1,5},{3,7},... | collective-permute-start | bytes 786440 | tf_op jit(solution)/shard_map/ppermute | solution.py:12
  19.1 0.7 copy-start.3
  19.9 13.2 %collective-permute-start.2 = (bf16[128,1024]{1,0:T(8,128)(2,1)S(1)}, bf16[128,1024]{1,0:T(8,128)(2,1)S(1)}, u32[]{:S(2)}, u32[]{:S(2)}) collective-permute-start(bf16[128,1024]{1,0:T(8,128)(2,1)S(1)} %fusion.18), channel_id=1, source_target_pairs={{0,8},{2,10},{4,12},{6,14},{8,0},{10,2},{12,4},{14,6},{1,9},{3,11}... | collective-permute-start | bytes 786440 | tf_op jit(solution)/shard_map/ppermute | solution.py:12
  33.1 2.2 %copy-start.7 = (f32[1024]{0:T(1024)S(1)}, f32[1024]{0:T(1024)}, u32[]{:S(2)}) copy-start(f32[1024]{0:T(1024)} %param.14) | copy-start | bytes 12292
  33.4 1.8 %collective-permute-start.3 = (f32[128]{0:T(128)S(1)}, f32[128]{0:T(128)S(1)}, u32[]{:S(2)}, u32[]{:S(2)}) collective-permute-start(f32[128]{0:T(128)S(1)} %get-tuple-element.13), channel_id=1, source_target_pairs={{0,1},{1,0},{2,3},{3,2},{4,5},{5,4},{6,7},{7,6},{8,9},{9,8},{10,11... | collective-permute-start | bytes 1544 | tf_op jit(solution)/shard_map/ppermute | solution.py:20
  46.5 18.2 %copy-start.4 = (bf16[128,1024]{1,0:T(8,128)(2,1)S(1)}, bf16[128,1024]{1,0:T(8,128)(2,1)}, u32[]{:S(2)}) copy-start(bf16[128,1024]{1,0:T(8,128)(2,1)} %copy-done.3) | copy-start | bytes 786436
  46.7 1.4 %collective-permute-start.4 = (f32[128]{0:T(128)S(1)}, f32[128]{0:T(128)S(1)}, u32[]{:S(2)}, u32[]{:S(2)}) collective-permute-start(f32[128]{0:T(128)S(1)} %multiply_reduce_fusion), channel_id=1, source_target_pairs={{0,1},{1,0},{2,3},{3,2},{4,5},{5,4},{6,7},{7,6},{8,9},{9,8},{10,11... | collective-permute-start | bytes 1544 | tf_op jit(solution)/shard_map/ppermute | solution.py:20
  49.6 33.2 %copy-start.6 = (bf16[128,1024]{1,0:T(8,128)(2,1)S(1)}, bf16[128,1024]{1,0:T(8,128)(2,1)}, u32[]{:S(2)}) copy-start(bf16[128,1024]{1,0:T(8,128)(2,1)} %param.10) | copy-start | bytes 786436
  49.6 33.2 %copy-start.8 = (bf16[1,128,128]{2,1,0:T(8,128)(2,1)S(1)}, bf16[1,128,128]{2,1,0:T(8,128)(2,1)}, u32[]{:S(2)}) copy-start(bf16[1,128,128]{2,1,0:T(8,128)(2,1)} %param.11) | copy-start | bytes 98308
  49.6 15.1 %collective-permute-start.5 = (bf16[128,1024]{1,0:T(8,128)(2,1)S(1)}, bf16[128,1024]{1,0:T(8,128)(2,1)S(1)}, u32[]{:S(2)}, u32[]{:S(2)}) collective-permute-start(bf16[128,1024]{1,0:T(8,128)(2,1)S(1)} %fusion.24), channel_id=1, source_target_pairs={{0,8},{2,10},{4,12},{6,14},{8,0},{10,2},{12,4},{14,6},{1,9},{3,11}... | collective-permute-start | bytes 786440 | tf_op jit(solution)/shard_map/ppermute | solution.py:12
  65.2 7.9 %collective-permute-start.6 = (bf16[128,1024]{1,0:T(8,128)(2,1)S(1)}, bf16[128,1024]{1,0:T(8,128)(2,1)S(1)}, u32[]{:S(2)}, u32[]{:S(2)}) collective-permute-start(bf16[128,1024]{1,0:T(8,128)(2,1)S(1)} %fusion.29), channel_id=1, source_target_pairs={{0,4},{2,6},{4,0},{6,2},{8,12},{10,14},{12,8},{14,10},{1,5},{3,7},... | collective-permute-start | bytes 786440 | tf_op jit(solution)/shard_map/ppermute | solution.py:12
  73.4 1.8 %collective-permute-start.9 = (f32[3,128]{1,0:T(4,128)S(1)}, f32[3,128]{1,0:T(4,128)S(1)}, u32[]{:S(2)}, u32[]{:S(2)}) collective-permute-start(f32[3,128]{1,0:T(4,128)S(1)} %pad_maximum_fusion.1), channel_id=1, source_target_pairs={{0,1},{1,0},{2,3},{3,2},{4,5},{5,4},{6,7},{7,6},{8,9},{9,8},{10,11... | collective-permute-start | bytes 4616 | tf_op jit(solution)/shard_map/ppermute | solution.py:20
  73.5 2.3 %collective-permute-start.8 = (f32[3,128]{1,0:T(4,128)S(1)}, f32[3,128]{1,0:T(4,128)S(1)}, u32[]{:S(2)}, u32[]{:S(2)}) collective-permute-start(f32[3,128]{1,0:T(4,128)S(1)} %pad_maximum_fusion), channel_id=1, source_target_pairs={{0,1},{1,0},{2,3},{3,2},{4,5},{5,4},{6,7},{7,6},{8,9},{9,8},{10,11... | collective-permute-start | bytes 4616 | tf_op jit(solution)/shard_map/ppermute | solution.py:20
  74.2 8.3 %collective-permute-start.7 = (bf16[128,1024]{1,0:T(8,128)(2,1)S(1)}, bf16[128,1024]{1,0:T(8,128)(2,1)S(1)}, u32[]{:S(2)}, u32[]{:S(2)}) collective-permute-start(bf16[128,1024]{1,0:T(8,128)(2,1)S(1)} %fusion.34), channel_id=1, source_target_pairs={{0,2},{2,0},{4,6},{6,4},{8,10},{10,8},{12,14},{14,12},{1,3},{3,1},... | collective-permute-start | bytes 786440 | tf_op jit(solution)/shard_map/ppermute | solution.py:12
  82.8 1.3 %collective-permute-start.10 = (f32[1,128,128]{2,1,0:T(8,128)S(1)}, f32[1,128,128]{2,1,0:T(8,128)S(1)}, u32[]{:S(2)}, u32[]{:S(2)}) collective-permute-start(f32[1,128,128]{2,1,0:T(8,128)S(1)} %convolution_bitcast_fusion.1), channel_id=1, source_target_pairs={{0,1},{1,0},{2,3},{3,2},{4,5},{5,4},{6,7},{7,6},{8,9},{9,8},{10,11... | collective-permute-start | bytes 196616 | tf_op jit(solution)/shard_map/ppermute | solution.py:20

commit v2 on v1

--- a/solution.py
+++ b/solution.py
@@ -4,6 +4,7 @@
 from jax.sharding import PartitionSpec as P
 
 D = 2048
+CHUNKS = 2
 
 
 def from_partner(value, axis, distance):
@@ -21,16 +22,11 @@
     return total
 
 
-def body(tokens, cotangent, blocks, coef_self, coef_cross, norm_gain, w_gate, w_up, w_down):
+def chain(local, tokens, cotangent, coef_self, coef_cross, norm_gain, w_gate, w_up, w_down):
     tok, width = tokens.shape
-    sections = lax.axis_size("seq").bit_length() - 1
-    nblk = blocks.shape[0]
-    blen = blocks.shape[1]
+    sections = coef_self.shape[0]
     groups_here = w_gate.shape[0]
     cblock = w_gate.shape[1]
-    tok_blocks = tokens.reshape(nblk, blen, width)
-    local = jnp.einsum("kij,kjd->kid", blocks, tok_blocks, preferred_element_type=jnp.float32)
-    local = local.astype(jnp.bfloat16).reshape(tok, width)
     states = []
     mates = []
     current = local
@@ -83,8 +79,32 @@
         back = (coef_self[section][:, None] * back_f + received.astype(jnp.float32)).astype(
             jnp.bfloat16
         )
-    part_self = jnp.stack(grads_self)
-    part_cross = jnp.stack(grads_cross)
+    direct = d_resid * (1.0 + mixed_f)
+    return back, direct, jnp.stack(grads_self), jnp.stack(grads_cross)
+
+
+def body(tokens, cotangent, blocks, coef_self, coef_cross, norm_gain, w_gate, w_up, w_down):
+    tok, width = tokens.shape
+    nblk = blocks.shape[0]
+    blen = blocks.shape[1]
+    tok_blocks = tokens.reshape(nblk, blen, width)
+    local = jnp.einsum("kij,kjd->kid", blocks, tok_blocks, preferred_element_type=jnp.float32)
+    local = local.astype(jnp.bfloat16).reshape(tok, width)
+    chunks = CHUNKS if tok % CHUNKS == 0 else 1
+    rows = tok // chunks
+    results = []
+    for chunk in range(chunks):
+        rs = slice(chunk * rows, (chunk + 1) * rows)
+        results.append(
+            chain(
+                local[rs], tokens[rs], cotangent[rs], coef_self[:, rs], coef_cross[:, rs],
+                norm_gain, w_gate, w_up, w_down,
+            )
+        )
+    back = jnp.concatenate([r[0] for r in results], axis=0)
+    direct = jnp.concatenate([r[1] for r in results], axis=0)
+    part_self = jnp.concatenate([r[2] for r in results], axis=1)
+    part_cross = jnp.concatenate([r[3] for r in results], axis=1)
     back_blocks = back.reshape(nblk, blen, width)
     part_blocks = jnp.einsum(
         "kid,kjd->kij", back_blocks, tok_blocks, preferred_element_type=jnp.float32
@@ -93,7 +113,7 @@
         "kij,kid->kjd", blocks, back_blocks, preferred_element_type=jnp.float32
     ).reshape(tok, width)
     grad_self, grad_cross, grad_blocks = jax.tree.map(hid_sum, (part_self, part_cross, part_blocks))
-    grad_x = (d_resid * (1.0 + mixed_f) + from_blocks).astype(jnp.bfloat16)
+    grad_x = (direct + from_blocks).astype(jnp.bfloat16)
     return (grad_x, grad_self, grad_cross, grad_blocks)
 
 

time: 85 us -> 80.6 us (0.948)
  waiting for transfers between devices: 51.6 us -> 36.2 us
  starting transfers between devices: 9.97 us -> 17.4 us
  local copies, waits for them, and re-layouts: 2.79 us -> 7.23 us
  matrix products: 14.4 us -> 12.8 us
    ppermute x6 -> x12, waiting for transfers between devices: 50.6 us -> 34.2 us  [from_partner(): return lax.ppermute(value, axis, pairs)]
    ppermute x6 -> x12, starting transfers between devices: 8.67 us -> 15.6 us  [from_partner(): return lax.ppermute(value, axis, pairs)]
    unnamed x18 -> x87, local copies, waits for them, and re-layouts: 0.75 us -> 7.13 us
    dot_general x4 -> x8, matrix products: 11.7 us -> 10.3 us  [the longest x2 5.53 us: chain(): jnp.einsum('tge,gce->tgc', d_gate, w_gate, preferred_element_type=jnp.flo...]
    reshape x1 -> x0, local copies, waits for them, and re-layouts: 1.24 us -> none  [body(): scaled = norm_gain * d_normed.reshape(tok, width)]
    ppermute x5 -> x7, waiting for transfers between devices: 0.91 us -> 1.99 us  [hid_sum(): total = total + lax.ppermute(value, 'hid', pairs)]
    reduce_sum x5 -> x7, other arithmetic: 2.61 us -> 2.14 us  [the longest x4 1.13 us: chain(): jnp.sum(back_f * mates[section].astype(jnp.float32), axis=-1)]
    ppermute x5 -> x7, starting transfers between devices: 1.3 us -> 1.73 us  [hid_sum(): total = total + lax.ppermute(value, 'hid', pairs)]
  transfers between devices with their start and end apart: 11 -> 19, of which waited for: 8 -> 14; matrix products, arithmetic and copies ran while one was open for 6% -> 8% of each run, Pallas kernels for 0% -> 0%
where the time goes in v2:
time: 80.6 us; the launch traced here: 80.3 us
  waiting for transfers between devices  36.2 us (45%)
  starting transfers between devices  17.4 us (22%)
  matrix products  12.8 us (16%)
  local copies, waits for them, and re-layouts  7.23 us (9%)
  other arithmetic  5.54 us (7%)
  between operations  1.09 us (1%)
    ppermute x12, waiting for transfers between devices, from_partner(): return lax.ppermute(value, axis, pairs)  34.2 us
    ppermute x12, starting transfers between devices, from_partner(): return lax.ppermute(value, axis, pairs)  15.6 us
    unnamed x87, local copies, waits for them, and re-layouts  7.13 us
    dot_general x2, matrix products, chain(): jnp.einsum('tge,gce->tgc', d_gate, w_gate, preferred_element_type=jnp.flo...  5.53 us
    dot_general x2, matrix products, chain(): jnp.einsum('tge,gce->tgc', d_up, w_up, preferred_element_type=jnp.float32)  2.25 us
    ppermute x7, waiting for transfers between devices, hid_sum(): total = total + lax.ppermute(value, 'hid', pairs)  1.99 us
    dot_general x2, matrix products, chain(): jnp.einsum('tgc,gec->tge', cotangent.reshape(tok, groups_here, cblock), w...  1.97 us
    add x3, other arithmetic, hid_sum(): total = total + lax.ppermute(value, 'hid', pairs)  1.95 us
  transfers between devices with their start and end apart: 19, of which 14 were waited for; matrix products, arithmetic and copies ran while one was open for 8% of the time, Pallas kernels for 0%

profile of v2, /device:TPU:0, one launch (start us, length us, event | category | flops | bytes accessed | tf_op | source)
XLA Modules:
  0.0 80.3 jit_solution(2462346340504996268)
XLA Ops:
  0.6 1.3 %fusion.14 = bf16[1,128,1024]{2,1,0:T(8,128)(2,1)S(1)} fusion(bf16[128,1024]{1,0:T(8,128)(2,1)} %param.9, bf16[1,128,128]{2,1,0:T(8,128)(2,1)} %param.11), kind=kOutput, calls=%fused_computation.22 | convolution fusion | flops 33685504 | bytes 557056 | tf_op jit(solution)/shard_map/kij,kjd->kid/dot_general | solution.py:91
  2.0 3.0 %collective-permute-start = (bf16[64,1024]{1,0:T(8,128)(2,1)S(1)}, bf16[64,1024]{1,0:T(8,128)(2,1)S(1)}, u32[]{:S(2)}, u32[]{:S(2)}) collective-permute-start(bf16[64,1024]{1,0:T(8,128)(2,1)S(1)} %get-tuple-element.37), channel_id=1, source_target_pairs={{0,2},{2,0},{4,6},{6,4},{8,10},{10,8},{12,14},{14,12},{1,3},{3,1},... | collective-permute-start | bytes 393224 | tf_op jit(solution)/shard_map/ppermute | solution.py:13
  5.2 4.1 %collective-permute-done = bf16[64,1024]{1,0:T(8,128)(2,1)S(1)} collective-permute-done((bf16[64,1024]{1,0:T(8,128)(2,1)S(1)}, bf16[64,1024]{1,0:T(8,128)(2,1)S(1)}, u32[]{:S(2)}, u32[]{:S(2)}) %collective-permute-start) | collective-permute-done | bytes 131104 | tf_op jit(solution)/shard_map/ppermute | solution.py:13
  9.3 2.0 %collective-permute-done.5 = bf16[64,1024]{1,0:T(8,128)(2,1)S(1)} collective-permute-done((bf16[64,1024]{1,0:T(8,128)(2,1)S(1)}, bf16[64,1024]{1,0:T(8,128)(2,1)S(1)}, u32[]{:S(2)}, u32[]{:S(2)}) %collective-permute-start.5) | collective-permute-done | bytes 131104 | tf_op jit(solution)/shard_map/ppermute | solution.py:13
  11.9 1.8 %collective-permute-start.1 = (bf16[64,1024]{1,0:T(8,128)(2,1)S(1)}, bf16[64,1024]{1,0:T(8,128)(2,1)S(1)}, u32[]{:S(2)}, u32[]{:S(2)}) collective-permute-start(bf16[64,1024]{1,0:T(8,128)(2,1)S(1)} %get-tuple-element.35), channel_id=1, source_target_pairs={{0,4},{2,6},{4,0},{6,2},{8,12},{10,14},{12,8},{14,10},{1,5},{3,7},... | collective-permute-start | bytes 393224 | tf_op jit(solution)/shard_map/ppermute | solution.py:13
  14.1 4.0 %collective-permute-done.1 = bf16[64,1024]{1,0:T(8,128)(2,1)S(1)} collective-permute-done((bf16[64,1024]{1,0:T(8,128)(2,1)S(1)}, bf16[64,1024]{1,0:T(8,128)(2,1)S(1)}, u32[]{:S(2)}, u32[]{:S(2)}) %collective-permute-start.1) | collective-permute-done | bytes 131104 | tf_op jit(solution)/shard_map/ppermute | solution.py:13
  18.7 2.5 %collective-permute-start.2 = (bf16[64,1024]{1,0:T(8,128)(2,1)S(1)}, bf16[64,1024]{1,0:T(8,128)(2,1)S(1)}, u32[]{:S(2)}, u32[]{:S(2)}) collective-permute-start(bf16[64,1024]{1,0:T(8,128)(2,1)S(1)} %fusion.31), channel_id=1, source_target_pairs={{0,8},{2,10},{4,12},{6,14},{8,0},{10,2},{12,4},{14,6},{1,9},{3,11}... | collective-permute-start | bytes 393224 | tf_op jit(solution)/shard_map/ppermute | solution.py:13
  21.9 1.9 %collective-permute-start.7 = (bf16[64,1024]{1,0:T(8,128)(2,1)S(1)}, bf16[64,1024]{1,0:T(8,128)(2,1)S(1)}, u32[]{:S(2)}, u32[]{:S(2)}) collective-permute-start(bf16[64,1024]{1,0:T(8,128)(2,1)S(1)} %fusion.39), channel_id=1, source_target_pairs={{0,8},{2,10},{4,12},{6,14},{8,0},{10,2},{12,4},{14,6},{1,9},{3,11}... | collective-permute-start | bytes 393224 | tf_op jit(solution)/shard_map/ppermute | solution.py:13
  24.3 5.3 %collective-permute-done.2 = bf16[64,1024]{1,0:T(8,128)(2,1)S(1)} collective-permute-done((bf16[64,1024]{1,0:T(8,128)(2,1)S(1)}, bf16[64,1024]{1,0:T(8,128)(2,1)S(1)}, u32[]{:S(2)}, u32[]{:S(2)}) %collective-permute-start.2) | collective-permute-done | bytes 131104 | tf_op jit(solution)/shard_map/ppermute | solution.py:13
  29.6 1.4 %collective-permute-done.7 = bf16[64,1024]{1,0:T(8,128)(2,1)S(1)} collective-permute-done((bf16[64,1024]{1,0:T(8,128)(2,1)S(1)}, bf16[64,1024]{1,0:T(8,128)(2,1)S(1)}, u32[]{:S(2)}, u32[]{:S(2)}) %collective-permute-start.7) | collective-permute-done | bytes 131104 | tf_op jit(solution)/shard_map/ppermute | solution.py:13
  31.4 1.5 %convolution_bitcast_fusion.5 = f32[64,8,512]{2,0,1:T(8,128)} fusion(bf16[8,512,128]{2,1,0:T(8,128)(2,1)S(1)} %copy-done.2, bf16[8,8,8,128]{3,2,1,0:T(8,128)(2,1)S(1)} %get-tuple-element.33), kind=kOutput, calls=%fused_computation.9 | convolution fusion | flops 67108864 | bytes 2228224 | tf_op jit(solution)/shard_map/tgc,gec->tge/dot_general | solution.py:51
  33.5 0.8 %collective-permute-done.8 = f32[64]{0:T(128)S(1)} collective-permute-done((f32[64]{0:T(128)S(1)}, f32[64]{0:T(128)S(1)}, u32[]{:S(2)}, u32[]{:S(2)}) %collective-permute-start.8) | collective-permute-done | bytes 288 | tf_op jit(solution)/shard_map/ppermute | solution.py:21
  35.3 1.0 %copy-done.6 = f32[64,8,512]{2,0,1:T(8,128)} copy-done((f32[64,8,512]{2,0,1:T(8,128)}, f32[64,8,512]{2,0,1:T(8,128)S(1)}, u32[]{:S(2)}) %copy-start.6) | copy-done | bytes 1048600
  36.3 1.1 %fusion.26 = f32[8,64,128]{2,1,0:T(8,128)} fusion(bf16[8,128,512]{2,1,0:T(8,128)(2,1)S(1)} %copy-done.41, f32[64,8,512]{2,0,1:T(8,128)S(1)} %convolution_bitcast_fusion.2, f32[64,8,512]{2,0,1:T(8,128)S(1)} %convolution_bitcast_fusion), kind=kOutput, calls=%fused_computation.39 | convolution fusion | flops 68681728 | bytes 3407872 | tf_op jit(solution)/shard_map/tge,gce->tgc/dot_general | solution.py:61
  37.4 2.7 %fusion.16 = f32[8,8,8,128]{3,2,1,0:T(8,128)S(1)} fusion(f32[8,64,128]{2,1,0:T(8,128)} %fusion.26, bf16[8,128,512]{2,1,0:T(8,128)(2,1)S(1)} %copy-done, f32[64,8,512]{2,0,1:T(8,128)} %copy-done.4, bf16[8,128,512]{2,1,0:T(8,128)(2,1)} %param.16, f32[64,8,512]{2,0,1:T(8,128)} %copy-done.6, bf16[8,8,8,128]{3,2,1,0:T(8,128)(2,1)S(1)} %get-tuple-element.30), kind=kOutput, calls=%fused_computation.24 | convolution fusion | flops 136904704 | bytes 4849664 | tf_op jit(solution)/shard_map/tge,gce->tgc/dot_general | solution.py:60
  40.5 1.0 %copy-done.7 = f32[64,8,512]{2,0,1:T(8,128)} copy-done((f32[64,8,512]{2,0,1:T(8,128)}, f32[64,8,512]{2,0,1:T(8,128)S(1)}, u32[]{:S(2)}) %copy-start.7) | copy-done | bytes 1048600
  42.1 1.1 %fusion.25 = f32[8,64,128]{2,1,0:T(8,128)} fusion(bf16[8,128,512]{2,1,0:T(8,128)(2,1)S(1)} %copy-done.42, f32[64,8,512]{2,0,1:T(8,128)S(1)} %copy-done.5, f32[64,8,512]{2,0,1:T(8,128)S(1)} %convolution_bitcast_fusion.3), kind=kOutput, calls=%fused_computation.38 | convolution fusion | flops 68681728 | bytes 3407872 | tf_op jit(solution)/shard_map/tge,gce->tgc/dot_general | solution.py:61
  43.2 2.8 %fusion.15 = f32[8,8,8,128]{3,2,1,0:T(8,128)S(1)} fusion(f32[8,64,128]{2,1,0:T(8,128)} %fusion.25, bf16[8,128,512]{2,1,0:T(8,128)(2,1)S(1)} %copy-done, f32[64,8,512]{2,0,1:T(8,128)} %convolution_bitcast_fusion.5, bf16[8,128,512]{2,1,0:T(8,128)(2,1)} %param.16, f32[64,8,512]{2,0,1:T(8,128)} %copy-done.7, bf16[8,8,8,128]{3,2,1,0:T(8,128)(2,1)} %copy-done.14), kind=kOutput, calls=%fused_computation.23 | convolution fusion | flops 136904704 | bytes 4849664 | tf_op jit(solution)/shard_map/tge,gce->tgc/dot_general | solution.py:60
  48.4 3.0 %collective-permute-start.10 = (bf16[64,1024]{1,0:T(8,128)(2,1)S(1)}, bf16[64,1024]{1,0:T(8,128)(2,1)S(1)}, u32[]{:S(2)}, u32[]{:S(2)}) collective-permute-start(bf16[64,1024]{1,0:T(8,128)(2,1)S(1)} %fusion.45), channel_id=1, source_target_pairs={{0,8},{2,10},{4,12},{6,14},{8,0},{10,2},{12,4},{14,6},{1,9},{3,11}... | collective-permute-start | bytes 393224 | tf_op jit(solution)/shard_map/ppermute | solution.py:13
  51.3 9.2 %collective-permute-done.13 = bf16[64,1024]{1,0:T(8,128)(2,1)S(1)} collective-permute-done((bf16[64,1024]{1,0:T(8,128)(2,1)S(1)}, bf16[64,1024]{1,0:T(8,128)(2,1)S(1)}, u32[]{:S(2)}, u32[]{:S(2)}) %collective-permute-start.13) | collective-permute-done | bytes 131104 | tf_op jit(solution)/shard_map/ppermute | solution.py:13
  61.6 1.4 %collective-permute-done.10 = bf16[64,1024]{1,0:T(8,128)(2,1)S(1)} collective-permute-done((bf16[64,1024]{1,0:T(8,128)(2,1)S(1)}, bf16[64,1024]{1,0:T(8,128)(2,1)S(1)}, u32[]{:S(2)}, u32[]{:S(2)}) %collective-permute-start.10) | collective-permute-done | bytes 131104 | tf_op jit(solution)/shard_map/ppermute | solution.py:13
  63.2 0.6 copy-done.36
  64.0 0.7 collective-permute-start.11
  64.7 2.0 %collective-permute-done.14 = bf16[64,1024]{1,0:T(8,128)(2,1)S(1)} collective-permute-done((bf16[64,1024]{1,0:T(8,128)(2,1)S(1)}, bf16[64,1024]{1,0:T(8,128)(2,1)S(1)}, u32[]{:S(2)}, u32[]{:S(2)}) %collective-permute-start.14) | collective-permute-done | bytes 131104 | tf_op jit(solution)/shard_map/ppermute | solution.py:13
  66.6 2.7 %collective-permute-done.11 = bf16[64,1024]{1,0:T(8,128)(2,1)S(1)} collective-permute-done((bf16[64,1024]{1,0:T(8,128)(2,1)S(1)}, bf16[64,1024]{1,0:T(8,128)(2,1)S(1)}, u32[]{:S(2)}, u32[]{:S(2)}) %collective-permute-start.11) | collective-permute-done | bytes 131104 | tf_op jit(solution)/shard_map/ppermute | solution.py:13
  70.5 1.6 %collective-permute-start.12 = (bf16[64,1024]{1,0:T(8,128)(2,1)S(1)}, bf16[64,1024]{1,0:T(8,128)(2,1)S(1)}, u32[]{:S(2)}, u32[]{:S(2)}) collective-permute-start(bf16[64,1024]{1,0:T(8,128)(2,1)S(1)} %fusion.55), channel_id=1, source_target_pairs={{0,2},{2,0},{4,6},{6,4},{8,10},{10,8},{12,14},{14,12},{1,3},{3,1},... | collective-permute-start | bytes 393224 | tf_op jit(solution)/shard_map/ppermute | solution.py:13
  72.1 0.7 collective-permute-start.15
  74.0 0.7 fusion.123
  74.7 0.7 fusion.124
  75.3 1.0 %collective-permute-done.12 = bf16[64,1024]{1,0:T(8,128)(2,1)S(1)} collective-permute-done((bf16[64,1024]{1,0:T(8,128)(2,1)S(1)}, bf16[64,1024]{1,0:T(8,128)(2,1)S(1)}, u32[]{:S(2)}, u32[]{:S(2)}) %collective-permute-start.12) | collective-permute-done | bytes 131104 | tf_op jit(solution)/shard_map/ppermute | solution.py:13
  76.5 1.3 %collective-permute-done.15 = bf16[64,1024]{1,0:T(8,128)(2,1)S(1)} collective-permute-done((bf16[64,1024]{1,0:T(8,128)(2,1)S(1)}, bf16[64,1024]{1,0:T(8,128)(2,1)S(1)}, u32[]{:S(2)}, u32[]{:S(2)}) %collective-permute-start.15) | collective-permute-done | bytes 131104 | tf_op jit(solution)/shard_map/ppermute | solution.py:13
  78.6 1.0 %fusion.11 = bf16[128,1024]{1,0:T(8,128)(2,1)} fusion(f32[64,1024]{1,0:T(8,128)S(1)} %get-tuple-element.28, f32[64,1024]{1,0:T(8,128)S(1)} %get-tuple-element.29, bf16[64,1024]{1,0:T(8,128)(2,1)S(1)} %fusion.69, bf16[64,1024]{1,0:T(8,128)(2,1)S(1)} %fusion.54, bf16[1,128,128]{2,1,0:T(8,128)(2,1)S(1)} %copy-done.15), kind=kOutput, calls=%fused_computation.18 | convolution fusion | flops 34471936 | bytes 1081344 | tf_op jit(solution)/shard_map/kij,kid->kjd/dot_general | solution.py:112
  (134 shorter events, 13.6 us)
Async XLA Ops:
  0.6 34.3 %copy-start = (bf16[8,128,512]{2,1,0:T(8,128)(2,1)S(1)}, bf16[8,128,512]{2,1,0:T(8,128)(2,1)}, u32[]{:S(2)}) copy-start(bf16[8,128,512]{2,1,0:T(8,128)(2,1)} %param.15) | copy-start | bytes 3145732
  2.0 7.3 %collective-permute-start = (bf16[64,1024]{1,0:T(8,128)(2,1)S(1)}, bf16[64,1024]{1,0:T(8,128)(2,1)S(1)}, u32[]{:S(2)}, u32[]{:S(2)}) collective-permute-start(bf16[64,1024]{1,0:T(8,128)(2,1)S(1)} %get-tuple-element.37), channel_id=1, source_target_pairs={{0,2},{2,0},{4,6},{6,4},{8,10},{10,8},{12,14},{14,12},{1,3},{3,1},... | collective-permute-start | bytes 393224 | tf_op jit(solution)/shard_map/ppermute | solution.py:13
  5.0 6.3 %collective-permute-start.5 = (bf16[64,1024]{1,0:T(8,128)(2,1)S(1)}, bf16[64,1024]{1,0:T(8,128)(2,1)S(1)}, u32[]{:S(2)}, u32[]{:S(2)}) collective-permute-start(bf16[64,1024]{1,0:T(8,128)(2,1)S(1)} %get-tuple-element.36), channel_id=1, source_target_pairs={{0,2},{2,0},{4,6},{6,4},{8,10},{10,8},{12,14},{14,12},{1,3},{3,1},... | collective-permute-start | bytes 393224 | tf_op jit(solution)/shard_map/ppermute | solution.py:13
  5.1 8.7 %copy-start.3 = (bf16[128,1024]{1,0:T(8,128)(2,1)S(1)}, bf16[128,1024]{1,0:T(8,128)(2,1)}, u32[]{:S(2)}) copy-start(bf16[128,1024]{1,0:T(8,128)(2,1)} %param.10) | copy-start | bytes 786436
  5.2 12.9 %copy-start.33 = (f32[64]{0:T(128)}, f32[64]{0:T(128)S(1)}, u32[]{:S(2)}) copy-start(f32[64]{0:T(128)S(1)} %get-tuple-element.53) | copy-start | bytes 772
  5.2 12.9 %copy-start.35 = (f32[64]{0:T(128)}, f32[64]{0:T(128)S(1)}, u32[]{:S(2)}) copy-start(f32[64]{0:T(128)S(1)} %get-tuple-element.47) | copy-start | bytes 772
  5.2 16.0 %copy-start.31 = (f32[64]{0:T(128)}, f32[64]{0:T(128)S(1)}, u32[]{:S(2)}) copy-start(f32[64]{0:T(128)S(1)} %get-tuple-element.50) | copy-start | bytes 772
  5.2 16.0 %copy-start.37 = (f32[64]{0:T(128)}, f32[64]{0:T(128)S(1)}, u32[]{:S(2)}) copy-start(f32[64]{0:T(128)S(1)} %get-tuple-element.49) | copy-start | bytes 772
  5.2 25.8 %copy-start.19 = (f32[64]{0:T(128)}, f32[64]{0:T(128)S(1)}, u32[]{:S(2)}) copy-start(f32[64]{0:T(128)S(1)} %get-tuple-element.52) | copy-start | bytes 772
  5.2 25.8 %copy-start.21 = (f32[64]{0:T(128)}, f32[64]{0:T(128)S(1)}, u32[]{:S(2)}) copy-start(f32[64]{0:T(128)S(1)} %get-tuple-element.55) | copy-start | bytes 772
  11.3 12.5 %copy-start.2 = (bf16[8,512,128]{2,1,0:T(8,128)(2,1)S(1)}, bf16[8,512,128]{2,1,0:T(8,128)(2,1)}, u32[]{:S(2)}) copy-start(bf16[8,512,128]{2,1,0:T(8,128)(2,1)} %param.17) | copy-start | bytes 3145732
  11.9 6.1 %collective-permute-start.1 = (bf16[64,1024]{1,0:T(8,128)(2,1)S(1)}, bf16[64,1024]{1,0:T(8,128)(2,1)S(1)}, u32[]{:S(2)}, u32[]{:S(2)}) collective-permute-start(bf16[64,1024]{1,0:T(8,128)(2,1)S(1)} %get-tuple-element.35), channel_id=1, source_target_pairs={{0,4},{2,6},{4,0},{6,2},{8,12},{10,14},{12,8},{14,10},{1,5},{3,7},... | collective-permute-start | bytes 393224 | tf_op jit(solution)/shard_map/ppermute | solution.py:13
  13.8 7.4 %collective-permute-start.6 = (bf16[64,1024]{1,0:T(8,128)(2,1)S(1)}, bf16[64,1024]{1,0:T(8,128)(2,1)S(1)}, u32[]{:S(2)}, u32[]{:S(2)}) collective-permute-start(bf16[64,1024]{1,0:T(8,128)(2,1)S(1)} %get-tuple-element.34), channel_id=1, source_target_pairs={{0,4},{2,6},{4,0},{6,2},{8,12},{10,14},{12,8},{14,10},{1,5},{3,7},... | collective-permute-start | bytes 393224 | tf_op jit(solution)/shard_map/ppermute | solution.py:13
  18.7 10.9 %collective-permute-start.2 = (bf16[64,1024]{1,0:T(8,128)(2,1)S(1)}, bf16[64,1024]{1,0:T(8,128)(2,1)S(1)}, u32[]{:S(2)}, u32[]{:S(2)}) collective-permute-start(bf16[64,1024]{1,0:T(8,128)(2,1)S(1)} %fusion.31), channel_id=1, source_target_pairs={{0,8},{2,10},{4,12},{6,14},{8,0},{10,2},{12,4},{14,6},{1,9},{3,11}... | collective-permute-start | bytes 393224 | tf_op jit(solution)/shard_map/ppermute | solution.py:13
  21.9 9.1 %collective-permute-start.7 = (bf16[64,1024]{1,0:T(8,128)(2,1)S(1)}, bf16[64,1024]{1,0:T(8,128)(2,1)S(1)}, u32[]{:S(2)}, u32[]{:S(2)}) collective-permute-start(bf16[64,1024]{1,0:T(8,128)(2,1)S(1)} %fusion.39), channel_id=1, source_target_pairs={{0,8},{2,10},{4,12},{6,14},{8,0},{10,2},{12,4},{14,6},{1,9},{3,11}... | collective-permute-start | bytes 393224 | tf_op jit(solution)/shard_map/ppermute | solution.py:13
  23.8 7.2 %copy-start.1 = (bf16[128,1024]{1,0:T(8,128)(2,1)S(1)}, bf16[128,1024]{1,0:T(8,128)(2,1)}, u32[]{:S(2)}) copy-start(bf16[128,1024]{1,0:T(8,128)(2,1)} %param.9) | copy-start | bytes 786436
  24.3 11.0 %copy-start.4 = (f32[64,8,512]{2,0,1:T(8,128)}, f32[64,8,512]{2,0,1:T(8,128)S(1)}, u32[]{:S(2)}) copy-start(f32[64,8,512]{2,0,1:T(8,128)S(1)} %convolution_bitcast_fusion.2) | copy-start | bytes 3145732
  31.4 2.1 %collective-permute-start.3 = (f32[64]{0:T(128)S(1)}, f32[64]{0:T(128)S(1)}, u32[]{:S(2)}, u32[]{:S(2)}) collective-permute-start(f32[64]{0:T(128)S(1)} %get-tuple-element.8), channel_id=1, source_target_pairs={{0,1},{1,0},{2,3},{3,2},{4,5},{5,4},{6,7},{7,6},{8,9},{9,8},{10,11... | collective-permute-start | bytes 776 | tf_op jit(solution)/shard_map/ppermute | solution.py:21
  32.9 1.3 %collective-permute-start.8 = (f32[64]{0:T(128)S(1)}, f32[64]{0:T(128)S(1)}, u32[]{:S(2)}, u32[]{:S(2)}) collective-permute-start(f32[64]{0:T(128)S(1)} %get-tuple-element.9), channel_id=1, source_target_pairs={{0,1},{1,0},{2,3},{3,2},{4,5},{5,4},{6,7},{7,6},{8,9},{9,8},{10,11... | collective-permute-start | bytes 776 | tf_op jit(solution)/shard_map/ppermute | solution.py:21
  46.2 1.2 %collective-permute-start.9 = (f32[64]{0:T(128)S(1)}, f32[64]{0:T(128)S(1)}, u32[]{:S(2)}, u32[]{:S(2)}) collective-permute-start(f32[64]{0:T(128)S(1)} %get-tuple-element.5), channel_id=1, source_target_pairs={{0,1},{1,0},{2,3},{3,2},{4,5},{5,4},{6,7},{7,6},{8,9},{9,8},{10,11... | collective-permute-start | bytes 776 | tf_op jit(solution)/shard_map/ppermute | solution.py:21
  46.6 1.3 %collective-permute-start.4 = (f32[64]{0:T(128)S(1)}, f32[64]{0:T(128)S(1)}, u32[]{:S(2)}, u32[]{:S(2)}) collective-permute-start(f32[64]{0:T(128)S(1)} %get-tuple-element.4), channel_id=1, source_target_pairs={{0,1},{1,0},{2,3},{3,2},{4,5},{5,4},{6,7},{7,6},{8,9},{9,8},{10,11... | collective-permute-start | bytes 776 | tf_op jit(solution)/shard_map/ppermute | solution.py:21
  47.9 12.6 %collective-permute-start.13 = (bf16[64,1024]{1,0:T(8,128)(2,1)S(1)}, bf16[64,1024]{1,0:T(8,128)(2,1)S(1)}, u32[]{:S(2)}, u32[]{:S(2)}) collective-permute-start(bf16[64,1024]{1,0:T(8,128)(2,1)S(1)} %fusion.60), channel_id=1, source_target_pairs={{0,8},{2,10},{4,12},{6,14},{8,0},{10,2},{12,4},{14,6},{1,9},{3,11}... | collective-permute-start | bytes 393224 | tf_op jit(solution)/shard_map/ppermute | solution.py:13
  48.3 12.2 %copy-start.13 = (bf16[64,1024]{1,0:T(8,128)(2,1)S(1)}, bf16[64,1024]{1,0:T(8,128)(2,1)}, u32[]{:S(2)}) copy-start(bf16[64,1024]{1,0:T(8,128)(2,1)} %copy-done.12) | copy-start | bytes 393220
  48.3 12.2 %copy-start.22 = (f32[64]{0:T(128)S(1)}, f32[64]{0:T(128)}, u32[]{:S(2)}) copy-start(f32[64]{0:T(128)} %copy-done.21) | copy-start | bytes 772
  48.4 14.6 %collective-permute-start.10 = (bf16[64,1024]{1,0:T(8,128)(2,1)S(1)}, bf16[64,1024]{1,0:T(8,128)(2,1)S(1)}, u32[]{:S(2)}, u32[]{:S(2)}) collective-permute-start(bf16[64,1024]{1,0:T(8,128)(2,1)S(1)} %fusion.45), channel_id=1, source_target_pairs={{0,8},{2,10},{4,12},{6,14},{8,0},{10,2},{12,4},{14,6},{1,9},{3,11}... | collective-permute-start | bytes 393224 | tf_op jit(solution)/shard_map/ppermute | solution.py:13
  61.5 5.1 %collective-permute-start.14 = (bf16[64,1024]{1,0:T(8,128)(2,1)S(1)}, bf16[64,1024]{1,0:T(8,128)(2,1)S(1)}, u32[]{:S(2)}, u32[]{:S(2)}) collective-permute-start(bf16[64,1024]{1,0:T(8,128)(2,1)S(1)} %fusion.65), channel_id=1, source_target_pairs={{0,4},{2,6},{4,0},{6,2},{8,12},{10,14},{12,8},{14,10},{1,5},{3,7},... | collective-permute-start | bytes 393224 | tf_op jit(solution)/shard_map/ppermute | solution.py:13
  64.0 5.4 %collective-permute-start.11 = (bf16[64,1024]{1,0:T(8,128)(2,1)S(1)}, bf16[64,1024]{1,0:T(8,128)(2,1)S(1)}, u32[]{:S(2)}, u32[]{:S(2)}) collective-permute-start(bf16[64,1024]{1,0:T(8,128)(2,1)S(1)} %fusion.50), channel_id=1, source_target_pairs={{0,4},{2,6},{4,0},{6,2},{8,12},{10,14},{12,8},{14,10},{1,5},{3,7},... | collective-permute-start | bytes 393224 | tf_op jit(solution)/shard_map/ppermute | solution.py:13
  70.5 5.9 %collective-permute-start.12 = (bf16[64,1024]{1,0:T(8,128)(2,1)S(1)}, bf16[64,1024]{1,0:T(8,128)(2,1)S(1)}, u32[]{:S(2)}, u32[]{:S(2)}) collective-permute-start(bf16[64,1024]{1,0:T(8,128)(2,1)S(1)} %fusion.55), channel_id=1, source_target_pairs={{0,2},{2,0},{4,6},{6,4},{8,10},{10,8},{12,14},{14,12},{1,3},{3,1},... | collective-permute-start | bytes 393224 | tf_op jit(solution)/shard_map/ppermute | solution.py:13
  72.1 5.6 %collective-permute-start.15 = (bf16[64,1024]{1,0:T(8,128)(2,1)S(1)}, bf16[64,1024]{1,0:T(8,128)(2,1)S(1)}, u32[]{:S(2)}, u32[]{:S(2)}) collective-permute-start(bf16[64,1024]{1,0:T(8,128)(2,1)S(1)} %fusion.70), channel_id=1, source_target_pairs={{0,2},{2,0},{4,6},{6,4},{8,10},{10,8},{12,14},{14,12},{1,3},{3,1},... | collective-permute-start | bytes 393224 | tf_op jit(solution)/shard_map/ppermute | solution.py:13
  72.9 1.2 %collective-permute-start.17 = (f32[3,128]{1,0:T(4,128)S(1)}, f32[3,128]{1,0:T(4,128)S(1)}, u32[]{:S(2)}, u32[]{:S(2)}) collective-permute-start(f32[3,128]{1,0:T(4,128)S(1)} %maximum_maximum_fusion.1), channel_id=1, source_target_pairs={{0,1},{1,0},{2,3},{3,2},{4,5},{5,4},{6,7},{7,6},{8,9},{9,8},{10,11... | collective-permute-start | bytes 4616 | tf_op jit(solution)/shard_map/ppermute | solution.py:21
  73.0 1.7 %collective-permute-start.16 = (f32[3,128]{1,0:T(4,128)S(1)}, f32[3,128]{1,0:T(4,128)S(1)}, u32[]{:S(2)}, u32[]{:S(2)}) collective-permute-start(f32[3,128]{1,0:T(4,128)S(1)} %maximum_maximum_fusion), channel_id=1, source_target_pairs={{0,1},{1,0},{2,3},{3,2},{4,5},{5,4},{6,7},{7,6},{8,9},{9,8},{10,11... | collective-permute-start | bytes 4616 | tf_op jit(solution)/shard_map/ppermute | solution.py:21
  78.1 1.5 %collective-permute-start.18 = (f32[1,128,128]{2,1,0:T(8,128)S(1)}, f32[1,128,128]{2,1,0:T(8,128)S(1)}, u32[]{:S(2)}, u32[]{:S(2)}) collective-permute-start(f32[1,128,128]{2,1,0:T(8,128)S(1)} %convolution_bitcast_fusion.7), channel_id=1, source_target_pairs={{0,1},{1,0},{2,3},{3,2},{4,5},{5,4},{6,7},{7,6},{8,9},{9,8},{10,11... | collective-permute-start | bytes 196616 | tf_op jit(solution)/shard_map/ppermute | solution.py:21
  (30 other events, 76.0 us)

commit v3 on v1

v3 whole, which is shorter than its diff:
```python
import jax
import jax.numpy as jnp
from jax import lax
from jax.sharding import PartitionSpec as P

D = 2048
CHUNKS = 2


def from_partner(value, axis, distance):
    mask = 2**distance
    pairs = [(source, source ^ mask) for source in range(lax.axis_size(axis))]
    return lax.ppermute(value, axis, pairs)


def hid_sum(value):
    size = lax.axis_size("hid")
    total = value
    for shift in range(1, size):
        pairs = [(source, (source + shift) % size) for source in range(size)]
        total = total + lax.ppermute(value, "hid", pairs)
    return total


def tie(value, after):
    if after is None:
        return value
    return lax.optimization_barrier((value, after))[0]


def body(tokens, cotangent, blocks, coef_self, coef_cross, norm_gain, w_gate, w_up, w_down):
    tok, width = tokens.shape
    sections = coef_self.shape[0]
    nblk = blocks.shape[0]
    blen = blocks.shape[1]
    groups_here = w_gate.shape[0]
    cblock = w_gate.shape[1]
    tok_blocks = tokens.reshape(nblk, blen, width)
    local = jnp.einsum("kij,kjd->kid", blocks, tok_blocks, preferred_element_type=jnp.float32)
    local = local.astype(jnp.bfloat16).reshape(tok, width)
    chunks = CHUNKS if tok % CHUNKS == 0 else 1
    rows = tok // chunks
    spans = [slice(chunk * rows, (chunk + 1) * rows) for chunk in range(chunks)]

    states = [[None] * sections for _ in spans]
    mates = [[None] * sections for _ in spans]
    current = [local[rs] for rs in spans]
    for section in range(sections):
        previous = None
        for chunk, rs in enumerate(spans):
            value = tie(current[chunk], previous)
            mate = from_partner(value, "seq", section)
            previous = mate
            states[chunk][section] = value
            mates[chunk][section] = mate
            current[chunk] = (
                coef_self[section, rs][:, None] * value.astype(jnp.float32)
                + coef_cross[section, rs][:, None] * mate.astype(jnp.float32)
            ).astype(jnp.bfloat16)

    backs = []
    directs = []
    tok_fs = []
    for chunk, rs in enumerate(spans):
        tok_f = tokens[rs].astype(jnp.float32)
        cot = cotangent[rs]
        mixed_f = current[chunk].astype(jnp.float32)
        resid = tok_f + tok_f * mixed_f
        square = hid_sum(jnp.sum(resid * resid, axis=-1))
        inv = lax.rsqrt(square / D + 1e-06)
        normed = (
            (resid * inv[:, None] * norm_gain).astype(jnp.bfloat16).reshape(rows, groups_here, cblock)
        )
        gate_pre = jnp.einsum("tgc,gce->tge", normed, w_gate, preferred_element_type=jnp.float32)
        up_val = jnp.einsum("tgc,gce->tge", normed, w_up, preferred_element_type=jnp.float32)
        d_hidden = jnp.einsum(
            "tgc,gec->tge",
            cot.reshape(rows, groups_here, cblock),
            w_down,
            preferred_element_type=jnp.float32,
        )
        sig = jax.nn.sigmoid(gate_pre)
        d_up = (d_hidden * gate_pre * sig).astype(jnp.bfloat16)
        d_gate = (d_hidden * up_val * sig * (1.0 + gate_pre * (1.0 - sig))).astype(jnp.bfloat16)
        d_normed = jnp.einsum("tge,gce->tgc", d_gate, w_gate, preferred_element_type=jnp.float32)
        d_normed = d_normed + jnp.einsum(
            "tge,gce->tgc", d_up, w_up, preferred_element_type=jnp.float32
        )
        scaled = norm_gain * d_normed.reshape(rows, width)
        inner = hid_sum(jnp.sum(resid * scaled, axis=-1))
        d_resid = (
            cot.astype(jnp.float32)
            + inv[:, None] * scaled
            - resid * (inv**3 * inner / D)[:, None]
        )
        backs.append((d_resid * tok_f).astype(jnp.bfloat16))
        directs.append(d_resid * (1.0 + mixed_f))

    grads_self = [[None] * sections for _ in spans]
    grads_cross = [[None] * sections for _ in spans]
    for section in range(sections - 1, -1, -1):
        previous = None
        for chunk, rs in enumerate(spans):
            back_f = backs[chunk].astype(jnp.float32)
            grads_self[chunk][section] = jnp.sum(
                back_f * states[chunk][section].astype(jnp.float32), axis=-1
            )
            grads_cross[chunk][section] = jnp.sum(
                back_f * mates[chunk][section].astype(jnp.float32), axis=-1
            )
            sent = tie((coef_cross[section, rs][:, None] * back_f).astype(jnp.bfloat16), previous)
            received = from_partner(sent, "seq", section)
            previous = received
            backs[chunk] = (
                coef_self[section, rs][:, None] * back_f + received.astype(jnp.float32)
            ).astype(jnp.bfloat16)

    back = jnp.concatenate(backs, axis=0)
    direct = jnp.concatenate(directs, axis=0)
    part_self = jnp.concatenate([jnp.stack(g) for g in grads_self], axis=1)
    part_cross = jnp.concatenate([jnp.stack(g) for g in grads_cross], axis=1)
    back_blocks = back.reshape(nblk, blen, width)
    part_blocks = jnp.einsum(
        "kid,kjd->kij", back_blocks, tok_blocks, preferred_element_type=jnp.float32
    )
    from_blocks = jnp.einsum(
        "kij,kid->kjd", blocks, back_blocks, preferred_element_type=jnp.float32
    ).reshape(tok, width)
    grad_self, grad_cross, grad_blocks = jax.tree.map(hid_sum, (part_self, part_cross, part_blocks))
    grad_x = (direct + from_blocks).astype(jnp.bfloat16)
    return (grad_x, grad_self, grad_cross, grad_blocks)


def solution(mesh):
    return jax.shard_map(
        body,
        mesh=mesh,
        in_specs=(
            P(("groups", "seq"), "hid"),
            P(("groups", "seq"), "hid"),
            P("seq", None, None),
            P(None, "seq"),
            P(None, "seq"),
            P("hid"),
            P("hid", None, None),
            P("hid", None, None),
            P("hid", None, None),
        ),
        out_specs=(
            P(("groups", "seq"), "hid"),
            P(None, ("groups", "seq")),
            P(None, ("groups", "seq")),
            P(("groups", "seq"), None, None),
        ),
        check_vma=False,
    )
```

time: 85 us -> 87.6 us (1.031)
  waiting for transfers between devices: 51.6 us -> 45.8 us
  local copies, waits for them, and re-layouts: 2.79 us -> 8.46 us
  starting transfers between devices: 9.97 us -> 13.5 us
  matrix products: 14.4 us -> 12.8 us
    unnamed x18 -> x91, local copies, waits for them, and re-layouts: 0.75 us -> 8.29 us
    ppermute x6 -> x12, waiting for transfers between devices: 50.6 us -> 44 us  [from_partner(): return lax.ppermute(value, axis, pairs)]
    ppermute x6 -> x12, starting transfers between devices: 8.67 us -> 11.9 us  [from_partner(): return lax.ppermute(value, axis, pairs)]
    dot_general x1 -> x2, matrix products: 4.17 us -> 2.25 us  [body(): jnp.einsum('tge,gce->tgc', d_up, w_up, preferred_element_type=jnp.float32)]
    dot_general x1 -> x2, matrix products: 3.9 us -> 5.53 us  [body(): jnp.einsum('tge,gce->tgc', d_gate, w_gate, preferred_element_type=jnp.flo...]
    dot_general x1 -> x2, matrix products: 1.89 us -> 0.59 us  [body(): jnp.einsum('tgc,gce->tge', normed, w_gate, preferred_element_type=jnp.flo...]
    reshape x1 -> x0, local copies, waits for them, and re-layouts: 1.24 us -> none  [body(): scaled = norm_gain * d_normed.reshape(tok, width)]
    ppermute x5 -> x7, waiting for transfers between devices: 0.91 us -> 1.81 us  [hid_sum(): total = total + lax.ppermute(value, 'hid', pairs)]
  transfers between devices with their start and end apart: 11 -> 19, of which waited for: 8 -> 15; matrix products, arithmetic and copies ran while one was open for 6% -> 8% of each run, Pallas kernels for 0% -> 0%
where the time goes in v3:
time: 87.6 us; the launch traced here: 87.2 us
  waiting for transfers between devices  45.8 us (52%)
  starting transfers between devices  13.5 us (15%)
  matrix products  12.8 us (15%)
  local copies, waits for them, and re-layouts  8.46 us (10%)
  other arithmetic  5.53 us (6%)
  between operations  1.08 us (1%)
    ppermute x12, waiting for transfers between devices, from_partner(): return lax.ppermute(value, axis, pairs)  44 us
    ppermute x12, starting transfers between devices, from_partner(): return lax.ppermute(value, axis, pairs)  11.9 us
    unnamed x91, local copies, waits for them, and re-layouts  8.29 us
    dot_general x2, matrix products, body(): jnp.einsum('tge,gce->tgc', d_gate, w_gate, preferred_element_type=jnp.flo...  5.53 us
    dot_general x2, matrix products, body(): jnp.einsum('tge,gce->tgc', d_up, w_up, preferred_element_type=jnp.float32)  2.25 us
    dot_general x2, matrix products, body(): jnp.einsum('tgc,gec->tge', cot.reshape(rows, groups_here, cblock), w_down...  1.96 us
    add x3, other arithmetic, hid_sum(): total = total + lax.ppermute(value, 'hid', pairs)  1.95 us
    ppermute x7, waiting for transfers between devices, hid_sum(): total = total + lax.ppermute(value, 'hid', pairs)  1.81 us
  transfers between devices with their start and end apart: 19, of which 15 were waited for; matrix products, arithmetic and copies ran while one was open for 8% of the time, Pallas kernels for 0%

profile of v3, /device:TPU:0, one launch (start us, length us, event | category | flops | bytes accessed | tf_op | source)
XLA Modules:
  0.0 87.2 jit_solution(2578141737738665767)
XLA Ops:
  0.6 1.3 %fusion.14 = bf16[1,128,1024]{2,1,0:T(8,128)(2,1)S(1)} fusion(bf16[128,1024]{1,0:T(8,128)(2,1)} %param.9, bf16[1,128,128]{2,1,0:T(8,128)(2,1)} %param.11), kind=kOutput, calls=%fused_computation.22 | convolution fusion | flops 33685504 | bytes 557056 | tf_op jit(solution)/shard_map/kij,kjd->kid/dot_general | solution.py:39
  2.0 3.0 %collective-permute-start = (bf16[64,1024]{1,0:T(8,128)(2,1)S(1)}, bf16[64,1024]{1,0:T(8,128)(2,1)S(1)}, u32[]{:S(2)}, u32[]{:S(2)}) collective-permute-start(bf16[64,1024]{1,0:T(8,128)(2,1)S(1)} %get-tuple-element.47), channel_id=1, source_target_pairs={{0,2},{2,0},{4,6},{6,4},{8,10},{10,8},{12,14},{14,12},{1,3},{3,1},... | collective-permute-start | bytes 393224 | tf_op jit(solution)/shard_map/ppermute | solution.py:13
  5.2 3.2 %collective-permute-done = bf16[64,1024]{1,0:T(8,128)(2,1)S(1)} collective-permute-done((bf16[64,1024]{1,0:T(8,128)(2,1)S(1)}, bf16[64,1024]{1,0:T(8,128)(2,1)S(1)}, u32[]{:S(2)}, u32[]{:S(2)}) %collective-permute-start) | collective-permute-done | bytes 131104 | tf_op jit(solution)/shard_map/ppermute | solution.py:13
  8.5 1.7 %collective-permute-start.5 = (bf16[64,1024]{1,0:T(8,128)(2,1)S(1)}, bf16[64,1024]{1,0:T(8,128)(2,1)S(1)}, u32[]{:S(2)}, u32[]{:S(2)}) collective-permute-start(bf16[64,1024]{1,0:T(8,128)(2,1)S(1)} %get-tuple-element.10), channel_id=1, source_target_pairs={{0,2},{2,0},{4,6},{6,4},{8,10},{10,8},{12,14},{14,12},{1,3},{3,1},... | collective-permute-start | bytes 393224 | tf_op jit(solution)/shard_map/ppermute | solution.py:13
  10.4 1.6 %collective-permute-start.1 = (bf16[64,1024]{1,0:T(8,128)(2,1)S(1)}, bf16[64,1024]{1,0:T(8,128)(2,1)S(1)}, u32[]{:S(2)}, u32[]{:S(2)}) collective-permute-start(bf16[64,1024]{1,0:T(8,128)(2,1)S(1)} %fusion.29), channel_id=1, source_target_pairs={{0,4},{2,6},{4,0},{6,2},{8,12},{10,14},{12,8},{14,10},{1,5},{3,7},... | collective-permute-start | bytes 393224 | tf_op jit(solution)/shard_map/ppermute | solution.py:13
  12.0 1.4 %collective-permute-done.5 = bf16[64,1024]{1,0:T(8,128)(2,1)S(1)} collective-permute-done((bf16[64,1024]{1,0:T(8,128)(2,1)S(1)}, bf16[64,1024]{1,0:T(8,128)(2,1)S(1)}, u32[]{:S(2)}, u32[]{:S(2)}) %collective-permute-start.5) | collective-permute-done | bytes 131104 | tf_op jit(solution)/shard_map/ppermute | solution.py:13
  14.1 1.3 %collective-permute-done.1 = bf16[64,1024]{1,0:T(8,128)(2,1)S(1)} collective-permute-done((bf16[64,1024]{1,0:T(8,128)(2,1)S(1)}, bf16[64,1024]{1,0:T(8,128)(2,1)S(1)}, u32[]{:S(2)}, u32[]{:S(2)}) %collective-permute-start.1) | collective-permute-done | bytes 131104 | tf_op jit(solution)/shard_map/ppermute | solution.py:13
  15.4 1.6 %collective-permute-start.6 = (bf16[64,1024]{1,0:T(8,128)(2,1)S(1)}, bf16[64,1024]{1,0:T(8,128)(2,1)S(1)}, u32[]{:S(2)}, u32[]{:S(2)}) collective-permute-start(bf16[64,1024]{1,0:T(8,128)(2,1)S(1)} %fusion.37), channel_id=1, source_target_pairs={{0,4},{2,6},{4,0},{6,2},{8,12},{10,14},{12,8},{14,10},{1,5},{3,7},... | collective-permute-start | bytes 393224 | tf_op jit(solution)/shard_map/ppermute | solution.py:13
  17.1 2.7 %collective-permute-start.2 = (bf16[64,1024]{1,0:T(8,128)(2,1)S(1)}, bf16[64,1024]{1,0:T(8,128)(2,1)S(1)}, u32[]{:S(2)}, u32[]{:S(2)}) collective-permute-start(bf16[64,1024]{1,0:T(8,128)(2,1)S(1)} %fusion.31), channel_id=1, source_target_pairs={{0,8},{2,10},{4,12},{6,14},{8,0},{10,2},{12,4},{14,6},{1,9},{3,11}... | collective-permute-start | bytes 393224 | tf_op jit(solution)/shard_map/ppermute | solution.py:13
  19.8 1.0 %collective-permute-done.6 = bf16[64,1024]{1,0:T(8,128)(2,1)S(1)} collective-permute-done((bf16[64,1024]{1,0:T(8,128)(2,1)S(1)}, bf16[64,1024]{1,0:T(8,128)(2,1)S(1)}, u32[]{:S(2)}, u32[]{:S(2)}) %collective-permute-start.6) | collective-permute-done | bytes 131104 | tf_op jit(solution)/shard_map/ppermute | solution.py:13
  20.9 5.3 %collective-permute-done.2 = bf16[64,1024]{1,0:T(8,128)(2,1)S(1)} collective-permute-done((bf16[64,1024]{1,0:T(8,128)(2,1)S(1)}, bf16[64,1024]{1,0:T(8,128)(2,1)S(1)}, u32[]{:S(2)}, u32[]{:S(2)}) %collective-permute-start.2) | collective-permute-done | bytes 131104 | tf_op jit(solution)/shard_map/ppermute | solution.py:13
  26.7 5.4 %collective-permute-done.7 = bf16[64,1024]{1,0:T(8,128)(2,1)S(1)} collective-permute-done((bf16[64,1024]{1,0:T(8,128)(2,1)S(1)}, bf16[64,1024]{1,0:T(8,128)(2,1)S(1)}, u32[]{:S(2)}, u32[]{:S(2)}) %collective-permute-start.7) | collective-permute-done | bytes 131104 | tf_op jit(solution)/shard_map/ppermute | solution.py:13
  32.7 1.5 %convolution_bitcast_fusion.5 = f32[64,8,512]{2,0,1:T(8,128)} fusion(bf16[8,512,128]{2,1,0:T(8,128)(2,1)S(1)} %copy-done.2, bf16[8,8,8,128]{3,2,1,0:T(8,128)(2,1)S(1)} %get-tuple-element.45), kind=kOutput, calls=%fused_computation.9 | convolution fusion | flops 67108864 | bytes 2228224 | tf_op jit(solution)/shard_map/tgc,gec->tge/dot_general | solution.py:76
  34.7 0.8 collective-permute-done.8
  36.5 1.0 %copy-done.6 = f32[64,8,512]{2,0,1:T(8,128)} copy-done((f32[64,8,512]{2,0,1:T(8,128)}, f32[64,8,512]{2,0,1:T(8,128)S(1)}, u32[]{:S(2)}) %copy-start.6) | copy-done | bytes 1048600
  37.5 1.1 %fusion.26 = f32[8,64,128]{2,1,0:T(8,128)} fusion(bf16[8,128,512]{2,1,0:T(8,128)(2,1)S(1)} %copy-done.43, f32[64,8,512]{2,0,1:T(8,128)S(1)} %convolution_bitcast_fusion.2, f32[64,8,512]{2,0,1:T(8,128)S(1)} %convolution_bitcast_fusion), kind=kOutput, calls=%fused_computation.39 | convolution fusion | flops 68681728 | bytes 3407872 | tf_op jit(solution)/shard_map/tge,gce->tgc/dot_general | solution.py:86
  38.7 2.7 %fusion.16 = f32[8,8,8,128]{3,2,1,0:T(8,128)S(1)} fusion(f32[8,64,128]{2,1,0:T(8,128)} %fusion.26, bf16[8,128,512]{2,1,0:T(8,128)(2,1)S(1)} %copy-done, f32[64,8,512]{2,0,1:T(8,128)} %copy-done.4, bf16[8,128,512]{2,1,0:T(8,128)(2,1)} %param.16, f32[64,8,512]{2,0,1:T(8,128)} %copy-done.6, bf16[8,8,8,128]{3,2,1,0:T(8,128)(2,1)S(1)} %get-tuple-element.42), kind=kOutput, calls=%fused_computation.24 | convolution fusion | flops 136904704 | bytes 4849664 | tf_op jit(solution)/shard_map/tge,gce->tgc/dot_general | solution.py:85
  41.8 1.0 %copy-done.7 = f32[64,8,512]{2,0,1:T(8,128)} copy-done((f32[64,8,512]{2,0,1:T(8,128)}, f32[64,8,512]{2,0,1:T(8,128)S(1)}, u32[]{:S(2)}) %copy-start.7) | copy-done | bytes 1048600
  42.7 0.6 copy-done.44
  43.3 1.1 %fusion.25 = f32[8,64,128]{2,1,0:T(8,128)} fusion(bf16[8,128,512]{2,1,0:T(8,128)(2,1)S(1)} %copy-done.44, f32[64,8,512]{2,0,1:T(8,128)S(1)} %copy-done.5, f32[64,8,512]{2,0,1:T(8,128)S(1)} %convolution_bitcast_fusion.3), kind=kOutput, calls=%fused_computation.38 | convolution fusion | flops 68681728 | bytes 3407872 | tf_op jit(solution)/shard_map/tge,gce->tgc/dot_general | solution.py:86
  44.5 2.8 %fusion.15 = f32[8,8,8,128]{3,2,1,0:T(8,128)S(1)} fusion(f32[8,64,128]{2,1,0:T(8,128)} %fusion.25, bf16[8,128,512]{2,1,0:T(8,128)(2,1)S(1)} %copy-done, f32[64,8,512]{2,0,1:T(8,128)} %convolution_bitcast_fusion.5, bf16[8,128,512]{2,1,0:T(8,128)(2,1)} %param.16, f32[64,8,512]{2,0,1:T(8,128)} %copy-done.7, bf16[8,8,8,128]{3,2,1,0:T(8,128)(2,1)} %copy-done.16), kind=kOutput, calls=%fused_computation.23 | convolution fusion | flops 136904704 | bytes 4849664 | tf_op jit(solution)/shard_map/tge,gce->tgc/dot_general | solution.py:85
  49.0 0.6 copy-done.20
  51.0 7.9 %collective-permute-done.10 = bf16[64,1024]{1,0:T(8,128)(2,1)S(1)} collective-permute-done((bf16[64,1024]{1,0:T(8,128)(2,1)S(1)}, bf16[64,1024]{1,0:T(8,128)(2,1)S(1)}, u32[]{:S(2)}, u32[]{:S(2)}) %collective-permute-start.10) | collective-permute-done | bytes 131104 | tf_op jit(solution)/shard_map/ppermute | solution.py:13
  58.9 8.0 %collective-permute-done.13 = bf16[64,1024]{1,0:T(8,128)(2,1)S(1)} collective-permute-done((bf16[64,1024]{1,0:T(8,128)(2,1)S(1)}, bf16[64,1024]{1,0:T(8,128)(2,1)S(1)}, u32[]{:S(2)}, u32[]{:S(2)}) %collective-permute-start.13) | collective-permute-done | bytes 131104 | tf_op jit(solution)/shard_map/ppermute | solution.py:13
  68.7 4.7 %collective-permute-done.11 = bf16[64,1024]{1,0:T(8,128)(2,1)S(1)} collective-permute-done((bf16[64,1024]{1,0:T(8,128)(2,1)S(1)}, bf16[64,1024]{1,0:T(8,128)(2,1)S(1)}, u32[]{:S(2)}, u32[]{:S(2)}) %collective-permute-start.11) | collective-permute-done | bytes 131104 | tf_op jit(solution)/shard_map/ppermute | solution.py:13
  75.1 3.3 %collective-permute-done.14 = bf16[64,1024]{1,0:T(8,128)(2,1)S(1)} collective-permute-done((bf16[64,1024]{1,0:T(8,128)(2,1)S(1)}, bf16[64,1024]{1,0:T(8,128)(2,1)S(1)}, u32[]{:S(2)}, u32[]{:S(2)}) %collective-permute-start.14) | collective-permute-done | bytes 131104 | tf_op jit(solution)/shard_map/ppermute | solution.py:13
  78.7 0.6 copy-done.30
  81.3 0.7 fusion.123
  82.0 0.7 fusion.124
  82.7 2.1 %collective-permute-done.15 = bf16[64,1024]{1,0:T(8,128)(2,1)S(1)} collective-permute-done((bf16[64,1024]{1,0:T(8,128)(2,1)S(1)}, bf16[64,1024]{1,0:T(8,128)(2,1)S(1)}, u32[]{:S(2)}, u32[]{:S(2)}) %collective-permute-start.15) | collective-permute-done | bytes 131104 | tf_op jit(solution)/shard_map/ppermute | solution.py:13
  85.6 1.0 %fusion.11 = bf16[128,1024]{1,0:T(8,128)(2,1)} fusion(f32[64,1024]{1,0:T(8,128)S(1)} %get-tuple-element.41, f32[64,1024]{1,0:T(8,128)S(1)} %get-tuple-element.40, bf16[64,1024]{1,0:T(8,128)(2,1)S(1)} %fusion.69, bf16[64,1024]{1,0:T(8,128)(2,1)S(1)} %fusion.54, bf16[1,128,128]{2,1,0:T(8,128)(2,1)S(1)} %copy-done.17), kind=kOutput, calls=%fused_computation.18 | convolution fusion | flops 34471936 | bytes 1081344 | tf_op jit(solution)/shard_map/kij,kid->kjd/dot_general | solution.py:126
  86.6 0.6 add.143
  (140 shorter events, 13.7 us)
Async XLA Ops:
  0.6 35.6 %copy-start = (bf16[8,128,512]{2,1,0:T(8,128)(2,1)S(1)}, bf16[8,128,512]{2,1,0:T(8,128)(2,1)}, u32[]{:S(2)}) copy-start(bf16[8,128,512]{2,1,0:T(8,128)(2,1)} %param.15) | copy-start | bytes 3145732
  2.0 6.5 %collective-permute-start = (bf16[64,1024]{1,0:T(8,128)(2,1)S(1)}, bf16[64,1024]{1,0:T(8,128)(2,1)S(1)}, u32[]{:S(2)}, u32[]{:S(2)}) collective-permute-start(bf16[64,1024]{1,0:T(8,128)(2,1)S(1)} %get-tuple-element.47), channel_id=1, source_target_pairs={{0,2},{2,0},{4,6},{6,4},{8,10},{10,8},{12,14},{14,12},{1,3},{3,1},... | collective-permute-start | bytes 393224 | tf_op jit(solution)/shard_map/ppermute | solution.py:13
  5.1 8.4 %copy-start.25 = (f32[64]{0:T(128)}, f32[64]{0:T(128)S(1)}, u32[]{:S(2)}) copy-start(f32[64]{0:T(128)S(1)} %get-tuple-element.52) | copy-start | bytes 772
  5.1 11.9 %copy-start.41 = (f32[64]{0:T(128)}, f32[64]{0:T(128)S(1)}, u32[]{:S(2)}) copy-start(f32[64]{0:T(128)S(1)} %get-tuple-element.50) | copy-start | bytes 772
  5.1 15.7 %copy-start.39 = (f32[64]{0:T(128)}, f32[64]{0:T(128)S(1)}, u32[]{:S(2)}) copy-start(f32[64]{0:T(128)S(1)} %get-tuple-element.53) | copy-start | bytes 772
  5.1 21.1 %copy-start.2 = (bf16[8,512,128]{2,1,0:T(8,128)(2,1)S(1)}, bf16[8,512,128]{2,1,0:T(8,128)(2,1)}, u32[]{:S(2)}) copy-start(bf16[8,512,128]{2,1,0:T(8,128)(2,1)} %param.17) | copy-start | bytes 3145732
  5.2 8.2 %copy-start.29 = (f32[64]{0:T(128)}, f32[64]{0:T(128)S(1)}, u32[]{:S(2)}) copy-start(f32[64]{0:T(128)S(1)} %get-tuple-element.55) | copy-start | bytes 772
  5.2 11.8 %copy-start.35 = (f32[64]{0:T(128)}, f32[64]{0:T(128)S(1)}, u32[]{:S(2)}) copy-start(f32[64]{0:T(128)S(1)} %get-tuple-element.57) | copy-start | bytes 772
  5.2 15.5 %copy-start.33 = (f32[64]{0:T(128)}, f32[64]{0:T(128)S(1)}, u32[]{:S(2)}) copy-start(f32[64]{0:T(128)S(1)} %get-tuple-element.59) | copy-start | bytes 772
  5.2 26.8 %copy-start.19 = (f32[64]{0:T(128)}, f32[64]{0:T(128)S(1)}, u32[]{:S(2)}) copy-start(f32[64]{0:T(128)S(1)} %get-tuple-element.56) | copy-start | bytes 772
  8.5 5.0 %collective-permute-start.5 = (bf16[64,1024]{1,0:T(8,128)(2,1)S(1)}, bf16[64,1024]{1,0:T(8,128)(2,1)S(1)}, u32[]{:S(2)}, u32[]{:S(2)}) collective-permute-start(bf16[64,1024]{1,0:T(8,128)(2,1)S(1)} %get-tuple-element.10), channel_id=1, source_target_pairs={{0,2},{2,0},{4,6},{6,4},{8,10},{10,8},{12,14},{14,12},{1,3},{3,1},... | collective-permute-start | bytes 393224 | tf_op jit(solution)/shard_map/ppermute | solution.py:13
  10.4 5.0 %collective-permute-start.1 = (bf16[64,1024]{1,0:T(8,128)(2,1)S(1)}, bf16[64,1024]{1,0:T(8,128)(2,1)S(1)}, u32[]{:S(2)}, u32[]{:S(2)}) collective-permute-start(bf16[64,1024]{1,0:T(8,128)(2,1)S(1)} %fusion.29), channel_id=1, source_target_pairs={{0,4},{2,6},{4,0},{6,2},{8,12},{10,14},{12,8},{14,10},{1,5},{3,7},... | collective-permute-start | bytes 393224 | tf_op jit(solution)/shard_map/ppermute | solution.py:13
  15.4 5.4 %collective-permute-start.6 = (bf16[64,1024]{1,0:T(8,128)(2,1)S(1)}, bf16[64,1024]{1,0:T(8,128)(2,1)S(1)}, u32[]{:S(2)}, u32[]{:S(2)}) collective-permute-start(bf16[64,1024]{1,0:T(8,128)(2,1)S(1)} %fusion.37), channel_id=1, source_target_pairs={{0,4},{2,6},{4,0},{6,2},{8,12},{10,14},{12,8},{14,10},{1,5},{3,7},... | collective-permute-start | bytes 393224 | tf_op jit(solution)/shard_map/ppermute | solution.py:13
  17.1 9.0 %collective-permute-start.2 = (bf16[64,1024]{1,0:T(8,128)(2,1)S(1)}, bf16[64,1024]{1,0:T(8,128)(2,1)S(1)}, u32[]{:S(2)}, u32[]{:S(2)}) collective-permute-start(bf16[64,1024]{1,0:T(8,128)(2,1)S(1)} %fusion.31), channel_id=1, source_target_pairs={{0,8},{2,10},{4,12},{6,14},{8,0},{10,2},{12,4},{14,6},{1,9},{3,11}... | collective-permute-start | bytes 393224 | tf_op jit(solution)/shard_map/ppermute | solution.py:13
  26.1 5.9 %copy-start.10 = (bf16[64,1024]{1,0:T(8,128)(2,1)}, bf16[64,1024]{1,0:T(8,128)(2,1)S(1)}, u32[]{:S(2)}) copy-start(bf16[64,1024]{1,0:T(8,128)(2,1)S(1)} %collective-permute-done.2) | copy-start | bytes 393220
  26.1 5.9 %collective-permute-start.7 = (bf16[64,1024]{1,0:T(8,128)(2,1)S(1)}, bf16[64,1024]{1,0:T(8,128)(2,1)S(1)}, u32[]{:S(2)}, u32[]{:S(2)}) collective-permute-start(bf16[64,1024]{1,0:T(8,128)(2,1)S(1)} %fusion.39), channel_id=1, source_target_pairs={{0,8},{2,10},{4,12},{6,14},{8,0},{10,2},{12,4},{14,6},{1,9},{3,11}... | collective-permute-start | bytes 393224 | tf_op jit(solution)/shard_map/ppermute | solution.py:13
  26.2 5.9 %copy-start.1 = (bf16[128,1024]{1,0:T(8,128)(2,1)S(1)}, bf16[128,1024]{1,0:T(8,128)(2,1)}, u32[]{:S(2)}) copy-start(bf16[128,1024]{1,0:T(8,128)(2,1)} %param.9) | copy-start | bytes 786436
  26.6 9.9 %copy-start.4 = (f32[64,8,512]{2,0,1:T(8,128)}, f32[64,8,512]{2,0,1:T(8,128)S(1)}, u32[]{:S(2)}) copy-start(f32[64,8,512]{2,0,1:T(8,128)S(1)} %convolution_bitcast_fusion.2) | copy-start | bytes 3145732
  32.7 2.0 %collective-permute-start.3 = (f32[64]{0:T(128)S(1)}, f32[64]{0:T(128)S(1)}, u32[]{:S(2)}, u32[]{:S(2)}) collective-permute-start(f32[64]{0:T(128)S(1)} %get-tuple-element.18), channel_id=1, source_target_pairs={{0,1},{1,0},{2,3},{3,2},{4,5},{5,4},{6,7},{7,6},{8,9},{9,8},{10,11... | collective-permute-start | bytes 776 | tf_op jit(solution)/shard_map/ppermute | solution.py:21
  34.2 1.3 %collective-permute-start.8 = (f32[64]{0:T(128)S(1)}, f32[64]{0:T(128)S(1)}, u32[]{:S(2)}, u32[]{:S(2)}) collective-permute-start(f32[64]{0:T(128)S(1)} %get-tuple-element.19), channel_id=1, source_target_pairs={{0,1},{1,0},{2,3},{3,2},{4,5},{5,4},{6,7},{7,6},{8,9},{9,8},{10,11... | collective-permute-start | bytes 776 | tf_op jit(solution)/shard_map/ppermute | solution.py:21
  36.2 5.2 %copy-start.16 = (bf16[8,8,8,128]{3,2,1,0:T(8,128)(2,1)}, bf16[8,8,8,128]{3,2,1,0:T(8,128)(2,1)S(1)}, u32[]{:S(2)}) copy-start(bf16[8,8,8,128]{3,2,1,0:T(8,128)(2,1)S(1)} %get-tuple-element.43) | copy-start | bytes 393220
  47.5 1.2 %collective-permute-start.4 = (f32[64]{0:T(128)S(1)}, f32[64]{0:T(128)S(1)}, u32[]{:S(2)}, u32[]{:S(2)}) collective-permute-start(f32[64]{0:T(128)S(1)} %get-tuple-element.16), channel_id=1, source_target_pairs={{0,1},{1,0},{2,3},{3,2},{4,5},{5,4},{6,7},{7,6},{8,9},{9,8},{10,11... | collective-permute-start | bytes 776 | tf_op jit(solution)/shard_map/ppermute | solution.py:21
  47.9 2.1 %collective-permute-start.9 = (f32[64]{0:T(128)S(1)}, f32[64]{0:T(128)S(1)}, u32[]{:S(2)}, u32[]{:S(2)}) collective-permute-start(f32[64]{0:T(128)S(1)} %get-tuple-element.17), channel_id=1, source_target_pairs={{0,1},{1,0},{2,3},{3,2},{4,5},{5,4},{6,7},{7,6},{8,9},{9,8},{10,11... | collective-permute-start | bytes 776 | tf_op jit(solution)/shard_map/ppermute | solution.py:21
  49.8 9.2 %collective-permute-start.10 = (bf16[64,1024]{1,0:T(8,128)(2,1)S(1)}, bf16[64,1024]{1,0:T(8,128)(2,1)S(1)}, u32[]{:S(2)}, u32[]{:S(2)}) collective-permute-start(bf16[64,1024]{1,0:T(8,128)(2,1)S(1)} %fusion.45), channel_id=1, source_target_pairs={{0,8},{2,10},{4,12},{6,14},{8,0},{10,2},{12,4},{14,6},{1,9},{3,11}... | collective-permute-start | bytes 393224 | tf_op jit(solution)/shard_map/ppermute | solution.py:13
  58.9 8.0 %collective-permute-start.13 = (bf16[64,1024]{1,0:T(8,128)(2,1)S(1)}, bf16[64,1024]{1,0:T(8,128)(2,1)S(1)}, u32[]{:S(2)}, u32[]{:S(2)}) collective-permute-start(bf16[64,1024]{1,0:T(8,128)(2,1)S(1)} %fusion.60), channel_id=1, source_target_pairs={{0,8},{2,10},{4,12},{6,14},{8,0},{10,2},{12,4},{14,6},{1,9},{3,11}... | collective-permute-start | bytes 393224 | tf_op jit(solution)/shard_map/ppermute | solution.py:13
  68.0 5.5 %collective-permute-start.11 = (bf16[64,1024]{1,0:T(8,128)(2,1)S(1)}, bf16[64,1024]{1,0:T(8,128)(2,1)S(1)}, u32[]{:S(2)}, u32[]{:S(2)}) collective-permute-start(bf16[64,1024]{1,0:T(8,128)(2,1)S(1)} %fusion.50), channel_id=1, source_target_pairs={{0,4},{2,6},{4,0},{6,2},{8,12},{10,14},{12,8},{14,10},{1,5},{3,7},... | collective-permute-start | bytes 393224 | tf_op jit(solution)/shard_map/ppermute | solution.py:13
  73.5 5.0 %collective-permute-start.14 = (bf16[64,1024]{1,0:T(8,128)(2,1)S(1)}, bf16[64,1024]{1,0:T(8,128)(2,1)S(1)}, u32[]{:S(2)}, u32[]{:S(2)}) collective-permute-start(bf16[64,1024]{1,0:T(8,128)(2,1)S(1)} %fusion.65), channel_id=1, source_target_pairs={{0,4},{2,6},{4,0},{6,2},{8,12},{10,14},{12,8},{14,10},{1,5},{3,7},... | collective-permute-start | bytes 393224 | tf_op jit(solution)/shard_map/ppermute | solution.py:13
  74.7 5.0 %collective-permute-start.12 = (bf16[64,1024]{1,0:T(8,128)(2,1)S(1)}, bf16[64,1024]{1,0:T(8,128)(2,1)S(1)}, u32[]{:S(2)}, u32[]{:S(2)}) collective-permute-start(bf16[64,1024]{1,0:T(8,128)(2,1)S(1)} %fusion.55), channel_id=1, source_target_pairs={{0,2},{2,0},{4,6},{6,4},{8,10},{10,8},{12,14},{14,12},{1,3},{3,1},... | collective-permute-start | bytes 393224 | tf_op jit(solution)/shard_map/ppermute | solution.py:13
  79.8 5.0 %collective-permute-start.15 = (bf16[64,1024]{1,0:T(8,128)(2,1)S(1)}, bf16[64,1024]{1,0:T(8,128)(2,1)S(1)}, u32[]{:S(2)}, u32[]{:S(2)}) collective-permute-start(bf16[64,1024]{1,0:T(8,128)(2,1)S(1)} %fusion.70), channel_id=1, source_target_pairs={{0,2},{2,0},{4,6},{6,4},{8,10},{10,8},{12,14},{14,12},{1,3},{3,1},... | collective-permute-start | bytes 393224 | tf_op jit(solution)/shard_map/ppermute | solution.py:13
  80.2 1.2 %collective-permute-start.17 = (f32[3,128]{1,0:T(4,128)S(1)}, f32[3,128]{1,0:T(4,128)S(1)}, u32[]{:S(2)}, u32[]{:S(2)}) collective-permute-start(f32[3,128]{1,0:T(4,128)S(1)} %maximum_maximum_fusion.1), channel_id=1, source_target_pairs={{0,1},{1,0},{2,3},{3,2},{4,5},{5,4},{6,7},{7,6},{8,9},{9,8},{10,11... | collective-permute-start | bytes 4616 | tf_op jit(solution)/shard_map/ppermute | solution.py:21
  80.3 1.7 %collective-permute-start.16 = (f32[3,128]{1,0:T(4,128)S(1)}, f32[3,128]{1,0:T(4,128)S(1)}, u32[]{:S(2)}, u32[]{:S(2)}) collective-permute-start(f32[3,128]{1,0:T(4,128)S(1)} %maximum_maximum_fusion), channel_id=1, source_target_pairs={{0,1},{1,0},{2,3},{3,2},{4,5},{5,4},{6,7},{7,6},{8,9},{9,8},{10,11... | collective-permute-start | bytes 4616 | tf_op jit(solution)/shard_map/ppermute | solution.py:21
  85.1 1.5 %collective-permute-start.18 = (f32[1,128,128]{2,1,0:T(8,128)S(1)}, f32[1,128,128]{2,1,0:T(8,128)S(1)}, u32[]{:S(2)}, u32[]{:S(2)}) collective-permute-start(f32[1,128,128]{2,1,0:T(8,128)S(1)} %convolution_bitcast_fusion.7), channel_id=1, source_target_pairs={{0,1},{1,0},{2,3},{3,2},{4,5},{5,4},{6,7},{7,6},{8,9},{9,8},{10,11... | collective-permute-start | bytes 196616 | tf_op jit(solution)/shard_map/ppermute | solution.py:21
  (32 other events, 61.9 us)

commit v4 on v2

--- a/solution.py
+++ b/solution.py
@@ -2,6 +2,7 @@
 import jax.numpy as jnp
 from jax import lax
 from jax.sharding import PartitionSpec as P
+from jax.experimental import pallas as pl
 
 D = 2048
 CHUNKS = 2
@@ -11,6 +12,43 @@
     mask = 2**distance
     pairs = [(source, source ^ mask) for source in range(lax.axis_size(axis))]
     return lax.ppermute(value, axis, pairs)
+
+
+def ffn_kernel(normed_ref, cot_ref, wg_ref, wu_ref, wd_ref, out_ref):
+    normed = normed_ref[...]
+    w_gate = wg_ref[0]
+    w_up = wu_ref[0]
+    contract_last = (((1,), (1,)), ((), ()))
+    gate_pre = jnp.dot(normed, w_gate, preferred_element_type=jnp.float32)
+    up_val = jnp.dot(normed, w_up, preferred_element_type=jnp.float32)
+    d_hidden = lax.dot_general(
+        cot_ref[...], wd_ref[0], contract_last, preferred_element_type=jnp.float32
+    )
+    sig = 1.0 / (1.0 + jnp.exp(-gate_pre))
+    d_up = (d_hidden * gate_pre * sig).astype(jnp.bfloat16)
+    d_gate = (d_hidden * up_val * sig * (1.0 + gate_pre * (1.0 - sig))).astype(jnp.bfloat16)
+    out_ref[...] = lax.dot_general(
+        d_gate, w_gate, contract_last, preferred_element_type=jnp.float32
+    ) + lax.dot_general(d_up, w_up, contract_last, preferred_element_type=jnp.float32)
+
+
+def ffn_grad(normed, cotangent, w_gate, w_up, w_down):
+    tok, width = normed.shape
+    groups_here, cblock, hidden = w_gate.shape
+    act = pl.BlockSpec((tok, cblock), lambda g: (0, g))
+    return pl.pallas_call(
+        ffn_kernel,
+        grid=(groups_here,),
+        in_specs=[
+            act,
+            act,
+            pl.BlockSpec((1, cblock, hidden), lambda g: (g, 0, 0)),
+            pl.BlockSpec((1, cblock, hidden), lambda g: (g, 0, 0)),
+            pl.BlockSpec((1, hidden, cblock), lambda g: (g, 0, 0)),
+        ],
+        out_specs=act,
+        out_shape=jax.ShapeDtypeStruct((tok, width), jnp.float32),
+    )(normed, cotangent, w_gate, w_up, w_down)
 
 
 def hid_sum(value):
@@ -43,23 +81,9 @@
     resid = tok_f + tok_f * mixed_f
     square = hid_sum(jnp.sum(resid * resid, axis=-1))
     inv = lax.rsqrt(square / D + 1e-06)
-    normed = (
-        (resid * inv[:, None] * norm_gain).astype(jnp.bfloat16).reshape(tok, groups_here, cblock)
-    )
-    gate_pre = jnp.einsum("tgc,gce->tge", normed, w_gate, preferred_element_type=jnp.float32)
-    up_val = jnp.einsum("tgc,gce->tge", normed, w_up, preferred_element_type=jnp.float32)
-    d_hidden = jnp.einsum(
-        "tgc,gec->tge",
-        cotangent.reshape(tok, groups_here, cblock),
-        w_down,
-        preferred_element_type=jnp.float32,
-    )
-    sig = jax.nn.sigmoid(gate_pre)
-    d_up = (d_hidden * gate_pre * sig).astype(jnp.bfloat16)
-    d_gate = (d_hidden * up_val * sig * (1.0 + gate_pre * (1.0 - sig))).astype(jnp.bfloat16)
-    d_normed = jnp.einsum("tge,gce->tgc", d_gate, w_gate, preferred_element_type=jnp.float32)
-    d_normed = d_normed + jnp.einsum("tge,gce->tgc", d_up, w_up, preferred_element_type=jnp.float32)
-    scaled = norm_gain * d_normed.reshape(tok, width)
+    normed = (resid * inv[:, None] * norm_gain).astype(jnp.bfloat16)
+    d_normed = ffn_grad(normed, cotangent, w_gate, w_up, w_down)
+    scaled = norm_gain * d_normed
     inner = hid_sum(jnp.sum(resid * scaled, axis=-1))
     d_resid = (
         cotangent.astype(jnp.float32)

time: 80.6 us -> 85.2 us (1.057)
  Pallas kernels: 0 us -> 14.8 us
  matrix products: 12.8 us -> 2.36 us
  local copies, waits for them, and re-layouts: 7.23 us -> 2.09 us
  waiting for transfers between devices: 36.2 us -> 40 us
  other arithmetic: 5.54 us -> 7.23 us
    pallas_call x0 -> x2, Pallas kernels: none -> 14.8 us  [ffn_grad(): pl.pallas_call(ffn_kernel, grid=(groups_here,), in_specs=[act, act, pl.Bl...]
    dot_general x8 -> x0, matrix products: 10.3 us -> none  [the longest x2 5.53 us: chain(): jnp.einsum('tge,gce->tgc', d_gate, w_gate, preferred_element_type=jnp.flo...]
    unnamed x87 -> x16, local copies, waits for them, and re-layouts: 7.13 us -> 1.29 us
    ppermute x12, waiting for transfers between devices: 34.2 us -> 38.1 us  [from_partner(): return lax.ppermute(value, axis, pairs)]
    reduce_sum x1, other arithmetic: 0.22 us -> 1.24 us  [chain(): inner = hid_sum(jnp.sum(resid * scaled, axis=-1))]
  transfers between devices with their start and end apart: 19 -> 19, of which waited for: 14 -> 14; matrix products, arithmetic and copies ran while one was open for 8% -> 6% of each run, Pallas kernels for 0% -> 0%
where the time goes in v4:
time: 85.2 us; the launch traced here: 84.6 us
  waiting for transfers between devices  40 us (47%)
  starting transfers between devices  17.3 us (20%)
  Pallas kernels  14.8 us (17%)
  other arithmetic  7.23 us (8%)
  matrix products  2.36 us (3%)
  local copies, waits for them, and re-layouts  2.09 us (2%)
    ppermute x12, waiting for transfers between devices, from_partner(): return lax.ppermute(value, axis, pairs)  38.1 us
    ppermute x12, starting transfers between devices, from_partner(): return lax.ppermute(value, axis, pairs)  16 us
    pallas_call x2, Pallas kernels, ffn_grad(): pl.pallas_call(ffn_kernel, grid=(groups_here,), in_specs=[act, act, pl.Bl...  14.8 us
    ppermute x7, waiting for transfers between devices, hid_sum(): total = total + lax.ppermute(value, 'hid', pairs)  1.99 us
    add x3, other arithmetic, hid_sum(): total = total + lax.ppermute(value, 'hid', pairs)  1.95 us
  transfers between devices with their start and end apart: 19, of which 14 were waited for; matrix products, arithmetic and copies ran while one was open for 6% of the time, Pallas kernels for 0%

profile of v4, /device:TPU:0, one launch (start us, length us, event | category | flops | bytes accessed | tf_op | source)
XLA Modules:
  0.0 84.6 jit_solution(74801532160621846)
XLA Ops:
  0.6 0.7 copy-done
  1.4 1.2 %fusion.2 = bf16[1,128,1024]{2,1,0:T(8,128)(2,1)S(1)} fusion(bf16[128,1024]{1,0:T(8,128)(2,1)} %param.9, bf16[1,128,128]{2,1,0:T(8,128)(2,1)S(1)} %copy-done), kind=kOutput, calls=%fused_computation.4 | convolution fusion | flops 33685504 | bytes 557056 | tf_op jit(solution)/shard_map/kij,kjd->kid/dot_general | solution.py:115
  2.6 3.0 %collective-permute-start.5 = (bf16[64,1024]{1,0:T(8,128)(2,1)S(1)}, bf16[64,1024]{1,0:T(8,128)(2,1)S(1)}, u32[]{:S(2)}, u32[]{:S(2)}) collective-permute-start(bf16[64,1024]{1,0:T(8,128)(2,1)S(1)} %get-tuple-element.36), channel_id=1, source_target_pairs={{0,2},{2,0},{4,6},{6,4},{8,10},{10,8},{12,14},{14,12},{1,3},{3,1},... | collective-permute-start | bytes 393224 | tf_op jit(solution)/shard_map/ppermute | solution.py:14
  5.8 4.2 %collective-permute-done.5 = bf16[64,1024]{1,0:T(8,128)(2,1)S(1)} collective-permute-done((bf16[64,1024]{1,0:T(8,128)(2,1)S(1)}, bf16[64,1024]{1,0:T(8,128)(2,1)S(1)}, u32[]{:S(2)}, u32[]{:S(2)}) %collective-permute-start.5) | collective-permute-done | bytes 131104 | tf_op jit(solution)/shard_map/ppermute | solution.py:14
  9.9 2.0 %collective-permute-done = bf16[64,1024]{1,0:T(8,128)(2,1)S(1)} collective-permute-done((bf16[64,1024]{1,0:T(8,128)(2,1)S(1)}, bf16[64,1024]{1,0:T(8,128)(2,1)S(1)}, u32[]{:S(2)}, u32[]{:S(2)}) %collective-permute-start) | collective-permute-done | bytes 131104 | tf_op jit(solution)/shard_map/ppermute | solution.py:14
  12.1 1.9 %collective-permute-start.6 = (bf16[64,1024]{1,0:T(8,128)(2,1)S(1)}, bf16[64,1024]{1,0:T(8,128)(2,1)S(1)}, u32[]{:S(2)}, u32[]{:S(2)}) collective-permute-start(bf16[64,1024]{1,0:T(8,128)(2,1)S(1)} %get-tuple-element.34), channel_id=1, source_target_pairs={{0,4},{2,6},{4,0},{6,2},{8,12},{10,14},{12,8},{14,10},{1,5},{3,7},... | collective-permute-start | bytes 393224 | tf_op jit(solution)/shard_map/ppermute | solution.py:14
  14.2 4.1 %collective-permute-done.6 = bf16[64,1024]{1,0:T(8,128)(2,1)S(1)} collective-permute-done((bf16[64,1024]{1,0:T(8,128)(2,1)S(1)}, bf16[64,1024]{1,0:T(8,128)(2,1)S(1)}, u32[]{:S(2)}, u32[]{:S(2)}) %collective-permute-start.6) | collective-permute-done | bytes 131104 | tf_op jit(solution)/shard_map/ppermute | solution.py:14
  18.4 2.8 %collective-permute-start.7 = (bf16[64,1024]{1,0:T(8,128)(2,1)S(1)}, bf16[64,1024]{1,0:T(8,128)(2,1)S(1)}, u32[]{:S(2)}, u32[]{:S(2)}) collective-permute-start(bf16[64,1024]{1,0:T(8,128)(2,1)S(1)} %fusion.15), channel_id=1, source_target_pairs={{0,8},{2,10},{4,12},{6,14},{8,0},{10,2},{12,4},{14,6},{1,9},{3,11}... | collective-permute-start | bytes 393224 | tf_op jit(solution)/shard_map/ppermute | solution.py:14
  21.3 2.7 %collective-permute-start.2 = (bf16[64,1024]{1,0:T(8,128)(2,1)S(1)}, bf16[64,1024]{1,0:T(8,128)(2,1)S(1)}, u32[]{:S(2)}, u32[]{:S(2)}) collective-permute-start(bf16[64,1024]{1,0:T(8,128)(2,1)S(1)} %fusion.7), channel_id=1, source_target_pairs={{0,8},{2,10},{4,12},{6,14},{8,0},{10,2},{12,4},{14,6},{1,9},{3,11}... | collective-permute-start | bytes 393224 | tf_op jit(solution)/shard_map/ppermute | solution.py:14
  24.0 5.2 %collective-permute-done.7 = bf16[64,1024]{1,0:T(8,128)(2,1)S(1)} collective-permute-done((bf16[64,1024]{1,0:T(8,128)(2,1)S(1)}, bf16[64,1024]{1,0:T(8,128)(2,1)S(1)}, u32[]{:S(2)}, u32[]{:S(2)}) %collective-permute-start.7) | collective-permute-done | bytes 131104 | tf_op jit(solution)/shard_map/ppermute | solution.py:14
  29.2 1.4 %collective-permute-done.2 = bf16[64,1024]{1,0:T(8,128)(2,1)S(1)} collective-permute-done((bf16[64,1024]{1,0:T(8,128)(2,1)S(1)}, bf16[64,1024]{1,0:T(8,128)(2,1)S(1)}, u32[]{:S(2)}, u32[]{:S(2)}) %collective-permute-start.2) | collective-permute-done | bytes 131104 | tf_op jit(solution)/shard_map/ppermute | solution.py:14
  31.6 0.7 fusion.65
  32.3 1.1 %collective-permute-done.8 = f32[64]{0:T(128)S(1)} collective-permute-done((f32[64]{0:T(128)S(1)}, f32[64]{0:T(128)S(1)}, u32[]{:S(2)}, u32[]{:S(2)}) %collective-permute-start.8) | collective-permute-done | bytes 288 | tf_op jit(solution)/shard_map/ppermute | solution.py:59
  33.5 0.8 multiply_convert_fusion
  34.3 7.4 %shard_map.121 = f32[64,1024]{1,0:T(8,128)} custom-call(bf16[64,1024]{1,0:T(8,128)(2,1)} %get-tuple-element.30.normed_ref, bf16[64,1024]{1,0:T(8,128)(2,1)} %get-tuple-element.32.cot_ref, bf16[8,128,512]{2,1,0:T(8,128)(2,1)} %wg_ref.3, bf16[8,128,512]{2,1,0:T(8,128)(2,1)} %wu_ref.3, bf16[8,512,128]{2,1,0:T(8,128)(2,1)} %wd_ref.3), custom_call_target="tpu_custom_call" | custom-call | tf_op jit(solution)/shard_map/pallas_call | solution.py:39
  41.6 7.4 %shard_map.120 = f32[64,1024]{1,0:T(8,128)} custom-call(bf16[64,1024]{1,0:T(8,128)(2,1)} %get-tuple-element.31.normed_ref, bf16[64,1024]{1,0:T(8,128)(2,1)} %get-tuple-element.33.cot_ref, bf16[8,128,512]{2,1,0:T(8,128)(2,1)} %wg_ref.3, bf16[8,128,512]{2,1,0:T(8,128)(2,1)} %wu_ref.3, bf16[8,512,128]{2,1,0:T(8,128)(2,1)} %wd_ref.3), custom_call_target="tpu_custom_call" | custom-call | tf_op jit(solution)/shard_map/pallas_call | solution.py:39
  49.1 1.2 %multiply_reduce_fusion.2 = (f32[64]{0:T(128)S(1)}, f32[64]{0:T(128)S(1)}) fusion(f32[64,1024]{1,0:T(8,128)} %shard_map.120, bf16[64,1024]{1,0:T(8,128)(2,1)S(1)} %get-tuple-element.26, f32[1024]{0:T(1024)S(1)} %copy-done.5, bf16[128,1024]{1,0:T(8,128)(2,1)S(1)} %copy-done.1, f32[64,1024]{1,0:T(8,128)S(1)} %copy-done.2, ...), kind=kLoop, calls=%fused_computation.100 | loop fusion | flops 917376 | bytes 1053184 | tf_op jit(solution)/shard_map/reduce_sum | solution.py:87
  50.9 0.6 collective-permute-done.4
  52.4 3.0 %collective-permute-start.13 = (bf16[64,1024]{1,0:T(8,128)(2,1)S(1)}, bf16[64,1024]{1,0:T(8,128)(2,1)S(1)}, u32[]{:S(2)}, u32[]{:S(2)}) collective-permute-start(bf16[64,1024]{1,0:T(8,128)(2,1)S(1)} %fusion.36), channel_id=1, source_target_pairs={{0,8},{2,10},{4,12},{6,14},{8,0},{10,2},{12,4},{14,6},{1,9},{3,11}... | collective-permute-start | bytes 393224 | tf_op jit(solution)/shard_map/ppermute | solution.py:14
  55.4 9.2 %collective-permute-done.10 = bf16[64,1024]{1,0:T(8,128)(2,1)S(1)} collective-permute-done((bf16[64,1024]{1,0:T(8,128)(2,1)S(1)}, bf16[64,1024]{1,0:T(8,128)(2,1)S(1)}, u32[]{:S(2)}, u32[]{:S(2)}) %collective-permute-start.10) | collective-permute-done | bytes 131104 | tf_op jit(solution)/shard_map/ppermute | solution.py:14
  65.0 1.9 %collective-permute-done.13 = bf16[64,1024]{1,0:T(8,128)(2,1)S(1)} collective-permute-done((bf16[64,1024]{1,0:T(8,128)(2,1)S(1)}, bf16[64,1024]{1,0:T(8,128)(2,1)S(1)}, u32[]{:S(2)}, u32[]{:S(2)}) %collective-permute-start.13) | collective-permute-done | bytes 131104 | tf_op jit(solution)/shard_map/ppermute | solution.py:14
  67.4 2.9 %collective-permute-done.11 = bf16[64,1024]{1,0:T(8,128)(2,1)S(1)} collective-permute-done((bf16[64,1024]{1,0:T(8,128)(2,1)S(1)}, bf16[64,1024]{1,0:T(8,128)(2,1)S(1)}, u32[]{:S(2)}, u32[]{:S(2)}) %collective-permute-start.11) | collective-permute-done | bytes 131104 | tf_op jit(solution)/shard_map/ppermute | solution.py:14
  70.3 2.5 %collective-permute-done.14 = bf16[64,1024]{1,0:T(8,128)(2,1)S(1)} collective-permute-done((bf16[64,1024]{1,0:T(8,128)(2,1)S(1)}, bf16[64,1024]{1,0:T(8,128)(2,1)S(1)}, u32[]{:S(2)}, u32[]{:S(2)}) %collective-permute-start.14) | collective-permute-done | bytes 131104 | tf_op jit(solution)/shard_map/ppermute | solution.py:14
  73.3 0.5 collective-permute-start.16
  74.0 1.6 %collective-permute-start.15 = (bf16[64,1024]{1,0:T(8,128)(2,1)S(1)}, bf16[64,1024]{1,0:T(8,128)(2,1)S(1)}, u32[]{:S(2)}, u32[]{:S(2)}) collective-permute-start(bf16[64,1024]{1,0:T(8,128)(2,1)S(1)} %fusion.46), channel_id=1, source_target_pairs={{0,2},{2,0},{4,6},{6,4},{8,10},{10,8},{12,14},{14,12},{1,3},{3,1},... | collective-permute-start | bytes 393224 | tf_op jit(solution)/shard_map/ppermute | solution.py:14
  75.6 0.5 collective-permute-start.12
  76.1 0.7 fusion.68
  76.8 0.7 fusion.69
  77.4 3.0 %collective-permute-done.15 = bf16[64,1024]{1,0:T(8,128)(2,1)S(1)} collective-permute-done((bf16[64,1024]{1,0:T(8,128)(2,1)S(1)}, bf16[64,1024]{1,0:T(8,128)(2,1)S(1)}, u32[]{:S(2)}, u32[]{:S(2)}) %collective-permute-start.15) | collective-permute-done | bytes 131104 | tf_op jit(solution)/shard_map/ppermute | solution.py:14
  80.5 1.8 %collective-permute-done.12 = bf16[64,1024]{1,0:T(8,128)(2,1)S(1)} collective-permute-done((bf16[64,1024]{1,0:T(8,128)(2,1)S(1)}, bf16[64,1024]{1,0:T(8,128)(2,1)S(1)}, u32[]{:S(2)}, u32[]{:S(2)}) %collective-permute-start.12) | collective-permute-done | bytes 131104 | tf_op jit(solution)/shard_map/ppermute | solution.py:14
  82.7 1.0 %fusion.1 = bf16[128,1024]{1,0:T(8,128)(2,1)} fusion(f32[64,1024]{1,0:T(8,128)S(1)} %get-tuple-element.28, f32[64,1024]{1,0:T(8,128)S(1)} %get-tuple-element.29, bf16[64,1024]{1,0:T(8,128)(2,1)S(1)} %fusion.45, bf16[64,1024]{1,0:T(8,128)(2,1)S(1)} %fusion.30, bf16[1,128,128]{2,1,0:T(8,128)(2,1)S(1)} %copy-done), kind=kOutput, calls=%fused_computation.2 | convolution fusion | flops 34471936 | bytes 1081344 | tf_op jit(solution)/shard_map/kij,kid->kjd/dot_general | solution.py:136
  84.0 0.6 add.111
  (58 shorter events, 5.7 us)
Async XLA Ops:
  0.6 0.8 copy-start
  2.6 3.1 %copy-start.7 = (f32[3,128]{1,0:T(4,128)S(1)}, f32[3,128]{1,0:T(4,128)}, u32[]{:S(2)}) copy-start(f32[3,128]{1,0:T(4,128)} %param.12) | copy-start | bytes 4612
  2.6 3.1 %copy-start.6 = (f32[3,128]{1,0:T(4,128)S(1)}, f32[3,128]{1,0:T(4,128)}, u32[]{:S(2)}) copy-start(f32[3,128]{1,0:T(4,128)} %param.13) | copy-start | bytes 4612
  2.6 7.3 %collective-permute-start.5 = (bf16[64,1024]{1,0:T(8,128)(2,1)S(1)}, bf16[64,1024]{1,0:T(8,128)(2,1)S(1)}, u32[]{:S(2)}, u32[]{:S(2)}) collective-permute-start(bf16[64,1024]{1,0:T(8,128)(2,1)S(1)} %get-tuple-element.36), channel_id=1, source_target_pairs={{0,2},{2,0},{4,6},{6,4},{8,10},{10,8},{12,14},{14,12},{1,3},{3,1},... | collective-permute-start | bytes 393224 | tf_op jit(solution)/shard_map/ppermute | solution.py:14
  5.6 6.3 %collective-permute-start = (bf16[64,1024]{1,0:T(8,128)(2,1)S(1)}, bf16[64,1024]{1,0:T(8,128)(2,1)S(1)}, u32[]{:S(2)}, u32[]{:S(2)}) collective-permute-start(bf16[64,1024]{1,0:T(8,128)(2,1)S(1)} %get-tuple-element.37), channel_id=1, source_target_pairs={{0,2},{2,0},{4,6},{6,4},{8,10},{10,8},{12,14},{14,12},{1,3},{3,1},... | collective-permute-start | bytes 393224 | tf_op jit(solution)/shard_map/ppermute | solution.py:14
  12.1 6.2 %collective-permute-start.6 = (bf16[64,1024]{1,0:T(8,128)(2,1)S(1)}, bf16[64,1024]{1,0:T(8,128)(2,1)S(1)}, u32[]{:S(2)}, u32[]{:S(2)}) collective-permute-start(bf16[64,1024]{1,0:T(8,128)(2,1)S(1)} %get-tuple-element.34), channel_id=1, source_target_pairs={{0,4},{2,6},{4,0},{6,2},{8,12},{10,14},{12,8},{14,10},{1,5},{3,7},... | collective-permute-start | bytes 393224 | tf_op jit(solution)/shard_map/ppermute | solution.py:14
  14.0 7.2 %collective-permute-start.1 = (bf16[64,1024]{1,0:T(8,128)(2,1)S(1)}, bf16[64,1024]{1,0:T(8,128)(2,1)S(1)}, u32[]{:S(2)}, u32[]{:S(2)}) collective-permute-start(bf16[64,1024]{1,0:T(8,128)(2,1)S(1)} %get-tuple-element.35), channel_id=1, source_target_pairs={{0,4},{2,6},{4,0},{6,2},{8,12},{10,14},{12,8},{14,10},{1,5},{3,7},... | collective-permute-start | bytes 393224 | tf_op jit(solution)/shard_map/ppermute | solution.py:14
  18.4 12.3 %copy-start.1 = (bf16[128,1024]{1,0:T(8,128)(2,1)S(1)}, bf16[128,1024]{1,0:T(8,128)(2,1)}, u32[]{:S(2)}) copy-start(bf16[128,1024]{1,0:T(8,128)(2,1)} %param.9) | copy-start | bytes 786436
  18.4 10.9 %collective-permute-start.7 = (bf16[64,1024]{1,0:T(8,128)(2,1)S(1)}, bf16[64,1024]{1,0:T(8,128)(2,1)S(1)}, u32[]{:S(2)}, u32[]{:S(2)}) collective-permute-start(bf16[64,1024]{1,0:T(8,128)(2,1)S(1)} %fusion.15), channel_id=1, source_target_pairs={{0,8},{2,10},{4,12},{6,14},{8,0},{10,2},{12,4},{14,6},{1,9},{3,11}... | collective-permute-start | bytes 393224 | tf_op jit(solution)/shard_map/ppermute | solution.py:14
  21.3 9.3 %collective-permute-start.2 = (bf16[64,1024]{1,0:T(8,128)(2,1)S(1)}, bf16[64,1024]{1,0:T(8,128)(2,1)S(1)}, u32[]{:S(2)}, u32[]{:S(2)}) collective-permute-start(bf16[64,1024]{1,0:T(8,128)(2,1)S(1)} %fusion.7), channel_id=1, source_target_pairs={{0,8},{2,10},{4,12},{6,14},{8,0},{10,2},{12,4},{14,6},{1,9},{3,11}... | collective-permute-start | bytes 393224 | tf_op jit(solution)/shard_map/ppermute | solution.py:14
  30.7 1.0 %copy-start.4 = (bf16[128,1024]{1,0:T(8,128)(2,1)S(1)}, bf16[128,1024]{1,0:T(8,128)(2,1)}, u32[]{:S(2)}) copy-start(bf16[128,1024]{1,0:T(8,128)(2,1)} %param.10) | copy-start | bytes 786436
  31.0 1.3 %collective-permute-start.3 = (f32[64]{0:T(128)S(1)}, f32[64]{0:T(128)S(1)}, u32[]{:S(2)}, u32[]{:S(2)}) collective-permute-start(f32[64]{0:T(128)S(1)} %get-tuple-element.8), channel_id=1, source_target_pairs={{0,1},{1,0},{2,3},{3,2},{4,5},{5,4},{6,7},{7,6},{8,9},{9,8},{10,11... | collective-permute-start | bytes 776 | tf_op jit(solution)/shard_map/ppermute | solution.py:59
  32.3 1.1 %copy-start.5 = (f32[1024]{0:T(1024)S(1)}, f32[1024]{0:T(1024)}, u32[]{:S(2)}) copy-start(f32[1024]{0:T(1024)} %param.14) | copy-start | bytes 12292
  32.3 1.1 %collective-permute-start.8 = (f32[64]{0:T(128)S(1)}, f32[64]{0:T(128)S(1)}, u32[]{:S(2)}, u32[]{:S(2)}) collective-permute-start(f32[64]{0:T(128)S(1)} %get-tuple-element.9), channel_id=1, source_target_pairs={{0,1},{1,0},{2,3},{3,2},{4,5},{5,4},{6,7},{7,6},{8,9},{9,8},{10,11... | collective-permute-start | bytes 776 | tf_op jit(solution)/shard_map/ppermute | solution.py:59
  41.6 7.4 %copy-start.2 = (f32[64,1024]{1,0:T(8,128)S(1)}, f32[64,1024]{1,0:T(8,128)}, u32[]{:S(2)}) copy-start(f32[64,1024]{1,0:T(8,128)} %shard_map.121) | copy-start | bytes 786436
  49.0 2.4 %copy-start.3 = (f32[64,1024]{1,0:T(8,128)S(1)}, f32[64,1024]{1,0:T(8,128)}, u32[]{:S(2)}) copy-start(f32[64,1024]{1,0:T(8,128)} %shard_map.120) | copy-start | bytes 786436
  50.3 1.2 %collective-permute-start.4 = (f32[64]{0:T(128)S(1)}, f32[64]{0:T(128)S(1)}, u32[]{:S(2)}, u32[]{:S(2)}) collective-permute-start(f32[64]{0:T(128)S(1)} %get-tuple-element.4), channel_id=1, source_target_pairs={{0,1},{1,0},{2,3},{3,2},{4,5},{5,4},{6,7},{7,6},{8,9},{9,8},{10,11... | collective-permute-start | bytes 776 | tf_op jit(solution)/shard_map/ppermute | solution.py:59
  50.6 1.4 %collective-permute-start.9 = (f32[64]{0:T(128)S(1)}, f32[64]{0:T(128)S(1)}, u32[]{:S(2)}, u32[]{:S(2)}) collective-permute-start(f32[64]{0:T(128)S(1)} %get-tuple-element.5), channel_id=1, source_target_pairs={{0,1},{1,0},{2,3},{3,2},{4,5},{5,4},{6,7},{7,6},{8,9},{9,8},{10,11... | collective-permute-start | bytes 776 | tf_op jit(solution)/shard_map/ppermute | solution.py:59
  51.9 12.6 %collective-permute-start.10 = (bf16[64,1024]{1,0:T(8,128)(2,1)S(1)}, bf16[64,1024]{1,0:T(8,128)(2,1)S(1)}, u32[]{:S(2)}, u32[]{:S(2)}) collective-permute-start(bf16[64,1024]{1,0:T(8,128)(2,1)S(1)} %fusion.21), channel_id=1, source_target_pairs={{0,8},{2,10},{4,12},{6,14},{8,0},{10,2},{12,4},{14,6},{1,9},{3,11}... | collective-permute-start | bytes 393224 | tf_op jit(solution)/shard_map/ppermute | solution.py:14
  52.4 14.5 %collective-permute-start.13 = (bf16[64,1024]{1,0:T(8,128)(2,1)S(1)}, bf16[64,1024]{1,0:T(8,128)(2,1)S(1)}, u32[]{:S(2)}, u32[]{:S(2)}) collective-permute-start(bf16[64,1024]{1,0:T(8,128)(2,1)S(1)} %fusion.36), channel_id=1, source_target_pairs={{0,8},{2,10},{4,12},{6,14},{8,0},{10,2},{12,4},{14,6},{1,9},{3,11}... | collective-permute-start | bytes 393224 | tf_op jit(solution)/shard_map/ppermute | solution.py:14
  64.9 5.4 %collective-permute-start.11 = (bf16[64,1024]{1,0:T(8,128)(2,1)S(1)}, bf16[64,1024]{1,0:T(8,128)(2,1)S(1)}, u32[]{:S(2)}, u32[]{:S(2)}) collective-permute-start(bf16[64,1024]{1,0:T(8,128)(2,1)S(1)} %fusion.26), channel_id=1, source_target_pairs={{0,4},{2,6},{4,0},{6,2},{8,12},{10,14},{12,8},{14,10},{1,5},{3,7},... | collective-permute-start | bytes 393224 | tf_op jit(solution)/shard_map/ppermute | solution.py:14
  67.3 5.5 %collective-permute-start.14 = (bf16[64,1024]{1,0:T(8,128)(2,1)S(1)}, bf16[64,1024]{1,0:T(8,128)(2,1)S(1)}, u32[]{:S(2)}, u32[]{:S(2)}) collective-permute-start(bf16[64,1024]{1,0:T(8,128)(2,1)S(1)} %fusion.41), channel_id=1, source_target_pairs={{0,4},{2,6},{4,0},{6,2},{8,12},{10,14},{12,8},{14,10},{1,5},{3,7},... | collective-permute-start | bytes 393224 | tf_op jit(solution)/shard_map/ppermute | solution.py:14
  73.2 2.9 %collective-permute-start.17 = (f32[3,128]{1,0:T(4,128)S(1)}, f32[3,128]{1,0:T(4,128)S(1)}, u32[]{:S(2)}, u32[]{:S(2)}) collective-permute-start(f32[3,128]{1,0:T(4,128)S(1)} %maximum_maximum_fusion.1), channel_id=1, source_target_pairs={{0,1},{1,0},{2,3},{3,2},{4,5},{5,4},{6,7},{7,6},{8,9},{9,8},{10,11... | collective-permute-start | bytes 4616 | tf_op jit(solution)/shard_map/ppermute | solution.py:59
  73.3 3.4 %collective-permute-start.16 = (f32[3,128]{1,0:T(4,128)S(1)}, f32[3,128]{1,0:T(4,128)S(1)}, u32[]{:S(2)}, u32[]{:S(2)}) collective-permute-start(f32[3,128]{1,0:T(4,128)S(1)} %maximum_maximum_fusion), channel_id=1, source_target_pairs={{0,1},{1,0},{2,3},{3,2},{4,5},{5,4},{6,7},{7,6},{8,9},{9,8},{10,11... | collective-permute-start | bytes 4616 | tf_op jit(solution)/shard_map/ppermute | solution.py:59
  74.0 6.4 %collective-permute-start.15 = (bf16[64,1024]{1,0:T(8,128)(2,1)S(1)}, bf16[64,1024]{1,0:T(8,128)(2,1)S(1)}, u32[]{:S(2)}, u32[]{:S(2)}) collective-permute-start(bf16[64,1024]{1,0:T(8,128)(2,1)S(1)} %fusion.46), channel_id=1, source_target_pairs={{0,2},{2,0},{4,6},{6,4},{8,10},{10,8},{12,14},{14,12},{1,3},{3,1},... | collective-permute-start | bytes 393224 | tf_op jit(solution)/shard_map/ppermute | solution.py:14
  75.6 6.7 %collective-permute-start.12 = (bf16[64,1024]{1,0:T(8,128)(2,1)S(1)}, bf16[64,1024]{1,0:T(8,128)(2,1)S(1)}, u32[]{:S(2)}, u32[]{:S(2)}) collective-permute-start(bf16[64,1024]{1,0:T(8,128)(2,1)S(1)} %fusion.31), channel_id=1, source_target_pairs={{0,2},{2,0},{4,6},{6,4},{8,10},{10,8},{12,14},{14,12},{1,3},{3,1},... | collective-permute-start | bytes 393224 | tf_op jit(solution)/shard_map/ppermute | solution.py:14
  82.7 1.3 %collective-permute-start.18 = (f32[1,128,128]{2,1,0:T(8,128)S(1)}, f32[1,128,128]{2,1,0:T(8,128)S(1)}, u32[]{:S(2)}, u32[]{:S(2)}) collective-permute-start(f32[1,128,128]{2,1,0:T(8,128)S(1)} %convolution_bitcast_fusion.1), channel_id=1, source_target_pairs={{0,1},{1,0},{2,3},{3,2},{4,5},{5,4},{6,7},{7,6},{8,9},{9,8},{10,11... | collective-permute-start | bytes 196616 | tf_op jit(solution)/shard_map/ppermute | solution.py:59

commit v5 on v1

--- a/solution.py
+++ b/solution.py
@@ -2,6 +2,7 @@
 import jax.numpy as jnp
 from jax import lax
 from jax.sharding import PartitionSpec as P
+from jax.experimental import pallas as pl
 
 D = 2048
 
@@ -10,6 +11,48 @@
     mask = 2**distance
     pairs = [(source, source ^ mask) for source in range(lax.axis_size(axis))]
     return lax.ppermute(value, axis, pairs)
+
+
+def ffn_kernel(normed_ref, cot_ref, wg_ref, wu_ref, wd_ref, out_ref):
+    cblock = wg_ref.shape[1]
+    contract_last = (((1,), (1,)), ((), ()))
+    for group in range(wg_ref.shape[0]):
+        cols = slice(group * cblock, (group + 1) * cblock)
+        normed = normed_ref[:, cols]
+        w_gate = wg_ref[group]
+        w_up = wu_ref[group]
+        gate_pre = jnp.dot(normed, w_gate, preferred_element_type=jnp.float32)
+        up_val = jnp.dot(normed, w_up, preferred_element_type=jnp.float32)
+        d_hidden = lax.dot_general(
+            cot_ref[:, cols], wd_ref[group], contract_last, preferred_element_type=jnp.float32
+        )
+        sig = 1.0 / (1.0 + jnp.exp(-gate_pre))
+        d_up = (d_hidden * gate_pre * sig).astype(jnp.bfloat16)
+        d_gate = (d_hidden * up_val * sig * (1.0 + gate_pre * (1.0 - sig))).astype(jnp.bfloat16)
+        out_ref[:, cols] = lax.dot_general(
+            d_gate, w_gate, contract_last, preferred_element_type=jnp.float32
+        ) + lax.dot_general(d_up, w_up, contract_last, preferred_element_type=jnp.float32)
+
+
+def ffn_grad(normed, cotangent, w_gate, w_up, w_down, per_step=4):
+    tok, width = normed.shape
+    groups_here, cblock, hidden = w_gate.shape
+    if groups_here % per_step:
+        per_step = 1
+    act = pl.BlockSpec((tok, cblock * per_step), lambda g: (0, g))
+    return pl.pallas_call(
+        ffn_kernel,
+        grid=(groups_here // per_step,),
+        in_specs=[
+            act,
+            act,
+            pl.BlockSpec((per_step, cblock, hidden), lambda g: (g, 0, 0)),
+            pl.BlockSpec((per_step, cblock, hidden), lambda g: (g, 0, 0)),
+            pl.BlockSpec((per_step, hidden, cblock), lambda g: (g, 0, 0)),
+        ],
+        out_specs=act,
+        out_shape=jax.ShapeDtypeStruct((tok, width), jnp.float32),
+    )(normed, cotangent, w_gate, w_up, w_down)
 
 
 def hid_sum(value):
@@ -26,8 +69,6 @@
     sections = lax.axis_size("seq").bit_length() - 1
     nblk = blocks.shape[0]
     blen = blocks.shape[1]
-    groups_here = w_gate.shape[0]
-    cblock = w_gate.shape[1]
     tok_blocks = tokens.reshape(nblk, blen, width)
     local = jnp.einsum("kij,kjd->kid", blocks, tok_blocks, preferred_element_type=jnp.float32)
     local = local.astype(jnp.bfloat16).reshape(tok, width)
@@ -47,23 +88,9 @@
     resid = tok_f + tok_f * mixed_f
     square = hid_sum(jnp.sum(resid * resid, axis=-1))
     inv = lax.rsqrt(square / D + 1e-06)
-    normed = (
-        (resid * inv[:, None] * norm_gain).astype(jnp.bfloat16).reshape(tok, groups_here, cblock)
-    )
-    gate_pre = jnp.einsum("tgc,gce->tge", normed, w_gate, preferred_element_type=jnp.float32)
-    up_val = jnp.einsum("tgc,gce->tge", normed, w_up, preferred_element_type=jnp.float32)
-    d_hidden = jnp.einsum(
-        "tgc,gec->tge",
-        cotangent.reshape(tok, groups_here, cblock),
-        w_down,
-        preferred_element_type=jnp.float32,
-    )
-    sig = jax.nn.sigmoid(gate_pre)
-    d_up = (d_hidden * gate_pre * sig).astype(jnp.bfloat16)
-    d_gate = (d_hidden * up_val * sig * (1.0 + gate_pre * (1.0 - sig))).astype(jnp.bfloat16)
-    d_normed = jnp.einsum("tge,gce->tgc", d_gate, w_gate, preferred_element_type=jnp.float32)
-    d_normed = d_normed + jnp.einsum("tge,gce->tgc", d_up, w_up, preferred_element_type=jnp.float32)
-    scaled = norm_gain * d_normed.reshape(tok, width)
+    normed = (resid * inv[:, None] * norm_gain).astype(jnp.bfloat16)
+    d_normed = ffn_grad(normed, cotangent, w_gate, w_up, w_down)
+    scaled = norm_gain * d_normed
     inner = hid_sum(jnp.sum(resid * scaled, axis=-1))
     d_resid = (
         cotangent.astype(jnp.float32)

time: 85 us -> 78.4 us (0.922)
  matrix products: 14.4 us -> 2.58 us
  Pallas kernels: 0 us -> 4.81 us
  local copies, waits for them, and re-layouts: 2.79 us -> 0.76 us
  waiting for transfers between devices: 51.6 us -> 53.5 us
  other arithmetic: 5.11 us -> 6.09 us
    dot_general x4 -> x0, matrix products: 11.7 us -> none  [the longest x1 4.17 us: body(): jnp.einsum('tge,gce->tgc', d_up, w_up, preferred_element_type=jnp.float32)]
    pallas_call x0 -> x1, Pallas kernels: none -> 4.81 us  [ffn_grad(): pl.pallas_call(ffn_kernel, grid=(groups_here // per_step,), in_specs=[act...]
    reshape x1 -> x0, local copies, waits for them, and re-layouts: 1.24 us -> none  [body(): scaled = norm_gain * d_normed.reshape(tok, width)]
    ppermute x5, waiting for transfers between devices: 0.91 us -> 2.14 us  [hid_sum(): total = total + lax.ppermute(value, 'hid', pairs)]
    reduce_sum x1, other arithmetic: 0.2 us -> 1.31 us  [body(): inner = hid_sum(jnp.sum(resid * scaled, axis=-1))]
    reduce_sum x3, other arithmetic: 2.05 us -> 1.1 us  [body(): jnp.sum(back_f * mates[section].astype(jnp.float32), axis=-1)]
  transfers between devices with their start and end apart: 11 -> 11, of which waited for: 8 -> 9; matrix products, arithmetic and copies ran while one was open for 6% -> 3% of each run, Pallas kernels for 0% -> 0%
where the time goes in v5:
time: 78.4 us; the launch traced here: 78.2 us
  waiting for transfers between devices  53.5 us (68%)
  starting transfers between devices  9.63 us (12%)
  other arithmetic  6.09 us (8%)
  Pallas kernels  4.81 us (6%)
  matrix products  2.58 us (3%)
    ppermute x6, waiting for transfers between devices, from_partner(): return lax.ppermute(value, axis, pairs)  51.4 us
    ppermute x6, starting transfers between devices, from_partner(): return lax.ppermute(value, axis, pairs)  8.6 us
    pallas_call x1, Pallas kernels, ffn_grad(): pl.pallas_call(ffn_kernel, grid=(groups_here // per_step,), in_specs=[act...  4.81 us
    ppermute x5, waiting for transfers between devices, hid_sum(): total = total + lax.ppermute(value, 'hid', pairs)  2.14 us
    add x3, other arithmetic, hid_sum(): total = total + lax.ppermute(value, 'hid', pairs)  1.81 us
  transfers between devices with their start and end apart: 11, of which 9 were waited for; matrix products, arithmetic and copies ran while one was open for 3% of the time, Pallas kernels for 0%

profile of v5, /device:TPU:0, one launch (start us, length us, event | category | flops | bytes accessed | tf_op | source)
XLA Modules:
  0.0 78.2 jit_solution(10729940081137293834)
XLA Ops:
  0.7 0.7 copy-done
  1.4 1.2 %convolution_convert_fusion = bf16[128,1024]{1,0:T(8,128)(2,1)S(1)} fusion(bf16[128,1024]{1,0:T(8,128)(2,1)} %param.9, bf16[1,128,128]{2,1,0:T(8,128)(2,1)S(1)} %copy-done), kind=kOutput, calls=%fused_computation.3 | convolution fusion | flops 33685504 | bytes 557056 | tf_op jit(solution)/shard_map/kij,kjd->kid/dot_general | solution.py:73
  2.6 3.0 %collective-permute-start = (bf16[128,1024]{1,0:T(8,128)(2,1)S(1)}, bf16[128,1024]{1,0:T(8,128)(2,1)S(1)}, u32[]{:S(2)}, u32[]{:S(2)}) collective-permute-start(bf16[128,1024]{1,0:T(8,128)(2,1)S(1)} %convolution_convert_fusion), channel_id=1, source_target_pairs={{0,2},{2,0},{4,6},{6,4},{8,10},{10,8},{12,14},{14,12},{1,3},{3,1},... | collective-permute-start | bytes 786440 | tf_op jit(solution)/shard_map/ppermute | solution.py:13
  5.6 6.3 %collective-permute-done = bf16[128,1024]{1,0:T(8,128)(2,1)S(1)} collective-permute-done((bf16[128,1024]{1,0:T(8,128)(2,1)S(1)}, bf16[128,1024]{1,0:T(8,128)(2,1)S(1)}, u32[]{:S(2)}, u32[]{:S(2)}) %collective-permute-start) | collective-permute-done | bytes 262176 | tf_op jit(solution)/shard_map/ppermute | solution.py:13
  11.9 0.2 fusion.4
  12.0 1.9 %collective-permute-start.1 = (bf16[128,1024]{1,0:T(8,128)(2,1)S(1)}, bf16[128,1024]{1,0:T(8,128)(2,1)S(1)}, u32[]{:S(2)}, u32[]{:S(2)}) collective-permute-start(bf16[128,1024]{1,0:T(8,128)(2,1)S(1)} %fusion.4), channel_id=1, source_target_pairs={{0,4},{2,6},{4,0},{6,2},{8,12},{10,14},{12,8},{14,10},{1,5},{3,7},... | collective-permute-start | bytes 786440 | tf_op jit(solution)/shard_map/ppermute | solution.py:13
  13.9 5.7 %collective-permute-done.1 = bf16[128,1024]{1,0:T(8,128)(2,1)S(1)} collective-permute-done((bf16[128,1024]{1,0:T(8,128)(2,1)S(1)}, bf16[128,1024]{1,0:T(8,128)(2,1)S(1)}, u32[]{:S(2)}, u32[]{:S(2)}) %collective-permute-start.1) | collective-permute-done | bytes 262176 | tf_op jit(solution)/shard_map/ppermute | solution.py:13
  19.6 0.2 fusion.6
  19.8 2.6 %collective-permute-start.2 = (bf16[128,1024]{1,0:T(8,128)(2,1)S(1)}, bf16[128,1024]{1,0:T(8,128)(2,1)S(1)}, u32[]{:S(2)}, u32[]{:S(2)}) collective-permute-start(bf16[128,1024]{1,0:T(8,128)(2,1)S(1)} %fusion.6), channel_id=1, source_target_pairs={{0,8},{2,10},{4,12},{6,14},{8,0},{10,2},{12,4},{14,6},{1,9},{3,11}... | collective-permute-start | bytes 786440 | tf_op jit(solution)/shard_map/ppermute | solution.py:13
  22.4 10.6 %collective-permute-done.2 = bf16[128,1024]{1,0:T(8,128)(2,1)S(1)} collective-permute-done((bf16[128,1024]{1,0:T(8,128)(2,1)S(1)}, bf16[128,1024]{1,0:T(8,128)(2,1)S(1)}, u32[]{:S(2)}, u32[]{:S(2)}) %collective-permute-start.2) | collective-permute-done | bytes 262176 | tf_op jit(solution)/shard_map/ppermute | solution.py:13
  32.9 0.4 multiply_reduce_fusion.1
  33.4 1.1 %collective-permute-done.3 = f32[128]{0:T(128)S(1)} collective-permute-done((f32[128]{0:T(128)S(1)}, f32[128]{0:T(128)S(1)}, u32[]{:S(2)}, u32[]{:S(2)}) %collective-permute-start.3) | collective-permute-done | bytes 544 | tf_op jit(solution)/shard_map/ppermute | solution.py:63
  34.5 0.8 %multiply_convert_fusion.normed_ref = bf16[128,1024]{1,0:T(8,128)(2,1)} fusion(bf16[128,1024]{1,0:T(8,128)(2,1)S(1)} %get-tuple-element.14, bf16[128,1024]{1,0:T(8,128)(2,1)S(1)} %copy-done.1, f32[1024]{0:T(1024)S(1)} %copy-done.4, f32[128]{0:T(128)S(1)} %add_rsqrt_fusion), kind=kLoop, calls=%fused_computation.51 | loop fusion | flops 917504 | bytes 791040 | tf_op jit(solution)/shard_map/convert_element_type | solution.py:91
  35.3 4.8 %shard_map.120 = f32[128,1024]{1,0:T(8,128)} custom-call(bf16[128,1024]{1,0:T(8,128)(2,1)} %multiply_convert_fusion.normed_ref, bf16[128,1024]{1,0:T(8,128)(2,1)} %cot_ref.1, bf16[8,128,512]{2,1,0:T(8,128)(2,1)} %wg_ref.1, bf16[8,128,512]{2,1,0:T(8,128)(2,1)} %wu_ref.1, bf16[8,512,128]{2,1,0:T(8,128)(2,1)} %wd_ref.1), custom_call_target="tpu_custom_call" | custom-call | tf_op jit(solution)/shard_map/pallas_call | solution.py:43
  40.1 1.3 %multiply_reduce_fusion = f32[128]{0:T(128)S(1)} fusion(f32[128,1024]{1,0:T(8,128)} %shard_map.120, bf16[128,1024]{1,0:T(8,128)(2,1)S(1)} %get-tuple-element.14, bf16[128,1024]{1,0:T(8,128)(2,1)S(1)} %copy-done.1, f32[1024]{0:T(1024)S(1)} %copy-done.4), kind=kLoop, calls=%fused_computation.50 | loop fusion | flops 917376 | bytes 1053184 | tf_op jit(solution)/shard_map/reduce_sum | solution.py:94
  41.4 0.3 collective-permute-start.4
  41.7 0.9 %collective-permute-done.4 = f32[128]{0:T(128)S(1)} collective-permute-done((f32[128]{0:T(128)S(1)}, f32[128]{0:T(128)S(1)}, u32[]{:S(2)}, u32[]{:S(2)}) %collective-permute-start.4) | collective-permute-done | bytes 544 | tf_op jit(solution)/shard_map/ppermute | solution.py:63
  42.6 0.4 fusion.14
  43.1 0.1 fusion.12
  43.3 14.9 %collective-permute-done.5 = bf16[128,1024]{1,0:T(8,128)(2,1)S(1)} collective-permute-done((bf16[128,1024]{1,0:T(8,128)(2,1)S(1)}, bf16[128,1024]{1,0:T(8,128)(2,1)S(1)}, u32[]{:S(2)}, u32[]{:S(2)}) %collective-permute-start.5) | collective-permute-done | bytes 262176 | tf_op jit(solution)/shard_map/ppermute | solution.py:13
  58.2 0.3 fusion.19
  58.7 7.8 %collective-permute-done.6 = bf16[128,1024]{1,0:T(8,128)(2,1)S(1)} collective-permute-done((bf16[128,1024]{1,0:T(8,128)(2,1)S(1)}, bf16[128,1024]{1,0:T(8,128)(2,1)S(1)}, u32[]{:S(2)}, u32[]{:S(2)}) %collective-permute-start.6) | collective-permute-done | bytes 262176 | tf_op jit(solution)/shard_map/ppermute | solution.py:13
  66.5 0.3 fusion.24
  66.9 0.5 collective-permute-start.8
  67.6 1.0 %collective-permute-start.7 = (bf16[128,1024]{1,0:T(8,128)(2,1)S(1)}, bf16[128,1024]{1,0:T(8,128)(2,1)S(1)}, u32[]{:S(2)}, u32[]{:S(2)}) collective-permute-start(bf16[128,1024]{1,0:T(8,128)(2,1)S(1)} %fusion.22), channel_id=1, source_target_pairs={{0,2},{2,0},{4,6},{6,4},{8,10},{10,8},{12,14},{14,12},{1,3},{3,1},... | collective-permute-start | bytes 786440 | tf_op jit(solution)/shard_map/ppermute | solution.py:13
  68.6 0.6 fusion.29
  69.2 0.6 fusion.30
  69.8 6.1 %collective-permute-done.7 = bf16[128,1024]{1,0:T(8,128)(2,1)S(1)} collective-permute-done((bf16[128,1024]{1,0:T(8,128)(2,1)S(1)}, bf16[128,1024]{1,0:T(8,128)(2,1)S(1)}, u32[]{:S(2)}, u32[]{:S(2)}) %collective-permute-start.7) | collective-permute-done | bytes 262176 | tf_op jit(solution)/shard_map/ppermute | solution.py:13
  75.9 0.3 convolution_bitcast_fusion.1
  76.3 1.1 %fusion.1 = bf16[128,1024]{1,0:T(8,128)(2,1)} fusion(bf16[128,1024]{1,0:T(8,128)(2,1)S(1)} %get-tuple-element.14, bf16[1,128,128]{2,1,0:T(8,128)(2,1)S(1)} %copy-done, bf16[128,1024]{1,0:T(8,128)(2,1)S(1)} %get-tuple-element.10, bf16[128,1024]{1,0:T(8,128)(2,1)S(1)} %collective-permute-done.7, f32[128]{0:T(128)S(1)} %get-tuple-element.22, ...), kind=kOutput, calls=%fused_computation.2 | convolution fusion | flops 36044800 | bytes 2135552 | tf_op jit(solution)/shard_map/kij,kid->kjd/dot_general | solution.py:119
  77.4 0.1 collective-permute-done.10
  77.5 0.6 add.71
  (27 shorter events, 0.6 us)
Async XLA Ops:
  0.6 0.8 copy-start
  0.6 4.9 %copy-start.5 = (f32[3,128]{1,0:T(4,128)S(1)}, f32[3,128]{1,0:T(4,128)}, u32[]{:S(2)}) copy-start(f32[3,128]{1,0:T(4,128)} %param.13) | copy-start | bytes 4612
  0.7 4.9 %copy-start.6 = (f32[3,128]{1,0:T(4,128)S(1)}, f32[3,128]{1,0:T(4,128)}, u32[]{:S(2)}) copy-start(f32[3,128]{1,0:T(4,128)} %param.12) | copy-start | bytes 4612
  2.6 9.3 %collective-permute-start = (bf16[128,1024]{1,0:T(8,128)(2,1)S(1)}, bf16[128,1024]{1,0:T(8,128)(2,1)S(1)}, u32[]{:S(2)}, u32[]{:S(2)}) collective-permute-start(bf16[128,1024]{1,0:T(8,128)(2,1)S(1)} %convolution_convert_fusion), channel_id=1, source_target_pairs={{0,2},{2,0},{4,6},{6,4},{8,10},{10,8},{12,14},{14,12},{1,3},{3,1},... | collective-permute-start | bytes 786440 | tf_op jit(solution)/shard_map/ppermute | solution.py:13
  12.0 7.6 %collective-permute-start.1 = (bf16[128,1024]{1,0:T(8,128)(2,1)S(1)}, bf16[128,1024]{1,0:T(8,128)(2,1)S(1)}, u32[]{:S(2)}, u32[]{:S(2)}) collective-permute-start(bf16[128,1024]{1,0:T(8,128)(2,1)S(1)} %fusion.4), channel_id=1, source_target_pairs={{0,4},{2,6},{4,0},{6,2},{8,12},{10,14},{12,8},{14,10},{1,5},{3,7},... | collective-permute-start | bytes 786440 | tf_op jit(solution)/shard_map/ppermute | solution.py:13
  19.6 13.3 %copy-start.1 = (bf16[128,1024]{1,0:T(8,128)(2,1)S(1)}, bf16[128,1024]{1,0:T(8,128)(2,1)}, u32[]{:S(2)}) copy-start(bf16[128,1024]{1,0:T(8,128)(2,1)} %param.9) | copy-start | bytes 786436
  19.8 13.2 %collective-permute-start.2 = (bf16[128,1024]{1,0:T(8,128)(2,1)S(1)}, bf16[128,1024]{1,0:T(8,128)(2,1)S(1)}, u32[]{:S(2)}, u32[]{:S(2)}) collective-permute-start(bf16[128,1024]{1,0:T(8,128)(2,1)S(1)} %fusion.6), channel_id=1, source_target_pairs={{0,8},{2,10},{4,12},{6,14},{8,0},{10,2},{12,4},{14,6},{1,9},{3,11}... | collective-permute-start | bytes 786440 | tf_op jit(solution)/shard_map/ppermute | solution.py:13
  33.3 1.2 %copy-start.4 = (f32[1024]{0:T(1024)S(1)}, f32[1024]{0:T(1024)}, u32[]{:S(2)}) copy-start(f32[1024]{0:T(1024)} %param.14) | copy-start | bytes 12292
  33.3 1.2 %collective-permute-start.3 = (f32[128]{0:T(128)S(1)}, f32[128]{0:T(128)S(1)}, u32[]{:S(2)}, u32[]{:S(2)}) collective-permute-start(f32[128]{0:T(128)S(1)} %get-tuple-element.13), channel_id=1, source_target_pairs={{0,1},{1,0},{2,3},{3,2},{4,5},{5,4},{6,7},{7,6},{8,9},{9,8},{10,11... | collective-permute-start | bytes 1544 | tf_op jit(solution)/shard_map/ppermute | solution.py:63
  40.1 2.5 %copy-start.2 = (f32[128,1024]{1,0:T(8,128)S(1)}, f32[128,1024]{1,0:T(8,128)}, u32[]{:S(2)}) copy-start(f32[128,1024]{1,0:T(8,128)} %shard_map.120) | copy-start | bytes 1572868
  40.1 2.5 %copy-start.3 = (bf16[128,1024]{1,0:T(8,128)(2,1)S(1)}, bf16[128,1024]{1,0:T(8,128)(2,1)}, u32[]{:S(2)}) copy-start(bf16[128,1024]{1,0:T(8,128)(2,1)} %cot_ref.1) | copy-start | bytes 786436
  41.4 1.2 %collective-permute-start.4 = (f32[128]{0:T(128)S(1)}, f32[128]{0:T(128)S(1)}, u32[]{:S(2)}, u32[]{:S(2)}) collective-permute-start(f32[128]{0:T(128)S(1)} %multiply_reduce_fusion), channel_id=1, source_target_pairs={{0,1},{1,0},{2,3},{3,2},{4,5},{5,4},{6,7},{7,6},{8,9},{9,8},{10,11... | collective-permute-start | bytes 1544 | tf_op jit(solution)/shard_map/ppermute | solution.py:63
  43.2 15.0 %collective-permute-start.5 = (bf16[128,1024]{1,0:T(8,128)(2,1)S(1)}, bf16[128,1024]{1,0:T(8,128)(2,1)S(1)}, u32[]{:S(2)}, u32[]{:S(2)}) collective-permute-start(bf16[128,1024]{1,0:T(8,128)(2,1)S(1)} %fusion.12), channel_id=1, source_target_pairs={{0,8},{2,10},{4,12},{6,14},{8,0},{10,2},{12,4},{14,6},{1,9},{3,11}... | collective-permute-start | bytes 786440 | tf_op jit(solution)/shard_map/ppermute | solution.py:13
  58.6 7.9 %collective-permute-start.6 = (bf16[128,1024]{1,0:T(8,128)(2,1)S(1)}, bf16[128,1024]{1,0:T(8,128)(2,1)S(1)}, u32[]{:S(2)}, u32[]{:S(2)}) collective-permute-start(bf16[128,1024]{1,0:T(8,128)(2,1)S(1)} %fusion.17), channel_id=1, source_target_pairs={{0,4},{2,6},{4,0},{6,2},{8,12},{10,14},{12,8},{14,10},{1,5},{3,7},... | collective-permute-start | bytes 786440 | tf_op jit(solution)/shard_map/ppermute | solution.py:13
  66.8 1.7 %collective-permute-start.9 = (f32[3,128]{1,0:T(4,128)S(1)}, f32[3,128]{1,0:T(4,128)S(1)}, u32[]{:S(2)}, u32[]{:S(2)}) collective-permute-start(f32[3,128]{1,0:T(4,128)S(1)} %pad_maximum_fusion.1), channel_id=1, source_target_pairs={{0,1},{1,0},{2,3},{3,2},{4,5},{5,4},{6,7},{7,6},{8,9},{9,8},{10,11... | collective-permute-start | bytes 4616 | tf_op jit(solution)/shard_map/ppermute | solution.py:63
  66.9 2.2 %collective-permute-start.8 = (f32[3,128]{1,0:T(4,128)S(1)}, f32[3,128]{1,0:T(4,128)S(1)}, u32[]{:S(2)}, u32[]{:S(2)}) collective-permute-start(f32[3,128]{1,0:T(4,128)S(1)} %pad_maximum_fusion), channel_id=1, source_target_pairs={{0,1},{1,0},{2,3},{3,2},{4,5},{5,4},{6,7},{7,6},{8,9},{9,8},{10,11... | collective-permute-start | bytes 4616 | tf_op jit(solution)/shard_map/ppermute | solution.py:63
  67.6 8.3 %collective-permute-start.7 = (bf16[128,1024]{1,0:T(8,128)(2,1)S(1)}, bf16[128,1024]{1,0:T(8,128)(2,1)S(1)}, u32[]{:S(2)}, u32[]{:S(2)}) collective-permute-start(bf16[128,1024]{1,0:T(8,128)(2,1)S(1)} %fusion.22), channel_id=1, source_target_pairs={{0,2},{2,0},{4,6},{6,4},{8,10},{10,8},{12,14},{14,12},{1,3},{3,1},... | collective-permute-start | bytes 786440 | tf_op jit(solution)/shard_map/ppermute | solution.py:13
  76.2 1.3 %collective-permute-start.10 = (f32[1,128,128]{2,1,0:T(8,128)S(1)}, f32[1,128,128]{2,1,0:T(8,128)S(1)}, u32[]{:S(2)}, u32[]{:S(2)}) collective-permute-start(f32[1,128,128]{2,1,0:T(8,128)S(1)} %convolution_bitcast_fusion.1), channel_id=1, source_target_pairs={{0,1},{1,0},{2,3},{3,2},{4,5},{5,4},{6,7},{7,6},{8,9},{9,8},{10,11... | collective-permute-start | bytes 196616 | tf_op jit(solution)/shard_map/ppermute | solution.py:63

commit v6 on v5

--- a/solution.py
+++ b/solution.py
@@ -5,6 +5,7 @@
 from jax.experimental import pallas as pl
 
 D = 2048
+CHUNKS = 2
 
 
 def from_partner(value, axis, distance):
@@ -72,17 +73,23 @@
     tok_blocks = tokens.reshape(nblk, blen, width)
     local = jnp.einsum("kij,kjd->kid", blocks, tok_blocks, preferred_element_type=jnp.float32)
     local = local.astype(jnp.bfloat16).reshape(tok, width)
-    states = []
-    mates = []
-    current = local
+    chunks = CHUNKS if tok % CHUNKS == 0 else 1
+    rows = tok // chunks
+    spans = [slice(chunk * rows, (chunk + 1) * rows) for chunk in range(chunks)]
+    states = [[None] * sections for _ in spans]
+    mates = [[None] * sections for _ in spans]
+    pieces = [local[rs] for rs in spans]
     for section in range(sections):
-        mate = from_partner(current, "seq", section)
-        states.append(current)
-        mates.append(mate)
-        current = (
-            coef_self[section][:, None] * current.astype(jnp.float32)
-            + coef_cross[section][:, None] * mate.astype(jnp.float32)
-        ).astype(jnp.bfloat16)
+        for chunk, rs in enumerate(spans):
+            value = pieces[chunk]
+            mate = from_partner(value, "seq", section)
+            states[chunk][section] = value
+            mates[chunk][section] = mate
+            pieces[chunk] = (
+                coef_self[section, rs][:, None] * value.astype(jnp.float32)
+                + coef_cross[section, rs][:, None] * mate.astype(jnp.float32)
+            ).astype(jnp.bfloat16)
+    current = jnp.concatenate(pieces, axis=0)
     tok_f = tokens.astype(jnp.float32)
     mixed_f = current.astype(jnp.float32)
     resid = tok_f + tok_f * mixed_f
@@ -98,20 +105,26 @@
         - resid * (inv**3 * inner / D)[:, None]
     )
     d_mixed = (d_resid * tok_f).astype(jnp.bfloat16)
-    grads_self = [None] * sections
-    grads_cross = [None] * sections
-    back = d_mixed
+    grads_self = [[None] * sections for _ in spans]
+    grads_cross = [[None] * sections for _ in spans]
+    backs = [d_mixed[rs] for rs in spans]
     for section in range(sections - 1, -1, -1):
-        back_f = back.astype(jnp.float32)
-        grads_self[section] = jnp.sum(back_f * states[section].astype(jnp.float32), axis=-1)
-        grads_cross[section] = jnp.sum(back_f * mates[section].astype(jnp.float32), axis=-1)
-        sent = (coef_cross[section][:, None] * back_f).astype(jnp.bfloat16)
-        received = from_partner(sent, "seq", section)
-        back = (coef_self[section][:, None] * back_f + received.astype(jnp.float32)).astype(
-            jnp.bfloat16
-        )
-    part_self = jnp.stack(grads_self)
-    part_cross = jnp.stack(grads_cross)
+        for chunk, rs in enumerate(spans):
+            back_f = backs[chunk].astype(jnp.float32)
+            grads_self[chunk][section] = jnp.sum(
+                back_f * states[chunk][section].astype(jnp.float32), axis=-1
+            )
+            grads_cross[chunk][section] = jnp.sum(
+                back_f * mates[chunk][section].astype(jnp.float32), axis=-1
+            )
+            sent = (coef_cross[section, rs][:, None] * back_f).astype(jnp.bfloat16)
+            received = from_partner(sent, "seq", section)
+            backs[chunk] = (
+                coef_self[section, rs][:, None] * back_f + received.astype(jnp.float32)
+            ).astype(jnp.bfloat16)
+    back = jnp.concatenate(backs, axis=0)
+    part_self = jnp.concatenate([jnp.stack(g) for g in grads_self], axis=1)
+    part_cross = jnp.concatenate([jnp.stack(g) for g in grads_cross], axis=1)
     back_blocks = back.reshape(nblk, blen, width)
     part_blocks = jnp.einsum(
         "kid,kjd->kij", back_blocks, tok_blocks, preferred_element_type=jnp.float32

time: 78.4 us -> 76.4 us (0.974)
  waiting for transfers between devices: 53.5 us -> 41.5 us
  starting transfers between devices: 9.63 us -> 18.8 us
  other arithmetic: 6.09 us -> 6.93 us
    ppermute x6 -> x12, waiting for transfers between devices: 51.4 us -> 39.3 us  [from_partner(): return lax.ppermute(value, axis, pairs)]
    ppermute x6 -> x12, starting transfers between devices: 8.6 us -> 17.9 us  [from_partner(): return lax.ppermute(value, axis, pairs)]
    convert_element_type x5 -> x12, other arithmetic: 0.65 us -> 1.49 us  [the longest x5 0.61 us: body(): pieces[chunk] = (coef_self[section, rs][:, None] * value.astype(jnp.float...]
  transfers between devices with their start and end apart: 11 -> 17, of which waited for: 9 -> 14; matrix products, arithmetic and copies ran while one was open for 3% -> 4% of each run, Pallas kernels for 0% -> 0%
where the time goes in v6:
time: 76.4 us; the launch traced here: 76.2 us
  waiting for transfers between devices  41.5 us (54%)
  starting transfers between devices  18.8 us (25%)
  other arithmetic  6.93 us (9%)
  Pallas kernels  4.81 us (6%)
  matrix products  2.47 us (3%)
  local copies, waits for them, and re-layouts  0.88 us (1%)
  between operations  0.83 us (1%)
    ppermute x12, waiting for transfers between devices, from_partner(): return lax.ppermute(value, axis, pairs)  39.3 us
    ppermute x12, starting transfers between devices, from_partner(): return lax.ppermute(value, axis, pairs)  17.9 us
    pallas_call x1, Pallas kernels, ffn_grad(): pl.pallas_call(ffn_kernel, grid=(groups_here // per_step,), in_specs=[act...  4.81 us
    ppermute x5, waiting for transfers between devices, hid_sum(): total = total + lax.ppermute(value, 'hid', pairs)  2.19 us
    add x3, other arithmetic, hid_sum(): total = total + lax.ppermute(value, 'hid', pairs)  1.95 us
  transfers between devices with their start and end apart: 17, of which 14 were waited for; matrix products, arithmetic and copies ran while one was open for 4% of the time, Pallas kernels for 0%

profile of v6, /device:TPU:0, one launch (start us, length us, event | category | flops | bytes accessed | tf_op | source)
XLA Modules:
  0.0 76.2 jit_solution(15082447082628187784)
XLA Ops:
  0.6 0.7 copy-done
  1.4 1.2 %fusion.2 = bf16[1,128,1024]{2,1,0:T(8,128)(2,1)S(1)} fusion(bf16[128,1024]{1,0:T(8,128)(2,1)} %param.9, bf16[1,128,128]{2,1,0:T(8,128)(2,1)S(1)} %copy-done), kind=kOutput, calls=%fused_computation.4 | convolution fusion | flops 33685504 | bytes 557056 | tf_op jit(solution)/shard_map/kij,kjd->kid/dot_general | solution.py:74
  2.6 3.0 %collective-permute-start = (bf16[64,1024]{1,0:T(8,128)(2,1)S(1)}, bf16[64,1024]{1,0:T(8,128)(2,1)S(1)}, u32[]{:S(2)}, u32[]{:S(2)}) collective-permute-start(bf16[64,1024]{1,0:T(8,128)(2,1)S(1)} %get-tuple-element.27), channel_id=1, source_target_pairs={{0,2},{2,0},{4,6},{6,4},{8,10},{10,8},{12,14},{14,12},{1,3},{3,1},... | collective-permute-start | bytes 393224 | tf_op jit(solution)/shard_map/ppermute | solution.py:14
  5.8 4.2 %collective-permute-done = bf16[64,1024]{1,0:T(8,128)(2,1)S(1)} collective-permute-done((bf16[64,1024]{1,0:T(8,128)(2,1)S(1)}, bf16[64,1024]{1,0:T(8,128)(2,1)S(1)}, u32[]{:S(2)}, u32[]{:S(2)}) %collective-permute-start) | collective-permute-done | bytes 131104 | tf_op jit(solution)/shard_map/ppermute | solution.py:14
  9.9 2.0 %collective-permute-done.3 = bf16[64,1024]{1,0:T(8,128)(2,1)S(1)} collective-permute-done((bf16[64,1024]{1,0:T(8,128)(2,1)S(1)}, bf16[64,1024]{1,0:T(8,128)(2,1)S(1)}, u32[]{:S(2)}, u32[]{:S(2)}) %collective-permute-start.3) | collective-permute-done | bytes 131104 | tf_op jit(solution)/shard_map/ppermute | solution.py:14
  12.1 1.9 %collective-permute-start.4 = (bf16[64,1024]{1,0:T(8,128)(2,1)S(1)}, bf16[64,1024]{1,0:T(8,128)(2,1)S(1)}, u32[]{:S(2)}, u32[]{:S(2)}) collective-permute-start(bf16[64,1024]{1,0:T(8,128)(2,1)S(1)} %get-tuple-element.25), channel_id=1, source_target_pairs={{0,4},{2,6},{4,0},{6,2},{8,12},{10,14},{12,8},{14,10},{1,5},{3,7},... | collective-permute-start | bytes 393224 | tf_op jit(solution)/shard_map/ppermute | solution.py:14
  14.2 4.1 %collective-permute-done.4 = bf16[64,1024]{1,0:T(8,128)(2,1)S(1)} collective-permute-done((bf16[64,1024]{1,0:T(8,128)(2,1)S(1)}, bf16[64,1024]{1,0:T(8,128)(2,1)S(1)}, u32[]{:S(2)}, u32[]{:S(2)}) %collective-permute-start.4) | collective-permute-done | bytes 131104 | tf_op jit(solution)/shard_map/ppermute | solution.py:14
  18.4 2.8 %collective-permute-start.5 = (bf16[64,1024]{1,0:T(8,128)(2,1)S(1)}, bf16[64,1024]{1,0:T(8,128)(2,1)S(1)}, u32[]{:S(2)}, u32[]{:S(2)}) collective-permute-start(bf16[64,1024]{1,0:T(8,128)(2,1)S(1)} %fusion.14), channel_id=1, source_target_pairs={{0,8},{2,10},{4,12},{6,14},{8,0},{10,2},{12,4},{14,6},{1,9},{3,11}... | collective-permute-start | bytes 393224 | tf_op jit(solution)/shard_map/ppermute | solution.py:14
  21.3 2.7 %collective-permute-start.2 = (bf16[64,1024]{1,0:T(8,128)(2,1)S(1)}, bf16[64,1024]{1,0:T(8,128)(2,1)S(1)}, u32[]{:S(2)}, u32[]{:S(2)}) collective-permute-start(bf16[64,1024]{1,0:T(8,128)(2,1)S(1)} %fusion.8), channel_id=1, source_target_pairs={{0,8},{2,10},{4,12},{6,14},{8,0},{10,2},{12,4},{14,6},{1,9},{3,11}... | collective-permute-start | bytes 393224 | tf_op jit(solution)/shard_map/ppermute | solution.py:14
  24.0 5.2 %collective-permute-done.5 = bf16[64,1024]{1,0:T(8,128)(2,1)S(1)} collective-permute-done((bf16[64,1024]{1,0:T(8,128)(2,1)S(1)}, bf16[64,1024]{1,0:T(8,128)(2,1)S(1)}, u32[]{:S(2)}, u32[]{:S(2)}) %collective-permute-start.5) | collective-permute-done | bytes 131104 | tf_op jit(solution)/shard_map/ppermute | solution.py:14
  29.4 1.3 %collective-permute-done.2 = bf16[64,1024]{1,0:T(8,128)(2,1)S(1)} collective-permute-done((bf16[64,1024]{1,0:T(8,128)(2,1)S(1)}, bf16[64,1024]{1,0:T(8,128)(2,1)S(1)}, u32[]{:S(2)}, u32[]{:S(2)}) %collective-permute-start.2) | collective-permute-done | bytes 131104 | tf_op jit(solution)/shard_map/ppermute | solution.py:14
  31.0 1.1 %collective-permute-done.6 = f32[128]{0:T(128)S(1)} collective-permute-done((f32[128]{0:T(128)S(1)}, f32[128]{0:T(128)S(1)}, u32[]{:S(2)}, u32[]{:S(2)}) %collective-permute-start.6) | collective-permute-done | bytes 544 | tf_op jit(solution)/shard_map/ppermute | solution.py:64
  32.2 0.8 %multiply_convert_fusion.normed_ref = bf16[128,1024]{1,0:T(8,128)(2,1)} fusion(bf16[128,1024]{1,0:T(8,128)(2,1)S(1)} %copy-done.1, f32[1024]{0:T(1024)S(1)} %copy-done.4, f32[128]{0:T(128)S(1)} %add_rsqrt_fusion, bf16[64,1024]{1,0:T(8,128)(2,1)S(1)} %fusion.16, bf16[64,1024]{1,0:T(8,128)(2,1)S(1)} %fusion.10), kind=kLoop, calls=%fused_computation.13 | loop fusion | flops 1310720 | bytes 791040 | tf_op jit(solution)/shard_map/convert_element_type | solution.py:98
  33.0 4.8 %shard_map.120 = f32[128,1024]{1,0:T(8,128)} custom-call(bf16[128,1024]{1,0:T(8,128)(2,1)} %multiply_convert_fusion.normed_ref, bf16[128,1024]{1,0:T(8,128)(2,1)} %cot_ref.1, bf16[8,128,512]{2,1,0:T(8,128)(2,1)} %wg_ref.1, bf16[8,128,512]{2,1,0:T(8,128)(2,1)} %wu_ref.1, bf16[8,512,128]{2,1,0:T(8,128)(2,1)} %wd_ref.1), custom_call_target="tpu_custom_call" | custom-call | tf_op jit(solution)/shard_map/pallas_call | solution.py:44
  37.8 1.3 %multiply_reduce_fusion = f32[128]{0:T(128)S(1)} fusion(f32[128,1024]{1,0:T(8,128)} %shard_map.120, bf16[128,1024]{1,0:T(8,128)(2,1)S(1)} %copy-done.1, f32[1024]{0:T(1024)S(1)} %copy-done.4, bf16[64,1024]{1,0:T(8,128)(2,1)S(1)} %fusion.16, bf16[64,1024]{1,0:T(8,128)(2,1)S(1)} %fusion.10), kind=kLoop, calls=%fused_computation.12 | loop fusion | flops 1310592 | bytes 1053184 | tf_op jit(solution)/shard_map/reduce_sum | solution.py:101
  39.4 0.9 %collective-permute-done.7 = f32[128]{0:T(128)S(1)} collective-permute-done((f32[128]{0:T(128)S(1)}, f32[128]{0:T(128)S(1)}, u32[]{:S(2)}, u32[]{:S(2)}) %collective-permute-start.7) | collective-permute-done | bytes 544 | tf_op jit(solution)/shard_map/ppermute | solution.py:64
  40.9 2.9 %collective-permute-start.11 = (bf16[64,1024]{1,0:T(8,128)(2,1)S(1)}, bf16[64,1024]{1,0:T(8,128)(2,1)S(1)}, u32[]{:S(2)}, u32[]{:S(2)}) collective-permute-start(bf16[64,1024]{1,0:T(8,128)(2,1)S(1)} %get-tuple-element.21), channel_id=1, source_target_pairs={{0,8},{2,10},{4,12},{6,14},{8,0},{10,2},{12,4},{14,6},{1,9},{3,11}... | collective-permute-start | bytes 393224 | tf_op jit(solution)/shard_map/ppermute | solution.py:14
  43.9 9.7 %collective-permute-done.8 = bf16[64,1024]{1,0:T(8,128)(2,1)S(1)} collective-permute-done((bf16[64,1024]{1,0:T(8,128)(2,1)S(1)}, bf16[64,1024]{1,0:T(8,128)(2,1)S(1)}, u32[]{:S(2)}, u32[]{:S(2)}) %collective-permute-start.8) | collective-permute-done | bytes 131104 | tf_op jit(solution)/shard_map/ppermute | solution.py:14
  53.5 2.4 %collective-permute-done.11 = bf16[64,1024]{1,0:T(8,128)(2,1)S(1)} collective-permute-done((bf16[64,1024]{1,0:T(8,128)(2,1)S(1)}, bf16[64,1024]{1,0:T(8,128)(2,1)S(1)}, u32[]{:S(2)}, u32[]{:S(2)}) %collective-permute-start.11) | collective-permute-done | bytes 131104 | tf_op jit(solution)/shard_map/ppermute | solution.py:14
  56.5 2.0 %collective-permute-start.12 = (bf16[64,1024]{1,0:T(8,128)(2,1)S(1)}, bf16[64,1024]{1,0:T(8,128)(2,1)S(1)}, u32[]{:S(2)}, u32[]{:S(2)}) collective-permute-start(bf16[64,1024]{1,0:T(8,128)(2,1)S(1)} %fusion.39), channel_id=1, source_target_pairs={{0,4},{2,6},{4,0},{6,2},{8,12},{10,14},{12,8},{14,10},{1,5},{3,7},... | collective-permute-start | bytes 393224 | tf_op jit(solution)/shard_map/ppermute | solution.py:14
  58.5 4.4 %collective-permute-done.9 = bf16[64,1024]{1,0:T(8,128)(2,1)S(1)} collective-permute-done((bf16[64,1024]{1,0:T(8,128)(2,1)S(1)}, bf16[64,1024]{1,0:T(8,128)(2,1)S(1)}, u32[]{:S(2)}, u32[]{:S(2)}) %collective-permute-start.9) | collective-permute-done | bytes 131104 | tf_op jit(solution)/shard_map/ppermute | solution.py:14
  62.9 1.5 %collective-permute-done.12 = bf16[64,1024]{1,0:T(8,128)(2,1)S(1)} collective-permute-done((bf16[64,1024]{1,0:T(8,128)(2,1)S(1)}, bf16[64,1024]{1,0:T(8,128)(2,1)S(1)}, u32[]{:S(2)}, u32[]{:S(2)}) %collective-permute-start.12) | collective-permute-done | bytes 131104 | tf_op jit(solution)/shard_map/ppermute | solution.py:14
  64.3 0.4 fusion.30
  64.9 0.5 collective-permute-start.14
  65.6 1.2 %collective-permute-start.13 = (bf16[64,1024]{1,0:T(8,128)(2,1)S(1)}, bf16[64,1024]{1,0:T(8,128)(2,1)S(1)}, u32[]{:S(2)}, u32[]{:S(2)}) collective-permute-start(bf16[64,1024]{1,0:T(8,128)(2,1)S(1)} %fusion.44), channel_id=1, source_target_pairs={{0,2},{2,0},{4,6},{6,4},{8,10},{10,8},{12,14},{14,12},{1,3},{3,1},... | collective-permute-start | bytes 393224 | tf_op jit(solution)/shard_map/ppermute | solution.py:14
  66.8 0.9 %collective-permute-start.10 = (bf16[64,1024]{1,0:T(8,128)(2,1)S(1)}, bf16[64,1024]{1,0:T(8,128)(2,1)S(1)}, u32[]{:S(2)}, u32[]{:S(2)}) collective-permute-start(bf16[64,1024]{1,0:T(8,128)(2,1)S(1)} %fusion.29), channel_id=1, source_target_pairs={{0,2},{2,0},{4,6},{6,4},{8,10},{10,8},{12,14},{14,12},{1,3},{3,1},... | collective-permute-start | bytes 393224 | tf_op jit(solution)/shard_map/ppermute | solution.py:14
  67.7 0.7 fusion.59
  68.4 0.7 fusion.60
  69.0 3.0 %collective-permute-done.13 = bf16[64,1024]{1,0:T(8,128)(2,1)S(1)} collective-permute-done((bf16[64,1024]{1,0:T(8,128)(2,1)S(1)}, bf16[64,1024]{1,0:T(8,128)(2,1)S(1)}, u32[]{:S(2)}, u32[]{:S(2)}) %collective-permute-start.13) | collective-permute-done | bytes 131104 | tf_op jit(solution)/shard_map/ppermute | solution.py:14
  72.1 1.8 %collective-permute-done.10 = bf16[64,1024]{1,0:T(8,128)(2,1)S(1)} collective-permute-done((bf16[64,1024]{1,0:T(8,128)(2,1)S(1)}, bf16[64,1024]{1,0:T(8,128)(2,1)S(1)}, u32[]{:S(2)}, u32[]{:S(2)}) %collective-permute-start.10) | collective-permute-done | bytes 131104 | tf_op jit(solution)/shard_map/ppermute | solution.py:14
  74.3 1.1 %fusion.1 = bf16[128,1024]{1,0:T(8,128)(2,1)} fusion(bf16[64,1024]{1,0:T(8,128)(2,1)S(1)} %fusion.43, bf16[64,1024]{1,0:T(8,128)(2,1)S(1)} %fusion.28, bf16[1,128,128]{2,1,0:T(8,128)(2,1)S(1)} %copy-done, f32[128]{0:T(128)S(1)} %fusion.50, bf16[128,1024]{1,0:T(8,128)(2,1)S(1)} %copy-done.1, f32[128,1024]{1,0:T(8,128)S(1)} %copy-done.2, ...), kind=kOutput, calls=%fused_computation.2 | convolution fusion | flops 36306944 | bytes 1872896 | tf_op jit(solution)/shard_map/kij,kid->kjd/dot_general | solution.py:132
  75.6 0.6 add.95
  (47 shorter events, 3.8 us)
Async XLA Ops:
  0.6 0.8 %copy-start = (bf16[1,128,128]{2,1,0:T(8,128)(2,1)S(1)}, bf16[1,128,128]{2,1,0:T(8,128)(2,1)}, u32[]{:S(2)}) copy-start(bf16[1,128,128]{2,1,0:T(8,128)(2,1)} %param.11) | copy-start | bytes 98308
  2.6 3.1 %copy-start.6 = (f32[3,128]{1,0:T(4,128)S(1)}, f32[3,128]{1,0:T(4,128)}, u32[]{:S(2)}) copy-start(f32[3,128]{1,0:T(4,128)} %param.12) | copy-start | bytes 4612
  2.6 3.1 %copy-start.5 = (f32[3,128]{1,0:T(4,128)S(1)}, f32[3,128]{1,0:T(4,128)}, u32[]{:S(2)}) copy-start(f32[3,128]{1,0:T(4,128)} %param.13) | copy-start | bytes 4612
  2.6 7.3 %collective-permute-start = (bf16[64,1024]{1,0:T(8,128)(2,1)S(1)}, bf16[64,1024]{1,0:T(8,128)(2,1)S(1)}, u32[]{:S(2)}, u32[]{:S(2)}) collective-permute-start(bf16[64,1024]{1,0:T(8,128)(2,1)S(1)} %get-tuple-element.27), channel_id=1, source_target_pairs={{0,2},{2,0},{4,6},{6,4},{8,10},{10,8},{12,14},{14,12},{1,3},{3,1},... | collective-permute-start | bytes 393224 | tf_op jit(solution)/shard_map/ppermute | solution.py:14
  5.6 6.3 %collective-permute-start.3 = (bf16[64,1024]{1,0:T(8,128)(2,1)S(1)}, bf16[64,1024]{1,0:T(8,128)(2,1)S(1)}, u32[]{:S(2)}, u32[]{:S(2)}) collective-permute-start(bf16[64,1024]{1,0:T(8,128)(2,1)S(1)} %get-tuple-element.28), channel_id=1, source_target_pairs={{0,2},{2,0},{4,6},{6,4},{8,10},{10,8},{12,14},{14,12},{1,3},{3,1},... | collective-permute-start | bytes 393224 | tf_op jit(solution)/shard_map/ppermute | solution.py:14
  12.1 6.2 %collective-permute-start.4 = (bf16[64,1024]{1,0:T(8,128)(2,1)S(1)}, bf16[64,1024]{1,0:T(8,128)(2,1)S(1)}, u32[]{:S(2)}, u32[]{:S(2)}) collective-permute-start(bf16[64,1024]{1,0:T(8,128)(2,1)S(1)} %get-tuple-element.25), channel_id=1, source_target_pairs={{0,4},{2,6},{4,0},{6,2},{8,12},{10,14},{12,8},{14,10},{1,5},{3,7},... | collective-permute-start | bytes 393224 | tf_op jit(solution)/shard_map/ppermute | solution.py:14
  14.0 7.2 %collective-permute-start.1 = (bf16[64,1024]{1,0:T(8,128)(2,1)S(1)}, bf16[64,1024]{1,0:T(8,128)(2,1)S(1)}, u32[]{:S(2)}, u32[]{:S(2)}) collective-permute-start(bf16[64,1024]{1,0:T(8,128)(2,1)S(1)} %get-tuple-element.26), channel_id=1, source_target_pairs={{0,4},{2,6},{4,0},{6,2},{8,12},{10,14},{12,8},{14,10},{1,5},{3,7},... | collective-permute-start | bytes 393224 | tf_op jit(solution)/shard_map/ppermute | solution.py:14
  18.4 10.9 %collective-permute-start.5 = (bf16[64,1024]{1,0:T(8,128)(2,1)S(1)}, bf16[64,1024]{1,0:T(8,128)(2,1)S(1)}, u32[]{:S(2)}, u32[]{:S(2)}) collective-permute-start(bf16[64,1024]{1,0:T(8,128)(2,1)S(1)} %fusion.14), channel_id=1, source_target_pairs={{0,8},{2,10},{4,12},{6,14},{8,0},{10,2},{12,4},{14,6},{1,9},{3,11}... | collective-permute-start | bytes 393224 | tf_op jit(solution)/shard_map/ppermute | solution.py:14
  21.3 9.3 %collective-permute-start.2 = (bf16[64,1024]{1,0:T(8,128)(2,1)S(1)}, bf16[64,1024]{1,0:T(8,128)(2,1)S(1)}, u32[]{:S(2)}, u32[]{:S(2)}) collective-permute-start(bf16[64,1024]{1,0:T(8,128)(2,1)S(1)} %fusion.8), channel_id=1, source_target_pairs={{0,8},{2,10},{4,12},{6,14},{8,0},{10,2},{12,4},{14,6},{1,9},{3,11}... | collective-permute-start | bytes 393224 | tf_op jit(solution)/shard_map/ppermute | solution.py:14
  29.4 1.4 %copy-start.1 = (bf16[128,1024]{1,0:T(8,128)(2,1)S(1)}, bf16[128,1024]{1,0:T(8,128)(2,1)}, u32[]{:S(2)}) copy-start(bf16[128,1024]{1,0:T(8,128)(2,1)} %param.9) | copy-start | bytes 786436
  30.8 1.4 %copy-start.4 = (f32[1024]{0:T(1024)S(1)}, f32[1024]{0:T(1024)}, u32[]{:S(2)}) copy-start(f32[1024]{0:T(1024)} %param.14) | copy-start | bytes 12292
  31.0 1.2 %collective-permute-start.6 = (f32[128]{0:T(128)S(1)}, f32[128]{0:T(128)S(1)}, u32[]{:S(2)}, u32[]{:S(2)}) collective-permute-start(f32[128]{0:T(128)S(1)} %multiply_reduce_fusion.1), channel_id=1, source_target_pairs={{0,1},{1,0},{2,3},{3,2},{4,5},{5,4},{6,7},{7,6},{8,9},{9,8},{10,11... | collective-permute-start | bytes 1544 | tf_op jit(solution)/shard_map/ppermute | solution.py:64
  37.8 2.5 %copy-start.2 = (f32[128,1024]{1,0:T(8,128)S(1)}, f32[128,1024]{1,0:T(8,128)}, u32[]{:S(2)}) copy-start(f32[128,1024]{1,0:T(8,128)} %shard_map.120) | copy-start | bytes 1572868
  37.8 2.5 %copy-start.3 = (bf16[128,1024]{1,0:T(8,128)(2,1)S(1)}, bf16[128,1024]{1,0:T(8,128)(2,1)}, u32[]{:S(2)}) copy-start(bf16[128,1024]{1,0:T(8,128)(2,1)} %cot_ref.1) | copy-start | bytes 786436
  39.1 1.2 %collective-permute-start.7 = (f32[128]{0:T(128)S(1)}, f32[128]{0:T(128)S(1)}, u32[]{:S(2)}, u32[]{:S(2)}) collective-permute-start(f32[128]{0:T(128)S(1)} %multiply_reduce_fusion), channel_id=1, source_target_pairs={{0,1},{1,0},{2,3},{3,2},{4,5},{5,4},{6,7},{7,6},{8,9},{9,8},{10,11... | collective-permute-start | bytes 1544 | tf_op jit(solution)/shard_map/ppermute | solution.py:64
  40.9 12.6 %collective-permute-start.8 = (bf16[64,1024]{1,0:T(8,128)(2,1)S(1)}, bf16[64,1024]{1,0:T(8,128)(2,1)S(1)}, u32[]{:S(2)}, u32[]{:S(2)}) collective-permute-start(bf16[64,1024]{1,0:T(8,128)(2,1)S(1)} %get-tuple-element.20), channel_id=1, source_target_pairs={{0,8},{2,10},{4,12},{6,14},{8,0},{10,2},{12,4},{14,6},{1,9},{3,11}... | collective-permute-start | bytes 393224 | tf_op jit(solution)/shard_map/ppermute | solution.py:14
  40.9 14.9 %collective-permute-start.11 = (bf16[64,1024]{1,0:T(8,128)(2,1)S(1)}, bf16[64,1024]{1,0:T(8,128)(2,1)S(1)}, u32[]{:S(2)}, u32[]{:S(2)}) collective-permute-start(bf16[64,1024]{1,0:T(8,128)(2,1)S(1)} %get-tuple-element.21), channel_id=1, source_target_pairs={{0,8},{2,10},{4,12},{6,14},{8,0},{10,2},{12,4},{14,6},{1,9},{3,11}... | collective-permute-start | bytes 393224 | tf_op jit(solution)/shard_map/ppermute | solution.py:14
  56.4 6.5 %collective-permute-start.9 = (bf16[64,1024]{1,0:T(8,128)(2,1)S(1)}, bf16[64,1024]{1,0:T(8,128)(2,1)S(1)}, u32[]{:S(2)}, u32[]{:S(2)}) collective-permute-start(bf16[64,1024]{1,0:T(8,128)(2,1)S(1)} %fusion.24), channel_id=1, source_target_pairs={{0,4},{2,6},{4,0},{6,2},{8,12},{10,14},{12,8},{14,10},{1,5},{3,7},... | collective-permute-start | bytes 393224 | tf_op jit(solution)/shard_map/ppermute | solution.py:14
  56.5 7.9 %collective-permute-start.12 = (bf16[64,1024]{1,0:T(8,128)(2,1)S(1)}, bf16[64,1024]{1,0:T(8,128)(2,1)S(1)}, u32[]{:S(2)}, u32[]{:S(2)}) collective-permute-start(bf16[64,1024]{1,0:T(8,128)(2,1)S(1)} %fusion.39), channel_id=1, source_target_pairs={{0,4},{2,6},{4,0},{6,2},{8,12},{10,14},{12,8},{14,10},{1,5},{3,7},... | collective-permute-start | bytes 393224 | tf_op jit(solution)/shard_map/ppermute | solution.py:14
  64.8 2.9 %collective-permute-start.15 = (f32[3,128]{1,0:T(4,128)S(1)}, f32[3,128]{1,0:T(4,128)S(1)}, u32[]{:S(2)}, u32[]{:S(2)}) collective-permute-start(f32[3,128]{1,0:T(4,128)S(1)} %maximum_maximum_fusion.1), channel_id=1, source_target_pairs={{0,1},{1,0},{2,3},{3,2},{4,5},{5,4},{6,7},{7,6},{8,9},{9,8},{10,11... | collective-permute-start | bytes 4616 | tf_op jit(solution)/shard_map/ppermute | solution.py:64
  64.9 3.4 %collective-permute-start.14 = (f32[3,128]{1,0:T(4,128)S(1)}, f32[3,128]{1,0:T(4,128)S(1)}, u32[]{:S(2)}, u32[]{:S(2)}) collective-permute-start(f32[3,128]{1,0:T(4,128)S(1)} %maximum_maximum_fusion), channel_id=1, source_target_pairs={{0,1},{1,0},{2,3},{3,2},{4,5},{5,4},{6,7},{7,6},{8,9},{9,8},{10,11... | collective-permute-start | bytes 4616 | tf_op jit(solution)/shard_map/ppermute | solution.py:64
  65.6 6.4 %collective-permute-start.13 = (bf16[64,1024]{1,0:T(8,128)(2,1)S(1)}, bf16[64,1024]{1,0:T(8,128)(2,1)S(1)}, u32[]{:S(2)}, u32[]{:S(2)}) collective-permute-start(bf16[64,1024]{1,0:T(8,128)(2,1)S(1)} %fusion.44), channel_id=1, source_target_pairs={{0,2},{2,0},{4,6},{6,4},{8,10},{10,8},{12,14},{14,12},{1,3},{3,1},... | collective-permute-start | bytes 393224 | tf_op jit(solution)/shard_map/ppermute | solution.py:14
  66.8 7.1 %collective-permute-start.10 = (bf16[64,1024]{1,0:T(8,128)(2,1)S(1)}, bf16[64,1024]{1,0:T(8,128)(2,1)S(1)}, u32[]{:S(2)}, u32[]{:S(2)}) collective-permute-start(bf16[64,1024]{1,0:T(8,128)(2,1)S(1)} %fusion.29), channel_id=1, source_target_pairs={{0,2},{2,0},{4,6},{6,4},{8,10},{10,8},{12,14},{14,12},{1,3},{3,1},... | collective-permute-start | bytes 393224 | tf_op jit(solution)/shard_map/ppermute | solution.py:14
  74.2 1.3 %collective-permute-start.16 = (f32[1,128,128]{2,1,0:T(8,128)S(1)}, f32[1,128,128]{2,1,0:T(8,128)S(1)}, u32[]{:S(2)}, u32[]{:S(2)}) collective-permute-start(f32[1,128,128]{2,1,0:T(8,128)S(1)} %convolution_bitcast_fusion.1), channel_id=1, source_target_pairs={{0,1},{1,0},{2,3},{3,2},{4,5},{5,4},{6,7},{7,6},{8,9},{9,8},{10,11... | collective-permute-start | bytes 196616 | tf_op jit(solution)/shard_map/ppermute | solution.py:64

commit v7 on v6

--- a/solution.py
+++ b/solution.py
@@ -5,7 +5,7 @@
 from jax.experimental import pallas as pl
 
 D = 2048
-CHUNKS = 2
+CHUNKS = 4
 
 
 def from_partner(value, axis, distance):

time: 76.4 us -> 76.2 us (level)
  waiting for transfers between devices: 41.5 us -> 28.4 us
  starting transfers between devices: 18.8 us -> 30 us
  other arithmetic: 6.93 us -> 7.86 us
    ppermute x12 -> x24, waiting for transfers between devices: 39.3 us -> 26.2 us  [from_partner(): return lax.ppermute(value, axis, pairs)]
    ppermute x12 -> x24, starting transfers between devices: 17.9 us -> 29 us  [from_partner(): return lax.ppermute(value, axis, pairs)]
  transfers between devices with their start and end apart: 17 -> 29, of which waited for: 14 -> 18; matrix products, arithmetic and copies ran while one was open for 4% -> 6% of each run, Pallas kernels for 0% -> 0%
where the time goes in v7:
time: 76.2 us; the launch traced here: 75.9 us
  starting transfers between devices  30 us (39%)
  waiting for transfers between devices  28.4 us (37%)
  other arithmetic  7.86 us (10%)
  Pallas kernels  4.81 us (6%)
  matrix products  2.48 us (3%)
  local copies, waits for them, and re-layouts  1.55 us (2%)
  between operations  0.83 us (1%)
    ppermute x24, starting transfers between devices, from_partner(): return lax.ppermute(value, axis, pairs)  29 us
    ppermute x24, waiting for transfers between devices, from_partner(): return lax.ppermute(value, axis, pairs)  26.2 us
    pallas_call x1, Pallas kernels, ffn_grad(): pl.pallas_call(ffn_kernel, grid=(groups_here // per_step,), in_specs=[act...  4.81 us
    ppermute x5, waiting for transfers between devices, hid_sum(): total = total + lax.ppermute(value, 'hid', pairs)  2.18 us
    add x3, other arithmetic, hid_sum(): total = total + lax.ppermute(value, 'hid', pairs)  1.96 us
  transfers between devices with their start and end apart: 29, of which 18 were waited for; matrix products, arithmetic and copies ran while one was open for 6% of the time, Pallas kernels for 0%

profile of v7, /device:TPU:0, one launch (start us, length us, event | category | flops | bytes accessed | tf_op | source)
XLA Modules:
  0.0 75.9 jit_solution(17121349049510068073)
XLA Ops:
  0.6 0.7 copy-done
  1.4 1.2 %fusion.2 = bf16[1,128,1024]{2,1,0:T(8,128)(2,1)S(1)} fusion(bf16[128,1024]{1,0:T(8,128)(2,1)} %param.9, bf16[1,128,128]{2,1,0:T(8,128)(2,1)S(1)} %copy-done), kind=kOutput, calls=%fused_computation.4 | convolution fusion | flops 33685504 | bytes 557056 | tf_op jit(solution)/shard_map/kij,kjd->kid/dot_general | solution.py:74
  2.6 3.0 %collective-permute-start = (bf16[32,1024]{1,0:T(8,128)(2,1)S(1)}, bf16[32,1024]{1,0:T(8,128)(2,1)S(1)}, u32[]{:S(2)}, u32[]{:S(2)}) collective-permute-start(bf16[32,1024]{1,0:T(8,128)(2,1)S(1)} %get-tuple-element.50), channel_id=1, source_target_pairs={{0,2},{2,0},{4,6},{6,4},{8,10},{10,8},{12,14},{14,12},{1,3},{3,1},... | collective-permute-start | bytes 196616 | tf_op jit(solution)/shard_map/ppermute | solution.py:14
  5.7 1.9 %collective-permute-start.6 = (bf16[32,1024]{1,0:T(8,128)(2,1)S(1)}, bf16[32,1024]{1,0:T(8,128)(2,1)S(1)}, u32[]{:S(2)}, u32[]{:S(2)}) collective-permute-start(bf16[32,1024]{1,0:T(8,128)(2,1)S(1)} %get-tuple-element.52), channel_id=1, source_target_pairs={{0,2},{2,0},{4,6},{6,4},{8,10},{10,8},{12,14},{14,12},{1,3},{3,1},... | collective-permute-start | bytes 196616 | tf_op jit(solution)/shard_map/ppermute | solution.py:14
  8.5 2.1 %collective-permute-done.9 = bf16[32,1024]{1,0:T(8,128)(2,1)S(1)} collective-permute-done((bf16[32,1024]{1,0:T(8,128)(2,1)S(1)}, bf16[32,1024]{1,0:T(8,128)(2,1)S(1)}, u32[]{:S(2)}, u32[]{:S(2)}) %collective-permute-start.9) | collective-permute-done | bytes 65568 | tf_op jit(solution)/shard_map/ppermute | solution.py:14
  12.2 2.2 %collective-permute-start.4 = (bf16[32,1024]{1,0:T(8,128)(2,1)S(1)}, bf16[32,1024]{1,0:T(8,128)(2,1)S(1)}, u32[]{:S(2)}, u32[]{:S(2)}) collective-permute-start(bf16[32,1024]{1,0:T(8,128)(2,1)S(1)} %get-tuple-element.46), channel_id=1, source_target_pairs={{0,4},{2,6},{4,0},{6,2},{8,12},{10,14},{12,8},{14,10},{1,5},{3,7},... | collective-permute-start | bytes 196616 | tf_op jit(solution)/shard_map/ppermute | solution.py:14
  14.5 1.9 %collective-permute-start.7 = (bf16[32,1024]{1,0:T(8,128)(2,1)S(1)}, bf16[32,1024]{1,0:T(8,128)(2,1)S(1)}, u32[]{:S(2)}, u32[]{:S(2)}) collective-permute-start(bf16[32,1024]{1,0:T(8,128)(2,1)S(1)} %get-tuple-element.48), channel_id=1, source_target_pairs={{0,4},{2,6},{4,0},{6,2},{8,12},{10,14},{12,8},{14,10},{1,5},{3,7},... | collective-permute-start | bytes 196616 | tf_op jit(solution)/shard_map/ppermute | solution.py:14
  16.5 0.8 %collective-permute-done.4 = bf16[32,1024]{1,0:T(8,128)(2,1)S(1)} collective-permute-done((bf16[32,1024]{1,0:T(8,128)(2,1)S(1)}, bf16[32,1024]{1,0:T(8,128)(2,1)S(1)}, u32[]{:S(2)}, u32[]{:S(2)}) %collective-permute-start.4) | collective-permute-done | bytes 65568 | tf_op jit(solution)/shard_map/ppermute | solution.py:14
  17.4 3.0 %collective-permute-start.5 = (bf16[32,1024]{1,0:T(8,128)(2,1)S(1)}, bf16[32,1024]{1,0:T(8,128)(2,1)S(1)}, u32[]{:S(2)}, u32[]{:S(2)}) collective-permute-start(bf16[32,1024]{1,0:T(8,128)(2,1)S(1)} %fusion.14), channel_id=1, source_target_pairs={{0,8},{2,10},{4,12},{6,14},{8,0},{10,2},{12,4},{14,6},{1,9},{3,11}... | collective-permute-start | bytes 196616 | tf_op jit(solution)/shard_map/ppermute | solution.py:14
  20.5 1.6 %collective-permute-start.11 = (bf16[32,1024]{1,0:T(8,128)(2,1)S(1)}, bf16[32,1024]{1,0:T(8,128)(2,1)S(1)}, u32[]{:S(2)}, u32[]{:S(2)}) collective-permute-start(bf16[32,1024]{1,0:T(8,128)(2,1)S(1)} %fusion.26), channel_id=1, source_target_pairs={{0,8},{2,10},{4,12},{6,14},{8,0},{10,2},{12,4},{14,6},{1,9},{3,11}... | collective-permute-start | bytes 196616 | tf_op jit(solution)/shard_map/ppermute | solution.py:14
  22.3 1.4 %collective-permute-start.8 = (bf16[32,1024]{1,0:T(8,128)(2,1)S(1)}, bf16[32,1024]{1,0:T(8,128)(2,1)S(1)}, u32[]{:S(2)}, u32[]{:S(2)}) collective-permute-start(bf16[32,1024]{1,0:T(8,128)(2,1)S(1)} %fusion.20), channel_id=1, source_target_pairs={{0,8},{2,10},{4,12},{6,14},{8,0},{10,2},{12,4},{14,6},{1,9},{3,11}... | collective-permute-start | bytes 196616 | tf_op jit(solution)/shard_map/ppermute | solution.py:14
  23.8 1.6 %collective-permute-start.2 = (bf16[32,1024]{1,0:T(8,128)(2,1)S(1)}, bf16[32,1024]{1,0:T(8,128)(2,1)S(1)}, u32[]{:S(2)}, u32[]{:S(2)}) collective-permute-start(bf16[32,1024]{1,0:T(8,128)(2,1)S(1)} %fusion.8), channel_id=1, source_target_pairs={{0,8},{2,10},{4,12},{6,14},{8,0},{10,2},{12,4},{14,6},{1,9},{3,11}... | collective-permute-start | bytes 196616 | tf_op jit(solution)/shard_map/ppermute | solution.py:14
  25.5 3.8 %collective-permute-done.11 = bf16[32,1024]{1,0:T(8,128)(2,1)S(1)} collective-permute-done((bf16[32,1024]{1,0:T(8,128)(2,1)S(1)}, bf16[32,1024]{1,0:T(8,128)(2,1)S(1)}, u32[]{:S(2)}, u32[]{:S(2)}) %collective-permute-start.11) | collective-permute-done | bytes 65568 | tf_op jit(solution)/shard_map/ppermute | solution.py:14
  29.4 1.7 %collective-permute-done.8 = bf16[32,1024]{1,0:T(8,128)(2,1)S(1)} collective-permute-done((bf16[32,1024]{1,0:T(8,128)(2,1)S(1)}, bf16[32,1024]{1,0:T(8,128)(2,1)S(1)}, u32[]{:S(2)}, u32[]{:S(2)}) %collective-permute-start.8) | collective-permute-done | bytes 65568 | tf_op jit(solution)/shard_map/ppermute | solution.py:14
  32.2 1.1 %collective-permute-done.12 = f32[128]{0:T(128)S(1)} collective-permute-done((f32[128]{0:T(128)S(1)}, f32[128]{0:T(128)S(1)}, u32[]{:S(2)}, u32[]{:S(2)}) %collective-permute-start.12) | collective-permute-done | bytes 544 | tf_op jit(solution)/shard_map/ppermute | solution.py:64
  33.3 0.8 %multiply_convert_fusion.normed_ref = bf16[128,1024]{1,0:T(8,128)(2,1)} fusion(bf16[128,1024]{1,0:T(8,128)(2,1)S(1)} %copy-done.1, f32[1024]{0:T(1024)S(1)} %copy-done.4, f32[128]{0:T(128)S(1)} %add_rsqrt_fusion, bf16[32,1024]{1,0:T(8,128)(2,1)S(1)} %fusion.28, bf16[32,1024]{1,0:T(8,128)(2,1)S(1)} %fusion.22, bf16[32,1024]{1,0:T(8,128)(2,1)S(1)} %fusion.16, ...), kind=kLoop, calls=%fused_computation.13 | loop fusion | flops 1835008 | bytes 791040 | tf_op jit(solution)/shard_map/convert_element_type | solution.py:98
  34.2 4.8 %shard_map.120 = f32[128,1024]{1,0:T(8,128)} custom-call(bf16[128,1024]{1,0:T(8,128)(2,1)} %multiply_convert_fusion.normed_ref, bf16[128,1024]{1,0:T(8,128)(2,1)} %cot_ref.1, bf16[8,128,512]{2,1,0:T(8,128)(2,1)} %wg_ref.1, bf16[8,128,512]{2,1,0:T(8,128)(2,1)} %wu_ref.1, bf16[8,512,128]{2,1,0:T(8,128)(2,1)} %wd_ref.1), custom_call_target="tpu_custom_call" | custom-call | tf_op jit(solution)/shard_map/pallas_call | solution.py:44
  39.0 1.3 %multiply_reduce_fusion = f32[128]{0:T(128)S(1)} fusion(f32[128,1024]{1,0:T(8,128)} %shard_map.120, bf16[128,1024]{1,0:T(8,128)(2,1)S(1)} %copy-done.1, f32[1024]{0:T(1024)S(1)} %copy-done.4, bf16[32,1024]{1,0:T(8,128)(2,1)S(1)} %fusion.28, bf16[32,1024]{1,0:T(8,128)(2,1)S(1)} %fusion.22, bf16[32,1024]{1,0:T(8,128)(2,1)S(1)} %fusion.16, ...), kind=kLoop, calls=%fused_computation.12 | loop fusion | flops 1834880 | bytes 1053184 | tf_op jit(solution)/shard_map/reduce_sum | solution.py:101
  40.6 0.9 %collective-permute-done.13 = f32[128]{0:T(128)S(1)} collective-permute-done((f32[128]{0:T(128)S(1)}, f32[128]{0:T(128)S(1)}, u32[]{:S(2)}, u32[]{:S(2)}) %collective-permute-start.13) | collective-permute-done | bytes 544 | tf_op jit(solution)/shard_map/ppermute | solution.py:64
  42.2 2.9 %collective-permute-start.20 = (bf16[32,1024]{1,0:T(8,128)(2,1)S(1)}, bf16[32,1024]{1,0:T(8,128)(2,1)S(1)}, u32[]{:S(2)}, u32[]{:S(2)}) collective-permute-start(bf16[32,1024]{1,0:T(8,128)(2,1)S(1)} %get-tuple-element.37), channel_id=1, source_target_pairs={{0,8},{2,10},{4,12},{6,14},{8,0},{10,2},{12,4},{14,6},{1,9},{3,11}... | collective-permute-start | bytes 196616 | tf_op jit(solution)/shard_map/ppermute | solution.py:14
  45.2 5.7 %collective-permute-done.14 = bf16[32,1024]{1,0:T(8,128)(2,1)S(1)} collective-permute-done((bf16[32,1024]{1,0:T(8,128)(2,1)S(1)}, bf16[32,1024]{1,0:T(8,128)(2,1)S(1)}, u32[]{:S(2)}, u32[]{:S(2)}) %collective-permute-start.14) | collective-permute-done | bytes 65568 | tf_op jit(solution)/shard_map/ppermute | solution.py:14
  51.2 2.5 %collective-permute-start.15 = (bf16[32,1024]{1,0:T(8,128)(2,1)S(1)}, bf16[32,1024]{1,0:T(8,128)(2,1)S(1)}, u32[]{:S(2)}, u32[]{:S(2)}) collective-permute-start(bf16[32,1024]{1,0:T(8,128)(2,1)S(1)} %fusion.36), channel_id=1, source_target_pairs={{0,4},{2,6},{4,0},{6,2},{8,12},{10,14},{12,8},{14,10},{1,5},{3,7},... | collective-permute-start | bytes 196616 | tf_op jit(solution)/shard_map/ppermute | solution.py:14
  53.7 3.1 %collective-permute-done.23 = bf16[32,1024]{1,0:T(8,128)(2,1)S(1)} collective-permute-done((bf16[32,1024]{1,0:T(8,128)(2,1)S(1)}, bf16[32,1024]{1,0:T(8,128)(2,1)S(1)}, u32[]{:S(2)}, u32[]{:S(2)}) %collective-permute-start.23) | collective-permute-done | bytes 65568 | tf_op jit(solution)/shard_map/ppermute | solution.py:14
  57.4 2.0 %collective-permute-start.21 = (bf16[32,1024]{1,0:T(8,128)(2,1)S(1)}, bf16[32,1024]{1,0:T(8,128)(2,1)S(1)}, u32[]{:S(2)}, u32[]{:S(2)}) collective-permute-start(bf16[32,1024]{1,0:T(8,128)(2,1)S(1)} %fusion.66), channel_id=1, source_target_pairs={{0,4},{2,6},{4,0},{6,2},{8,12},{10,14},{12,8},{14,10},{1,5},{3,7},... | collective-permute-start | bytes 196616 | tf_op jit(solution)/shard_map/ppermute | solution.py:14
  59.5 2.9 %collective-permute-done.18 = bf16[32,1024]{1,0:T(8,128)(2,1)S(1)} collective-permute-done((bf16[32,1024]{1,0:T(8,128)(2,1)S(1)}, bf16[32,1024]{1,0:T(8,128)(2,1)S(1)}, u32[]{:S(2)}, u32[]{:S(2)}) %collective-permute-start.18) | collective-permute-done | bytes 65568 | tf_op jit(solution)/shard_map/ppermute | solution.py:14
  62.4 0.8 %collective-permute-done.21 = bf16[32,1024]{1,0:T(8,128)(2,1)S(1)} collective-permute-done((bf16[32,1024]{1,0:T(8,128)(2,1)S(1)}, bf16[32,1024]{1,0:T(8,128)(2,1)S(1)}, u32[]{:S(2)}, u32[]{:S(2)}) %collective-permute-start.21) | collective-permute-done | bytes 65568 | tf_op jit(solution)/shard_map/ppermute | solution.py:14
  65.3 0.8 %collective-permute-start.25 = (bf16[32,1024]{1,0:T(8,128)(2,1)S(1)}, bf16[32,1024]{1,0:T(8,128)(2,1)S(1)}, u32[]{:S(2)}, u32[]{:S(2)}) collective-permute-start(bf16[32,1024]{1,0:T(8,128)(2,1)S(1)} %fusion.86), channel_id=1, source_target_pairs={{0,2},{2,0},{4,6},{6,4},{8,10},{10,8},{12,14},{14,12},{1,3},{3,1},... | collective-permute-start | bytes 196616 | tf_op jit(solution)/shard_map/ppermute | solution.py:14
  66.1 1.3 %collective-permute-start.22 = (bf16[32,1024]{1,0:T(8,128)(2,1)S(1)}, bf16[32,1024]{1,0:T(8,128)(2,1)S(1)}, u32[]{:S(2)}, u32[]{:S(2)}) collective-permute-start(bf16[32,1024]{1,0:T(8,128)(2,1)S(1)} %fusion.71), channel_id=1, source_target_pairs={{0,2},{2,0},{4,6},{6,4},{8,10},{10,8},{12,14},{14,12},{1,3},{3,1},... | collective-permute-start | bytes 196616 | tf_op jit(solution)/shard_map/ppermute | solution.py:14
  68.1 1.3 %collective-permute-start.16 = (bf16[32,1024]{1,0:T(8,128)(2,1)S(1)}, bf16[32,1024]{1,0:T(8,128)(2,1)S(1)}, u32[]{:S(2)}, u32[]{:S(2)}) collective-permute-start(bf16[32,1024]{1,0:T(8,128)(2,1)S(1)} %fusion.41), channel_id=1, source_target_pairs={{0,2},{2,0},{4,6},{6,4},{8,10},{10,8},{12,14},{14,12},{1,3},{3,1},... | collective-permute-start | bytes 196616 | tf_op jit(solution)/shard_map/ppermute | solution.py:14
  70.9 0.9 %collective-permute-done.22 = bf16[32,1024]{1,0:T(8,128)(2,1)S(1)} collective-permute-done((bf16[32,1024]{1,0:T(8,128)(2,1)S(1)}, bf16[32,1024]{1,0:T(8,128)(2,1)S(1)}, u32[]{:S(2)}, u32[]{:S(2)}) %collective-permute-start.22) | collective-permute-done | bytes 65568 | tf_op jit(solution)/shard_map/ppermute | solution.py:14
  71.8 1.1 %collective-permute-done.19 = bf16[32,1024]{1,0:T(8,128)(2,1)S(1)} collective-permute-done((bf16[32,1024]{1,0:T(8,128)(2,1)S(1)}, bf16[32,1024]{1,0:T(8,128)(2,1)S(1)}, u32[]{:S(2)}, u32[]{:S(2)}) %collective-permute-start.19) | collective-permute-done | bytes 65568 | tf_op jit(solution)/shard_map/ppermute | solution.py:14
  74.0 1.1 %fusion.1 = bf16[128,1024]{1,0:T(8,128)(2,1)} fusion(bf16[32,1024]{1,0:T(8,128)(2,1)S(1)} %fusion.85, bf16[32,1024]{1,0:T(8,128)(2,1)S(1)} %fusion.70, bf16[32,1024]{1,0:T(8,128)(2,1)S(1)} %fusion.55, bf16[32,1024]{1,0:T(8,128)(2,1)S(1)} %fusion.40, bf16[1,128,128]{2,1,0:T(8,128)(2,1)S(1)} %copy-done, f32[128]{0:T(128)S(1)} %fusion.92, ...), kind=kOutput, calls=%fused_computation.2 | convolution fusion | flops 37355520 | bytes 1872896 | tf_op jit(solution)/shard_map/kij,kid->kjd/dot_general | solution.py:132
  (83 shorter events, 12.7 us)
Async XLA Ops:
  2.6 5.9 %collective-permute-start = (bf16[32,1024]{1,0:T(8,128)(2,1)S(1)}, bf16[32,1024]{1,0:T(8,128)(2,1)S(1)}, u32[]{:S(2)}, u32[]{:S(2)}) collective-permute-start(bf16[32,1024]{1,0:T(8,128)(2,1)S(1)} %get-tuple-element.50), channel_id=1, source_target_pairs={{0,2},{2,0},{4,6},{6,4},{8,10},{10,8},{12,14},{14,12},{1,3},{3,1},... | collective-permute-start | bytes 196616 | tf_op jit(solution)/shard_map/ppermute | solution.py:14
  5.6 5.0 %collective-permute-start.9 = (bf16[32,1024]{1,0:T(8,128)(2,1)S(1)}, bf16[32,1024]{1,0:T(8,128)(2,1)S(1)}, u32[]{:S(2)}, u32[]{:S(2)}) collective-permute-start(bf16[32,1024]{1,0:T(8,128)(2,1)S(1)} %get-tuple-element.51), channel_id=1, source_target_pairs={{0,2},{2,0},{4,6},{6,4},{8,10},{10,8},{12,14},{14,12},{1,3},{3,1},... | collective-permute-start | bytes 196616 | tf_op jit(solution)/shard_map/ppermute | solution.py:14
  5.7 5.7 %collective-permute-start.6 = (bf16[32,1024]{1,0:T(8,128)(2,1)S(1)}, bf16[32,1024]{1,0:T(8,128)(2,1)S(1)}, u32[]{:S(2)}, u32[]{:S(2)}) collective-permute-start(bf16[32,1024]{1,0:T(8,128)(2,1)S(1)} %get-tuple-element.52), channel_id=1, source_target_pairs={{0,2},{2,0},{4,6},{6,4},{8,10},{10,8},{12,14},{14,12},{1,3},{3,1},... | collective-permute-start | bytes 196616 | tf_op jit(solution)/shard_map/ppermute | solution.py:14
  7.6 4.4 %collective-permute-start.3 = (bf16[32,1024]{1,0:T(8,128)(2,1)S(1)}, bf16[32,1024]{1,0:T(8,128)(2,1)S(1)}, u32[]{:S(2)}, u32[]{:S(2)}) collective-permute-start(bf16[32,1024]{1,0:T(8,128)(2,1)S(1)} %get-tuple-element.53), channel_id=1, source_target_pairs={{0,2},{2,0},{4,6},{6,4},{8,10},{10,8},{12,14},{14,12},{1,3},{3,1},... | collective-permute-start | bytes 196616 | tf_op jit(solution)/shard_map/ppermute | solution.py:14
  12.2 5.1 %collective-permute-start.4 = (bf16[32,1024]{1,0:T(8,128)(2,1)S(1)}, bf16[32,1024]{1,0:T(8,128)(2,1)S(1)}, u32[]{:S(2)}, u32[]{:S(2)}) collective-permute-start(bf16[32,1024]{1,0:T(8,128)(2,1)S(1)} %get-tuple-element.46), channel_id=1, source_target_pairs={{0,4},{2,6},{4,0},{6,2},{8,12},{10,14},{12,8},{14,10},{1,5},{3,7},... | collective-permute-start | bytes 196616 | tf_op jit(solution)/shard_map/ppermute | solution.py:14
  14.4 6.1 %collective-permute-start.10 = (bf16[32,1024]{1,0:T(8,128)(2,1)S(1)}, bf16[32,1024]{1,0:T(8,128)(2,1)S(1)}, u32[]{:S(2)}, u32[]{:S(2)}) collective-permute-start(bf16[32,1024]{1,0:T(8,128)(2,1)S(1)} %get-tuple-element.47), channel_id=1, source_target_pairs={{0,4},{2,6},{4,0},{6,2},{8,12},{10,14},{12,8},{14,10},{1,5},{3,7},... | collective-permute-start | bytes 196616 | tf_op jit(solution)/shard_map/ppermute | solution.py:14
  14.5 7.7 %collective-permute-start.7 = (bf16[32,1024]{1,0:T(8,128)(2,1)S(1)}, bf16[32,1024]{1,0:T(8,128)(2,1)S(1)}, u32[]{:S(2)}, u32[]{:S(2)}) collective-permute-start(bf16[32,1024]{1,0:T(8,128)(2,1)S(1)} %get-tuple-element.48), channel_id=1, source_target_pairs={{0,4},{2,6},{4,0},{6,2},{8,12},{10,14},{12,8},{14,10},{1,5},{3,7},... | collective-permute-start | bytes 196616 | tf_op jit(solution)/shard_map/ppermute | solution.py:14
  16.4 7.3 %collective-permute-start.1 = (bf16[32,1024]{1,0:T(8,128)(2,1)S(1)}, bf16[32,1024]{1,0:T(8,128)(2,1)S(1)}, u32[]{:S(2)}, u32[]{:S(2)}) collective-permute-start(bf16[32,1024]{1,0:T(8,128)(2,1)S(1)} %get-tuple-element.49), channel_id=1, source_target_pairs={{0,4},{2,6},{4,0},{6,2},{8,12},{10,14},{12,8},{14,10},{1,5},{3,7},... | collective-permute-start | bytes 196616 | tf_op jit(solution)/shard_map/ppermute | solution.py:14
  17.4 8.0 %collective-permute-start.5 = (bf16[32,1024]{1,0:T(8,128)(2,1)S(1)}, bf16[32,1024]{1,0:T(8,128)(2,1)S(1)}, u32[]{:S(2)}, u32[]{:S(2)}) collective-permute-start(bf16[32,1024]{1,0:T(8,128)(2,1)S(1)} %fusion.14), channel_id=1, source_target_pairs={{0,8},{2,10},{4,12},{6,14},{8,0},{10,2},{12,4},{14,6},{1,9},{3,11}... | collective-permute-start | bytes 196616 | tf_op jit(solution)/shard_map/ppermute | solution.py:14
  20.5 8.8 %collective-permute-start.11 = (bf16[32,1024]{1,0:T(8,128)(2,1)S(1)}, bf16[32,1024]{1,0:T(8,128)(2,1)S(1)}, u32[]{:S(2)}, u32[]{:S(2)}) collective-permute-start(bf16[32,1024]{1,0:T(8,128)(2,1)S(1)} %fusion.26), channel_id=1, source_target_pairs={{0,8},{2,10},{4,12},{6,14},{8,0},{10,2},{12,4},{14,6},{1,9},{3,11}... | collective-permute-start | bytes 196616 | tf_op jit(solution)/shard_map/ppermute | solution.py:14
  22.3 8.9 %collective-permute-start.8 = (bf16[32,1024]{1,0:T(8,128)(2,1)S(1)}, bf16[32,1024]{1,0:T(8,128)(2,1)S(1)}, u32[]{:S(2)}, u32[]{:S(2)}) collective-permute-start(bf16[32,1024]{1,0:T(8,128)(2,1)S(1)} %fusion.20), channel_id=1, source_target_pairs={{0,8},{2,10},{4,12},{6,14},{8,0},{10,2},{12,4},{14,6},{1,9},{3,11}... | collective-permute-start | bytes 196616 | tf_op jit(solution)/shard_map/ppermute | solution.py:14
  23.8 8.1 %collective-permute-start.2 = (bf16[32,1024]{1,0:T(8,128)(2,1)S(1)}, bf16[32,1024]{1,0:T(8,128)(2,1)S(1)}, u32[]{:S(2)}, u32[]{:S(2)}) collective-permute-start(bf16[32,1024]{1,0:T(8,128)(2,1)S(1)} %fusion.8), channel_id=1, source_target_pairs={{0,8},{2,10},{4,12},{6,14},{8,0},{10,2},{12,4},{14,6},{1,9},{3,11}... | collective-permute-start | bytes 196616 | tf_op jit(solution)/shard_map/ppermute | solution.py:14
  29.3 2.6 %copy-start.1 = (bf16[128,1024]{1,0:T(8,128)(2,1)S(1)}, bf16[128,1024]{1,0:T(8,128)(2,1)}, u32[]{:S(2)}) copy-start(bf16[128,1024]{1,0:T(8,128)(2,1)} %param.9) | copy-start | bytes 786436
  32.2 1.2 %collective-permute-start.12 = (f32[128]{0:T(128)S(1)}, f32[128]{0:T(128)S(1)}, u32[]{:S(2)}, u32[]{:S(2)}) collective-permute-start(f32[128]{0:T(128)S(1)} %multiply_reduce_fusion.1), channel_id=1, source_target_pairs={{0,1},{1,0},{2,3},{3,2},{4,5},{5,4},{6,7},{7,6},{8,9},{9,8},{10,11... | collective-permute-start | bytes 1544 | tf_op jit(solution)/shard_map/ppermute | solution.py:64
  39.0 2.5 %copy-start.2 = (f32[128,1024]{1,0:T(8,128)S(1)}, f32[128,1024]{1,0:T(8,128)}, u32[]{:S(2)}) copy-start(f32[128,1024]{1,0:T(8,128)} %shard_map.120) | copy-start | bytes 1572868
  39.0 2.5 %copy-start.3 = (bf16[128,1024]{1,0:T(8,128)(2,1)S(1)}, bf16[128,1024]{1,0:T(8,128)(2,1)}, u32[]{:S(2)}) copy-start(bf16[128,1024]{1,0:T(8,128)(2,1)} %cot_ref.1) | copy-start | bytes 786436
  40.3 1.2 %collective-permute-start.13 = (f32[128]{0:T(128)S(1)}, f32[128]{0:T(128)S(1)}, u32[]{:S(2)}, u32[]{:S(2)}) collective-permute-start(f32[128]{0:T(128)S(1)} %multiply_reduce_fusion), channel_id=1, source_target_pairs={{0,1},{1,0},{2,3},{3,2},{4,5},{5,4},{6,7},{7,6},{8,9},{9,8},{10,11... | collective-permute-start | bytes 1544 | tf_op jit(solution)/shard_map/ppermute | solution.py:64
  42.1 8.7 %collective-permute-start.14 = (bf16[32,1024]{1,0:T(8,128)(2,1)S(1)}, bf16[32,1024]{1,0:T(8,128)(2,1)S(1)}, u32[]{:S(2)}, u32[]{:S(2)}) collective-permute-start(bf16[32,1024]{1,0:T(8,128)(2,1)S(1)} %get-tuple-element.36), channel_id=1, source_target_pairs={{0,8},{2,10},{4,12},{6,14},{8,0},{10,2},{12,4},{14,6},{1,9},{3,11}... | collective-permute-start | bytes 196616 | tf_op jit(solution)/shard_map/ppermute | solution.py:14
  42.2 11.5 %collective-permute-start.20 = (bf16[32,1024]{1,0:T(8,128)(2,1)S(1)}, bf16[32,1024]{1,0:T(8,128)(2,1)S(1)}, u32[]{:S(2)}, u32[]{:S(2)}) collective-permute-start(bf16[32,1024]{1,0:T(8,128)(2,1)S(1)} %get-tuple-element.37), channel_id=1, source_target_pairs={{0,8},{2,10},{4,12},{6,14},{8,0},{10,2},{12,4},{14,6},{1,9},{3,11}... | collective-permute-start | bytes 196616 | tf_op jit(solution)/shard_map/ppermute | solution.py:14
  45.1 8.6 %collective-permute-start.17 = (bf16[32,1024]{1,0:T(8,128)(2,1)S(1)}, bf16[32,1024]{1,0:T(8,128)(2,1)S(1)}, u32[]{:S(2)}, u32[]{:S(2)}) collective-permute-start(bf16[32,1024]{1,0:T(8,128)(2,1)S(1)} %get-tuple-element.38), channel_id=1, source_target_pairs={{0,8},{2,10},{4,12},{6,14},{8,0},{10,2},{12,4},{14,6},{1,9},{3,11}... | collective-permute-start | bytes 196616 | tf_op jit(solution)/shard_map/ppermute | solution.py:14
  51.1 5.7 %collective-permute-start.23 = (bf16[32,1024]{1,0:T(8,128)(2,1)S(1)}, bf16[32,1024]{1,0:T(8,128)(2,1)S(1)}, u32[]{:S(2)}, u32[]{:S(2)}) collective-permute-start(bf16[32,1024]{1,0:T(8,128)(2,1)S(1)} %get-tuple-element.45), channel_id=1, source_target_pairs={{0,8},{2,10},{4,12},{6,14},{8,0},{10,2},{12,4},{14,6},{1,9},{3,11}... | collective-permute-start | bytes 196616 | tf_op jit(solution)/shard_map/ppermute | solution.py:14
  51.2 8.3 %collective-permute-start.15 = (bf16[32,1024]{1,0:T(8,128)(2,1)S(1)}, bf16[32,1024]{1,0:T(8,128)(2,1)S(1)}, u32[]{:S(2)}, u32[]{:S(2)}) collective-permute-start(bf16[32,1024]{1,0:T(8,128)(2,1)S(1)} %fusion.36), channel_id=1, source_target_pairs={{0,4},{2,6},{4,0},{6,2},{8,12},{10,14},{12,8},{14,10},{1,5},{3,7},... | collective-permute-start | bytes 196616 | tf_op jit(solution)/shard_map/ppermute | solution.py:14
  57.3 5.0 %collective-permute-start.18 = (bf16[32,1024]{1,0:T(8,128)(2,1)S(1)}, bf16[32,1024]{1,0:T(8,128)(2,1)S(1)}, u32[]{:S(2)}, u32[]{:S(2)}) collective-permute-start(bf16[32,1024]{1,0:T(8,128)(2,1)S(1)} %fusion.51), channel_id=1, source_target_pairs={{0,4},{2,6},{4,0},{6,2},{8,12},{10,14},{12,8},{14,10},{1,5},{3,7},... | collective-permute-start | bytes 196616 | tf_op jit(solution)/shard_map/ppermute | solution.py:14
  57.4 5.8 %collective-permute-start.21 = (bf16[32,1024]{1,0:T(8,128)(2,1)S(1)}, bf16[32,1024]{1,0:T(8,128)(2,1)S(1)}, u32[]{:S(2)}, u32[]{:S(2)}) collective-permute-start(bf16[32,1024]{1,0:T(8,128)(2,1)S(1)} %fusion.66), channel_id=1, source_target_pairs={{0,4},{2,6},{4,0},{6,2},{8,12},{10,14},{12,8},{14,10},{1,5},{3,7},... | collective-permute-start | bytes 196616 | tf_op jit(solution)/shard_map/ppermute | solution.py:14
  59.4 4.5 %collective-permute-start.24 = (bf16[32,1024]{1,0:T(8,128)(2,1)S(1)}, bf16[32,1024]{1,0:T(8,128)(2,1)S(1)}, u32[]{:S(2)}, u32[]{:S(2)}) collective-permute-start(bf16[32,1024]{1,0:T(8,128)(2,1)S(1)} %fusion.81), channel_id=1, source_target_pairs={{0,4},{2,6},{4,0},{6,2},{8,12},{10,14},{12,8},{14,10},{1,5},{3,7},... | collective-permute-start | bytes 196616 | tf_op jit(solution)/shard_map/ppermute | solution.py:14
  64.4 3.8 %collective-permute-start.27 = (f32[3,128]{1,0:T(4,128)S(1)}, f32[3,128]{1,0:T(4,128)S(1)}, u32[]{:S(2)}, u32[]{:S(2)}) collective-permute-start(f32[3,128]{1,0:T(4,128)S(1)} %maximum_maximum_fusion.1), channel_id=1, source_target_pairs={{0,1},{1,0},{2,3},{3,2},{4,5},{5,4},{6,7},{7,6},{8,9},{9,8},{10,11... | collective-permute-start | bytes 4616 | tf_op jit(solution)/shard_map/ppermute | solution.py:64
  64.5 5.6 %collective-permute-start.26 = (f32[3,128]{1,0:T(4,128)S(1)}, f32[3,128]{1,0:T(4,128)S(1)}, u32[]{:S(2)}, u32[]{:S(2)}) collective-permute-start(f32[3,128]{1,0:T(4,128)S(1)} %maximum_maximum_fusion), channel_id=1, source_target_pairs={{0,1},{1,0},{2,3},{3,2},{4,5},{5,4},{6,7},{7,6},{8,9},{9,8},{10,11... | collective-permute-start | bytes 4616 | tf_op jit(solution)/shard_map/ppermute | solution.py:64
  65.3 5.4 %collective-permute-start.25 = (bf16[32,1024]{1,0:T(8,128)(2,1)S(1)}, bf16[32,1024]{1,0:T(8,128)(2,1)S(1)}, u32[]{:S(2)}, u32[]{:S(2)}) collective-permute-start(bf16[32,1024]{1,0:T(8,128)(2,1)S(1)} %fusion.86), channel_id=1, source_target_pairs={{0,2},{2,0},{4,6},{6,4},{8,10},{10,8},{12,14},{14,12},{1,3},{3,1},... | collective-permute-start | bytes 196616 | tf_op jit(solution)/shard_map/ppermute | solution.py:14
  66.1 5.6 %collective-permute-start.22 = (bf16[32,1024]{1,0:T(8,128)(2,1)S(1)}, bf16[32,1024]{1,0:T(8,128)(2,1)S(1)}, u32[]{:S(2)}, u32[]{:S(2)}) collective-permute-start(bf16[32,1024]{1,0:T(8,128)(2,1)S(1)} %fusion.71), channel_id=1, source_target_pairs={{0,2},{2,0},{4,6},{6,4},{8,10},{10,8},{12,14},{14,12},{1,3},{3,1},... | collective-permute-start | bytes 196616 | tf_op jit(solution)/shard_map/ppermute | solution.py:14
  67.4 5.5 %collective-permute-start.19 = (bf16[32,1024]{1,0:T(8,128)(2,1)S(1)}, bf16[32,1024]{1,0:T(8,128)(2,1)S(1)}, u32[]{:S(2)}, u32[]{:S(2)}) collective-permute-start(bf16[32,1024]{1,0:T(8,128)(2,1)S(1)} %fusion.56), channel_id=1, source_target_pairs={{0,2},{2,0},{4,6},{6,4},{8,10},{10,8},{12,14},{14,12},{1,3},{3,1},... | collective-permute-start | bytes 196616 | tf_op jit(solution)/shard_map/ppermute | solution.py:14
  68.1 5.5 %collective-permute-start.16 = (bf16[32,1024]{1,0:T(8,128)(2,1)S(1)}, bf16[32,1024]{1,0:T(8,128)(2,1)S(1)}, u32[]{:S(2)}, u32[]{:S(2)}) collective-permute-start(bf16[32,1024]{1,0:T(8,128)(2,1)S(1)} %fusion.41), channel_id=1, source_target_pairs={{0,2},{2,0},{4,6},{6,4},{8,10},{10,8},{12,14},{14,12},{1,3},{3,1},... | collective-permute-start | bytes 196616 | tf_op jit(solution)/shard_map/ppermute | solution.py:14
  73.9 1.3 %collective-permute-start.28 = (f32[1,128,128]{2,1,0:T(8,128)S(1)}, f32[1,128,128]{2,1,0:T(8,128)S(1)}, u32[]{:S(2)}, u32[]{:S(2)}) collective-permute-start(f32[1,128,128]{2,1,0:T(8,128)S(1)} %convolution_bitcast_fusion.1), channel_id=1, source_target_pairs={{0,1},{1,0},{2,3},{3,2},{4,5},{5,4},{6,7},{7,6},{8,9},{9,8},{10,11... | collective-permute-start | bytes 196616 | tf_op jit(solution)/shard_map/ppermute | solution.py:64
  (4 other events, 5.0 us)

commit v8 on v6

--- a/solution.py
+++ b/solution.py
@@ -14,12 +14,18 @@
     return lax.ppermute(value, axis, pairs)
 
 
-def ffn_kernel(normed_ref, cot_ref, wg_ref, wu_ref, wd_ref, out_ref):
+def ffn_kernel(tok_ref, mix_ref, inv_ref, gain_ref, cot_ref, wg_ref, wu_ref, wd_ref,
+               scaled_ref, acc_ref):
     cblock = wg_ref.shape[1]
     contract_last = (((1,), (1,)), ((), ()))
+    inv = inv_ref[...]
+    acc = jnp.zeros(acc_ref.shape, jnp.float32)
     for group in range(wg_ref.shape[0]):
         cols = slice(group * cblock, (group + 1) * cblock)
-        normed = normed_ref[:, cols]
+        tok = tok_ref[:, cols].astype(jnp.float32)
+        resid = tok + tok * mix_ref[:, cols].astype(jnp.float32)
+        gain = gain_ref[:, cols]
+        normed = (resid * inv * gain).astype(jnp.bfloat16)
         w_gate = wg_ref[group]
         w_up = wu_ref[group]
         gate_pre = jnp.dot(normed, w_gate, preferred_element_type=jnp.float32)
@@ -30,13 +36,24 @@
         sig = 1.0 / (1.0 + jnp.exp(-gate_pre))
         d_up = (d_hidden * gate_pre * sig).astype(jnp.bfloat16)
         d_gate = (d_hidden * up_val * sig * (1.0 + gate_pre * (1.0 - sig))).astype(jnp.bfloat16)
-        out_ref[:, cols] = lax.dot_general(
+        d_normed = lax.dot_general(
             d_gate, w_gate, contract_last, preferred_element_type=jnp.float32
         ) + lax.dot_general(d_up, w_up, contract_last, preferred_element_type=jnp.float32)
+        scaled = gain * d_normed
+        scaled_ref[:, cols] = scaled
+        acc = acc + resid * scaled
+
+    @pl.when(pl.program_id(0) == 0)
+    def _():
+        acc_ref[...] = acc
+
+    @pl.when(pl.program_id(0) > 0)
+    def _():
+        acc_ref[...] += acc
 
 
-def ffn_grad(normed, cotangent, w_gate, w_up, w_down, per_step=4):
-    tok, width = normed.shape
+def ffn_grad(tokens, mixed, inv, norm_gain, cotangent, w_gate, w_up, w_down, per_step=4):
+    tok, width = tokens.shape
     groups_here, cblock, hidden = w_gate.shape
     if groups_here % per_step:
         per_step = 1
@@ -47,13 +64,19 @@
         in_specs=[
             act,
             act,
+            pl.BlockSpec((tok, 1), lambda g: (0, 0)),
+            pl.BlockSpec((1, cblock * per_step), lambda g: (0, g)),
+            act,
             pl.BlockSpec((per_step, cblock, hidden), lambda g: (g, 0, 0)),
             pl.BlockSpec((per_step, cblock, hidden), lambda g: (g, 0, 0)),
             pl.BlockSpec((per_step, hidden, cblock), lambda g: (g, 0, 0)),
         ],
-        out_specs=act,
-        out_shape=jax.ShapeDtypeStruct((tok, width), jnp.float32),
-    )(normed, cotangent, w_gate, w_up, w_down)
+        out_specs=[act, pl.BlockSpec((tok, cblock), lambda g: (0, 0))],
+        out_shape=[
+            jax.ShapeDtypeStruct((tok, width), jnp.float32),
+            jax.ShapeDtypeStruct((tok, cblock), jnp.float32),
+        ],
+    )(tokens, mixed, inv[:, None], norm_gain[None, :], cotangent, w_gate, w_up, w_down)
 
 
 def hid_sum(value):
@@ -95,10 +118,8 @@
     resid = tok_f + tok_f * mixed_f
     square = hid_sum(jnp.sum(resid * resid, axis=-1))
     inv = lax.rsqrt(square / D + 1e-06)
-    normed = (resid * inv[:, None] * norm_gain).astype(jnp.bfloat16)
-    d_normed = ffn_grad(normed, cotangent, w_gate, w_up, w_down)
-    scaled = norm_gain * d_normed
-    inner = hid_sum(jnp.sum(resid * scaled, axis=-1))
+    scaled, lanes = ffn_grad(tokens, current, inv, norm_gain, cotangent, w_gate, w_up, w_down)
+    inner = hid_sum(jnp.sum(lanes, axis=-1))
     d_resid = (
         cotangent.astype(jnp.float32)
         + inv[:, None] * scaled

time: 76.4 us -> 77.6 us (1.016)
    convert_element_type x1, other arithmetic: 0.31 us -> 1.27 us  [body(): d_mixed = (d_resid * tok_f).astype(jnp.bfloat16)]
    convert_element_type x1 -> x0, other arithmetic: 0.82 us -> none  [body(): normed = (resid * inv[:, None] * norm_gain).astype(jnp.bfloat16)]
  transfers between devices with their start and end apart: 17 -> 17, of which waited for: 14 -> 14; matrix products, arithmetic and copies ran while one was open for 4% -> 5% of each run, Pallas kernels for 0% -> 0%
where the time goes in v8:
time: 77.6 us; the launch traced here: 77.2 us
  waiting for transfers between devices  40.8 us (53%)
  starting transfers between devices  18.8 us (24%)
  other arithmetic  7.41 us (10%)
  Pallas kernels  5.35 us (7%)
  matrix products  2.45 us (3%)
  local copies, waits for them, and re-layouts  1.63 us (2%)
  between operations  0.85 us (1%)
    ppermute x12, waiting for transfers between devices, from_partner(): return lax.ppermute(value, axis, pairs)  39.3 us
    ppermute x12, starting transfers between devices, from_partner(): return lax.ppermute(value, axis, pairs)  17.9 us
    pallas_call x1, Pallas kernels, ffn_grad(): pl.pallas_call(ffn_kernel, grid=(groups_here // per_step,), in_specs=[act...  5.35 us
    add x3, other arithmetic, hid_sum(): total = total + lax.ppermute(value, 'hid', pairs)  1.95 us
  transfers between devices with their start and end apart: 17, of which 14 were waited for; matrix products, arithmetic and copies ran while one was open for 5% of the time, Pallas kernels for 0%

profile of v8, /device:TPU:0, one launch (start us, length us, event | category | flops | bytes accessed | tf_op | source)
XLA Modules:
  0.0 77.2 jit_solution(16964386406622678581)
XLA Ops:
  0.6 0.7 copy-done
  1.4 1.2 %fusion.2 = bf16[1,128,1024]{2,1,0:T(8,128)(2,1)S(1)} fusion(bf16[128,1024]{1,0:T(8,128)(2,1)} %tok_ref.1, bf16[1,128,128]{2,1,0:T(8,128)(2,1)S(1)} %copy-done), kind=kOutput, calls=%fused_computation.4 | convolution fusion | flops 33685504 | bytes 557056 | tf_op jit(solution)/shard_map/kij,kjd->kid/dot_general | solution.py:97
  2.6 3.0 %collective-permute-start = (bf16[64,1024]{1,0:T(8,128)(2,1)S(1)}, bf16[64,1024]{1,0:T(8,128)(2,1)S(1)}, u32[]{:S(2)}, u32[]{:S(2)}) collective-permute-start(bf16[64,1024]{1,0:T(8,128)(2,1)S(1)} %get-tuple-element.31), channel_id=1, source_target_pairs={{0,2},{2,0},{4,6},{6,4},{8,10},{10,8},{12,14},{14,12},{1,3},{3,1},... | collective-permute-start | bytes 393224 | tf_op jit(solution)/shard_map/ppermute | solution.py:14
  5.8 4.2 %collective-permute-done = bf16[64,1024]{1,0:T(8,128)(2,1)S(1)} collective-permute-done((bf16[64,1024]{1,0:T(8,128)(2,1)S(1)}, bf16[64,1024]{1,0:T(8,128)(2,1)S(1)}, u32[]{:S(2)}, u32[]{:S(2)}) %collective-permute-start) | collective-permute-done | bytes 131104 | tf_op jit(solution)/shard_map/ppermute | solution.py:14
  9.9 2.0 %collective-permute-done.3 = bf16[64,1024]{1,0:T(8,128)(2,1)S(1)} collective-permute-done((bf16[64,1024]{1,0:T(8,128)(2,1)S(1)}, bf16[64,1024]{1,0:T(8,128)(2,1)S(1)}, u32[]{:S(2)}, u32[]{:S(2)}) %collective-permute-start.3) | collective-permute-done | bytes 131104 | tf_op jit(solution)/shard_map/ppermute | solution.py:14
  12.1 1.9 %collective-permute-start.4 = (bf16[64,1024]{1,0:T(8,128)(2,1)S(1)}, bf16[64,1024]{1,0:T(8,128)(2,1)S(1)}, u32[]{:S(2)}, u32[]{:S(2)}) collective-permute-start(bf16[64,1024]{1,0:T(8,128)(2,1)S(1)} %get-tuple-element.29), channel_id=1, source_target_pairs={{0,4},{2,6},{4,0},{6,2},{8,12},{10,14},{12,8},{14,10},{1,5},{3,7},... | collective-permute-start | bytes 393224 | tf_op jit(solution)/shard_map/ppermute | solution.py:14
  14.2 4.1 %collective-permute-done.4 = bf16[64,1024]{1,0:T(8,128)(2,1)S(1)} collective-permute-done((bf16[64,1024]{1,0:T(8,128)(2,1)S(1)}, bf16[64,1024]{1,0:T(8,128)(2,1)S(1)}, u32[]{:S(2)}, u32[]{:S(2)}) %collective-permute-start.4) | collective-permute-done | bytes 131104 | tf_op jit(solution)/shard_map/ppermute | solution.py:14
  18.4 2.8 %collective-permute-start.5 = (bf16[64,1024]{1,0:T(8,128)(2,1)S(1)}, bf16[64,1024]{1,0:T(8,128)(2,1)S(1)}, u32[]{:S(2)}, u32[]{:S(2)}) collective-permute-start(bf16[64,1024]{1,0:T(8,128)(2,1)S(1)} %fusion.14), channel_id=1, source_target_pairs={{0,8},{2,10},{4,12},{6,14},{8,0},{10,2},{12,4},{14,6},{1,9},{3,11}... | collective-permute-start | bytes 393224 | tf_op jit(solution)/shard_map/ppermute | solution.py:14
  21.3 2.7 %collective-permute-start.2 = (bf16[64,1024]{1,0:T(8,128)(2,1)S(1)}, bf16[64,1024]{1,0:T(8,128)(2,1)S(1)}, u32[]{:S(2)}, u32[]{:S(2)}) collective-permute-start(bf16[64,1024]{1,0:T(8,128)(2,1)S(1)} %fusion.8), channel_id=1, source_target_pairs={{0,8},{2,10},{4,12},{6,14},{8,0},{10,2},{12,4},{14,6},{1,9},{3,11}... | collective-permute-start | bytes 393224 | tf_op jit(solution)/shard_map/ppermute | solution.py:14
  24.0 5.2 %collective-permute-done.5 = bf16[64,1024]{1,0:T(8,128)(2,1)S(1)} collective-permute-done((bf16[64,1024]{1,0:T(8,128)(2,1)S(1)}, bf16[64,1024]{1,0:T(8,128)(2,1)S(1)}, u32[]{:S(2)}, u32[]{:S(2)}) %collective-permute-start.5) | collective-permute-done | bytes 131104 | tf_op jit(solution)/shard_map/ppermute | solution.py:14
  29.4 1.3 %collective-permute-done.2 = bf16[64,1024]{1,0:T(8,128)(2,1)S(1)} collective-permute-done((bf16[64,1024]{1,0:T(8,128)(2,1)S(1)}, bf16[64,1024]{1,0:T(8,128)(2,1)S(1)}, u32[]{:S(2)}, u32[]{:S(2)}) %collective-permute-start.2) | collective-permute-done | bytes 131104 | tf_op jit(solution)/shard_map/ppermute | solution.py:14
  31.0 0.7 pad_maximum_fusion.mix_ref
  32.1 0.7 copy.13.inv_ref
  32.9 5.3 %shard_map.120 = (f32[128,1024]{1,0:T(8,128)}, f32[128,128]{1,0:T(8,128)}) custom-call(bf16[128,1024]{1,0:T(8,128)(2,1)} %tok_ref.1, bf16[128,1024]{1,0:T(8,128)(2,1)} %pad_maximum_fusion.mix_ref, f32[128,1]{1,0:T(8,128)} %copy.13.inv_ref, f32[1,1024]{1,0:T(1,128)} %bitcast.92, bf16[128,1024]{1,0:T(8,128)(2,1)} %cot_ref.1, bf16[8,128,512]{2,1,0:T(8,128)(2,1)} %wg_ref.1, ...), custom_call_target="tpu_custom_call" | custom-call | tf_op jit(solution)/shard_map/pallas_call | solution.py:61
  38.2 0.9 %reduce_sum.127 = f32[128]{0:T(128)S(1)} reduce(f32[128,128]{1,0:T(8,128)} %get-tuple-element.7, f32[]{:T(128)} %constant.2.clone.1), dimensions={1}, to_apply=%region_1.0 | reduce | flops 16256 | bytes 66052 | tf_op jit(solution)/shard_map/reduce_sum | solution.py:122
  39.5 0.9 %collective-permute-done.7 = f32[128]{0:T(128)S(1)} collective-permute-done((f32[128]{0:T(128)S(1)}, f32[128]{0:T(128)S(1)}, u32[]{:S(2)}, u32[]{:S(2)}) %collective-permute-start.7) | collective-permute-done | bytes 544 | tf_op jit(solution)/shard_map/ppermute | solution.py:87
  40.4 1.3 %fusion.3 = bf16[128,1024]{1,0:T(8,128)(2,1)S(1)} fusion(bf16[128,1024]{1,0:T(8,128)(2,1)S(1)} %copy-done.2, f32[128]{0:T(128)S(1)} %fusion.50, f32[128,1024]{1,0:T(8,128)} %get-tuple-element.6, f32[128]{0:T(128)S(1)} %add_rsqrt_fusion, bf16[128,1024]{1,0:T(8,128)(2,1)S(1)} %copy-done.3, bf16[64,1024]{1,0:T(8,128)(2,1)S(1)} %fusion.16, ...), kind=kLoop, calls=%fused_computation.9 | loop fusion | flops 1835008 | bytes 1573888 | tf_op jit(solution)/shard_map/convert_element_type | solution.py:128
  42.0 2.9 %collective-permute-start.11 = (bf16[64,1024]{1,0:T(8,128)(2,1)S(1)}, bf16[64,1024]{1,0:T(8,128)(2,1)S(1)}, u32[]{:S(2)}, u32[]{:S(2)}) collective-permute-start(bf16[64,1024]{1,0:T(8,128)(2,1)S(1)} %get-tuple-element.25), channel_id=1, source_target_pairs={{0,8},{2,10},{4,12},{6,14},{8,0},{10,2},{12,4},{14,6},{1,9},{3,11}... | collective-permute-start | bytes 393224 | tf_op jit(solution)/shard_map/ppermute | solution.py:14
  44.9 9.7 %collective-permute-done.8 = bf16[64,1024]{1,0:T(8,128)(2,1)S(1)} collective-permute-done((bf16[64,1024]{1,0:T(8,128)(2,1)S(1)}, bf16[64,1024]{1,0:T(8,128)(2,1)S(1)}, u32[]{:S(2)}, u32[]{:S(2)}) %collective-permute-start.8) | collective-permute-done | bytes 131104 | tf_op jit(solution)/shard_map/ppermute | solution.py:14
  54.6 2.4 %collective-permute-done.11 = bf16[64,1024]{1,0:T(8,128)(2,1)S(1)} collective-permute-done((bf16[64,1024]{1,0:T(8,128)(2,1)S(1)}, bf16[64,1024]{1,0:T(8,128)(2,1)S(1)}, u32[]{:S(2)}, u32[]{:S(2)}) %collective-permute-start.11) | collective-permute-done | bytes 131104 | tf_op jit(solution)/shard_map/ppermute | solution.py:14
  57.5 2.0 %collective-permute-start.12 = (bf16[64,1024]{1,0:T(8,128)(2,1)S(1)}, bf16[64,1024]{1,0:T(8,128)(2,1)S(1)}, u32[]{:S(2)}, u32[]{:S(2)}) collective-permute-start(bf16[64,1024]{1,0:T(8,128)(2,1)S(1)} %fusion.39), channel_id=1, source_target_pairs={{0,4},{2,6},{4,0},{6,2},{8,12},{10,14},{12,8},{14,10},{1,5},{3,7},... | collective-permute-start | bytes 393224 | tf_op jit(solution)/shard_map/ppermute | solution.py:14
  59.5 4.4 %collective-permute-done.9 = bf16[64,1024]{1,0:T(8,128)(2,1)S(1)} collective-permute-done((bf16[64,1024]{1,0:T(8,128)(2,1)S(1)}, bf16[64,1024]{1,0:T(8,128)(2,1)S(1)}, u32[]{:S(2)}, u32[]{:S(2)}) %collective-permute-start.9) | collective-permute-done | bytes 131104 | tf_op jit(solution)/shard_map/ppermute | solution.py:14
  63.9 1.5 %collective-permute-done.12 = bf16[64,1024]{1,0:T(8,128)(2,1)S(1)} collective-permute-done((bf16[64,1024]{1,0:T(8,128)(2,1)S(1)}, bf16[64,1024]{1,0:T(8,128)(2,1)S(1)}, u32[]{:S(2)}, u32[]{:S(2)}) %collective-permute-start.12) | collective-permute-done | bytes 131104 | tf_op jit(solution)/shard_map/ppermute | solution.py:14
  66.0 0.5 collective-permute-start.14
  66.6 1.2 %collective-permute-start.13 = (bf16[64,1024]{1,0:T(8,128)(2,1)S(1)}, bf16[64,1024]{1,0:T(8,128)(2,1)S(1)}, u32[]{:S(2)}, u32[]{:S(2)}) collective-permute-start(bf16[64,1024]{1,0:T(8,128)(2,1)S(1)} %fusion.44), channel_id=1, source_target_pairs={{0,2},{2,0},{4,6},{6,4},{8,10},{10,8},{12,14},{14,12},{1,3},{3,1},... | collective-permute-start | bytes 393224 | tf_op jit(solution)/shard_map/ppermute | solution.py:14
  67.9 0.9 %collective-permute-start.10 = (bf16[64,1024]{1,0:T(8,128)(2,1)S(1)}, bf16[64,1024]{1,0:T(8,128)(2,1)S(1)}, u32[]{:S(2)}, u32[]{:S(2)}) collective-permute-start(bf16[64,1024]{1,0:T(8,128)(2,1)S(1)} %fusion.29), channel_id=1, source_target_pairs={{0,2},{2,0},{4,6},{6,4},{8,10},{10,8},{12,14},{14,12},{1,3},{3,1},... | collective-permute-start | bytes 393224 | tf_op jit(solution)/shard_map/ppermute | solution.py:14
  68.7 0.7 fusion.59
  69.4 0.7 fusion.60
  70.1 3.0 %collective-permute-done.13 = bf16[64,1024]{1,0:T(8,128)(2,1)S(1)} collective-permute-done((bf16[64,1024]{1,0:T(8,128)(2,1)S(1)}, bf16[64,1024]{1,0:T(8,128)(2,1)S(1)}, u32[]{:S(2)}, u32[]{:S(2)}) %collective-permute-start.13) | collective-permute-done | bytes 131104 | tf_op jit(solution)/shard_map/ppermute | solution.py:14
  73.2 1.7 %collective-permute-done.10 = bf16[64,1024]{1,0:T(8,128)(2,1)S(1)} collective-permute-done((bf16[64,1024]{1,0:T(8,128)(2,1)S(1)}, bf16[64,1024]{1,0:T(8,128)(2,1)S(1)}, u32[]{:S(2)}, u32[]{:S(2)}) %collective-permute-start.10) | collective-permute-done | bytes 131104 | tf_op jit(solution)/shard_map/ppermute | solution.py:14
  75.4 1.1 %fusion.1 = bf16[128,1024]{1,0:T(8,128)(2,1)} fusion(bf16[64,1024]{1,0:T(8,128)(2,1)S(1)} %fusion.43, bf16[64,1024]{1,0:T(8,128)(2,1)S(1)} %fusion.28, bf16[1,128,128]{2,1,0:T(8,128)(2,1)S(1)} %copy-done, f32[128]{0:T(128)S(1)} %fusion.50, bf16[128,1024]{1,0:T(8,128)(2,1)S(1)} %copy-done.2, f32[128,1024]{1,0:T(8,128)S(1)} %copy-done.4, ...), kind=kOutput, calls=%fused_computation.2 | convolution fusion | flops 36175872 | bytes 1868800 | tf_op jit(solution)/shard_map/kij,kid->kjd/dot_general | solution.py:153
  76.6 0.6 add.95
  (48 shorter events, 4.3 us)
Async XLA Ops:
  0.6 0.8 copy-start
  2.6 3.1 %copy-start.6 = (f32[3,128]{1,0:T(4,128)S(1)}, f32[3,128]{1,0:T(4,128)}, u32[]{:S(2)}) copy-start(f32[3,128]{1,0:T(4,128)} %param.12) | copy-start | bytes 4612
  2.6 3.1 %copy-start.5 = (f32[3,128]{1,0:T(4,128)S(1)}, f32[3,128]{1,0:T(4,128)}, u32[]{:S(2)}) copy-start(f32[3,128]{1,0:T(4,128)} %param.13) | copy-start | bytes 4612
  2.6 7.3 %collective-permute-start = (bf16[64,1024]{1,0:T(8,128)(2,1)S(1)}, bf16[64,1024]{1,0:T(8,128)(2,1)S(1)}, u32[]{:S(2)}, u32[]{:S(2)}) collective-permute-start(bf16[64,1024]{1,0:T(8,128)(2,1)S(1)} %get-tuple-element.31), channel_id=1, source_target_pairs={{0,2},{2,0},{4,6},{6,4},{8,10},{10,8},{12,14},{14,12},{1,3},{3,1},... | collective-permute-start | bytes 393224 | tf_op jit(solution)/shard_map/ppermute | solution.py:14
  5.6 6.3 %collective-permute-start.3 = (bf16[64,1024]{1,0:T(8,128)(2,1)S(1)}, bf16[64,1024]{1,0:T(8,128)(2,1)S(1)}, u32[]{:S(2)}, u32[]{:S(2)}) collective-permute-start(bf16[64,1024]{1,0:T(8,128)(2,1)S(1)} %get-tuple-element.32), channel_id=1, source_target_pairs={{0,2},{2,0},{4,6},{6,4},{8,10},{10,8},{12,14},{14,12},{1,3},{3,1},... | collective-permute-start | bytes 393224 | tf_op jit(solution)/shard_map/ppermute | solution.py:14
  12.1 6.2 %collective-permute-start.4 = (bf16[64,1024]{1,0:T(8,128)(2,1)S(1)}, bf16[64,1024]{1,0:T(8,128)(2,1)S(1)}, u32[]{:S(2)}, u32[]{:S(2)}) collective-permute-start(bf16[64,1024]{1,0:T(8,128)(2,1)S(1)} %get-tuple-element.29), channel_id=1, source_target_pairs={{0,4},{2,6},{4,0},{6,2},{8,12},{10,14},{12,8},{14,10},{1,5},{3,7},... | collective-permute-start | bytes 393224 | tf_op jit(solution)/shard_map/ppermute | solution.py:14
  14.0 7.2 %collective-permute-start.1 = (bf16[64,1024]{1,0:T(8,128)(2,1)S(1)}, bf16[64,1024]{1,0:T(8,128)(2,1)S(1)}, u32[]{:S(2)}, u32[]{:S(2)}) collective-permute-start(bf16[64,1024]{1,0:T(8,128)(2,1)S(1)} %get-tuple-element.30), channel_id=1, source_target_pairs={{0,4},{2,6},{4,0},{6,2},{8,12},{10,14},{12,8},{14,10},{1,5},{3,7},... | collective-permute-start | bytes 393224 | tf_op jit(solution)/shard_map/ppermute | solution.py:14
  18.4 10.9 %collective-permute-start.5 = (bf16[64,1024]{1,0:T(8,128)(2,1)S(1)}, bf16[64,1024]{1,0:T(8,128)(2,1)S(1)}, u32[]{:S(2)}, u32[]{:S(2)}) collective-permute-start(bf16[64,1024]{1,0:T(8,128)(2,1)S(1)} %fusion.14), channel_id=1, source_target_pairs={{0,8},{2,10},{4,12},{6,14},{8,0},{10,2},{12,4},{14,6},{1,9},{3,11}... | collective-permute-start | bytes 393224 | tf_op jit(solution)/shard_map/ppermute | solution.py:14
  21.3 9.3 %collective-permute-start.2 = (bf16[64,1024]{1,0:T(8,128)(2,1)S(1)}, bf16[64,1024]{1,0:T(8,128)(2,1)S(1)}, u32[]{:S(2)}, u32[]{:S(2)}) collective-permute-start(bf16[64,1024]{1,0:T(8,128)(2,1)S(1)} %fusion.8), channel_id=1, source_target_pairs={{0,8},{2,10},{4,12},{6,14},{8,0},{10,2},{12,4},{14,6},{1,9},{3,11}... | collective-permute-start | bytes 393224 | tf_op jit(solution)/shard_map/ppermute | solution.py:14
  29.4 1.4 %copy-start.1 = (bf16[128,1024]{1,0:T(8,128)(2,1)S(1)}, bf16[128,1024]{1,0:T(8,128)(2,1)}, u32[]{:S(2)}) copy-start(bf16[128,1024]{1,0:T(8,128)(2,1)} %tok_ref.1) | copy-start | bytes 786436
  31.0 1.2 %collective-permute-start.6 = (f32[128]{0:T(128)S(1)}, f32[128]{0:T(128)S(1)}, u32[]{:S(2)}, u32[]{:S(2)}) collective-permute-start(f32[128]{0:T(128)S(1)} %multiply_reduce_fusion), channel_id=1, source_target_pairs={{0,1},{1,0},{2,3},{3,2},{4,5},{5,4},{6,7},{7,6},{8,9},{9,8},{10,11... | collective-permute-start | bytes 1544 | tf_op jit(solution)/shard_map/ppermute | solution.py:87
  32.9 7.5 %copy-start.2 = (bf16[128,1024]{1,0:T(8,128)(2,1)S(1)}, bf16[128,1024]{1,0:T(8,128)(2,1)}, u32[]{:S(2)}) copy-start(bf16[128,1024]{1,0:T(8,128)(2,1)} %tok_ref.1) | copy-start | bytes 786436
  32.9 7.5 %copy-start.3 = (bf16[128,1024]{1,0:T(8,128)(2,1)S(1)}, bf16[128,1024]{1,0:T(8,128)(2,1)}, u32[]{:S(2)}) copy-start(bf16[128,1024]{1,0:T(8,128)(2,1)} %cot_ref.1) | copy-start | bytes 786436
  39.2 1.2 %collective-permute-start.7 = (f32[128]{0:T(128)S(1)}, f32[128]{0:T(128)S(1)}, u32[]{:S(2)}, u32[]{:S(2)}) collective-permute-start(f32[128]{0:T(128)S(1)} %reduce_sum.127), channel_id=1, source_target_pairs={{0,1},{1,0},{2,3},{3,2},{4,5},{5,4},{6,7},{7,6},{8,9},{9,8},{10,11... | collective-permute-start | bytes 1544 | tf_op jit(solution)/shard_map/ppermute | solution.py:87
  41.9 12.6 %collective-permute-start.8 = (bf16[64,1024]{1,0:T(8,128)(2,1)S(1)}, bf16[64,1024]{1,0:T(8,128)(2,1)S(1)}, u32[]{:S(2)}, u32[]{:S(2)}) collective-permute-start(bf16[64,1024]{1,0:T(8,128)(2,1)S(1)} %get-tuple-element.24), channel_id=1, source_target_pairs={{0,8},{2,10},{4,12},{6,14},{8,0},{10,2},{12,4},{14,6},{1,9},{3,11}... | collective-permute-start | bytes 393224 | tf_op jit(solution)/shard_map/ppermute | solution.py:14
  42.0 14.9 %collective-permute-start.11 = (bf16[64,1024]{1,0:T(8,128)(2,1)S(1)}, bf16[64,1024]{1,0:T(8,128)(2,1)S(1)}, u32[]{:S(2)}, u32[]{:S(2)}) collective-permute-start(bf16[64,1024]{1,0:T(8,128)(2,1)S(1)} %get-tuple-element.25), channel_id=1, source_target_pairs={{0,8},{2,10},{4,12},{6,14},{8,0},{10,2},{12,4},{14,6},{1,9},{3,11}... | collective-permute-start | bytes 393224 | tf_op jit(solution)/shard_map/ppermute | solution.py:14
  57.4 6.5 %collective-permute-start.9 = (bf16[64,1024]{1,0:T(8,128)(2,1)S(1)}, bf16[64,1024]{1,0:T(8,128)(2,1)S(1)}, u32[]{:S(2)}, u32[]{:S(2)}) collective-permute-start(bf16[64,1024]{1,0:T(8,128)(2,1)S(1)} %fusion.24), channel_id=1, source_target_pairs={{0,4},{2,6},{4,0},{6,2},{8,12},{10,14},{12,8},{14,10},{1,5},{3,7},... | collective-permute-start | bytes 393224 | tf_op jit(solution)/shard_map/ppermute | solution.py:14
  57.5 7.9 %collective-permute-start.12 = (bf16[64,1024]{1,0:T(8,128)(2,1)S(1)}, bf16[64,1024]{1,0:T(8,128)(2,1)S(1)}, u32[]{:S(2)}, u32[]{:S(2)}) collective-permute-start(bf16[64,1024]{1,0:T(8,128)(2,1)S(1)} %fusion.39), channel_id=1, source_target_pairs={{0,4},{2,6},{4,0},{6,2},{8,12},{10,14},{12,8},{14,10},{1,5},{3,7},... | collective-permute-start | bytes 393224 | tf_op jit(solution)/shard_map/ppermute | solution.py:14
  65.9 2.9 %collective-permute-start.15 = (f32[3,128]{1,0:T(4,128)S(1)}, f32[3,128]{1,0:T(4,128)S(1)}, u32[]{:S(2)}, u32[]{:S(2)}) collective-permute-start(f32[3,128]{1,0:T(4,128)S(1)} %maximum_maximum_fusion.1), channel_id=1, source_target_pairs={{0,1},{1,0},{2,3},{3,2},{4,5},{5,4},{6,7},{7,6},{8,9},{9,8},{10,11... | collective-permute-start | bytes 4616 | tf_op jit(solution)/shard_map/ppermute | solution.py:87
  66.0 3.4 %collective-permute-start.14 = (f32[3,128]{1,0:T(4,128)S(1)}, f32[3,128]{1,0:T(4,128)S(1)}, u32[]{:S(2)}, u32[]{:S(2)}) collective-permute-start(f32[3,128]{1,0:T(4,128)S(1)} %maximum_maximum_fusion), channel_id=1, source_target_pairs={{0,1},{1,0},{2,3},{3,2},{4,5},{5,4},{6,7},{7,6},{8,9},{9,8},{10,11... | collective-permute-start | bytes 4616 | tf_op jit(solution)/shard_map/ppermute | solution.py:87
  66.6 6.4 %collective-permute-start.13 = (bf16[64,1024]{1,0:T(8,128)(2,1)S(1)}, bf16[64,1024]{1,0:T(8,128)(2,1)S(1)}, u32[]{:S(2)}, u32[]{:S(2)}) collective-permute-start(bf16[64,1024]{1,0:T(8,128)(2,1)S(1)} %fusion.44), channel_id=1, source_target_pairs={{0,2},{2,0},{4,6},{6,4},{8,10},{10,8},{12,14},{14,12},{1,3},{3,1},... | collective-permute-start | bytes 393224 | tf_op jit(solution)/shard_map/ppermute | solution.py:14
  67.9 7.1 %collective-permute-start.10 = (bf16[64,1024]{1,0:T(8,128)(2,1)S(1)}, bf16[64,1024]{1,0:T(8,128)(2,1)S(1)}, u32[]{:S(2)}, u32[]{:S(2)}) collective-permute-start(bf16[64,1024]{1,0:T(8,128)(2,1)S(1)} %fusion.29), channel_id=1, source_target_pairs={{0,2},{2,0},{4,6},{6,4},{8,10},{10,8},{12,14},{14,12},{1,3},{3,1},... | collective-permute-start | bytes 393224 | tf_op jit(solution)/shard_map/ppermute | solution.py:14
  73.2 2.2 %copy-start.4 = (f32[128,1024]{1,0:T(8,128)S(1)}, f32[128,1024]{1,0:T(8,128)}, u32[]{:S(2)}) copy-start(f32[128,1024]{1,0:T(8,128)} %get-tuple-element.6) | copy-start | bytes 1572868
  75.3 1.3 %collective-permute-start.16 = (f32[1,128,128]{2,1,0:T(8,128)S(1)}, f32[1,128,128]{2,1,0:T(8,128)S(1)}, u32[]{:S(2)}, u32[]{:S(2)}) collective-permute-start(f32[1,128,128]{2,1,0:T(8,128)S(1)} %convolution_bitcast_fusion.1), channel_id=1, source_target_pairs={{0,1},{1,0},{2,3},{3,2},{4,5},{5,4},{6,7},{7,6},{8,9},{9,8},{10,11... | collective-permute-start | bytes 196616 | tf_op jit(solution)/shard_map/ppermute | solution.py:87

commit v9 on v6

--- a/solution.py
+++ b/solution.py
@@ -71,14 +71,23 @@
     nblk = blocks.shape[0]
     blen = blocks.shape[1]
     tok_blocks = tokens.reshape(nblk, blen, width)
-    local = jnp.einsum("kij,kjd->kid", blocks, tok_blocks, preferred_element_type=jnp.float32)
-    local = local.astype(jnp.bfloat16).reshape(tok, width)
     chunks = CHUNKS if tok % CHUNKS == 0 else 1
     rows = tok // chunks
     spans = [slice(chunk * rows, (chunk + 1) * rows) for chunk in range(chunks)]
     states = [[None] * sections for _ in spans]
     mates = [[None] * sections for _ in spans]
-    pieces = [local[rs] for rs in spans]
+    if nblk == 1:
+        pieces = [
+            jnp.einsum(
+                "kij,kjd->kid", blocks[:, rs], tok_blocks, preferred_element_type=jnp.float32
+            ).astype(jnp.bfloat16).reshape(rows, width)
+            for rs in spans
+        ]
+    else:
+        local = jnp.einsum(
+            "kij,kjd->kid", blocks, tok_blocks, preferred_element_type=jnp.float32
+        ).astype(jnp.bfloat16).reshape(tok, width)
+        pieces = [local[rs] for rs in spans]
     for section in range(sections):
         for chunk, rs in enumerate(spans):
             value = pieces[chunk]

time: 76.4 us -> 74.7 us (0.978)
  waiting for transfers between devices: 41.5 us -> 39.5 us
    ppermute x12, waiting for transfers between devices: 39.3 us -> 37.3 us  [from_partner(): return lax.ppermute(value, axis, pairs)]
  transfers between devices with their start and end apart: 17 -> 17, of which waited for: 14 -> 13; matrix products, arithmetic and copies ran while one was open for 4% -> 5% of each run, Pallas kernels for 0% -> 0%
where the time goes in v9:
time: 74.7 us; the launch traced here: 74.5 us
  waiting for transfers between devices  39.5 us (53%)
  starting transfers between devices  19.1 us (26%)
  other arithmetic  6.93 us (9%)
  Pallas kernels  4.81 us (6%)
  matrix products  2.66 us (4%)
  between operations  0.82 us (1%)
    ppermute x12, waiting for transfers between devices, from_partner(): return lax.ppermute(value, axis, pairs)  37.3 us
    ppermute x12, starting transfers between devices, from_partner(): return lax.ppermute(value, axis, pairs)  18.2 us
    pallas_call x1, Pallas kernels, ffn_grad(): pl.pallas_call(ffn_kernel, grid=(groups_here // per_step,), in_specs=[act...  4.81 us
    ppermute x5, waiting for transfers between devices, hid_sum(): total = total + lax.ppermute(value, 'hid', pairs)  2.19 us
    add x3, other arithmetic, hid_sum(): total = total + lax.ppermute(value, 'hid', pairs)  1.95 us
  transfers between devices with their start and end apart: 17, of which 13 were waited for; matrix products, arithmetic and copies ran while one was open for 5% of the time, Pallas kernels for 0%

profile of v9, /device:TPU:0, one launch (start us, length us, event | category | flops | bytes accessed | tf_op | source)
XLA Modules:
  0.0 74.5 jit_solution(2826965512777258149)
XLA Ops:
  0.7 1.2 %convolution_convert_fusion = bf16[64,1024]{1,0:T(8,128)(2,1)S(1)} fusion(bf16[128,1024]{1,0:T(8,128)(2,1)} %param.9, bf16[1,128,128]{2,1,0:T(8,128)(2,1)} %param.11), kind=kOutput, calls=%fused_computation.3 | convolution fusion | flops 16842752 | bytes 409600 | tf_op jit(solution)/shard_map/kij,kjd->kid/dot_general | solution.py:81
  1.8 3.0 %collective-permute-start.3 = (bf16[64,1024]{1,0:T(8,128)(2,1)S(1)}, bf16[64,1024]{1,0:T(8,128)(2,1)S(1)}, u32[]{:S(2)}, u32[]{:S(2)}) collective-permute-start(bf16[64,1024]{1,0:T(8,128)(2,1)S(1)} %convolution_convert_fusion), channel_id=1, source_target_pairs={{0,2},{2,0},{4,6},{6,4},{8,10},{10,8},{12,14},{14,12},{1,3},{3,1},... | collective-permute-start | bytes 393224 | tf_op jit(solution)/shard_map/ppermute | solution.py:14
  5.2 0.4 copy-done.5
  5.8 3.4 %collective-permute-done.3 = bf16[64,1024]{1,0:T(8,128)(2,1)S(1)} collective-permute-done((bf16[64,1024]{1,0:T(8,128)(2,1)S(1)}, bf16[64,1024]{1,0:T(8,128)(2,1)S(1)}, u32[]{:S(2)}, u32[]{:S(2)}) %collective-permute-start.3) | collective-permute-done | bytes 131104 | tf_op jit(solution)/shard_map/ppermute | solution.py:14
  9.3 2.2 %collective-permute-start.4 = (bf16[64,1024]{1,0:T(8,128)(2,1)S(1)}, bf16[64,1024]{1,0:T(8,128)(2,1)S(1)}, u32[]{:S(2)}, u32[]{:S(2)}) collective-permute-start(bf16[64,1024]{1,0:T(8,128)(2,1)S(1)} %fusion.11), channel_id=1, source_target_pairs={{0,4},{2,6},{4,0},{6,2},{8,12},{10,14},{12,8},{14,10},{1,5},{3,7},... | collective-permute-start | bytes 393224 | tf_op jit(solution)/shard_map/ppermute | solution.py:14
  11.6 1.5 %collective-permute-start.1 = (bf16[64,1024]{1,0:T(8,128)(2,1)S(1)}, bf16[64,1024]{1,0:T(8,128)(2,1)S(1)}, u32[]{:S(2)}, u32[]{:S(2)}) collective-permute-start(bf16[64,1024]{1,0:T(8,128)(2,1)S(1)} %fusion.5), channel_id=1, source_target_pairs={{0,4},{2,6},{4,0},{6,2},{8,12},{10,14},{12,8},{14,10},{1,5},{3,7},... | collective-permute-start | bytes 393224 | tf_op jit(solution)/shard_map/ppermute | solution.py:14
  13.2 3.9 %collective-permute-done.4 = bf16[64,1024]{1,0:T(8,128)(2,1)S(1)} collective-permute-done((bf16[64,1024]{1,0:T(8,128)(2,1)S(1)}, bf16[64,1024]{1,0:T(8,128)(2,1)S(1)}, u32[]{:S(2)}, u32[]{:S(2)}) %collective-permute-start.4) | collective-permute-done | bytes 131104 | tf_op jit(solution)/shard_map/ppermute | solution.py:14
  17.2 1.9 %collective-permute-start.5 = (bf16[64,1024]{1,0:T(8,128)(2,1)S(1)}, bf16[64,1024]{1,0:T(8,128)(2,1)S(1)}, u32[]{:S(2)}, u32[]{:S(2)}) collective-permute-start(bf16[64,1024]{1,0:T(8,128)(2,1)S(1)} %fusion.13), channel_id=1, source_target_pairs={{0,8},{2,10},{4,12},{6,14},{8,0},{10,2},{12,4},{14,6},{1,9},{3,11}... | collective-permute-start | bytes 393224 | tf_op jit(solution)/shard_map/ppermute | solution.py:14
  19.2 2.3 %collective-permute-start.2 = (bf16[64,1024]{1,0:T(8,128)(2,1)S(1)}, bf16[64,1024]{1,0:T(8,128)(2,1)S(1)}, u32[]{:S(2)}, u32[]{:S(2)}) collective-permute-start(bf16[64,1024]{1,0:T(8,128)(2,1)S(1)} %fusion.7), channel_id=1, source_target_pairs={{0,8},{2,10},{4,12},{6,14},{8,0},{10,2},{12,4},{14,6},{1,9},{3,11}... | collective-permute-start | bytes 393224 | tf_op jit(solution)/shard_map/ppermute | solution.py:14
  21.5 6.5 %collective-permute-done.5 = bf16[64,1024]{1,0:T(8,128)(2,1)S(1)} collective-permute-done((bf16[64,1024]{1,0:T(8,128)(2,1)S(1)}, bf16[64,1024]{1,0:T(8,128)(2,1)S(1)}, u32[]{:S(2)}, u32[]{:S(2)}) %collective-permute-start.5) | collective-permute-done | bytes 131104 | tf_op jit(solution)/shard_map/ppermute | solution.py:14
  28.1 1.3 %collective-permute-done.2 = bf16[64,1024]{1,0:T(8,128)(2,1)S(1)} collective-permute-done((bf16[64,1024]{1,0:T(8,128)(2,1)S(1)}, bf16[64,1024]{1,0:T(8,128)(2,1)S(1)}, u32[]{:S(2)}, u32[]{:S(2)}) %collective-permute-start.2) | collective-permute-done | bytes 131104 | tf_op jit(solution)/shard_map/ppermute | solution.py:14
  29.8 1.1 %collective-permute-done.6 = f32[128]{0:T(128)S(1)} collective-permute-done((f32[128]{0:T(128)S(1)}, f32[128]{0:T(128)S(1)}, u32[]{:S(2)}, u32[]{:S(2)}) %collective-permute-start.6) | collective-permute-done | bytes 544 | tf_op jit(solution)/shard_map/ppermute | solution.py:64
  30.9 0.8 %multiply_convert_fusion.normed_ref = bf16[128,1024]{1,0:T(8,128)(2,1)} fusion(bf16[128,1024]{1,0:T(8,128)(2,1)S(1)} %copy-done, f32[1024]{0:T(1024)S(1)} %copy-done.3, f32[128]{0:T(128)S(1)} %add_rsqrt_fusion, bf16[64,1024]{1,0:T(8,128)(2,1)S(1)} %fusion.15, bf16[64,1024]{1,0:T(8,128)(2,1)S(1)} %fusion.9), kind=kLoop, calls=%fused_computation.13 | loop fusion | flops 1310720 | bytes 791040 | tf_op jit(solution)/shard_map/convert_element_type | solution.py:107
  31.7 4.8 %shard_map.120 = f32[128,1024]{1,0:T(8,128)} custom-call(bf16[128,1024]{1,0:T(8,128)(2,1)} %multiply_convert_fusion.normed_ref, bf16[128,1024]{1,0:T(8,128)(2,1)} %cot_ref.1, bf16[8,128,512]{2,1,0:T(8,128)(2,1)} %wg_ref.1, bf16[8,128,512]{2,1,0:T(8,128)(2,1)} %wu_ref.1, bf16[8,512,128]{2,1,0:T(8,128)(2,1)} %wd_ref.1), custom_call_target="tpu_custom_call" | custom-call | tf_op jit(solution)/shard_map/pallas_call | solution.py:44
  36.5 1.3 %multiply_reduce_fusion = f32[128]{0:T(128)S(1)} fusion(f32[128,1024]{1,0:T(8,128)} %shard_map.120, bf16[128,1024]{1,0:T(8,128)(2,1)S(1)} %copy-done, f32[1024]{0:T(1024)S(1)} %copy-done.3, bf16[64,1024]{1,0:T(8,128)(2,1)S(1)} %fusion.15, bf16[64,1024]{1,0:T(8,128)(2,1)S(1)} %fusion.9), kind=kLoop, calls=%fused_computation.12 | loop fusion | flops 1310592 | bytes 1053184 | tf_op jit(solution)/shard_map/reduce_sum | solution.py:110
  38.1 0.9 %collective-permute-done.7 = f32[128]{0:T(128)S(1)} collective-permute-done((f32[128]{0:T(128)S(1)}, f32[128]{0:T(128)S(1)}, u32[]{:S(2)}, u32[]{:S(2)}) %collective-permute-start.7) | collective-permute-done | bytes 544 | tf_op jit(solution)/shard_map/ppermute | solution.py:64
  39.7 2.9 %collective-permute-start.11 = (bf16[64,1024]{1,0:T(8,128)(2,1)S(1)}, bf16[64,1024]{1,0:T(8,128)(2,1)S(1)}, u32[]{:S(2)}, u32[]{:S(2)}) collective-permute-start(bf16[64,1024]{1,0:T(8,128)(2,1)S(1)} %get-tuple-element.21), channel_id=1, source_target_pairs={{0,8},{2,10},{4,12},{6,14},{8,0},{10,2},{12,4},{14,6},{1,9},{3,11}... | collective-permute-start | bytes 393224 | tf_op jit(solution)/shard_map/ppermute | solution.py:14
  42.6 8.5 %collective-permute-done.8 = bf16[64,1024]{1,0:T(8,128)(2,1)S(1)} collective-permute-done((bf16[64,1024]{1,0:T(8,128)(2,1)S(1)}, bf16[64,1024]{1,0:T(8,128)(2,1)S(1)}, u32[]{:S(2)}, u32[]{:S(2)}) %collective-permute-start.8) | collective-permute-done | bytes 131104 | tf_op jit(solution)/shard_map/ppermute | solution.py:14
  51.1 2.7 %collective-permute-done.11 = bf16[64,1024]{1,0:T(8,128)(2,1)S(1)} collective-permute-done((bf16[64,1024]{1,0:T(8,128)(2,1)S(1)}, bf16[64,1024]{1,0:T(8,128)(2,1)S(1)}, u32[]{:S(2)}, u32[]{:S(2)}) %collective-permute-start.11) | collective-permute-done | bytes 131104 | tf_op jit(solution)/shard_map/ppermute | solution.py:14
  53.9 0.3 fusion.25
  54.5 2.0 %collective-permute-start.9 = (bf16[64,1024]{1,0:T(8,128)(2,1)S(1)}, bf16[64,1024]{1,0:T(8,128)(2,1)S(1)}, u32[]{:S(2)}, u32[]{:S(2)}) collective-permute-start(bf16[64,1024]{1,0:T(8,128)(2,1)S(1)} %fusion.23), channel_id=1, source_target_pairs={{0,4},{2,6},{4,0},{6,2},{8,12},{10,14},{12,8},{14,10},{1,5},{3,7},... | collective-permute-start | bytes 393224 | tf_op jit(solution)/shard_map/ppermute | solution.py:14
  56.5 4.3 %collective-permute-done.12 = bf16[64,1024]{1,0:T(8,128)(2,1)S(1)} collective-permute-done((bf16[64,1024]{1,0:T(8,128)(2,1)S(1)}, bf16[64,1024]{1,0:T(8,128)(2,1)S(1)}, u32[]{:S(2)}, u32[]{:S(2)}) %collective-permute-start.12) | collective-permute-done | bytes 131104 | tf_op jit(solution)/shard_map/ppermute | solution.py:14
  60.8 1.9 %collective-permute-done.9 = bf16[64,1024]{1,0:T(8,128)(2,1)S(1)} collective-permute-done((bf16[64,1024]{1,0:T(8,128)(2,1)S(1)}, bf16[64,1024]{1,0:T(8,128)(2,1)S(1)}, u32[]{:S(2)}, u32[]{:S(2)}) %collective-permute-start.9) | collective-permute-done | bytes 131104 | tf_op jit(solution)/shard_map/ppermute | solution.py:14
  63.3 0.5 collective-permute-start.14
  63.9 0.9 %collective-permute-start.13 = (bf16[64,1024]{1,0:T(8,128)(2,1)S(1)}, bf16[64,1024]{1,0:T(8,128)(2,1)S(1)}, u32[]{:S(2)}, u32[]{:S(2)}) collective-permute-start(bf16[64,1024]{1,0:T(8,128)(2,1)S(1)} %fusion.43), channel_id=1, source_target_pairs={{0,2},{2,0},{4,6},{6,4},{8,10},{10,8},{12,14},{14,12},{1,3},{3,1},... | collective-permute-start | bytes 393224 | tf_op jit(solution)/shard_map/ppermute | solution.py:14
  64.9 1.2 %collective-permute-start.10 = (bf16[64,1024]{1,0:T(8,128)(2,1)S(1)}, bf16[64,1024]{1,0:T(8,128)(2,1)S(1)}, u32[]{:S(2)}, u32[]{:S(2)}) collective-permute-start(bf16[64,1024]{1,0:T(8,128)(2,1)S(1)} %fusion.28), channel_id=1, source_target_pairs={{0,2},{2,0},{4,6},{6,4},{8,10},{10,8},{12,14},{14,12},{1,3},{3,1},... | collective-permute-start | bytes 393224 | tf_op jit(solution)/shard_map/ppermute | solution.py:14
  66.0 0.7 fusion.62
  66.7 0.7 fusion.63
  67.3 3.0 %collective-permute-done.13 = bf16[64,1024]{1,0:T(8,128)(2,1)S(1)} collective-permute-done((bf16[64,1024]{1,0:T(8,128)(2,1)S(1)}, bf16[64,1024]{1,0:T(8,128)(2,1)S(1)}, u32[]{:S(2)}, u32[]{:S(2)}) %collective-permute-start.13) | collective-permute-done | bytes 131104 | tf_op jit(solution)/shard_map/ppermute | solution.py:14
  70.5 1.8 %collective-permute-done.10 = bf16[64,1024]{1,0:T(8,128)(2,1)S(1)} collective-permute-done((bf16[64,1024]{1,0:T(8,128)(2,1)S(1)}, bf16[64,1024]{1,0:T(8,128)(2,1)S(1)}, u32[]{:S(2)}, u32[]{:S(2)}) %collective-permute-start.10) | collective-permute-done | bytes 131104 | tf_op jit(solution)/shard_map/ppermute | solution.py:14
  72.7 1.1 %fusion.1 = bf16[128,1024]{1,0:T(8,128)(2,1)} fusion(bf16[64,1024]{1,0:T(8,128)(2,1)S(1)} %fusion.42, bf16[64,1024]{1,0:T(8,128)(2,1)S(1)} %fusion.27, bf16[1,128,128]{2,1,0:T(8,128)(2,1)S(1)} %copy-done.4, f32[128]{0:T(128)S(1)} %fusion.52, bf16[128,1024]{1,0:T(8,128)(2,1)S(1)} %copy-done, f32[128,1024]{1,0:T(8,128)S(1)} %copy-done.1, ...), kind=kOutput, calls=%fused_computation.2 | convolution fusion | flops 36306944 | bytes 1872896 | tf_op jit(solution)/shard_map/kij,kid->kjd/dot_general | solution.py:141
  73.9 0.6 add.95
  (49 shorter events, 4.0 us)
Async XLA Ops:
  0.6 4.2 %copy-start = (bf16[128,1024]{1,0:T(8,128)(2,1)S(1)}, bf16[128,1024]{1,0:T(8,128)(2,1)}, u32[]{:S(2)}) copy-start(bf16[128,1024]{1,0:T(8,128)(2,1)} %param.9) | copy-start | bytes 786436
  0.6 4.2 %copy-start.4 = (bf16[1,128,128]{2,1,0:T(8,128)(2,1)S(1)}, bf16[1,128,128]{2,1,0:T(8,128)(2,1)}, u32[]{:S(2)}) copy-start(bf16[1,128,128]{2,1,0:T(8,128)(2,1)} %param.11) | copy-start | bytes 98308
  1.8 7.3 %collective-permute-start.3 = (bf16[64,1024]{1,0:T(8,128)(2,1)S(1)}, bf16[64,1024]{1,0:T(8,128)(2,1)S(1)}, u32[]{:S(2)}, u32[]{:S(2)}) collective-permute-start(bf16[64,1024]{1,0:T(8,128)(2,1)S(1)} %convolution_convert_fusion), channel_id=1, source_target_pairs={{0,2},{2,0},{4,6},{6,4},{8,10},{10,8},{12,14},{14,12},{1,3},{3,1},... | collective-permute-start | bytes 393224 | tf_op jit(solution)/shard_map/ppermute | solution.py:14
  4.8 0.7 copy-start.5
  5.0 0.7 copy-start.6
  5.0 6.5 %collective-permute-start = (bf16[64,1024]{1,0:T(8,128)(2,1)S(1)}, bf16[64,1024]{1,0:T(8,128)(2,1)S(1)}, u32[]{:S(2)}, u32[]{:S(2)}) collective-permute-start(bf16[64,1024]{1,0:T(8,128)(2,1)S(1)} %convolution_convert_fusion.1), channel_id=1, source_target_pairs={{0,2},{2,0},{4,6},{6,4},{8,10},{10,8},{12,14},{14,12},{1,3},{3,1},... | collective-permute-start | bytes 393224 | tf_op jit(solution)/shard_map/ppermute | solution.py:14
  9.3 7.8 %collective-permute-start.4 = (bf16[64,1024]{1,0:T(8,128)(2,1)S(1)}, bf16[64,1024]{1,0:T(8,128)(2,1)S(1)}, u32[]{:S(2)}, u32[]{:S(2)}) collective-permute-start(bf16[64,1024]{1,0:T(8,128)(2,1)S(1)} %fusion.11), channel_id=1, source_target_pairs={{0,4},{2,6},{4,0},{6,2},{8,12},{10,14},{12,8},{14,10},{1,5},{3,7},... | collective-permute-start | bytes 393224 | tf_op jit(solution)/shard_map/ppermute | solution.py:14
  11.6 7.4 %collective-permute-start.1 = (bf16[64,1024]{1,0:T(8,128)(2,1)S(1)}, bf16[64,1024]{1,0:T(8,128)(2,1)S(1)}, u32[]{:S(2)}, u32[]{:S(2)}) collective-permute-start(bf16[64,1024]{1,0:T(8,128)(2,1)S(1)} %fusion.5), channel_id=1, source_target_pairs={{0,4},{2,6},{4,0},{6,2},{8,12},{10,14},{12,8},{14,10},{1,5},{3,7},... | collective-permute-start | bytes 393224 | tf_op jit(solution)/shard_map/ppermute | solution.py:14
  17.2 10.8 %collective-permute-start.5 = (bf16[64,1024]{1,0:T(8,128)(2,1)S(1)}, bf16[64,1024]{1,0:T(8,128)(2,1)S(1)}, u32[]{:S(2)}, u32[]{:S(2)}) collective-permute-start(bf16[64,1024]{1,0:T(8,128)(2,1)S(1)} %fusion.13), channel_id=1, source_target_pairs={{0,8},{2,10},{4,12},{6,14},{8,0},{10,2},{12,4},{14,6},{1,9},{3,11}... | collective-permute-start | bytes 393224 | tf_op jit(solution)/shard_map/ppermute | solution.py:14
  19.2 10.2 %collective-permute-start.2 = (bf16[64,1024]{1,0:T(8,128)(2,1)S(1)}, bf16[64,1024]{1,0:T(8,128)(2,1)S(1)}, u32[]{:S(2)}, u32[]{:S(2)}) collective-permute-start(bf16[64,1024]{1,0:T(8,128)(2,1)S(1)} %fusion.7), channel_id=1, source_target_pairs={{0,8},{2,10},{4,12},{6,14},{8,0},{10,2},{12,4},{14,6},{1,9},{3,11}... | collective-permute-start | bytes 393224 | tf_op jit(solution)/shard_map/ppermute | solution.py:14
  29.5 1.4 %copy-start.3 = (f32[1024]{0:T(1024)S(1)}, f32[1024]{0:T(1024)}, u32[]{:S(2)}) copy-start(f32[1024]{0:T(1024)} %param.14) | copy-start | bytes 12292
  29.7 1.2 %collective-permute-start.6 = (f32[128]{0:T(128)S(1)}, f32[128]{0:T(128)S(1)}, u32[]{:S(2)}, u32[]{:S(2)}) collective-permute-start(f32[128]{0:T(128)S(1)} %multiply_reduce_fusion.1), channel_id=1, source_target_pairs={{0,1},{1,0},{2,3},{3,2},{4,5},{5,4},{6,7},{7,6},{8,9},{9,8},{10,11... | collective-permute-start | bytes 1544 | tf_op jit(solution)/shard_map/ppermute | solution.py:64
  36.5 2.5 %copy-start.1 = (f32[128,1024]{1,0:T(8,128)S(1)}, f32[128,1024]{1,0:T(8,128)}, u32[]{:S(2)}) copy-start(f32[128,1024]{1,0:T(8,128)} %shard_map.120) | copy-start | bytes 1572868
  36.5 2.5 %copy-start.2 = (bf16[128,1024]{1,0:T(8,128)(2,1)S(1)}, bf16[128,1024]{1,0:T(8,128)(2,1)}, u32[]{:S(2)}) copy-start(bf16[128,1024]{1,0:T(8,128)(2,1)} %cot_ref.1) | copy-start | bytes 786436
  37.9 1.2 %collective-permute-start.7 = (f32[128]{0:T(128)S(1)}, f32[128]{0:T(128)S(1)}, u32[]{:S(2)}, u32[]{:S(2)}) collective-permute-start(f32[128]{0:T(128)S(1)} %multiply_reduce_fusion), channel_id=1, source_target_pairs={{0,1},{1,0},{2,3},{3,2},{4,5},{5,4},{6,7},{7,6},{8,9},{9,8},{10,11... | collective-permute-start | bytes 1544 | tf_op jit(solution)/shard_map/ppermute | solution.py:64
  39.6 11.5 %collective-permute-start.8 = (bf16[64,1024]{1,0:T(8,128)(2,1)S(1)}, bf16[64,1024]{1,0:T(8,128)(2,1)S(1)}, u32[]{:S(2)}, u32[]{:S(2)}) collective-permute-start(bf16[64,1024]{1,0:T(8,128)(2,1)S(1)} %get-tuple-element.20), channel_id=1, source_target_pairs={{0,8},{2,10},{4,12},{6,14},{8,0},{10,2},{12,4},{14,6},{1,9},{3,11}... | collective-permute-start | bytes 393224 | tf_op jit(solution)/shard_map/ppermute | solution.py:14
  39.7 14.2 %collective-permute-start.11 = (bf16[64,1024]{1,0:T(8,128)(2,1)S(1)}, bf16[64,1024]{1,0:T(8,128)(2,1)S(1)}, u32[]{:S(2)}, u32[]{:S(2)}) collective-permute-start(bf16[64,1024]{1,0:T(8,128)(2,1)S(1)} %get-tuple-element.21), channel_id=1, source_target_pairs={{0,8},{2,10},{4,12},{6,14},{8,0},{10,2},{12,4},{14,6},{1,9},{3,11}... | collective-permute-start | bytes 393224 | tf_op jit(solution)/shard_map/ppermute | solution.py:14
  54.4 6.4 %collective-permute-start.12 = (bf16[64,1024]{1,0:T(8,128)(2,1)S(1)}, bf16[64,1024]{1,0:T(8,128)(2,1)S(1)}, u32[]{:S(2)}, u32[]{:S(2)}) collective-permute-start(bf16[64,1024]{1,0:T(8,128)(2,1)S(1)} %fusion.38), channel_id=1, source_target_pairs={{0,4},{2,6},{4,0},{6,2},{8,12},{10,14},{12,8},{14,10},{1,5},{3,7},... | collective-permute-start | bytes 393224 | tf_op jit(solution)/shard_map/ppermute | solution.py:14
  54.5 8.2 %collective-permute-start.9 = (bf16[64,1024]{1,0:T(8,128)(2,1)S(1)}, bf16[64,1024]{1,0:T(8,128)(2,1)S(1)}, u32[]{:S(2)}, u32[]{:S(2)}) collective-permute-start(bf16[64,1024]{1,0:T(8,128)(2,1)S(1)} %fusion.23), channel_id=1, source_target_pairs={{0,4},{2,6},{4,0},{6,2},{8,12},{10,14},{12,8},{14,10},{1,5},{3,7},... | collective-permute-start | bytes 393224 | tf_op jit(solution)/shard_map/ppermute | solution.py:14
  63.2 2.9 %collective-permute-start.15 = (f32[3,128]{1,0:T(4,128)S(1)}, f32[3,128]{1,0:T(4,128)S(1)}, u32[]{:S(2)}, u32[]{:S(2)}) collective-permute-start(f32[3,128]{1,0:T(4,128)S(1)} %maximum_maximum_fusion.1), channel_id=1, source_target_pairs={{0,1},{1,0},{2,3},{3,2},{4,5},{5,4},{6,7},{7,6},{8,9},{9,8},{10,11... | collective-permute-start | bytes 4616 | tf_op jit(solution)/shard_map/ppermute | solution.py:64
  63.3 3.4 %collective-permute-start.14 = (f32[3,128]{1,0:T(4,128)S(1)}, f32[3,128]{1,0:T(4,128)S(1)}, u32[]{:S(2)}, u32[]{:S(2)}) collective-permute-start(f32[3,128]{1,0:T(4,128)S(1)} %maximum_maximum_fusion), channel_id=1, source_target_pairs={{0,1},{1,0},{2,3},{3,2},{4,5},{5,4},{6,7},{7,6},{8,9},{9,8},{10,11... | collective-permute-start | bytes 4616 | tf_op jit(solution)/shard_map/ppermute | solution.py:64
  63.9 6.4 %collective-permute-start.13 = (bf16[64,1024]{1,0:T(8,128)(2,1)S(1)}, bf16[64,1024]{1,0:T(8,128)(2,1)S(1)}, u32[]{:S(2)}, u32[]{:S(2)}) collective-permute-start(bf16[64,1024]{1,0:T(8,128)(2,1)S(1)} %fusion.43), channel_id=1, source_target_pairs={{0,2},{2,0},{4,6},{6,4},{8,10},{10,8},{12,14},{14,12},{1,3},{3,1},... | collective-permute-start | bytes 393224 | tf_op jit(solution)/shard_map/ppermute | solution.py:14
  64.9 7.4 %collective-permute-start.10 = (bf16[64,1024]{1,0:T(8,128)(2,1)S(1)}, bf16[64,1024]{1,0:T(8,128)(2,1)S(1)}, u32[]{:S(2)}, u32[]{:S(2)}) collective-permute-start(bf16[64,1024]{1,0:T(8,128)(2,1)S(1)} %fusion.28), channel_id=1, source_target_pairs={{0,2},{2,0},{4,6},{6,4},{8,10},{10,8},{12,14},{14,12},{1,3},{3,1},... | collective-permute-start | bytes 393224 | tf_op jit(solution)/shard_map/ppermute | solution.py:14
  72.6 1.3 %collective-permute-start.16 = (f32[1,128,128]{2,1,0:T(8,128)S(1)}, f32[1,128,128]{2,1,0:T(8,128)S(1)}, u32[]{:S(2)}, u32[]{:S(2)}) collective-permute-start(f32[1,128,128]{2,1,0:T(8,128)S(1)} %convolution_bitcast_fusion.1), channel_id=1, source_target_pairs={{0,1},{1,0},{2,3},{3,2},{4,5},{5,4},{6,7},{7,6},{8,9},{9,8},{10,11... | collective-permute-start | bytes 196616 | tf_op jit(solution)/shard_map/ppermute | solution.py:64

commit v10 on v9

--- a/solution.py
+++ b/solution.py
@@ -14,12 +14,19 @@
     return lax.ppermute(value, axis, pairs)
 
 
-def ffn_kernel(normed_ref, cot_ref, wg_ref, wu_ref, wd_ref, out_ref):
+def ffn_kernel(*refs):
+    *mix_refs, tok_ref, inv_ref, gain_ref, cot_ref, wg_ref, wu_ref, wd_ref, scaled_ref, inner_ref = refs
     cblock = wg_ref.shape[1]
     contract_last = (((1,), (1,)), ((), ()))
+    inv = inv_ref[...]
+    acc = jnp.zeros((tok_ref.shape[0], cblock), jnp.float32)
     for group in range(wg_ref.shape[0]):
         cols = slice(group * cblock, (group + 1) * cblock)
-        normed = normed_ref[:, cols]
+        mixed = jnp.concatenate([ref[:, cols] for ref in mix_refs], axis=0)
+        tok = tok_ref[:, cols].astype(jnp.float32)
+        resid = tok + tok * mixed.astype(jnp.float32)
+        gain = gain_ref[:, cols]
+        normed = (resid * inv * gain).astype(jnp.bfloat16)
         w_gate = wg_ref[group]
         w_up = wu_ref[group]
         gate_pre = jnp.dot(normed, w_gate, preferred_element_type=jnp.float32)
@@ -30,30 +37,49 @@
         sig = 1.0 / (1.0 + jnp.exp(-gate_pre))
         d_up = (d_hidden * gate_pre * sig).astype(jnp.bfloat16)
         d_gate = (d_hidden * up_val * sig * (1.0 + gate_pre * (1.0 - sig))).astype(jnp.bfloat16)
-        out_ref[:, cols] = lax.dot_general(
+        d_normed = lax.dot_general(
             d_gate, w_gate, contract_last, preferred_element_type=jnp.float32
         ) + lax.dot_general(d_up, w_up, contract_last, preferred_element_type=jnp.float32)
+        scaled = gain * d_normed
+        scaled_ref[:, cols] = scaled
+        acc = acc + resid * scaled
+    part = jnp.sum(acc, axis=1, keepdims=True)
+
+    @pl.when(pl.program_id(0) == 0)
+    def _():
+        inner_ref[...] = part
+
+    @pl.when(pl.program_id(0) > 0)
+    def _():
+        inner_ref[...] += part
 
 
-def ffn_grad(normed, cotangent, w_gate, w_up, w_down, per_step=4):
-    tok, width = normed.shape
+def ffn_grad(pieces, tokens, inv, norm_gain, cotangent, w_gate, w_up, w_down, per_step=4):
+    tok, width = tokens.shape
     groups_here, cblock, hidden = w_gate.shape
     if groups_here % per_step:
         per_step = 1
-    act = pl.BlockSpec((tok, cblock * per_step), lambda g: (0, g))
+    cols = cblock * per_step
+    act = pl.BlockSpec((tok, cols), lambda g: (0, g))
+    piece_specs = [pl.BlockSpec((piece.shape[0], cols), lambda g: (0, g)) for piece in pieces]
     return pl.pallas_call(
         ffn_kernel,
         grid=(groups_here // per_step,),
-        in_specs=[
+        in_specs=piece_specs + [
             act,
+            pl.BlockSpec((tok, 1), lambda g: (0, 0)),
+            pl.BlockSpec((1, cols), lambda g: (0, g)),
             act,
             pl.BlockSpec((per_step, cblock, hidden), lambda g: (g, 0, 0)),
             pl.BlockSpec((per_step, cblock, hidden), lambda g: (g, 0, 0)),
             pl.BlockSpec((per_step, hidden, cblock), lambda g: (g, 0, 0)),
         ],
-        out_specs=act,
-        out_shape=jax.ShapeDtypeStruct((tok, width), jnp.float32),
-    )(normed, cotangent, w_gate, w_up, w_down)
+        out_specs=[act, pl.BlockSpec((tok, 1), lambda g: (0, 0))],
+        out_shape=[
+            jax.ShapeDtypeStruct((tok, width), jnp.float32),
+            jax.ShapeDtypeStruct((tok, 1), jnp.float32),
+        ],
+    )(*pieces, tokens, inv, norm_gain[None, :], cotangent, w_gate, w_up, w_down)
 
 
 def hid_sum(value):
@@ -102,16 +128,14 @@
     tok_f = tokens.astype(jnp.float32)
     mixed_f = current.astype(jnp.float32)
     resid = tok_f + tok_f * mixed_f
-    square = hid_sum(jnp.sum(resid * resid, axis=-1))
+    square = hid_sum(jnp.sum(resid * resid, axis=-1, keepdims=True))
     inv = lax.rsqrt(square / D + 1e-06)
-    normed = (resid * inv[:, None] * norm_gain).astype(jnp.bfloat16)
-    d_normed = ffn_grad(normed, cotangent, w_gate, w_up, w_down)
-    scaled = norm_gain * d_normed
-    inner = hid_sum(jnp.sum(resid * scaled, axis=-1))
+    scaled, inner = ffn_grad(pieces, tokens, inv, norm_gain, cotangent, w_gate, w_up, w_down)
+    inner = hid_sum(inner)
     d_resid = (
         cotangent.astype(jnp.float32)
-        + inv[:, None] * scaled
-        - resid * (inv**3 * inner / D)[:, None]
+        + inv * scaled
+        - resid * (inv**3 * inner / D)
     )
     d_mixed = (d_resid * tok_f).astype(jnp.bfloat16)
     grads_self = [[None] * sections for _ in spans]

time: 74.7 us -> 77.3 us (1.035)
  Pallas kernels: 4.81 us -> 5.7 us
    rsqrt x1 -> x2, other arithmetic: 0.01 us -> 1.59 us  [body(): inv = lax.rsqrt(square / D + 1e-06)]
    reduce_sum x2 -> x1, other arithmetic: 1.5 us -> 0.19 us  [body(): square = hid_sum(jnp.sum(resid * resid, axis=-1, keepdims=True))]
    convert_element_type x1, other arithmetic: 0.31 us -> 1.27 us  [body(): d_mixed = (d_resid * tok_f).astype(jnp.bfloat16)]
    pallas_call x1, Pallas kernels: 4.81 us -> 5.7 us  [ffn_grad(): pl.pallas_call(ffn_kernel, grid=(groups_here // per_step,), in_specs=piec...]
    convert_element_type x1 -> x0, other arithmetic: 0.82 us -> none  [body(): normed = (resid * inv[:, None] * norm_gain).astype(jnp.bfloat16)]
where the time goes in v10:
time: 77.3 us; the launch traced here: 77 us
  waiting for transfers between devices  40.1 us (52%)
  starting transfers between devices  19.1 us (25%)
  other arithmetic  7.34 us (9%)
  Pallas kernels  5.7 us (7%)
  matrix products  2.65 us (3%)
  local copies, waits for them, and re-layouts  1.26 us (2%)
  between operations  0.91 us (1%)
    ppermute x12, waiting for transfers between devices, from_partner(): return lax.ppermute(value, axis, pairs)  37.3 us
    ppermute x12, starting transfers between devices, from_partner(): return lax.ppermute(value, axis, pairs)  18.2 us
    pallas_call x1, Pallas kernels, ffn_grad(): pl.pallas_call(ffn_kernel, grid=(groups_here // per_step,), in_specs=piec...  5.7 us
    ppermute x5, waiting for transfers between devices, hid_sum(): total = total + lax.ppermute(value, 'hid', pairs)  2.73 us
    add x3, other arithmetic, hid_sum(): total = total + lax.ppermute(value, 'hid', pairs)  1.95 us
    rsqrt x2, other arithmetic, body(): inv = lax.rsqrt(square / D + 1e-06)  1.59 us
  transfers between devices with their start and end apart: 17, of which 13 were waited for; matrix products, arithmetic and copies ran while one was open for 5% of the time, Pallas kernels for 0%

profile of v10, /device:TPU:0, one launch (start us, length us, event | category | flops | bytes accessed | tf_op | source)
XLA Modules:
  0.0 77.0 jit_solution(2602426760961632108)
XLA Ops:
  0.7 1.2 %convolution_convert_fusion = bf16[64,1024]{1,0:T(8,128)(2,1)S(1)} fusion(bf16[128,1024]{1,0:T(8,128)(2,1)} %refs_2_.1, bf16[1,128,128]{2,1,0:T(8,128)(2,1)} %param.11), kind=kOutput, calls=%fused_computation.3 | convolution fusion | flops 16842752 | bytes 409600 | tf_op jit(solution)/shard_map/kij,kjd->kid/dot_general | solution.py:107
  1.8 3.0 %collective-permute-start.3 = (bf16[64,1024]{1,0:T(8,128)(2,1)S(1)}, bf16[64,1024]{1,0:T(8,128)(2,1)S(1)}, u32[]{:S(2)}, u32[]{:S(2)}) collective-permute-start(bf16[64,1024]{1,0:T(8,128)(2,1)S(1)} %convolution_convert_fusion), channel_id=1, source_target_pairs={{0,2},{2,0},{4,6},{6,4},{8,10},{10,8},{12,14},{14,12},{1,3},{3,1},... | collective-permute-start | bytes 393224 | tf_op jit(solution)/shard_map/ppermute | solution.py:14
  5.8 3.4 %collective-permute-done.3 = bf16[64,1024]{1,0:T(8,128)(2,1)S(1)} collective-permute-done((bf16[64,1024]{1,0:T(8,128)(2,1)S(1)}, bf16[64,1024]{1,0:T(8,128)(2,1)S(1)}, u32[]{:S(2)}, u32[]{:S(2)}) %collective-permute-start.3) | collective-permute-done | bytes 131104 | tf_op jit(solution)/shard_map/ppermute | solution.py:14
  9.3 2.2 %collective-permute-start.4 = (bf16[64,1024]{1,0:T(8,128)(2,1)S(1)}, bf16[64,1024]{1,0:T(8,128)(2,1)S(1)}, u32[]{:S(2)}, u32[]{:S(2)}) collective-permute-start(bf16[64,1024]{1,0:T(8,128)(2,1)S(1)} %fusion.11), channel_id=1, source_target_pairs={{0,4},{2,6},{4,0},{6,2},{8,12},{10,14},{12,8},{14,10},{1,5},{3,7},... | collective-permute-start | bytes 393224 | tf_op jit(solution)/shard_map/ppermute | solution.py:14
  11.6 1.5 %collective-permute-start.1 = (bf16[64,1024]{1,0:T(8,128)(2,1)S(1)}, bf16[64,1024]{1,0:T(8,128)(2,1)S(1)}, u32[]{:S(2)}, u32[]{:S(2)}) collective-permute-start(bf16[64,1024]{1,0:T(8,128)(2,1)S(1)} %fusion.5), channel_id=1, source_target_pairs={{0,4},{2,6},{4,0},{6,2},{8,12},{10,14},{12,8},{14,10},{1,5},{3,7},... | collective-permute-start | bytes 393224 | tf_op jit(solution)/shard_map/ppermute | solution.py:14
  13.2 3.9 %collective-permute-done.4 = bf16[64,1024]{1,0:T(8,128)(2,1)S(1)} collective-permute-done((bf16[64,1024]{1,0:T(8,128)(2,1)S(1)}, bf16[64,1024]{1,0:T(8,128)(2,1)S(1)}, u32[]{:S(2)}, u32[]{:S(2)}) %collective-permute-start.4) | collective-permute-done | bytes 131104 | tf_op jit(solution)/shard_map/ppermute | solution.py:14
  17.2 1.8 %collective-permute-start.5 = (bf16[64,1024]{1,0:T(8,128)(2,1)S(1)}, bf16[64,1024]{1,0:T(8,128)(2,1)S(1)}, u32[]{:S(2)}, u32[]{:S(2)}) collective-permute-start(bf16[64,1024]{1,0:T(8,128)(2,1)S(1)} %fusion.13), channel_id=1, source_target_pairs={{0,8},{2,10},{4,12},{6,14},{8,0},{10,2},{12,4},{14,6},{1,9},{3,11}... | collective-permute-start | bytes 393224 | tf_op jit(solution)/shard_map/ppermute | solution.py:14
  19.1 2.4 %collective-permute-start.2 = (bf16[64,1024]{1,0:T(8,128)(2,1)S(1)}, bf16[64,1024]{1,0:T(8,128)(2,1)S(1)}, u32[]{:S(2)}, u32[]{:S(2)}) collective-permute-start(bf16[64,1024]{1,0:T(8,128)(2,1)S(1)} %fusion.7), channel_id=1, source_target_pairs={{0,8},{2,10},{4,12},{6,14},{8,0},{10,2},{12,4},{14,6},{1,9},{3,11}... | collective-permute-start | bytes 393224 | tf_op jit(solution)/shard_map/ppermute | solution.py:14
  21.5 6.4 %collective-permute-done.5 = bf16[64,1024]{1,0:T(8,128)(2,1)S(1)} collective-permute-done((bf16[64,1024]{1,0:T(8,128)(2,1)S(1)}, bf16[64,1024]{1,0:T(8,128)(2,1)S(1)}, u32[]{:S(2)}, u32[]{:S(2)}) %collective-permute-start.5) | collective-permute-done | bytes 131104 | tf_op jit(solution)/shard_map/ppermute | solution.py:14
  28.1 1.3 %collective-permute-done.2 = bf16[64,1024]{1,0:T(8,128)(2,1)S(1)} collective-permute-done((bf16[64,1024]{1,0:T(8,128)(2,1)S(1)}, bf16[64,1024]{1,0:T(8,128)(2,1)S(1)}, u32[]{:S(2)}, u32[]{:S(2)}) %collective-permute-start.2) | collective-permute-done | bytes 131104 | tf_op jit(solution)/shard_map/ppermute | solution.py:14
  29.7 0.5 copy-done.4
  30.4 1.2 %collective-permute-done.6 = f32[128,1]{1,0:T(8,128)S(1)} collective-permute-done((f32[128,1]{1,0:T(8,128)S(1)}, f32[128,1]{1,0:T(8,128)S(1)}, u32[]{:S(2)}, u32[]{:S(2)}) %collective-permute-start.6) | collective-permute-done | bytes 544 | tf_op jit(solution)/shard_map/ppermute | solution.py:90
  31.6 0.6 add_rsqrt_fusion.refs_3_
  32.3 5.7 %shard_map.120 = (f32[128,1024]{1,0:T(8,128)}, f32[128,1]{1,0:T(8,128)}) custom-call(bf16[64,1024]{1,0:T(8,128)(2,1)} %copy-done.4, bf16[64,1024]{1,0:T(8,128)(2,1)} %copy-done.2, bf16[128,1024]{1,0:T(8,128)(2,1)} %refs_2_.1, f32[128,1]{1,0:T(8,128)} %add_rsqrt_fusion.refs_3_, f32[1,1024]{1,0:T(1,128)} %bitcast.82, bf16[128,1024]{1,0:T(8,128)(2,1)} %refs_5_.1, ...), custom_call_target="tpu_custom_call" | custom-call | tf_op jit(solution)/shard_map/pallas_call | solution.py:65
  38.2 1.3 %collective-permute-done.7 = f32[128,1]{1,0:T(8,128)S(1)} collective-permute-done((f32[128,1]{1,0:T(8,128)}, f32[128,1]{1,0:T(8,128)S(1)}, u32[]{:S(2)}, u32[]{:S(2)}) %collective-permute-start.7) | collective-permute-done | bytes 544 | tf_op jit(solution)/shard_map/ppermute | solution.py:90
  39.5 0.9 %fusion.56 = (f32[128]{0:T(128)S(1)}, f32[128]{0:T(128)S(1)}) fusion(f32[128,1]{1,0:T(8,128)S(1)} %copy-done.7, f32[128,1]{1,0:T(8,128)} %get-tuple-element.7, f32[128,1]{1,0:T(8,128)S(1)} %collective-permute-done.7), kind=kLoop, calls=%fused_computation.119 | loop fusion | flops 640 | bytes 2560 | tf_op jit(solution)/shard_map/rsqrt | solution.py:132
  40.5 1.3 %fusion.2 = bf16[128,1024]{1,0:T(8,128)(2,1)S(1)} fusion(bf16[128,1024]{1,0:T(8,128)(2,1)S(1)} %copy-done.1, f32[128]{0:T(128)S(1)} %get-tuple-element.21, bf16[64,1024]{1,0:T(8,128)(2,1)S(1)} %copy-done.3, bf16[64,1024]{1,0:T(8,128)(2,1)S(1)} %copy-done.5, f32[128,1024]{1,0:T(8,128)} %get-tuple-element.6, f32[128]{0:T(128)S(1)} %get-tuple-element.20, ...), kind=kLoop, calls=%fused_computation.9 | loop fusion | flops 1835008 | bytes 1573888 | tf_op jit(solution)/shard_map/convert_element_type | solution.py:140
  42.1 2.9 %collective-permute-start.11 = (bf16[64,1024]{1,0:T(8,128)(2,1)S(1)}, bf16[64,1024]{1,0:T(8,128)(2,1)S(1)}, u32[]{:S(2)}, u32[]{:S(2)}) collective-permute-start(bf16[64,1024]{1,0:T(8,128)(2,1)S(1)} %get-tuple-element.27), channel_id=1, source_target_pairs={{0,8},{2,10},{4,12},{6,14},{8,0},{10,2},{12,4},{14,6},{1,9},{3,11}... | collective-permute-start | bytes 393224 | tf_op jit(solution)/shard_map/ppermute | solution.py:14
  45.0 8.6 %collective-permute-done.8 = bf16[64,1024]{1,0:T(8,128)(2,1)S(1)} collective-permute-done((bf16[64,1024]{1,0:T(8,128)(2,1)S(1)}, bf16[64,1024]{1,0:T(8,128)(2,1)S(1)}, u32[]{:S(2)}, u32[]{:S(2)}) %collective-permute-start.8) | collective-permute-done | bytes 131104 | tf_op jit(solution)/shard_map/ppermute | solution.py:14
  53.6 2.7 %collective-permute-done.11 = bf16[64,1024]{1,0:T(8,128)(2,1)S(1)} collective-permute-done((bf16[64,1024]{1,0:T(8,128)(2,1)S(1)}, bf16[64,1024]{1,0:T(8,128)(2,1)S(1)}, u32[]{:S(2)}, u32[]{:S(2)}) %collective-permute-start.11) | collective-permute-done | bytes 131104 | tf_op jit(solution)/shard_map/ppermute | solution.py:14
  56.9 2.0 %collective-permute-start.9 = (bf16[64,1024]{1,0:T(8,128)(2,1)S(1)}, bf16[64,1024]{1,0:T(8,128)(2,1)S(1)}, u32[]{:S(2)}, u32[]{:S(2)}) collective-permute-start(bf16[64,1024]{1,0:T(8,128)(2,1)S(1)} %fusion.23), channel_id=1, source_target_pairs={{0,4},{2,6},{4,0},{6,2},{8,12},{10,14},{12,8},{14,10},{1,5},{3,7},... | collective-permute-start | bytes 393224 | tf_op jit(solution)/shard_map/ppermute | solution.py:14
  59.0 4.3 %collective-permute-done.12 = bf16[64,1024]{1,0:T(8,128)(2,1)S(1)} collective-permute-done((bf16[64,1024]{1,0:T(8,128)(2,1)S(1)}, bf16[64,1024]{1,0:T(8,128)(2,1)S(1)}, u32[]{:S(2)}, u32[]{:S(2)}) %collective-permute-start.12) | collective-permute-done | bytes 131104 | tf_op jit(solution)/shard_map/ppermute | solution.py:14
  63.3 1.9 %collective-permute-done.9 = bf16[64,1024]{1,0:T(8,128)(2,1)S(1)} collective-permute-done((bf16[64,1024]{1,0:T(8,128)(2,1)S(1)}, bf16[64,1024]{1,0:T(8,128)(2,1)S(1)}, u32[]{:S(2)}, u32[]{:S(2)}) %collective-permute-start.9) | collective-permute-done | bytes 131104 | tf_op jit(solution)/shard_map/ppermute | solution.py:14
  65.7 0.5 collective-permute-start.14
  66.4 0.8 %collective-permute-start.13 = (bf16[64,1024]{1,0:T(8,128)(2,1)S(1)}, bf16[64,1024]{1,0:T(8,128)(2,1)S(1)}, u32[]{:S(2)}, u32[]{:S(2)}) collective-permute-start(bf16[64,1024]{1,0:T(8,128)(2,1)S(1)} %fusion.43), channel_id=1, source_target_pairs={{0,2},{2,0},{4,6},{6,4},{8,10},{10,8},{12,14},{14,12},{1,3},{3,1},... | collective-permute-start | bytes 393224 | tf_op jit(solution)/shard_map/ppermute | solution.py:14
  67.2 1.2 %collective-permute-start.10 = (bf16[64,1024]{1,0:T(8,128)(2,1)S(1)}, bf16[64,1024]{1,0:T(8,128)(2,1)S(1)}, u32[]{:S(2)}, u32[]{:S(2)}) collective-permute-start(bf16[64,1024]{1,0:T(8,128)(2,1)S(1)} %fusion.28), channel_id=1, source_target_pairs={{0,2},{2,0},{4,6},{6,4},{8,10},{10,8},{12,14},{14,12},{1,3},{3,1},... | collective-permute-start | bytes 393224 | tf_op jit(solution)/shard_map/ppermute | solution.py:14
  68.5 0.7 fusion.64
  69.1 0.7 fusion.65
  69.8 3.0 %collective-permute-done.13 = bf16[64,1024]{1,0:T(8,128)(2,1)S(1)} collective-permute-done((bf16[64,1024]{1,0:T(8,128)(2,1)S(1)}, bf16[64,1024]{1,0:T(8,128)(2,1)S(1)}, u32[]{:S(2)}, u32[]{:S(2)}) %collective-permute-start.13) | collective-permute-done | bytes 131104 | tf_op jit(solution)/shard_map/ppermute | solution.py:14
  72.9 1.7 %collective-permute-done.10 = bf16[64,1024]{1,0:T(8,128)(2,1)S(1)} collective-permute-done((bf16[64,1024]{1,0:T(8,128)(2,1)S(1)}, bf16[64,1024]{1,0:T(8,128)(2,1)S(1)}, u32[]{:S(2)}, u32[]{:S(2)}) %collective-permute-start.10) | collective-permute-done | bytes 131104 | tf_op jit(solution)/shard_map/ppermute | solution.py:14
  75.1 1.1 %fusion.1 = bf16[128,1024]{1,0:T(8,128)(2,1)} fusion(bf16[64,1024]{1,0:T(8,128)(2,1)S(1)} %fusion.42, bf16[64,1024]{1,0:T(8,128)(2,1)S(1)} %fusion.27, bf16[64,1024]{1,0:T(8,128)(2,1)S(1)} %copy-done.3, bf16[64,1024]{1,0:T(8,128)(2,1)S(1)} %copy-done.5, bf16[1,128,128]{2,1,0:T(8,128)(2,1)S(1)} %copy-done.9, f32[128]{0:T(128)S(1)} %get-tuple-element.21, ...), kind=kOutput, calls=%fused_computation.2 | convolution fusion | flops 36175872 | bytes 1868800 | tf_op jit(solution)/shard_map/kij,kid->kjd/dot_general | solution.py:165
  76.3 0.6 add.95
  (58 shorter events, 4.5 us)
Async XLA Ops:
  0.6 4.2 %copy-start = (bf16[128,1024]{1,0:T(8,128)(2,1)S(1)}, bf16[128,1024]{1,0:T(8,128)(2,1)}, u32[]{:S(2)}) copy-start(bf16[128,1024]{1,0:T(8,128)(2,1)} %refs_2_.1) | copy-start | bytes 786436
  0.6 4.2 %copy-start.9 = (bf16[1,128,128]{2,1,0:T(8,128)(2,1)S(1)}, bf16[1,128,128]{2,1,0:T(8,128)(2,1)}, u32[]{:S(2)}) copy-start(bf16[1,128,128]{2,1,0:T(8,128)(2,1)} %param.11) | copy-start | bytes 98308
  1.8 7.3 %collective-permute-start.3 = (bf16[64,1024]{1,0:T(8,128)(2,1)S(1)}, bf16[64,1024]{1,0:T(8,128)(2,1)S(1)}, u32[]{:S(2)}, u32[]{:S(2)}) collective-permute-start(bf16[64,1024]{1,0:T(8,128)(2,1)S(1)} %convolution_convert_fusion), channel_id=1, source_target_pairs={{0,2},{2,0},{4,6},{6,4},{8,10},{10,8},{12,14},{14,12},{1,3},{3,1},... | collective-permute-start | bytes 393224 | tf_op jit(solution)/shard_map/ppermute | solution.py:14
  4.9 0.7 copy-start.10
  5.0 0.7 copy-start.11
  5.0 6.5 %collective-permute-start = (bf16[64,1024]{1,0:T(8,128)(2,1)S(1)}, bf16[64,1024]{1,0:T(8,128)(2,1)S(1)}, u32[]{:S(2)}, u32[]{:S(2)}) collective-permute-start(bf16[64,1024]{1,0:T(8,128)(2,1)S(1)} %convolution_convert_fusion.1), channel_id=1, source_target_pairs={{0,2},{2,0},{4,6},{6,4},{8,10},{10,8},{12,14},{14,12},{1,3},{3,1},... | collective-permute-start | bytes 393224 | tf_op jit(solution)/shard_map/ppermute | solution.py:14
  9.3 7.8 %collective-permute-start.4 = (bf16[64,1024]{1,0:T(8,128)(2,1)S(1)}, bf16[64,1024]{1,0:T(8,128)(2,1)S(1)}, u32[]{:S(2)}, u32[]{:S(2)}) collective-permute-start(bf16[64,1024]{1,0:T(8,128)(2,1)S(1)} %fusion.11), channel_id=1, source_target_pairs={{0,4},{2,6},{4,0},{6,2},{8,12},{10,14},{12,8},{14,10},{1,5},{3,7},... | collective-permute-start | bytes 393224 | tf_op jit(solution)/shard_map/ppermute | solution.py:14
  11.6 7.4 %collective-permute-start.1 = (bf16[64,1024]{1,0:T(8,128)(2,1)S(1)}, bf16[64,1024]{1,0:T(8,128)(2,1)S(1)}, u32[]{:S(2)}, u32[]{:S(2)}) collective-permute-start(bf16[64,1024]{1,0:T(8,128)(2,1)S(1)} %fusion.5), channel_id=1, source_target_pairs={{0,4},{2,6},{4,0},{6,2},{8,12},{10,14},{12,8},{14,10},{1,5},{3,7},... | collective-permute-start | bytes 393224 | tf_op jit(solution)/shard_map/ppermute | solution.py:14
  17.2 10.8 %collective-permute-start.5 = (bf16[64,1024]{1,0:T(8,128)(2,1)S(1)}, bf16[64,1024]{1,0:T(8,128)(2,1)S(1)}, u32[]{:S(2)}, u32[]{:S(2)}) collective-permute-start(bf16[64,1024]{1,0:T(8,128)(2,1)S(1)} %fusion.13), channel_id=1, source_target_pairs={{0,8},{2,10},{4,12},{6,14},{8,0},{10,2},{12,4},{14,6},{1,9},{3,11}... | collective-permute-start | bytes 393224 | tf_op jit(solution)/shard_map/ppermute | solution.py:14
  19.1 10.3 %collective-permute-start.2 = (bf16[64,1024]{1,0:T(8,128)(2,1)S(1)}, bf16[64,1024]{1,0:T(8,128)(2,1)S(1)}, u32[]{:S(2)}, u32[]{:S(2)}) collective-permute-start(bf16[64,1024]{1,0:T(8,128)(2,1)S(1)} %fusion.7), channel_id=1, source_target_pairs={{0,8},{2,10},{4,12},{6,14},{8,0},{10,2},{12,4},{14,6},{1,9},{3,11}... | collective-permute-start | bytes 393224 | tf_op jit(solution)/shard_map/ppermute | solution.py:14
  28.1 1.4 %copy-start.2 = (bf16[64,1024]{1,0:T(8,128)(2,1)}, bf16[64,1024]{1,0:T(8,128)(2,1)S(1)}, u32[]{:S(2)}) copy-start(bf16[64,1024]{1,0:T(8,128)(2,1)S(1)} %fusion.15.refs_1_) | copy-start | bytes 393220
  29.5 0.7 copy-start.4
  30.3 1.3 %collective-permute-start.6 = (f32[128,1]{1,0:T(8,128)S(1)}, f32[128,1]{1,0:T(8,128)S(1)}, u32[]{:S(2)}, u32[]{:S(2)}) collective-permute-start(f32[128,1]{1,0:T(8,128)S(1)} %copy.17), channel_id=1, source_target_pairs={{0,1},{1,0},{2,3},{3,2},{4,5},{5,4},{6,7},{7,6},{8,9},{9,8},{10,11... | collective-permute-start | bytes 1544 | tf_op jit(solution)/shard_map/ppermute | solution.py:90
  32.2 7.3 %copy-start.7 = (f32[128,1]{1,0:T(8,128)S(1)}, f32[128,1]{1,0:T(8,128)}, u32[]{:S(2)}) copy-start(f32[128,1]{1,0:T(8,128)} %add_rsqrt_fusion.refs_3_) | copy-start | bytes 1540
  32.2 8.2 %copy-start.1 = (bf16[128,1024]{1,0:T(8,128)(2,1)S(1)}, bf16[128,1024]{1,0:T(8,128)(2,1)}, u32[]{:S(2)}) copy-start(bf16[128,1024]{1,0:T(8,128)(2,1)} %refs_2_.1) | copy-start | bytes 786436
  32.2 8.2 %copy-start.5 = (bf16[64,1024]{1,0:T(8,128)(2,1)S(1)}, bf16[64,1024]{1,0:T(8,128)(2,1)}, u32[]{:S(2)}) copy-start(bf16[64,1024]{1,0:T(8,128)(2,1)} %copy-done.4) | copy-start | bytes 393220
  32.2 8.2 %copy-start.6 = (bf16[128,1024]{1,0:T(8,128)(2,1)S(1)}, bf16[128,1024]{1,0:T(8,128)(2,1)}, u32[]{:S(2)}) copy-start(bf16[128,1024]{1,0:T(8,128)(2,1)} %refs_5_.1) | copy-start | bytes 786436
  38.0 2.5 %copy-start.3 = (bf16[64,1024]{1,0:T(8,128)(2,1)S(1)}, bf16[64,1024]{1,0:T(8,128)(2,1)}, u32[]{:S(2)}) copy-start(bf16[64,1024]{1,0:T(8,128)(2,1)} %copy-done.2) | copy-start | bytes 393220
  38.0 1.5 %collective-permute-start.7 = (f32[128,1]{1,0:T(8,128)}, f32[128,1]{1,0:T(8,128)S(1)}, u32[]{:S(2)}, u32[]{:S(2)}) collective-permute-start(f32[128,1]{1,0:T(8,128)} %get-tuple-element.7), channel_id=1, source_target_pairs={{0,1},{1,0},{2,3},{3,2},{4,5},{5,4},{6,7},{7,6},{8,9},{9,8},{10,11... | collective-permute-start | bytes 1544 | tf_op jit(solution)/shard_map/ppermute | solution.py:90
  42.0 11.6 %collective-permute-start.8 = (bf16[64,1024]{1,0:T(8,128)(2,1)S(1)}, bf16[64,1024]{1,0:T(8,128)(2,1)S(1)}, u32[]{:S(2)}, u32[]{:S(2)}) collective-permute-start(bf16[64,1024]{1,0:T(8,128)(2,1)S(1)} %get-tuple-element.26), channel_id=1, source_target_pairs={{0,8},{2,10},{4,12},{6,14},{8,0},{10,2},{12,4},{14,6},{1,9},{3,11}... | collective-permute-start | bytes 393224 | tf_op jit(solution)/shard_map/ppermute | solution.py:14
  42.1 14.2 %collective-permute-start.11 = (bf16[64,1024]{1,0:T(8,128)(2,1)S(1)}, bf16[64,1024]{1,0:T(8,128)(2,1)S(1)}, u32[]{:S(2)}, u32[]{:S(2)}) collective-permute-start(bf16[64,1024]{1,0:T(8,128)(2,1)S(1)} %get-tuple-element.27), channel_id=1, source_target_pairs={{0,8},{2,10},{4,12},{6,14},{8,0},{10,2},{12,4},{14,6},{1,9},{3,11}... | collective-permute-start | bytes 393224 | tf_op jit(solution)/shard_map/ppermute | solution.py:14
  56.9 6.4 %collective-permute-start.12 = (bf16[64,1024]{1,0:T(8,128)(2,1)S(1)}, bf16[64,1024]{1,0:T(8,128)(2,1)S(1)}, u32[]{:S(2)}, u32[]{:S(2)}) collective-permute-start(bf16[64,1024]{1,0:T(8,128)(2,1)S(1)} %fusion.38), channel_id=1, source_target_pairs={{0,4},{2,6},{4,0},{6,2},{8,12},{10,14},{12,8},{14,10},{1,5},{3,7},... | collective-permute-start | bytes 393224 | tf_op jit(solution)/shard_map/ppermute | solution.py:14
  56.9 8.2 %collective-permute-start.9 = (bf16[64,1024]{1,0:T(8,128)(2,1)S(1)}, bf16[64,1024]{1,0:T(8,128)(2,1)S(1)}, u32[]{:S(2)}, u32[]{:S(2)}) collective-permute-start(bf16[64,1024]{1,0:T(8,128)(2,1)S(1)} %fusion.23), channel_id=1, source_target_pairs={{0,4},{2,6},{4,0},{6,2},{8,12},{10,14},{12,8},{14,10},{1,5},{3,7},... | collective-permute-start | bytes 393224 | tf_op jit(solution)/shard_map/ppermute | solution.py:14
  65.6 2.9 %collective-permute-start.15 = (f32[3,128]{1,0:T(4,128)S(1)}, f32[3,128]{1,0:T(4,128)S(1)}, u32[]{:S(2)}, u32[]{:S(2)}) collective-permute-start(f32[3,128]{1,0:T(4,128)S(1)} %maximum_maximum_fusion.1), channel_id=1, source_target_pairs={{0,1},{1,0},{2,3},{3,2},{4,5},{5,4},{6,7},{7,6},{8,9},{9,8},{10,11... | collective-permute-start | bytes 4616 | tf_op jit(solution)/shard_map/ppermute | solution.py:90
  65.7 3.4 %collective-permute-start.14 = (f32[3,128]{1,0:T(4,128)S(1)}, f32[3,128]{1,0:T(4,128)S(1)}, u32[]{:S(2)}, u32[]{:S(2)}) collective-permute-start(f32[3,128]{1,0:T(4,128)S(1)} %maximum_maximum_fusion), channel_id=1, source_target_pairs={{0,1},{1,0},{2,3},{3,2},{4,5},{5,4},{6,7},{7,6},{8,9},{9,8},{10,11... | collective-permute-start | bytes 4616 | tf_op jit(solution)/shard_map/ppermute | solution.py:90
  66.4 6.4 %collective-permute-start.13 = (bf16[64,1024]{1,0:T(8,128)(2,1)S(1)}, bf16[64,1024]{1,0:T(8,128)(2,1)S(1)}, u32[]{:S(2)}, u32[]{:S(2)}) collective-permute-start(bf16[64,1024]{1,0:T(8,128)(2,1)S(1)} %fusion.43), channel_id=1, source_target_pairs={{0,2},{2,0},{4,6},{6,4},{8,10},{10,8},{12,14},{14,12},{1,3},{3,1},... | collective-permute-start | bytes 393224 | tf_op jit(solution)/shard_map/ppermute | solution.py:14
  67.2 7.5 %collective-permute-start.10 = (bf16[64,1024]{1,0:T(8,128)(2,1)S(1)}, bf16[64,1024]{1,0:T(8,128)(2,1)S(1)}, u32[]{:S(2)}, u32[]{:S(2)}) collective-permute-start(bf16[64,1024]{1,0:T(8,128)(2,1)S(1)} %fusion.28), channel_id=1, source_target_pairs={{0,2},{2,0},{4,6},{6,4},{8,10},{10,8},{12,14},{14,12},{1,3},{3,1},... | collective-permute-start | bytes 393224 | tf_op jit(solution)/shard_map/ppermute | solution.py:14
  72.9 2.2 %copy-start.8 = (f32[128,1024]{1,0:T(8,128)S(1)}, f32[128,1024]{1,0:T(8,128)}, u32[]{:S(2)}) copy-start(f32[128,1024]{1,0:T(8,128)} %get-tuple-element.6) | copy-start | bytes 1572868
  75.0 1.3 %collective-permute-start.16 = (f32[1,128,128]{2,1,0:T(8,128)S(1)}, f32[1,128,128]{2,1,0:T(8,128)S(1)}, u32[]{:S(2)}, u32[]{:S(2)}) collective-permute-start(f32[1,128,128]{2,1,0:T(8,128)S(1)} %convolution_bitcast_fusion.1), channel_id=1, source_target_pairs={{0,1},{1,0},{2,3},{3,2},{4,5},{5,4},{6,7},{7,6},{8,9},{9,8},{10,11... | collective-permute-start | bytes 196616 | tf_op jit(solution)/shard_map/ppermute | solution.py:90

commit v11 on v9

--- a/solution.py
+++ b/solution.py
@@ -53,6 +53,11 @@
         ],
         out_specs=act,
         out_shape=jax.ShapeDtypeStruct((tok, width), jnp.float32),
+        cost_estimate=pl.CostEstimate(
+            flops=10 * tok * cblock * hidden * groups_here,
+            transcendentals=tok * hidden * groups_here,
+            bytes_accessed=3 * groups_here * cblock * hidden * 2 + tok * width * 8,
+        ),
     )(normed, cotangent, w_gate, w_up, w_down)
 
 
@@ -63,6 +68,12 @@
         pairs = [(source, (source + shift) % size) for source in range(size)]
         total = total + lax.ppermute(value, "hid", pairs)
     return total
+
+
+def tie(value, after):
+    if after is None:
+        return value
+    return lax.optimization_barrier((value, after))[0]
 
 
 def body(tokens, cotangent, blocks, coef_self, coef_cross, norm_gain, w_gate, w_up, w_down):
@@ -98,25 +109,36 @@
                 coef_self[section, rs][:, None] * value.astype(jnp.float32)
                 + coef_cross[section, rs][:, None] * mate.astype(jnp.float32)
             ).astype(jnp.bfloat16)
-    current = jnp.concatenate(pieces, axis=0)
-    tok_f = tokens.astype(jnp.float32)
-    mixed_f = current.astype(jnp.float32)
-    resid = tok_f + tok_f * mixed_f
-    square = hid_sum(jnp.sum(resid * resid, axis=-1))
-    inv = lax.rsqrt(square / D + 1e-06)
-    normed = (resid * inv[:, None] * norm_gain).astype(jnp.bfloat16)
-    d_normed = ffn_grad(normed, cotangent, w_gate, w_up, w_down)
-    scaled = norm_gain * d_normed
-    inner = hid_sum(jnp.sum(resid * scaled, axis=-1))
-    d_resid = (
-        cotangent.astype(jnp.float32)
-        + inv[:, None] * scaled
-        - resid * (inv**3 * inner / D)[:, None]
-    )
-    d_mixed = (d_resid * tok_f).astype(jnp.bfloat16)
+    top = sections - 1
+    backs = []
+    sents = []
+    directs = []
+    previous = None
+    for chunk, rs in enumerate(spans):
+        mixed = tie(pieces[chunk], previous)
+        cot = cotangent[rs]
+        tok_f = tokens[rs].astype(jnp.float32)
+        mixed_f = mixed.astype(jnp.float32)
+        resid = tok_f + tok_f * mixed_f
+        square = hid_sum(jnp.sum(resid * resid, axis=-1))
+        inv = lax.rsqrt(square / D + 1e-06)
+        normed = (resid * inv[:, None] * norm_gain).astype(jnp.bfloat16)
+        d_normed = ffn_grad(normed, cot, w_gate, w_up, w_down)
+        scaled = norm_gain * d_normed
+        inner = hid_sum(jnp.sum(resid * scaled, axis=-1))
+        d_resid = (
+            cot.astype(jnp.float32)
+            + inv[:, None] * scaled
+            - resid * (inv**3 * inner / D)[:, None]
+        )
+        d_mixed = (d_resid * tok_f).astype(jnp.bfloat16)
+        sent = (coef_cross[top, rs][:, None] * d_mixed.astype(jnp.float32)).astype(jnp.bfloat16)
+        previous = sent
+        backs.append(d_mixed)
+        sents.append(sent)
+        directs.append(d_resid * (1.0 + mixed_f))
     grads_self = [[None] * sections for _ in spans]
     grads_cross = [[None] * sections for _ in spans]
-    backs = [d_mixed[rs] for rs in spans]
     for section in range(sections - 1, -1, -1):
         for chunk, rs in enumerate(spans):
             back_f = backs[chunk].astype(jnp.float32)
@@ -126,7 +148,10 @@
             grads_cross[chunk][section] = jnp.sum(
                 back_f * mates[chunk][section].astype(jnp.float32), axis=-1
             )
-            sent = (coef_cross[section, rs][:, None] * back_f).astype(jnp.bfloat16)
+            if section == top:
+                sent = sents[chunk]
+            else:
+                sent = (coef_cross[section, rs][:, None] * back_f).astype(jnp.bfloat16)
             received = from_partner(sent, "seq", section)
             backs[chunk] = (
                 coef_self[section, rs][:, None] * back_f + received.astype(jnp.float32)
@@ -142,7 +167,7 @@
         "kij,kid->kjd", blocks, back_blocks, preferred_element_type=jnp.float32
     ).reshape(tok, width)
     grad_self, grad_cross, grad_blocks = jax.tree.map(hid_sum, (part_self, part_cross, part_blocks))
-    grad_x = (d_resid * (1.0 + mixed_f) + from_blocks).astype(jnp.bfloat16)
+    grad_x = (jnp.concatenate(directs, axis=0) + from_blocks).astype(jnp.bfloat16)
     return (grad_x, grad_self, grad_cross, grad_blocks)
 
 

time: 74.7 us -> 70.8 us (0.948)
  waiting for transfers between devices: 39.5 us -> 29.7 us
  Pallas kernels: 4.81 us -> 8.11 us
  other arithmetic: 6.93 us -> 9.3 us
    ppermute x12, waiting for transfers between devices: 37.3 us -> 27.7 us  [from_partner(): return lax.ppermute(value, axis, pairs)]
    pallas_call x1 -> x2, Pallas kernels: 4.81 us -> 8.11 us  [ffn_grad(): pl.pallas_call(ffn_kernel, grid=(groups_here // per_step,), in_specs=[act...]
    reduce_sum x1 -> x2, other arithmetic: 1.31 us -> 2.29 us  [body(): inner = hid_sum(jnp.sum(resid * scaled, axis=-1))]
    reduce_sum x3 -> x6, other arithmetic: 0.93 us -> 1.64 us  [body(): jnp.sum(back_f * mates[chunk][section].astype(jnp.float32), axis=-1)]
    convert_element_type x1 -> x2, other arithmetic: 0.82 us -> 1.5 us  [body(): normed = (resid * inv[:, None] * norm_gain).astype(jnp.bfloat16)]
    ppermute x5 -> x7, waiting for transfers between devices: 2.19 us -> 1.95 us  [hid_sum(): total = total + lax.ppermute(value, 'hid', pairs)]
  transfers between devices with their start and end apart: 17 -> 19, of which waited for: 13 -> 13; matrix products, arithmetic and copies ran while one was open for 5% -> 11% of each run, Pallas kernels for 0% -> 6%
where the time goes in v11:
time: 70.8 us; the launch traced here: 70.5 us
  waiting for transfers between devices  29.7 us (42%)
  starting transfers between devices  18.8 us (27%)
  other arithmetic  9.3 us (13%)
  Pallas kernels  8.11 us (11%)
  matrix products  2.57 us (4%)
  local copies, waits for them, and re-layouts  1.2 us (2%)
  between operations  0.88 us (1%)
    ppermute x12, waiting for transfers between devices, from_partner(): return lax.ppermute(value, axis, pairs)  27.7 us
    ppermute x12, starting transfers between devices, from_partner(): return lax.ppermute(value, axis, pairs)  17.6 us
    pallas_call x2, Pallas kernels, ffn_grad(): pl.pallas_call(ffn_kernel, grid=(groups_here // per_step,), in_specs=[act...  8.11 us
    reduce_sum x2, other arithmetic, body(): inner = hid_sum(jnp.sum(resid * scaled, axis=-1))  2.29 us
    add x3, other arithmetic, hid_sum(): total = total + lax.ppermute(value, 'hid', pairs)  1.95 us
    ppermute x7, waiting for transfers between devices, hid_sum(): total = total + lax.ppermute(value, 'hid', pairs)  1.95 us
    reduce_sum x6, other arithmetic, body(): jnp.sum(back_f * mates[chunk][section].astype(jnp.float32), axis=-1)  1.64 us
    convert_element_type x2, other arithmetic, body(): normed = (resid * inv[:, None] * norm_gain).astype(jnp.bfloat16)  1.5 us
  transfers between devices with their start and end apart: 19, of which 13 were waited for; matrix products, arithmetic and copies ran while one was open for 11% of the time, Pallas kernels for 6%

profile of v11, /device:TPU:0, one launch (start us, length us, event | category | flops | bytes accessed | tf_op | source)
XLA Modules:
  0.0 70.5 jit_solution(13160427751710084424)
XLA Ops:
  0.7 1.2 %convolution_convert_fusion.1 = bf16[64,1024]{1,0:T(8,128)(2,1)S(1)} fusion(bf16[128,1024]{1,0:T(8,128)(2,1)} %param.9, bf16[1,128,128]{2,1,0:T(8,128)(2,1)} %param.11), kind=kOutput, calls=%fused_computation.4 | convolution fusion | flops 16842752 | bytes 409600 | tf_op jit(solution)/shard_map/kij,kjd->kid/dot_general | solution.py:92
  1.8 3.0 %collective-permute-start = (bf16[64,1024]{1,0:T(8,128)(2,1)S(1)}, bf16[64,1024]{1,0:T(8,128)(2,1)S(1)}, u32[]{:S(2)}, u32[]{:S(2)}) collective-permute-start(bf16[64,1024]{1,0:T(8,128)(2,1)S(1)} %convolution_convert_fusion.1), channel_id=1, source_target_pairs={{0,2},{2,0},{4,6},{6,4},{8,10},{10,8},{12,14},{14,12},{1,3},{3,1},... | collective-permute-start | bytes 393224 | tf_op jit(solution)/shard_map/ppermute | solution.py:14
  5.6 3.5 %collective-permute-done = bf16[64,1024]{1,0:T(8,128)(2,1)S(1)} collective-permute-done((bf16[64,1024]{1,0:T(8,128)(2,1)S(1)}, bf16[64,1024]{1,0:T(8,128)(2,1)S(1)}, u32[]{:S(2)}, u32[]{:S(2)}) %collective-permute-start) | collective-permute-done | bytes 131104 | tf_op jit(solution)/shard_map/ppermute | solution.py:14
  9.3 2.2 %collective-permute-start.1 = (bf16[64,1024]{1,0:T(8,128)(2,1)S(1)}, bf16[64,1024]{1,0:T(8,128)(2,1)S(1)}, u32[]{:S(2)}, u32[]{:S(2)}) collective-permute-start(bf16[64,1024]{1,0:T(8,128)(2,1)S(1)} %fusion.4), channel_id=1, source_target_pairs={{0,4},{2,6},{4,0},{6,2},{8,12},{10,14},{12,8},{14,10},{1,5},{3,7},... | collective-permute-start | bytes 393224 | tf_op jit(solution)/shard_map/ppermute | solution.py:14
  11.5 0.7 %fusion.66 = (bf16[64,1024]{1,0:T(8,128)(2,1)}, bf16[64,1024]{1,0:T(8,128)(2,1)}) fusion(bf16[128,1024]{1,0:T(8,128)(2,1)S(1)} %copy-done.3), kind=kLoop, calls=%fused_computation.132 | loop fusion | bytes 524288 | tf_op jit(solution)/shard_map/slice | solution.py:119
  12.2 2.2 %collective-permute-done.1 = bf16[64,1024]{1,0:T(8,128)(2,1)S(1)} collective-permute-done((bf16[64,1024]{1,0:T(8,128)(2,1)S(1)}, bf16[64,1024]{1,0:T(8,128)(2,1)S(1)}, u32[]{:S(2)}, u32[]{:S(2)}) %collective-permute-start.1) | collective-permute-done | bytes 131104 | tf_op jit(solution)/shard_map/ppermute | solution.py:14
  14.6 3.8 %collective-permute-start.2 = (bf16[64,1024]{1,0:T(8,128)(2,1)S(1)}, bf16[64,1024]{1,0:T(8,128)(2,1)S(1)}, u32[]{:S(2)}, u32[]{:S(2)}) collective-permute-start(bf16[64,1024]{1,0:T(8,128)(2,1)S(1)} %fusion.6), channel_id=1, source_target_pairs={{0,8},{2,10},{4,12},{6,14},{8,0},{10,2},{12,4},{14,6},{1,9},{3,11}... | collective-permute-start | bytes 393224 | tf_op jit(solution)/shard_map/ppermute | solution.py:14
  18.5 1.2 %collective-permute-start.6 = (bf16[64,1024]{1,0:T(8,128)(2,1)S(1)}, bf16[64,1024]{1,0:T(8,128)(2,1)S(1)}, u32[]{:S(2)}, u32[]{:S(2)}) collective-permute-start(bf16[64,1024]{1,0:T(8,128)(2,1)S(1)} %fusion.12), channel_id=1, source_target_pairs={{0,4},{2,6},{4,0},{6,2},{8,12},{10,14},{12,8},{14,10},{1,5},{3,7},... | collective-permute-start | bytes 393224 | tf_op jit(solution)/shard_map/ppermute | solution.py:14
  19.7 3.1 %collective-permute-done.2 = bf16[64,1024]{1,0:T(8,128)(2,1)S(1)} collective-permute-done((bf16[64,1024]{1,0:T(8,128)(2,1)S(1)}, bf16[64,1024]{1,0:T(8,128)(2,1)S(1)}, u32[]{:S(2)}, u32[]{:S(2)}) %collective-permute-start.2) | collective-permute-done | bytes 131104 | tf_op jit(solution)/shard_map/ppermute | solution.py:14
  23.1 1.0 %collective-permute-done.6 = bf16[64,1024]{1,0:T(8,128)(2,1)S(1)} collective-permute-done((bf16[64,1024]{1,0:T(8,128)(2,1)S(1)}, bf16[64,1024]{1,0:T(8,128)(2,1)S(1)}, u32[]{:S(2)}, u32[]{:S(2)}) %collective-permute-start.6) | collective-permute-done | bytes 131104 | tf_op jit(solution)/shard_map/ppermute | solution.py:14
  24.2 0.6 collective-permute-start.7
  24.9 0.8 %multiply_convert_fusion.1.normed_ref = bf16[64,1024]{1,0:T(8,128)(2,1)} fusion(bf16[64,1024]{1,0:T(8,128)(2,1)S(1)} %get-tuple-element.25, f32[1024]{0:T(1024)S(1)} %copy-done.4, f32[64]{0:T(128)S(1)} %add_rsqrt_fusion.1, bf16[128,1024]{1,0:T(8,128)(2,1)S(1)} %copy-done), kind=kLoop, calls=%fused_computation.101 | loop fusion | flops 458752 | bytes 397568 | tf_op jit(solution)/shard_map/convert_element_type | solution.py:125
  25.7 4.1 %shard_map.120 = f32[64,1024]{1,0:T(8,128)} custom-call(bf16[64,1024]{1,0:T(8,128)(2,1)} %multiply_convert_fusion.1.normed_ref, bf16[64,1024]{1,0:T(8,128)(2,1)} %get-tuple-element.29.cot_ref, bf16[8,128,512]{2,1,0:T(8,128)(2,1)} %wg_ref.3, bf16[8,128,512]{2,1,0:T(8,128)(2,1)} %wu_ref.3, bf16[8,512,128]{2,1,0:T(8,128)(2,1)} %wd_ref.3), custom_call_target="tpu_custom_call" | custom-call | flops 335544320 | bytes 3670016 | tf_op jit(solution)/shard_map/pallas_call | solution.py:44
  29.7 1.1 %multiply_reduce_fusion.2 = f32[64]{0:T(128)S(1)} fusion(f32[64,1024]{1,0:T(8,128)} %shard_map.120, bf16[64,1024]{1,0:T(8,128)(2,1)S(1)} %get-tuple-element.25, f32[1024]{0:T(1024)S(1)} %copy-done.4, bf16[128,1024]{1,0:T(8,128)(2,1)S(1)} %copy-done), kind=kLoop, calls=%fused_computation.100 | loop fusion | flops 458688 | bytes 528640 | tf_op jit(solution)/shard_map/reduce_sum | solution.py:128
  31.1 1.8 %collective-permute-done.7 = bf16[64,1024]{1,0:T(8,128)(2,1)S(1)} collective-permute-done((bf16[64,1024]{1,0:T(8,128)(2,1)S(1)}, bf16[64,1024]{1,0:T(8,128)(2,1)S(1)}, u32[]{:S(2)}, u32[]{:S(2)}) %collective-permute-start.7) | collective-permute-done | bytes 131104 | tf_op jit(solution)/shard_map/ppermute | solution.py:14
  33.7 1.1 %collective-permute-done.8 = f32[64]{0:T(128)S(1)} collective-permute-done((f32[64]{0:T(128)S(1)}, f32[64]{0:T(128)S(1)}, u32[]{:S(2)}, u32[]{:S(2)}) %collective-permute-start.8) | collective-permute-done | bytes 288 | tf_op jit(solution)/shard_map/ppermute | solution.py:69
  34.8 0.8 %multiply_convert_fusion.normed_ref = bf16[64,1024]{1,0:T(8,128)(2,1)} fusion(bf16[64,1024]{1,0:T(8,128)(2,1)S(1)} %fusion.16, f32[64]{0:T(128)S(1)} %add_rsqrt_fusion, f32[1024]{0:T(1024)S(1)} %copy-done.4, bf16[128,1024]{1,0:T(8,128)(2,1)S(1)} %copy-done), kind=kLoop, calls=%fused_computation.97 | loop fusion | flops 458752 | bytes 397568 | tf_op jit(solution)/shard_map/convert_element_type | solution.py:125
  35.6 4.1 %shard_map.121 = f32[64,1024]{1,0:T(8,128)} custom-call(bf16[64,1024]{1,0:T(8,128)(2,1)} %multiply_convert_fusion.normed_ref, bf16[64,1024]{1,0:T(8,128)(2,1)} %get-tuple-element.28.cot_ref, bf16[8,128,512]{2,1,0:T(8,128)(2,1)} %wg_ref.3, bf16[8,128,512]{2,1,0:T(8,128)(2,1)} %wu_ref.3, bf16[8,512,128]{2,1,0:T(8,128)(2,1)} %wd_ref.3), custom_call_target="tpu_custom_call" | custom-call | flops 335544320 | bytes 3670016 | tf_op jit(solution)/shard_map/pallas_call | solution.py:44
  39.6 1.2 %multiply_reduce_fusion = f32[64]{0:T(128)S(1)} fusion(f32[64,1024]{1,0:T(8,128)} %shard_map.121, bf16[64,1024]{1,0:T(8,128)(2,1)S(1)} %fusion.16, f32[1024]{0:T(1024)S(1)} %copy-done.4, bf16[128,1024]{1,0:T(8,128)(2,1)S(1)} %copy-done), kind=kLoop, calls=%fused_computation.96 | loop fusion | flops 458688 | bytes 528640 | tf_op jit(solution)/shard_map/reduce_sum | solution.py:128
  41.1 1.3 %collective-permute-start.10 = (bf16[64,1024]{1,0:T(8,128)(2,1)S(1)}, bf16[64,1024]{1,0:T(8,128)(2,1)S(1)}, u32[]{:S(2)}, u32[]{:S(2)}) collective-permute-start(bf16[64,1024]{1,0:T(8,128)(2,1)S(1)} %fusion.18), channel_id=1, source_target_pairs={{0,8},{2,10},{4,12},{6,14},{8,0},{10,2},{12,4},{14,6},{1,9},{3,11}... | collective-permute-start | bytes 393224 | tf_op jit(solution)/shard_map/ppermute | solution.py:14
  42.8 1.7 %collective-permute-start.13 = (bf16[64,1024]{1,0:T(8,128)(2,1)S(1)}, bf16[64,1024]{1,0:T(8,128)(2,1)S(1)}, u32[]{:S(2)}, u32[]{:S(2)}) collective-permute-start(bf16[64,1024]{1,0:T(8,128)(2,1)S(1)} %fusion.35), channel_id=1, source_target_pairs={{0,8},{2,10},{4,12},{6,14},{8,0},{10,2},{12,4},{14,6},{1,9},{3,11}... | collective-permute-start | bytes 393224 | tf_op jit(solution)/shard_map/ppermute | solution.py:14
  44.5 9.4 %collective-permute-done.10 = bf16[64,1024]{1,0:T(8,128)(2,1)S(1)} collective-permute-done((bf16[64,1024]{1,0:T(8,128)(2,1)S(1)}, bf16[64,1024]{1,0:T(8,128)(2,1)S(1)}, u32[]{:S(2)}, u32[]{:S(2)}) %collective-permute-start.10) | collective-permute-done | bytes 131104 | tf_op jit(solution)/shard_map/ppermute | solution.py:14
  54.4 1.8 %collective-permute-done.13 = bf16[64,1024]{1,0:T(8,128)(2,1)S(1)} collective-permute-done((bf16[64,1024]{1,0:T(8,128)(2,1)S(1)}, bf16[64,1024]{1,0:T(8,128)(2,1)S(1)}, u32[]{:S(2)}, u32[]{:S(2)}) %collective-permute-start.13) | collective-permute-done | bytes 131104 | tf_op jit(solution)/shard_map/ppermute | solution.py:14
  56.8 3.2 %collective-permute-done.11 = bf16[64,1024]{1,0:T(8,128)(2,1)S(1)} collective-permute-done((bf16[64,1024]{1,0:T(8,128)(2,1)S(1)}, bf16[64,1024]{1,0:T(8,128)(2,1)S(1)}, u32[]{:S(2)}, u32[]{:S(2)}) %collective-permute-start.11) | collective-permute-done | bytes 131104 | tf_op jit(solution)/shard_map/ppermute | solution.py:14
  60.4 1.6 %collective-permute-start.12 = (bf16[64,1024]{1,0:T(8,128)(2,1)S(1)}, bf16[64,1024]{1,0:T(8,128)(2,1)S(1)}, u32[]{:S(2)}, u32[]{:S(2)}) collective-permute-start(bf16[64,1024]{1,0:T(8,128)(2,1)S(1)} %fusion.30), channel_id=1, source_target_pairs={{0,2},{2,0},{4,6},{6,4},{8,10},{10,8},{12,14},{14,12},{1,3},{3,1},... | collective-permute-start | bytes 393224 | tf_op jit(solution)/shard_map/ppermute | solution.py:14
  62.5 1.6 %collective-permute-start.15 = (bf16[64,1024]{1,0:T(8,128)(2,1)S(1)}, bf16[64,1024]{1,0:T(8,128)(2,1)S(1)}, u32[]{:S(2)}, u32[]{:S(2)}) collective-permute-start(bf16[64,1024]{1,0:T(8,128)(2,1)S(1)} %fusion.45), channel_id=1, source_target_pairs={{0,2},{2,0},{4,6},{6,4},{8,10},{10,8},{12,14},{14,12},{1,3},{3,1},... | collective-permute-start | bytes 393224 | tf_op jit(solution)/shard_map/ppermute | solution.py:14
  64.8 0.6 collective-permute-done.17
  65.3 0.7 fusion.70
  66.0 0.7 fusion.71
  66.8 1.5 %collective-permute-done.15 = bf16[64,1024]{1,0:T(8,128)(2,1)S(1)} collective-permute-done((bf16[64,1024]{1,0:T(8,128)(2,1)S(1)}, bf16[64,1024]{1,0:T(8,128)(2,1)S(1)}, u32[]{:S(2)}, u32[]{:S(2)}) %collective-permute-start.15) | collective-permute-done | bytes 131104 | tf_op jit(solution)/shard_map/ppermute | solution.py:14
  68.7 1.0 %fusion.1 = bf16[128,1024]{1,0:T(8,128)(2,1)} fusion(f32[64,1024]{1,0:T(8,128)S(1)} %get-tuple-element.26, f32[64,1024]{1,0:T(8,128)S(1)} %get-tuple-element.27, bf16[64,1024]{1,0:T(8,128)(2,1)S(1)} %fusion.44, bf16[64,1024]{1,0:T(8,128)(2,1)S(1)} %fusion.29, bf16[1,128,128]{2,1,0:T(8,128)(2,1)S(1)} %copy-done.5), kind=kOutput, calls=%fused_computation.2 | convolution fusion | flops 34471936 | bytes 1081344 | tf_op jit(solution)/shard_map/kij,kid->kjd/dot_general | solution.py:166
  69.9 0.6 add.111
  (64 shorter events, 6.6 us)
Async XLA Ops:
  0.6 4.2 %copy-start.5 = (bf16[1,128,128]{2,1,0:T(8,128)(2,1)S(1)}, bf16[1,128,128]{2,1,0:T(8,128)(2,1)}, u32[]{:S(2)}) copy-start(bf16[1,128,128]{2,1,0:T(8,128)(2,1)} %param.11) | copy-start | bytes 98308
  0.6 4.2 %copy-start = (bf16[128,1024]{1,0:T(8,128)(2,1)S(1)}, bf16[128,1024]{1,0:T(8,128)(2,1)}, u32[]{:S(2)}) copy-start(bf16[128,1024]{1,0:T(8,128)(2,1)} %param.9) | copy-start | bytes 786436
  1.8 7.3 %collective-permute-start = (bf16[64,1024]{1,0:T(8,128)(2,1)S(1)}, bf16[64,1024]{1,0:T(8,128)(2,1)S(1)}, u32[]{:S(2)}, u32[]{:S(2)}) collective-permute-start(bf16[64,1024]{1,0:T(8,128)(2,1)S(1)} %convolution_convert_fusion.1), channel_id=1, source_target_pairs={{0,2},{2,0},{4,6},{6,4},{8,10},{10,8},{12,14},{14,12},{1,3},{3,1},... | collective-permute-start | bytes 393224 | tf_op jit(solution)/shard_map/ppermute | solution.py:14
  4.9 0.7 copy-start.6
  4.9 0.7 copy-start.7
  5.0 6.5 %copy-start.3 = (bf16[128,1024]{1,0:T(8,128)(2,1)S(1)}, bf16[128,1024]{1,0:T(8,128)(2,1)}, u32[]{:S(2)}) copy-start(bf16[128,1024]{1,0:T(8,128)(2,1)} %param.10) | copy-start | bytes 786436
  5.1 13.3 %collective-permute-start.5 = (bf16[64,1024]{1,0:T(8,128)(2,1)S(1)}, bf16[64,1024]{1,0:T(8,128)(2,1)S(1)}, u32[]{:S(2)}, u32[]{:S(2)}) collective-permute-start(bf16[64,1024]{1,0:T(8,128)(2,1)S(1)} %convolution_convert_fusion), channel_id=1, source_target_pairs={{0,2},{2,0},{4,6},{6,4},{8,10},{10,8},{12,14},{14,12},{1,3},{3,1},... | collective-permute-start | bytes 393224 | tf_op jit(solution)/shard_map/ppermute | solution.py:14
  9.3 5.2 %collective-permute-start.1 = (bf16[64,1024]{1,0:T(8,128)(2,1)S(1)}, bf16[64,1024]{1,0:T(8,128)(2,1)S(1)}, u32[]{:S(2)}, u32[]{:S(2)}) collective-permute-start(bf16[64,1024]{1,0:T(8,128)(2,1)S(1)} %fusion.4), channel_id=1, source_target_pairs={{0,4},{2,6},{4,0},{6,2},{8,12},{10,14},{12,8},{14,10},{1,5},{3,7},... | collective-permute-start | bytes 393224 | tf_op jit(solution)/shard_map/ppermute | solution.py:14
  14.6 8.2 %collective-permute-start.2 = (bf16[64,1024]{1,0:T(8,128)(2,1)S(1)}, bf16[64,1024]{1,0:T(8,128)(2,1)S(1)}, u32[]{:S(2)}, u32[]{:S(2)}) collective-permute-start(bf16[64,1024]{1,0:T(8,128)(2,1)S(1)} %fusion.6), channel_id=1, source_target_pairs={{0,8},{2,10},{4,12},{6,14},{8,0},{10,2},{12,4},{14,6},{1,9},{3,11}... | collective-permute-start | bytes 393224 | tf_op jit(solution)/shard_map/ppermute | solution.py:14
  18.5 5.6 %collective-permute-start.6 = (bf16[64,1024]{1,0:T(8,128)(2,1)S(1)}, bf16[64,1024]{1,0:T(8,128)(2,1)S(1)}, u32[]{:S(2)}, u32[]{:S(2)}) collective-permute-start(bf16[64,1024]{1,0:T(8,128)(2,1)S(1)} %fusion.12), channel_id=1, source_target_pairs={{0,4},{2,6},{4,0},{6,2},{8,12},{10,14},{12,8},{14,10},{1,5},{3,7},... | collective-permute-start | bytes 393224 | tf_op jit(solution)/shard_map/ppermute | solution.py:14
  23.1 1.8 %collective-permute-start.3 = (f32[64]{0:T(128)S(1)}, f32[64]{0:T(128)S(1)}, u32[]{:S(2)}, u32[]{:S(2)}) collective-permute-start(f32[64]{0:T(128)S(1)} %get-tuple-element.24), channel_id=1, source_target_pairs={{0,1},{1,0},{2,3},{3,2},{4,5},{5,4},{6,7},{7,6},{8,9},{9,8},{10,11... | collective-permute-start | bytes 776 | tf_op jit(solution)/shard_map/ppermute | solution.py:69
  24.1 0.8 %copy-start.4 = (f32[1024]{0:T(1024)S(1)}, f32[1024]{0:T(1024)}, u32[]{:S(2)}) copy-start(f32[1024]{0:T(1024)} %param.14) | copy-start | bytes 12292
  24.2 8.7 %collective-permute-start.7 = (bf16[64,1024]{1,0:T(8,128)(2,1)S(1)}, bf16[64,1024]{1,0:T(8,128)(2,1)S(1)}, u32[]{:S(2)}, u32[]{:S(2)}) collective-permute-start(bf16[64,1024]{1,0:T(8,128)(2,1)S(1)} %fusion.14), channel_id=1, source_target_pairs={{0,8},{2,10},{4,12},{6,14},{8,0},{10,2},{12,4},{14,6},{1,9},{3,11}... | collective-permute-start | bytes 393224 | tf_op jit(solution)/shard_map/ppermute | solution.py:14
  30.8 2.2 %copy-start.1 = (f32[64,1024]{1,0:T(8,128)S(1)}, f32[64,1024]{1,0:T(8,128)}, u32[]{:S(2)}) copy-start(f32[64,1024]{1,0:T(8,128)} %shard_map.120) | copy-start | bytes 786436
  30.8 2.2 %collective-permute-start.4 = (f32[64]{0:T(128)S(1)}, f32[64]{0:T(128)S(1)}, u32[]{:S(2)}, u32[]{:S(2)}) collective-permute-start(f32[64]{0:T(128)S(1)} %multiply_reduce_fusion.2), channel_id=1, source_target_pairs={{0,1},{1,0},{2,3},{3,2},{4,5},{5,4},{6,7},{7,6},{8,9},{9,8},{10,11... | collective-permute-start | bytes 776 | tf_op jit(solution)/shard_map/ppermute | solution.py:69
  33.6 1.2 %collective-permute-start.8 = (f32[64]{0:T(128)S(1)}, f32[64]{0:T(128)S(1)}, u32[]{:S(2)}, u32[]{:S(2)}) collective-permute-start(f32[64]{0:T(128)S(1)} %multiply_reduce_fusion.1), channel_id=1, source_target_pairs={{0,1},{1,0},{2,3},{3,2},{4,5},{5,4},{6,7},{7,6},{8,9},{9,8},{10,11... | collective-permute-start | bytes 776 | tf_op jit(solution)/shard_map/ppermute | solution.py:69
  39.6 2.8 %copy-start.2 = (f32[64,1024]{1,0:T(8,128)S(1)}, f32[64,1024]{1,0:T(8,128)}, u32[]{:S(2)}) copy-start(f32[64,1024]{1,0:T(8,128)} %shard_map.121) | copy-start | bytes 786436
  40.8 1.6 %collective-permute-start.9 = (f32[64]{0:T(128)S(1)}, f32[64]{0:T(128)S(1)}, u32[]{:S(2)}, u32[]{:S(2)}) collective-permute-start(f32[64]{0:T(128)S(1)} %multiply_reduce_fusion), channel_id=1, source_target_pairs={{0,1},{1,0},{2,3},{3,2},{4,5},{5,4},{6,7},{7,6},{8,9},{9,8},{10,11... | collective-permute-start | bytes 776 | tf_op jit(solution)/shard_map/ppermute | solution.py:69
  41.1 12.8 %collective-permute-start.10 = (bf16[64,1024]{1,0:T(8,128)(2,1)S(1)}, bf16[64,1024]{1,0:T(8,128)(2,1)S(1)}, u32[]{:S(2)}, u32[]{:S(2)}) collective-permute-start(bf16[64,1024]{1,0:T(8,128)(2,1)S(1)} %fusion.18), channel_id=1, source_target_pairs={{0,8},{2,10},{4,12},{6,14},{8,0},{10,2},{12,4},{14,6},{1,9},{3,11}... | collective-permute-start | bytes 393224 | tf_op jit(solution)/shard_map/ppermute | solution.py:14
  42.8 13.3 %collective-permute-start.13 = (bf16[64,1024]{1,0:T(8,128)(2,1)S(1)}, bf16[64,1024]{1,0:T(8,128)(2,1)S(1)}, u32[]{:S(2)}, u32[]{:S(2)}) collective-permute-start(bf16[64,1024]{1,0:T(8,128)(2,1)S(1)} %fusion.35), channel_id=1, source_target_pairs={{0,8},{2,10},{4,12},{6,14},{8,0},{10,2},{12,4},{14,6},{1,9},{3,11}... | collective-permute-start | bytes 393224 | tf_op jit(solution)/shard_map/ppermute | solution.py:14
  54.3 5.8 %collective-permute-start.11 = (bf16[64,1024]{1,0:T(8,128)(2,1)S(1)}, bf16[64,1024]{1,0:T(8,128)(2,1)S(1)}, u32[]{:S(2)}, u32[]{:S(2)}) collective-permute-start(bf16[64,1024]{1,0:T(8,128)(2,1)S(1)} %fusion.25), channel_id=1, source_target_pairs={{0,4},{2,6},{4,0},{6,2},{8,12},{10,14},{12,8},{14,10},{1,5},{3,7},... | collective-permute-start | bytes 393224 | tf_op jit(solution)/shard_map/ppermute | solution.py:14
  56.5 5.6 %collective-permute-start.14 = (bf16[64,1024]{1,0:T(8,128)(2,1)S(1)}, bf16[64,1024]{1,0:T(8,128)(2,1)S(1)}, u32[]{:S(2)}, u32[]{:S(2)}) collective-permute-start(bf16[64,1024]{1,0:T(8,128)(2,1)S(1)} %fusion.40), channel_id=1, source_target_pairs={{0,4},{2,6},{4,0},{6,2},{8,12},{10,14},{12,8},{14,10},{1,5},{3,7},... | collective-permute-start | bytes 393224 | tf_op jit(solution)/shard_map/ppermute | solution.py:14
  60.4 6.3 %collective-permute-start.12 = (bf16[64,1024]{1,0:T(8,128)(2,1)S(1)}, bf16[64,1024]{1,0:T(8,128)(2,1)S(1)}, u32[]{:S(2)}, u32[]{:S(2)}) collective-permute-start(bf16[64,1024]{1,0:T(8,128)(2,1)S(1)} %fusion.30), channel_id=1, source_target_pairs={{0,2},{2,0},{4,6},{6,4},{8,10},{10,8},{12,14},{14,12},{1,3},{3,1},... | collective-permute-start | bytes 393224 | tf_op jit(solution)/shard_map/ppermute | solution.py:14
  62.5 5.8 %collective-permute-start.15 = (bf16[64,1024]{1,0:T(8,128)(2,1)S(1)}, bf16[64,1024]{1,0:T(8,128)(2,1)S(1)}, u32[]{:S(2)}, u32[]{:S(2)}) collective-permute-start(bf16[64,1024]{1,0:T(8,128)(2,1)S(1)} %fusion.45), channel_id=1, source_target_pairs={{0,2},{2,0},{4,6},{6,4},{8,10},{10,8},{12,14},{14,12},{1,3},{3,1},... | collective-permute-start | bytes 393224 | tf_op jit(solution)/shard_map/ppermute | solution.py:14
  64.2 1.2 %collective-permute-start.17 = (f32[3,128]{1,0:T(4,128)S(1)}, f32[3,128]{1,0:T(4,128)S(1)}, u32[]{:S(2)}, u32[]{:S(2)}) collective-permute-start(f32[3,128]{1,0:T(4,128)S(1)} %maximum_maximum_fusion.1), channel_id=1, source_target_pairs={{0,1},{1,0},{2,3},{3,2},{4,5},{5,4},{6,7},{7,6},{8,9},{9,8},{10,11... | collective-permute-start | bytes 4616 | tf_op jit(solution)/shard_map/ppermute | solution.py:69
  64.3 1.7 %collective-permute-start.16 = (f32[3,128]{1,0:T(4,128)S(1)}, f32[3,128]{1,0:T(4,128)S(1)}, u32[]{:S(2)}, u32[]{:S(2)}) collective-permute-start(f32[3,128]{1,0:T(4,128)S(1)} %maximum_maximum_fusion), channel_id=1, source_target_pairs={{0,1},{1,0},{2,3},{3,2},{4,5},{5,4},{6,7},{7,6},{8,9},{9,8},{10,11... | collective-permute-start | bytes 4616 | tf_op jit(solution)/shard_map/ppermute | solution.py:69
  68.6 1.3 %collective-permute-start.18 = (f32[1,128,128]{2,1,0:T(8,128)S(1)}, f32[1,128,128]{2,1,0:T(8,128)S(1)}, u32[]{:S(2)}, u32[]{:S(2)}) collective-permute-start(f32[1,128,128]{2,1,0:T(8,128)S(1)} %convolution_bitcast_fusion.1), channel_id=1, source_target_pairs={{0,1},{1,0},{2,3},{3,2},{4,5},{5,4},{6,7},{7,6},{8,9},{9,8},{10,11... | collective-permute-start | bytes 196616 | tf_op jit(solution)/shard_map/ppermute | solution.py:69

commit v12 on v11

--- a/solution.py
+++ b/solution.py
@@ -120,12 +120,13 @@
         tok_f = tokens[rs].astype(jnp.float32)
         mixed_f = mixed.astype(jnp.float32)
         resid = tok_f + tok_f * mixed_f
-        square = hid_sum(jnp.sum(resid * resid, axis=-1))
+        reduce_hid = hid_sum if chunk == 0 else (lambda v: lax.psum(v, "hid"))
+        square = reduce_hid(jnp.sum(resid * resid, axis=-1))
         inv = lax.rsqrt(square / D + 1e-06)
         normed = (resid * inv[:, None] * norm_gain).astype(jnp.bfloat16)
         d_normed = ffn_grad(normed, cot, w_gate, w_up, w_down)
         scaled = norm_gain * d_normed
-        inner = hid_sum(jnp.sum(resid * scaled, axis=-1))
+        inner = reduce_hid(jnp.sum(resid * scaled, axis=-1))
         d_resid = (
             cot.astype(jnp.float32)
             + inv[:, None] * scaled
@@ -135,7 +136,7 @@
         sent = (coef_cross[top, rs][:, None] * d_mixed.astype(jnp.float32)).astype(jnp.bfloat16)
         previous = sent
         backs.append(d_mixed)
-        sents.append(sent)
+        sents.append(from_partner(sent, "seq", top))
         directs.append(d_resid * (1.0 + mixed_f))
     grads_self = [[None] * sections for _ in spans]
     grads_cross = [[None] * sections for _ in spans]
@@ -149,10 +150,10 @@
                 back_f * mates[chunk][section].astype(jnp.float32), axis=-1
             )
             if section == top:
-                sent = sents[chunk]
+                received = sents[chunk]
             else:
                 sent = (coef_cross[section, rs][:, None] * back_f).astype(jnp.bfloat16)
-            received = from_partner(sent, "seq", section)
+                received = from_partner(sent, "seq", section)
             backs[chunk] = (
                 coef_self[section, rs][:, None] * back_f + received.astype(jnp.float32)
             ).astype(jnp.bfloat16)

time: 70.8 us -> 69.1 us (0.976)
  waiting for transfers between devices: 29.7 us -> 22 us
  blocking collectives: 0 us -> 4.93 us
  starting transfers between devices: 18.8 us -> 19.8 us
    ppermute x12, waiting for transfers between devices: 27.7 us -> 21.2 us  [from_partner(): return lax.ppermute(value, axis, pairs)]
    psum x0 -> x2, blocking collectives: none -> 4.93 us  [body(): reduce_hid = hid_sum if chunk == 0 else lambda v: lax.psum(v, 'hid')]
    ppermute x12, starting transfers between devices: 17.6 us -> 18.9 us  [from_partner(): return lax.ppermute(value, axis, pairs)]
    ppermute x7 -> x5, waiting for transfers between devices: 1.95 us -> 0.84 us  [hid_sum(): total = total + lax.ppermute(value, 'hid', pairs)]
  transfers between devices with their start and end apart: 19 -> 17, of which waited for: 13 -> 10; matrix products, arithmetic and copies ran while one was open for 11% -> 15% of each run, Pallas kernels for 6% -> 12%
where the time goes in v12:
time: 69.1 us; the launch traced here: 68.8 us
  waiting for transfers between devices  22 us (32%)
  starting transfers between devices  19.8 us (29%)
  other arithmetic  9.31 us (13%)
  Pallas kernels  8.11 us (12%)
  blocking collectives  4.93 us (7%)
  matrix products  2.57 us (4%)
  local copies, waits for them, and re-layouts  1.2 us (2%)
  between operations  0.88 us (1%)
    ppermute x12, waiting for transfers between devices, from_partner(): return lax.ppermute(value, axis, pairs)  21.2 us
    ppermute x12, starting transfers between devices, from_partner(): return lax.ppermute(value, axis, pairs)  18.9 us
    pallas_call x2, Pallas kernels, ffn_grad(): pl.pallas_call(ffn_kernel, grid=(groups_here // per_step,), in_specs=[act...  8.11 us
    psum x2, blocking collectives, body(): reduce_hid = hid_sum if chunk == 0 else lambda v: lax.psum(v, 'hid')  4.93 us
    reduce_sum x2, other arithmetic, body(): inner = reduce_hid(jnp.sum(resid * scaled, axis=-1))  2.29 us
    add x3, other arithmetic, hid_sum(): total = total + lax.ppermute(value, 'hid', pairs)  1.95 us
    reduce_sum x6, other arithmetic, body(): jnp.sum(back_f * mates[chunk][section].astype(jnp.float32), axis=-1)  1.65 us
    convert_element_type x2, other arithmetic, body(): normed = (resid * inv[:, None] * norm_gain).astype(jnp.bfloat16)  1.5 us
  transfers between devices with their start and end apart: 17, of which 10 were waited for; matrix products, arithmetic and copies ran while one was open for 15% of the time, Pallas kernels for 12%

profile of v12, /device:TPU:0, one launch (start us, length us, event | category | flops | bytes accessed | tf_op | source)
XLA Modules:
  0.0 68.8 jit_solution(17752345775684800718)
XLA Ops:
  0.7 1.2 %convolution_convert_fusion.1 = bf16[64,1024]{1,0:T(8,128)(2,1)S(1)} fusion(bf16[128,1024]{1,0:T(8,128)(2,1)} %param.9, bf16[1,128,128]{2,1,0:T(8,128)(2,1)} %param.11), kind=kOutput, calls=%fused_computation.4 | convolution fusion | flops 16842752 | bytes 409600 | tf_op jit(solution)/shard_map/kij,kjd->kid/dot_general | solution.py:92
  1.8 3.0 %collective-permute-start = (bf16[64,1024]{1,0:T(8,128)(2,1)S(1)}, bf16[64,1024]{1,0:T(8,128)(2,1)S(1)}, u32[]{:S(2)}, u32[]{:S(2)}) collective-permute-start(bf16[64,1024]{1,0:T(8,128)(2,1)S(1)} %convolution_convert_fusion.1), channel_id=1, source_target_pairs={{0,2},{2,0},{4,6},{6,4},{8,10},{10,8},{12,14},{14,12},{1,3},{3,1},... | collective-permute-start | bytes 393224 | tf_op jit(solution)/shard_map/ppermute | solution.py:14
  5.6 3.5 %collective-permute-done = bf16[64,1024]{1,0:T(8,128)(2,1)S(1)} collective-permute-done((bf16[64,1024]{1,0:T(8,128)(2,1)S(1)}, bf16[64,1024]{1,0:T(8,128)(2,1)S(1)}, u32[]{:S(2)}, u32[]{:S(2)}) %collective-permute-start) | collective-permute-done | bytes 131104 | tf_op jit(solution)/shard_map/ppermute | solution.py:14
  9.3 2.2 %collective-permute-start.1 = (bf16[64,1024]{1,0:T(8,128)(2,1)S(1)}, bf16[64,1024]{1,0:T(8,128)(2,1)S(1)}, u32[]{:S(2)}, u32[]{:S(2)}) collective-permute-start(bf16[64,1024]{1,0:T(8,128)(2,1)S(1)} %fusion.4), channel_id=1, source_target_pairs={{0,4},{2,6},{4,0},{6,2},{8,12},{10,14},{12,8},{14,10},{1,5},{3,7},... | collective-permute-start | bytes 393224 | tf_op jit(solution)/shard_map/ppermute | solution.py:14
  11.5 0.7 %fusion.66 = (bf16[64,1024]{1,0:T(8,128)(2,1)}, bf16[64,1024]{1,0:T(8,128)(2,1)}) fusion(bf16[128,1024]{1,0:T(8,128)(2,1)S(1)} %copy-done.3), kind=kLoop, calls=%fused_computation.132 | loop fusion | bytes 524288 | tf_op jit(solution)/shard_map/slice | solution.py:119
  12.2 2.2 %collective-permute-done.1 = bf16[64,1024]{1,0:T(8,128)(2,1)S(1)} collective-permute-done((bf16[64,1024]{1,0:T(8,128)(2,1)S(1)}, bf16[64,1024]{1,0:T(8,128)(2,1)S(1)}, u32[]{:S(2)}, u32[]{:S(2)}) %collective-permute-start.1) | collective-permute-done | bytes 131104 | tf_op jit(solution)/shard_map/ppermute | solution.py:14
  14.6 3.8 %collective-permute-start.2 = (bf16[64,1024]{1,0:T(8,128)(2,1)S(1)}, bf16[64,1024]{1,0:T(8,128)(2,1)S(1)}, u32[]{:S(2)}, u32[]{:S(2)}) collective-permute-start(bf16[64,1024]{1,0:T(8,128)(2,1)S(1)} %fusion.6), channel_id=1, source_target_pairs={{0,8},{2,10},{4,12},{6,14},{8,0},{10,2},{12,4},{14,6},{1,9},{3,11}... | collective-permute-start | bytes 393224 | tf_op jit(solution)/shard_map/ppermute | solution.py:14
  18.5 1.2 %collective-permute-start.6 = (bf16[64,1024]{1,0:T(8,128)(2,1)S(1)}, bf16[64,1024]{1,0:T(8,128)(2,1)S(1)}, u32[]{:S(2)}, u32[]{:S(2)}) collective-permute-start(bf16[64,1024]{1,0:T(8,128)(2,1)S(1)} %fusion.12), channel_id=1, source_target_pairs={{0,4},{2,6},{4,0},{6,2},{8,12},{10,14},{12,8},{14,10},{1,5},{3,7},... | collective-permute-start | bytes 393224 | tf_op jit(solution)/shard_map/ppermute | solution.py:14
  19.7 3.1 %collective-permute-done.2 = bf16[64,1024]{1,0:T(8,128)(2,1)S(1)} collective-permute-done((bf16[64,1024]{1,0:T(8,128)(2,1)S(1)}, bf16[64,1024]{1,0:T(8,128)(2,1)S(1)}, u32[]{:S(2)}, u32[]{:S(2)}) %collective-permute-start.2) | collective-permute-done | bytes 131104 | tf_op jit(solution)/shard_map/ppermute | solution.py:14
  23.1 1.0 %collective-permute-done.6 = bf16[64,1024]{1,0:T(8,128)(2,1)S(1)} collective-permute-done((bf16[64,1024]{1,0:T(8,128)(2,1)S(1)}, bf16[64,1024]{1,0:T(8,128)(2,1)S(1)}, u32[]{:S(2)}, u32[]{:S(2)}) %collective-permute-start.6) | collective-permute-done | bytes 131104 | tf_op jit(solution)/shard_map/ppermute | solution.py:14
  24.3 0.6 collective-permute-start.7
  24.9 0.8 %multiply_convert_fusion.1.normed_ref = bf16[64,1024]{1,0:T(8,128)(2,1)} fusion(bf16[64,1024]{1,0:T(8,128)(2,1)S(1)} %get-tuple-element.25, f32[1024]{0:T(1024)S(1)} %copy-done.4, f32[64]{0:T(128)S(1)} %add_rsqrt_fusion.1, bf16[128,1024]{1,0:T(8,128)(2,1)S(1)} %copy-done), kind=kLoop, calls=%fused_computation.101 | loop fusion | flops 458752 | bytes 397568 | tf_op jit(solution)/shard_map/convert_element_type | solution.py:126
  25.7 4.1 %shard_map.120 = f32[64,1024]{1,0:T(8,128)} custom-call(bf16[64,1024]{1,0:T(8,128)(2,1)} %multiply_convert_fusion.1.normed_ref, bf16[64,1024]{1,0:T(8,128)(2,1)} %get-tuple-element.29.cot_ref, bf16[8,128,512]{2,1,0:T(8,128)(2,1)} %wg_ref.3, bf16[8,128,512]{2,1,0:T(8,128)(2,1)} %wu_ref.3, bf16[8,512,128]{2,1,0:T(8,128)(2,1)} %wd_ref.3), custom_call_target="tpu_custom_call" | custom-call | flops 335544320 | bytes 3670016 | tf_op jit(solution)/shard_map/pallas_call | solution.py:44
  29.7 1.1 %multiply_reduce_fusion.2 = f32[64]{0:T(128)S(1)} fusion(f32[64,1024]{1,0:T(8,128)} %shard_map.120, bf16[64,1024]{1,0:T(8,128)(2,1)S(1)} %get-tuple-element.25, f32[1024]{0:T(1024)S(1)} %copy-done.4, bf16[128,1024]{1,0:T(8,128)(2,1)S(1)} %copy-done), kind=kLoop, calls=%fused_computation.100 | loop fusion | flops 458688 | bytes 528640 | tf_op jit(solution)/shard_map/reduce_sum | solution.py:129
  31.1 1.8 %collective-permute-done.7 = bf16[64,1024]{1,0:T(8,128)(2,1)S(1)} collective-permute-done((bf16[64,1024]{1,0:T(8,128)(2,1)S(1)}, bf16[64,1024]{1,0:T(8,128)(2,1)S(1)}, u32[]{:S(2)}, u32[]{:S(2)}) %collective-permute-start.7) | collective-permute-done | bytes 131104 | tf_op jit(solution)/shard_map/ppermute | solution.py:14
  33.5 1.4 %collective-permute-start.8 = (bf16[64,1024]{1,0:T(8,128)(2,1)S(1)}, bf16[64,1024]{1,0:T(8,128)(2,1)S(1)}, u32[]{:S(2)}, u32[]{:S(2)}) collective-permute-start(bf16[64,1024]{1,0:T(8,128)(2,1)S(1)} %fusion.18), channel_id=1, source_target_pairs={{0,8},{2,10},{4,12},{6,14},{8,0},{10,2},{12,4},{14,6},{1,9},{3,11}... | collective-permute-start | bytes 393224 | tf_op jit(solution)/shard_map/ppermute | solution.py:14
  35.0 2.5 %psum.14 = f32[64]{0:T(128)S(1)} all-reduce(f32[64]{0:T(128)S(1)} %multiply_reduce_fusion.1), channel_id=1, replica_groups=mesh['groups'=2,'seq'=8,'hid'=2] {'hid'}, use_global_device_ids=true, to_apply=%region_3.0 | all-reduce | flops 64 | bytes 512 | tf_op jit(solution)/shard_map/psum | solution.py:123
  37.5 0.8 %multiply_convert_fusion.normed_ref = bf16[64,1024]{1,0:T(8,128)(2,1)} fusion(bf16[64,1024]{1,0:T(8,128)(2,1)S(1)} %fusion.16, f32[64]{0:T(128)S(1)} %add_rsqrt_fusion, f32[1024]{0:T(1024)S(1)} %copy-done.4, bf16[128,1024]{1,0:T(8,128)(2,1)S(1)} %copy-done), kind=kLoop, calls=%fused_computation.97 | loop fusion | flops 458752 | bytes 397568 | tf_op jit(solution)/shard_map/convert_element_type | solution.py:126
  38.2 4.1 %shard_map.121 = f32[64,1024]{1,0:T(8,128)} custom-call(bf16[64,1024]{1,0:T(8,128)(2,1)} %multiply_convert_fusion.normed_ref, bf16[64,1024]{1,0:T(8,128)(2,1)} %get-tuple-element.28.cot_ref, bf16[8,128,512]{2,1,0:T(8,128)(2,1)} %wg_ref.3, bf16[8,128,512]{2,1,0:T(8,128)(2,1)} %wu_ref.3, bf16[8,512,128]{2,1,0:T(8,128)(2,1)} %wd_ref.3), custom_call_target="tpu_custom_call" | custom-call | flops 335544320 | bytes 3670016 | tf_op jit(solution)/shard_map/pallas_call | solution.py:44
  42.3 1.2 %multiply_reduce_fusion = f32[64]{0:T(128)S(1)} fusion(f32[64,1024]{1,0:T(8,128)} %shard_map.121, bf16[64,1024]{1,0:T(8,128)(2,1)S(1)} %fusion.16, f32[1024]{0:T(1024)S(1)} %copy-done.4, bf16[128,1024]{1,0:T(8,128)(2,1)S(1)} %copy-done), kind=kLoop, calls=%fused_computation.96 | loop fusion | flops 458688 | bytes 528640 | tf_op jit(solution)/shard_map/reduce_sum | solution.py:129
  43.5 2.5 %psum.15 = f32[64]{0:T(128)S(1)} all-reduce(f32[64]{0:T(128)S(1)} %multiply_reduce_fusion), channel_id=1, replica_groups=mesh['groups'=2,'seq'=8,'hid'=2] {'hid'}, use_global_device_ids=true, to_apply=%region_5.0 | all-reduce | flops 64 | bytes 512 | tf_op jit(solution)/shard_map/psum | solution.py:123
  46.4 1.7 %collective-permute-start.11 = (bf16[64,1024]{1,0:T(8,128)(2,1)S(1)}, bf16[64,1024]{1,0:T(8,128)(2,1)S(1)}, u32[]{:S(2)}, u32[]{:S(2)}) collective-permute-start(bf16[64,1024]{1,0:T(8,128)(2,1)S(1)} %fusion.35), channel_id=1, source_target_pairs={{0,8},{2,10},{4,12},{6,14},{8,0},{10,2},{12,4},{14,6},{1,9},{3,11}... | collective-permute-start | bytes 393224 | tf_op jit(solution)/shard_map/ppermute | solution.py:14
  48.4 1.5 %collective-permute-start.9 = (bf16[64,1024]{1,0:T(8,128)(2,1)S(1)}, bf16[64,1024]{1,0:T(8,128)(2,1)S(1)}, u32[]{:S(2)}, u32[]{:S(2)}) collective-permute-start(bf16[64,1024]{1,0:T(8,128)(2,1)S(1)} %fusion.25), channel_id=1, source_target_pairs={{0,4},{2,6},{4,0},{6,2},{8,12},{10,14},{12,8},{14,10},{1,5},{3,7},... | collective-permute-start | bytes 393224 | tf_op jit(solution)/shard_map/ppermute | solution.py:14
  49.9 5.8 %collective-permute-done.11 = bf16[64,1024]{1,0:T(8,128)(2,1)S(1)} collective-permute-done((bf16[64,1024]{1,0:T(8,128)(2,1)S(1)}, bf16[64,1024]{1,0:T(8,128)(2,1)S(1)}, u32[]{:S(2)}, u32[]{:S(2)}) %collective-permute-start.11) | collective-permute-done | bytes 131104 | tf_op jit(solution)/shard_map/ppermute | solution.py:14
  56.5 1.6 %collective-permute-start.10 = (bf16[64,1024]{1,0:T(8,128)(2,1)S(1)}, bf16[64,1024]{1,0:T(8,128)(2,1)S(1)}, u32[]{:S(2)}, u32[]{:S(2)}) collective-permute-start(bf16[64,1024]{1,0:T(8,128)(2,1)S(1)} %fusion.30), channel_id=1, source_target_pairs={{0,2},{2,0},{4,6},{6,4},{8,10},{10,8},{12,14},{14,12},{1,3},{3,1},... | collective-permute-start | bytes 393224 | tf_op jit(solution)/shard_map/ppermute | solution.py:14
  58.1 3.0 %collective-permute-done.12 = bf16[64,1024]{1,0:T(8,128)(2,1)S(1)} collective-permute-done((bf16[64,1024]{1,0:T(8,128)(2,1)S(1)}, bf16[64,1024]{1,0:T(8,128)(2,1)S(1)}, u32[]{:S(2)}, u32[]{:S(2)}) %collective-permute-start.12) | collective-permute-done | bytes 131104 | tf_op jit(solution)/shard_map/ppermute | solution.py:14
  61.5 1.6 %collective-permute-start.13 = (bf16[64,1024]{1,0:T(8,128)(2,1)S(1)}, bf16[64,1024]{1,0:T(8,128)(2,1)S(1)}, u32[]{:S(2)}, u32[]{:S(2)}) collective-permute-start(bf16[64,1024]{1,0:T(8,128)(2,1)S(1)} %fusion.45), channel_id=1, source_target_pairs={{0,2},{2,0},{4,6},{6,4},{8,10},{10,8},{12,14},{14,12},{1,3},{3,1},... | collective-permute-start | bytes 393224 | tf_op jit(solution)/shard_map/ppermute | solution.py:14
  64.3 0.7 fusion.70
  65.0 0.7 fusion.71
  65.7 0.7 %collective-permute-done.13 = bf16[64,1024]{1,0:T(8,128)(2,1)S(1)} collective-permute-done((bf16[64,1024]{1,0:T(8,128)(2,1)S(1)}, bf16[64,1024]{1,0:T(8,128)(2,1)S(1)}, u32[]{:S(2)}, u32[]{:S(2)}) %collective-permute-start.13) | collective-permute-done | bytes 131104 | tf_op jit(solution)/shard_map/ppermute | solution.py:14
  66.9 1.0 %fusion.1 = bf16[128,1024]{1,0:T(8,128)(2,1)} fusion(f32[64,1024]{1,0:T(8,128)S(1)} %get-tuple-element.26, f32[64,1024]{1,0:T(8,128)S(1)} %get-tuple-element.27, bf16[64,1024]{1,0:T(8,128)(2,1)S(1)} %fusion.44, bf16[64,1024]{1,0:T(8,128)(2,1)S(1)} %fusion.29, bf16[1,128,128]{2,1,0:T(8,128)(2,1)S(1)} %copy-done.5), kind=kOutput, calls=%fused_computation.2 | convolution fusion | flops 34471936 | bytes 1081344 | tf_op jit(solution)/shard_map/kij,kid->kjd/dot_general | solution.py:167
  68.2 0.6 add.107
  (62 shorter events, 6.4 us)
Async XLA Ops:
  0.6 4.2 %copy-start.5 = (bf16[1,128,128]{2,1,0:T(8,128)(2,1)S(1)}, bf16[1,128,128]{2,1,0:T(8,128)(2,1)}, u32[]{:S(2)}) copy-start(bf16[1,128,128]{2,1,0:T(8,128)(2,1)} %param.11) | copy-start | bytes 98308
  0.6 4.2 %copy-start = (bf16[128,1024]{1,0:T(8,128)(2,1)S(1)}, bf16[128,1024]{1,0:T(8,128)(2,1)}, u32[]{:S(2)}) copy-start(bf16[128,1024]{1,0:T(8,128)(2,1)} %param.9) | copy-start | bytes 786436
  1.8 7.3 %collective-permute-start = (bf16[64,1024]{1,0:T(8,128)(2,1)S(1)}, bf16[64,1024]{1,0:T(8,128)(2,1)S(1)}, u32[]{:S(2)}, u32[]{:S(2)}) collective-permute-start(bf16[64,1024]{1,0:T(8,128)(2,1)S(1)} %convolution_convert_fusion.1), channel_id=1, source_target_pairs={{0,2},{2,0},{4,6},{6,4},{8,10},{10,8},{12,14},{14,12},{1,3},{3,1},... | collective-permute-start | bytes 393224 | tf_op jit(solution)/shard_map/ppermute | solution.py:14
  4.9 0.7 copy-start.6
  4.9 0.7 %copy-start.7 = (f32[3,128]{1,0:T(4,128)S(1)}, f32[3,128]{1,0:T(4,128)}, u32[]{:S(2)}) copy-start(f32[3,128]{1,0:T(4,128)} %param.12) | copy-start | bytes 4612
  5.0 6.5 %copy-start.3 = (bf16[128,1024]{1,0:T(8,128)(2,1)S(1)}, bf16[128,1024]{1,0:T(8,128)(2,1)}, u32[]{:S(2)}) copy-start(bf16[128,1024]{1,0:T(8,128)(2,1)} %param.10) | copy-start | bytes 786436
  5.1 13.3 %collective-permute-start.5 = (bf16[64,1024]{1,0:T(8,128)(2,1)S(1)}, bf16[64,1024]{1,0:T(8,128)(2,1)S(1)}, u32[]{:S(2)}, u32[]{:S(2)}) collective-permute-start(bf16[64,1024]{1,0:T(8,128)(2,1)S(1)} %convolution_convert_fusion), channel_id=1, source_target_pairs={{0,2},{2,0},{4,6},{6,4},{8,10},{10,8},{12,14},{14,12},{1,3},{3,1},... | collective-permute-start | bytes 393224 | tf_op jit(solution)/shard_map/ppermute | solution.py:14
  9.3 5.2 %collective-permute-start.1 = (bf16[64,1024]{1,0:T(8,128)(2,1)S(1)}, bf16[64,1024]{1,0:T(8,128)(2,1)S(1)}, u32[]{:S(2)}, u32[]{:S(2)}) collective-permute-start(bf16[64,1024]{1,0:T(8,128)(2,1)S(1)} %fusion.4), channel_id=1, source_target_pairs={{0,4},{2,6},{4,0},{6,2},{8,12},{10,14},{12,8},{14,10},{1,5},{3,7},... | collective-permute-start | bytes 393224 | tf_op jit(solution)/shard_map/ppermute | solution.py:14
  14.6 8.2 %collective-permute-start.2 = (bf16[64,1024]{1,0:T(8,128)(2,1)S(1)}, bf16[64,1024]{1,0:T(8,128)(2,1)S(1)}, u32[]{:S(2)}, u32[]{:S(2)}) collective-permute-start(bf16[64,1024]{1,0:T(8,128)(2,1)S(1)} %fusion.6), channel_id=1, source_target_pairs={{0,8},{2,10},{4,12},{6,14},{8,0},{10,2},{12,4},{14,6},{1,9},{3,11}... | collective-permute-start | bytes 393224 | tf_op jit(solution)/shard_map/ppermute | solution.py:14
  18.5 5.6 %collective-permute-start.6 = (bf16[64,1024]{1,0:T(8,128)(2,1)S(1)}, bf16[64,1024]{1,0:T(8,128)(2,1)S(1)}, u32[]{:S(2)}, u32[]{:S(2)}) collective-permute-start(bf16[64,1024]{1,0:T(8,128)(2,1)S(1)} %fusion.12), channel_id=1, source_target_pairs={{0,4},{2,6},{4,0},{6,2},{8,12},{10,14},{12,8},{14,10},{1,5},{3,7},... | collective-permute-start | bytes 393224 | tf_op jit(solution)/shard_map/ppermute | solution.py:14
  23.1 1.8 %collective-permute-start.3 = (f32[64]{0:T(128)S(1)}, f32[64]{0:T(128)S(1)}, u32[]{:S(2)}, u32[]{:S(2)}) collective-permute-start(f32[64]{0:T(128)S(1)} %get-tuple-element.24), channel_id=1, source_target_pairs={{0,1},{1,0},{2,3},{3,2},{4,5},{5,4},{6,7},{7,6},{8,9},{9,8},{10,11... | collective-permute-start | bytes 776 | tf_op jit(solution)/shard_map/ppermute | solution.py:69
  24.1 0.8 %copy-start.4 = (f32[1024]{0:T(1024)S(1)}, f32[1024]{0:T(1024)}, u32[]{:S(2)}) copy-start(f32[1024]{0:T(1024)} %param.14) | copy-start | bytes 12292
  24.3 8.7 %collective-permute-start.7 = (bf16[64,1024]{1,0:T(8,128)(2,1)S(1)}, bf16[64,1024]{1,0:T(8,128)(2,1)S(1)}, u32[]{:S(2)}, u32[]{:S(2)}) collective-permute-start(bf16[64,1024]{1,0:T(8,128)(2,1)S(1)} %fusion.14), channel_id=1, source_target_pairs={{0,8},{2,10},{4,12},{6,14},{8,0},{10,2},{12,4},{14,6},{1,9},{3,11}... | collective-permute-start | bytes 393224 | tf_op jit(solution)/shard_map/ppermute | solution.py:14
  30.8 2.2 %copy-start.1 = (f32[64,1024]{1,0:T(8,128)S(1)}, f32[64,1024]{1,0:T(8,128)}, u32[]{:S(2)}) copy-start(f32[64,1024]{1,0:T(8,128)} %shard_map.120) | copy-start | bytes 786436
  30.9 2.2 %collective-permute-start.4 = (f32[64]{0:T(128)S(1)}, f32[64]{0:T(128)S(1)}, u32[]{:S(2)}, u32[]{:S(2)}) collective-permute-start(f32[64]{0:T(128)S(1)} %multiply_reduce_fusion.2), channel_id=1, source_target_pairs={{0,1},{1,0},{2,3},{3,2},{4,5},{5,4},{6,7},{7,6},{8,9},{9,8},{10,11... | collective-permute-start | bytes 776 | tf_op jit(solution)/shard_map/ppermute | solution.py:69
  33.5 14.6 %collective-permute-start.8 = (bf16[64,1024]{1,0:T(8,128)(2,1)S(1)}, bf16[64,1024]{1,0:T(8,128)(2,1)S(1)}, u32[]{:S(2)}, u32[]{:S(2)}) collective-permute-start(bf16[64,1024]{1,0:T(8,128)(2,1)S(1)} %fusion.18), channel_id=1, source_target_pairs={{0,8},{2,10},{4,12},{6,14},{8,0},{10,2},{12,4},{14,6},{1,9},{3,11}... | collective-permute-start | bytes 393224 | tf_op jit(solution)/shard_map/ppermute | solution.py:14
  42.3 3.7 %copy-start.2 = (f32[64,1024]{1,0:T(8,128)S(1)}, f32[64,1024]{1,0:T(8,128)}, u32[]{:S(2)}) copy-start(f32[64,1024]{1,0:T(8,128)} %shard_map.121) | copy-start | bytes 786436
  46.4 9.3 %collective-permute-start.11 = (bf16[64,1024]{1,0:T(8,128)(2,1)S(1)}, bf16[64,1024]{1,0:T(8,128)(2,1)S(1)}, u32[]{:S(2)}, u32[]{:S(2)}) collective-permute-start(bf16[64,1024]{1,0:T(8,128)(2,1)S(1)} %fusion.35), channel_id=1, source_target_pairs={{0,8},{2,10},{4,12},{6,14},{8,0},{10,2},{12,4},{14,6},{1,9},{3,11}... | collective-permute-start | bytes 393224 | tf_op jit(solution)/shard_map/ppermute | solution.py:14
  48.4 7.8 %collective-permute-start.9 = (bf16[64,1024]{1,0:T(8,128)(2,1)S(1)}, bf16[64,1024]{1,0:T(8,128)(2,1)S(1)}, u32[]{:S(2)}, u32[]{:S(2)}) collective-permute-start(bf16[64,1024]{1,0:T(8,128)(2,1)S(1)} %fusion.25), channel_id=1, source_target_pairs={{0,4},{2,6},{4,0},{6,2},{8,12},{10,14},{12,8},{14,10},{1,5},{3,7},... | collective-permute-start | bytes 393224 | tf_op jit(solution)/shard_map/ppermute | solution.py:14
  56.1 5.0 %collective-permute-start.12 = (bf16[64,1024]{1,0:T(8,128)(2,1)S(1)}, bf16[64,1024]{1,0:T(8,128)(2,1)S(1)}, u32[]{:S(2)}, u32[]{:S(2)}) collective-permute-start(bf16[64,1024]{1,0:T(8,128)(2,1)S(1)} %fusion.40), channel_id=1, source_target_pairs={{0,4},{2,6},{4,0},{6,2},{8,12},{10,14},{12,8},{14,10},{1,5},{3,7},... | collective-permute-start | bytes 393224 | tf_op jit(solution)/shard_map/ppermute | solution.py:14
  56.5 9.1 %collective-permute-start.10 = (bf16[64,1024]{1,0:T(8,128)(2,1)S(1)}, bf16[64,1024]{1,0:T(8,128)(2,1)S(1)}, u32[]{:S(2)}, u32[]{:S(2)}) collective-permute-start(bf16[64,1024]{1,0:T(8,128)(2,1)S(1)} %fusion.30), channel_id=1, source_target_pairs={{0,2},{2,0},{4,6},{6,4},{8,10},{10,8},{12,14},{14,12},{1,3},{3,1},... | collective-permute-start | bytes 393224 | tf_op jit(solution)/shard_map/ppermute | solution.py:14
  61.5 5.0 %collective-permute-start.13 = (bf16[64,1024]{1,0:T(8,128)(2,1)S(1)}, bf16[64,1024]{1,0:T(8,128)(2,1)S(1)}, u32[]{:S(2)}, u32[]{:S(2)}) collective-permute-start(bf16[64,1024]{1,0:T(8,128)(2,1)S(1)} %fusion.45), channel_id=1, source_target_pairs={{0,2},{2,0},{4,6},{6,4},{8,10},{10,8},{12,14},{14,12},{1,3},{3,1},... | collective-permute-start | bytes 393224 | tf_op jit(solution)/shard_map/ppermute | solution.py:14
  63.1 1.2 %collective-permute-start.15 = (f32[3,128]{1,0:T(4,128)S(1)}, f32[3,128]{1,0:T(4,128)S(1)}, u32[]{:S(2)}, u32[]{:S(2)}) collective-permute-start(f32[3,128]{1,0:T(4,128)S(1)} %maximum_maximum_fusion.1), channel_id=1, source_target_pairs={{0,1},{1,0},{2,3},{3,2},{4,5},{5,4},{6,7},{7,6},{8,9},{9,8},{10,11... | collective-permute-start | bytes 4616 | tf_op jit(solution)/shard_map/ppermute | solution.py:69
  63.2 1.7 %collective-permute-start.14 = (f32[3,128]{1,0:T(4,128)S(1)}, f32[3,128]{1,0:T(4,128)S(1)}, u32[]{:S(2)}, u32[]{:S(2)}) collective-permute-start(f32[3,128]{1,0:T(4,128)S(1)} %maximum_maximum_fusion), channel_id=1, source_target_pairs={{0,1},{1,0},{2,3},{3,2},{4,5},{5,4},{6,7},{7,6},{8,9},{9,8},{10,11... | collective-permute-start | bytes 4616 | tf_op jit(solution)/shard_map/ppermute | solution.py:69
  66.8 1.3 %collective-permute-start.16 = (f32[1,128,128]{2,1,0:T(8,128)S(1)}, f32[1,128,128]{2,1,0:T(8,128)S(1)}, u32[]{:S(2)}, u32[]{:S(2)}) collective-permute-start(f32[1,128,128]{2,1,0:T(8,128)S(1)} %convolution_bitcast_fusion.1), channel_id=1, source_target_pairs={{0,1},{1,0},{2,3},{3,2},{4,5},{5,4},{6,7},{7,6},{8,9},{9,8},{10,11... | collective-permute-start | bytes 196616 | tf_op jit(solution)/shard_map/ppermute | solution.py:69

commit v13 on v12

--- a/solution.py
+++ b/solution.py
@@ -121,7 +121,7 @@
         mixed_f = mixed.astype(jnp.float32)
         resid = tok_f + tok_f * mixed_f
         reduce_hid = hid_sum if chunk == 0 else (lambda v: lax.psum(v, "hid"))
-        square = reduce_hid(jnp.sum(resid * resid, axis=-1))
+        square = hid_sum(jnp.sum(resid * resid, axis=-1))
         inv = lax.rsqrt(square / D + 1e-06)
         normed = (resid * inv[:, None] * norm_gain).astype(jnp.bfloat16)
         d_normed = ffn_grad(normed, cot, w_gate, w_up, w_down)

time: 69.1 us -> 66.8 us (0.967)
  blocking collectives: 4.93 us -> 2.47 us
    psum x2 -> x1, blocking collectives: 4.93 us -> 2.47 us  [body(): reduce_hid = hid_sum if chunk == 0 else lambda v: lax.psum(v, 'hid')]
  transfers between devices with their start and end apart: 17 -> 18, of which waited for: 10 -> 10; matrix products, arithmetic and copies ran while one was open for 15% -> 15% of each run, Pallas kernels for 12% -> 12%
where the time goes in v13:
time: 66.8 us; the launch traced here: 66.5 us
  waiting for transfers between devices  22.1 us (33%)
  starting transfers between devices  19.9 us (30%)
  other arithmetic  9.3 us (14%)
  Pallas kernels  8.12 us (12%)
  matrix products  2.57 us (4%)
  blocking collectives  2.47 us (4%)
  local copies, waits for them, and re-layouts  1.2 us (2%)
  between operations  0.89 us (1%)
    ppermute x12, waiting for transfers between devices, from_partner(): return lax.ppermute(value, axis, pairs)  21.2 us
    ppermute x12, starting transfers between devices, from_partner(): return lax.ppermute(value, axis, pairs)  19 us
    pallas_call x2, Pallas kernels, ffn_grad(): pl.pallas_call(ffn_kernel, grid=(groups_here // per_step,), in_specs=[act...  8.12 us
    psum x1, blocking collectives, body(): reduce_hid = hid_sum if chunk == 0 else lambda v: lax.psum(v, 'hid')  2.47 us
    reduce_sum x2, other arithmetic, body(): inner = reduce_hid(jnp.sum(resid * scaled, axis=-1))  2.29 us
    add x3, other arithmetic, hid_sum(): total = total + lax.ppermute(value, 'hid', pairs)  1.95 us
    reduce_sum x6, other arithmetic, body(): jnp.sum(back_f * mates[chunk][section].astype(jnp.float32), axis=-1)  1.65 us
    convert_element_type x2, other arithmetic, body(): normed = (resid * inv[:, None] * norm_gain).astype(jnp.bfloat16)  1.5 us
  transfers between devices with their start and end apart: 18, of which 10 were waited for; matrix products, arithmetic and copies ran while one was open for 15% of the time, Pallas kernels for 12%

profile of v13, /device:TPU:0, one launch (start us, length us, event | category | flops | bytes accessed | tf_op | source)
XLA Modules:
  0.0 66.5 jit_solution(9421647619297010347)
XLA Ops:
  0.7 1.2 %convolution_convert_fusion.1 = bf16[64,1024]{1,0:T(8,128)(2,1)S(1)} fusion(bf16[128,1024]{1,0:T(8,128)(2,1)} %param.9, bf16[1,128,128]{2,1,0:T(8,128)(2,1)} %param.11), kind=kOutput, calls=%fused_computation.4 | convolution fusion | flops 16842752 | bytes 409600 | tf_op jit(solution)/shard_map/kij,kjd->kid/dot_general | solution.py:92
  1.8 3.0 %collective-permute-start = (bf16[64,1024]{1,0:T(8,128)(2,1)S(1)}, bf16[64,1024]{1,0:T(8,128)(2,1)S(1)}, u32[]{:S(2)}, u32[]{:S(2)}) collective-permute-start(bf16[64,1024]{1,0:T(8,128)(2,1)S(1)} %convolution_convert_fusion.1), channel_id=1, source_target_pairs={{0,2},{2,0},{4,6},{6,4},{8,10},{10,8},{12,14},{14,12},{1,3},{3,1},... | collective-permute-start | bytes 393224 | tf_op jit(solution)/shard_map/ppermute | solution.py:14
  5.6 3.5 %collective-permute-done = bf16[64,1024]{1,0:T(8,128)(2,1)S(1)} collective-permute-done((bf16[64,1024]{1,0:T(8,128)(2,1)S(1)}, bf16[64,1024]{1,0:T(8,128)(2,1)S(1)}, u32[]{:S(2)}, u32[]{:S(2)}) %collective-permute-start) | collective-permute-done | bytes 131104 | tf_op jit(solution)/shard_map/ppermute | solution.py:14
  9.3 2.2 %collective-permute-start.1 = (bf16[64,1024]{1,0:T(8,128)(2,1)S(1)}, bf16[64,1024]{1,0:T(8,128)(2,1)S(1)}, u32[]{:S(2)}, u32[]{:S(2)}) collective-permute-start(bf16[64,1024]{1,0:T(8,128)(2,1)S(1)} %fusion.4), channel_id=1, source_target_pairs={{0,4},{2,6},{4,0},{6,2},{8,12},{10,14},{12,8},{14,10},{1,5},{3,7},... | collective-permute-start | bytes 393224 | tf_op jit(solution)/shard_map/ppermute | solution.py:14
  11.5 0.7 %fusion.66 = (bf16[64,1024]{1,0:T(8,128)(2,1)}, bf16[64,1024]{1,0:T(8,128)(2,1)}) fusion(bf16[128,1024]{1,0:T(8,128)(2,1)S(1)} %copy-done.3), kind=kLoop, calls=%fused_computation.132 | loop fusion | bytes 524288 | tf_op jit(solution)/shard_map/slice | solution.py:119
  12.2 2.2 %collective-permute-done.1 = bf16[64,1024]{1,0:T(8,128)(2,1)S(1)} collective-permute-done((bf16[64,1024]{1,0:T(8,128)(2,1)S(1)}, bf16[64,1024]{1,0:T(8,128)(2,1)S(1)}, u32[]{:S(2)}, u32[]{:S(2)}) %collective-permute-start.1) | collective-permute-done | bytes 131104 | tf_op jit(solution)/shard_map/ppermute | solution.py:14
  14.6 3.8 %collective-permute-start.2 = (bf16[64,1024]{1,0:T(8,128)(2,1)S(1)}, bf16[64,1024]{1,0:T(8,128)(2,1)S(1)}, u32[]{:S(2)}, u32[]{:S(2)}) collective-permute-start(bf16[64,1024]{1,0:T(8,128)(2,1)S(1)} %fusion.6), channel_id=1, source_target_pairs={{0,8},{2,10},{4,12},{6,14},{8,0},{10,2},{12,4},{14,6},{1,9},{3,11}... | collective-permute-start | bytes 393224 | tf_op jit(solution)/shard_map/ppermute | solution.py:14
  18.5 1.2 %collective-permute-start.6 = (bf16[64,1024]{1,0:T(8,128)(2,1)S(1)}, bf16[64,1024]{1,0:T(8,128)(2,1)S(1)}, u32[]{:S(2)}, u32[]{:S(2)}) collective-permute-start(bf16[64,1024]{1,0:T(8,128)(2,1)S(1)} %fusion.12), channel_id=1, source_target_pairs={{0,4},{2,6},{4,0},{6,2},{8,12},{10,14},{12,8},{14,10},{1,5},{3,7},... | collective-permute-start | bytes 393224 | tf_op jit(solution)/shard_map/ppermute | solution.py:14
  19.7 3.1 %collective-permute-done.2 = bf16[64,1024]{1,0:T(8,128)(2,1)S(1)} collective-permute-done((bf16[64,1024]{1,0:T(8,128)(2,1)S(1)}, bf16[64,1024]{1,0:T(8,128)(2,1)S(1)}, u32[]{:S(2)}, u32[]{:S(2)}) %collective-permute-start.2) | collective-permute-done | bytes 131104 | tf_op jit(solution)/shard_map/ppermute | solution.py:14
  23.1 1.0 %collective-permute-done.6 = bf16[64,1024]{1,0:T(8,128)(2,1)S(1)} collective-permute-done((bf16[64,1024]{1,0:T(8,128)(2,1)S(1)}, bf16[64,1024]{1,0:T(8,128)(2,1)S(1)}, u32[]{:S(2)}, u32[]{:S(2)}) %collective-permute-start.6) | collective-permute-done | bytes 131104 | tf_op jit(solution)/shard_map/ppermute | solution.py:14
  24.3 0.6 collective-permute-start.7
  24.9 0.8 %multiply_convert_fusion.1.normed_ref = bf16[64,1024]{1,0:T(8,128)(2,1)} fusion(bf16[64,1024]{1,0:T(8,128)(2,1)S(1)} %get-tuple-element.25, f32[1024]{0:T(1024)S(1)} %copy-done.4, f32[64]{0:T(128)S(1)} %add_rsqrt_fusion.1, bf16[128,1024]{1,0:T(8,128)(2,1)S(1)} %copy-done), kind=kLoop, calls=%fused_computation.101 | loop fusion | flops 458752 | bytes 397568 | tf_op jit(solution)/shard_map/convert_element_type | solution.py:126
  25.7 4.1 %shard_map.120 = f32[64,1024]{1,0:T(8,128)} custom-call(bf16[64,1024]{1,0:T(8,128)(2,1)} %multiply_convert_fusion.1.normed_ref, bf16[64,1024]{1,0:T(8,128)(2,1)} %get-tuple-element.29.cot_ref, bf16[8,128,512]{2,1,0:T(8,128)(2,1)} %wg_ref.3, bf16[8,128,512]{2,1,0:T(8,128)(2,1)} %wu_ref.3, bf16[8,512,128]{2,1,0:T(8,128)(2,1)} %wd_ref.3), custom_call_target="tpu_custom_call" | custom-call | flops 335544320 | bytes 3670016 | tf_op jit(solution)/shard_map/pallas_call | solution.py:44
  29.7 1.1 %multiply_reduce_fusion.2 = f32[64]{0:T(128)S(1)} fusion(f32[64,1024]{1,0:T(8,128)} %shard_map.120, bf16[64,1024]{1,0:T(8,128)(2,1)S(1)} %get-tuple-element.25, f32[1024]{0:T(1024)S(1)} %copy-done.4, bf16[128,1024]{1,0:T(8,128)(2,1)S(1)} %copy-done), kind=kLoop, calls=%fused_computation.100 | loop fusion | flops 458688 | bytes 528640 | tf_op jit(solution)/shard_map/reduce_sum | solution.py:129
  31.1 1.8 %collective-permute-done.7 = bf16[64,1024]{1,0:T(8,128)(2,1)S(1)} collective-permute-done((bf16[64,1024]{1,0:T(8,128)(2,1)S(1)}, bf16[64,1024]{1,0:T(8,128)(2,1)S(1)}, u32[]{:S(2)}, u32[]{:S(2)}) %collective-permute-start.7) | collective-permute-done | bytes 131104 | tf_op jit(solution)/shard_map/ppermute | solution.py:14
  33.7 1.5 %collective-permute-start.9 = (bf16[64,1024]{1,0:T(8,128)(2,1)S(1)}, bf16[64,1024]{1,0:T(8,128)(2,1)S(1)}, u32[]{:S(2)}, u32[]{:S(2)}) collective-permute-start(bf16[64,1024]{1,0:T(8,128)(2,1)S(1)} %fusion.18), channel_id=1, source_target_pairs={{0,8},{2,10},{4,12},{6,14},{8,0},{10,2},{12,4},{14,6},{1,9},{3,11}... | collective-permute-start | bytes 393224 | tf_op jit(solution)/shard_map/ppermute | solution.py:14
  35.2 0.8 %multiply_convert_fusion.normed_ref = bf16[64,1024]{1,0:T(8,128)(2,1)} fusion(bf16[64,1024]{1,0:T(8,128)(2,1)S(1)} %fusion.16, f32[64]{0:T(128)S(1)} %add_rsqrt_fusion, f32[1024]{0:T(1024)S(1)} %copy-done.4, bf16[128,1024]{1,0:T(8,128)(2,1)S(1)} %copy-done), kind=kLoop, calls=%fused_computation.97 | loop fusion | flops 458752 | bytes 397568 | tf_op jit(solution)/shard_map/convert_element_type | solution.py:126
  36.0 4.1 %shard_map.121 = f32[64,1024]{1,0:T(8,128)} custom-call(bf16[64,1024]{1,0:T(8,128)(2,1)} %multiply_convert_fusion.normed_ref, bf16[64,1024]{1,0:T(8,128)(2,1)} %get-tuple-element.28.cot_ref, bf16[8,128,512]{2,1,0:T(8,128)(2,1)} %wg_ref.3, bf16[8,128,512]{2,1,0:T(8,128)(2,1)} %wu_ref.3, bf16[8,512,128]{2,1,0:T(8,128)(2,1)} %wd_ref.3), custom_call_target="tpu_custom_call" | custom-call | flops 335544320 | bytes 3670016 | tf_op jit(solution)/shard_map/pallas_call | solution.py:44
  40.0 1.2 %multiply_reduce_fusion = f32[64]{0:T(128)S(1)} fusion(f32[64,1024]{1,0:T(8,128)} %shard_map.121, bf16[64,1024]{1,0:T(8,128)(2,1)S(1)} %fusion.16, f32[1024]{0:T(1024)S(1)} %copy-done.4, bf16[128,1024]{1,0:T(8,128)(2,1)S(1)} %copy-done), kind=kLoop, calls=%fused_computation.96 | loop fusion | flops 458688 | bytes 528640 | tf_op jit(solution)/shard_map/reduce_sum | solution.py:129
  41.2 2.5 %psum.7 = f32[64]{0:T(128)S(1)} all-reduce(f32[64]{0:T(128)S(1)} %multiply_reduce_fusion), channel_id=1, replica_groups=mesh['groups'=2,'seq'=8,'hid'=2] {'hid'}, use_global_device_ids=true, to_apply=%region_4.0 | all-reduce | flops 64 | bytes 512 | tf_op jit(solution)/shard_map/psum | solution.py:123
  44.1 1.5 %collective-permute-start.12 = (bf16[64,1024]{1,0:T(8,128)(2,1)S(1)}, bf16[64,1024]{1,0:T(8,128)(2,1)S(1)}, u32[]{:S(2)}, u32[]{:S(2)}) collective-permute-start(bf16[64,1024]{1,0:T(8,128)(2,1)S(1)} %fusion.35), channel_id=1, source_target_pairs={{0,8},{2,10},{4,12},{6,14},{8,0},{10,2},{12,4},{14,6},{1,9},{3,11}... | collective-permute-start | bytes 393224 | tf_op jit(solution)/shard_map/ppermute | solution.py:14
  46.0 1.6 %collective-permute-start.10 = (bf16[64,1024]{1,0:T(8,128)(2,1)S(1)}, bf16[64,1024]{1,0:T(8,128)(2,1)S(1)}, u32[]{:S(2)}, u32[]{:S(2)}) collective-permute-start(bf16[64,1024]{1,0:T(8,128)(2,1)S(1)} %fusion.25), channel_id=1, source_target_pairs={{0,4},{2,6},{4,0},{6,2},{8,12},{10,14},{12,8},{14,10},{1,5},{3,7},... | collective-permute-start | bytes 393224 | tf_op jit(solution)/shard_map/ppermute | solution.py:14
  47.6 5.8 %collective-permute-done.12 = bf16[64,1024]{1,0:T(8,128)(2,1)S(1)} collective-permute-done((bf16[64,1024]{1,0:T(8,128)(2,1)S(1)}, bf16[64,1024]{1,0:T(8,128)(2,1)S(1)}, u32[]{:S(2)}, u32[]{:S(2)}) %collective-permute-start.12) | collective-permute-done | bytes 131104 | tf_op jit(solution)/shard_map/ppermute | solution.py:14
  54.2 1.6 %collective-permute-start.11 = (bf16[64,1024]{1,0:T(8,128)(2,1)S(1)}, bf16[64,1024]{1,0:T(8,128)(2,1)S(1)}, u32[]{:S(2)}, u32[]{:S(2)}) collective-permute-start(bf16[64,1024]{1,0:T(8,128)(2,1)S(1)} %fusion.30), channel_id=1, source_target_pairs={{0,2},{2,0},{4,6},{6,4},{8,10},{10,8},{12,14},{14,12},{1,3},{3,1},... | collective-permute-start | bytes 393224 | tf_op jit(solution)/shard_map/ppermute | solution.py:14
  55.9 3.0 %collective-permute-done.13 = bf16[64,1024]{1,0:T(8,128)(2,1)S(1)} collective-permute-done((bf16[64,1024]{1,0:T(8,128)(2,1)S(1)}, bf16[64,1024]{1,0:T(8,128)(2,1)S(1)}, u32[]{:S(2)}, u32[]{:S(2)}) %collective-permute-start.13) | collective-permute-done | bytes 131104 | tf_op jit(solution)/shard_map/ppermute | solution.py:14
  59.2 1.6 %collective-permute-start.14 = (bf16[64,1024]{1,0:T(8,128)(2,1)S(1)}, bf16[64,1024]{1,0:T(8,128)(2,1)S(1)}, u32[]{:S(2)}, u32[]{:S(2)}) collective-permute-start(bf16[64,1024]{1,0:T(8,128)(2,1)S(1)} %fusion.45), channel_id=1, source_target_pairs={{0,2},{2,0},{4,6},{6,4},{8,10},{10,8},{12,14},{14,12},{1,3},{3,1},... | collective-permute-start | bytes 393224 | tf_op jit(solution)/shard_map/ppermute | solution.py:14
  61.5 0.6 collective-permute-done.16
  62.0 0.7 fusion.70
  62.7 0.7 fusion.71
  63.5 0.8 %collective-permute-done.14 = bf16[64,1024]{1,0:T(8,128)(2,1)S(1)} collective-permute-done((bf16[64,1024]{1,0:T(8,128)(2,1)S(1)}, bf16[64,1024]{1,0:T(8,128)(2,1)S(1)}, u32[]{:S(2)}, u32[]{:S(2)}) %collective-permute-start.14) | collective-permute-done | bytes 131104 | tf_op jit(solution)/shard_map/ppermute | solution.py:14
  64.7 1.0 %fusion.1 = bf16[128,1024]{1,0:T(8,128)(2,1)} fusion(f32[64,1024]{1,0:T(8,128)S(1)} %get-tuple-element.26, f32[64,1024]{1,0:T(8,128)S(1)} %get-tuple-element.27, bf16[64,1024]{1,0:T(8,128)(2,1)S(1)} %fusion.44, bf16[64,1024]{1,0:T(8,128)(2,1)S(1)} %fusion.29, bf16[1,128,128]{2,1,0:T(8,128)(2,1)S(1)} %copy-done.5), kind=kOutput, calls=%fused_computation.2 | convolution fusion | flops 34471936 | bytes 1081344 | tf_op jit(solution)/shard_map/kij,kid->kjd/dot_general | solution.py:167
  65.9 0.6 add.109
  (63 shorter events, 5.9 us)
Async XLA Ops:
  0.6 4.2 %copy-start.5 = (bf16[1,128,128]{2,1,0:T(8,128)(2,1)S(1)}, bf16[1,128,128]{2,1,0:T(8,128)(2,1)}, u32[]{:S(2)}) copy-start(bf16[1,128,128]{2,1,0:T(8,128)(2,1)} %param.11) | copy-start | bytes 98308
  0.6 4.2 %copy-start = (bf16[128,1024]{1,0:T(8,128)(2,1)S(1)}, bf16[128,1024]{1,0:T(8,128)(2,1)}, u32[]{:S(2)}) copy-start(bf16[128,1024]{1,0:T(8,128)(2,1)} %param.9) | copy-start | bytes 786436
  1.8 7.3 %collective-permute-start = (bf16[64,1024]{1,0:T(8,128)(2,1)S(1)}, bf16[64,1024]{1,0:T(8,128)(2,1)S(1)}, u32[]{:S(2)}, u32[]{:S(2)}) collective-permute-start(bf16[64,1024]{1,0:T(8,128)(2,1)S(1)} %convolution_convert_fusion.1), channel_id=1, source_target_pairs={{0,2},{2,0},{4,6},{6,4},{8,10},{10,8},{12,14},{14,12},{1,3},{3,1},... | collective-permute-start | bytes 393224 | tf_op jit(solution)/shard_map/ppermute | solution.py:14
  4.9 0.7 %copy-start.6 = (f32[3,128]{1,0:T(4,128)S(1)}, f32[3,128]{1,0:T(4,128)}, u32[]{:S(2)}) copy-start(f32[3,128]{1,0:T(4,128)} %param.13) | copy-start | bytes 4612
  4.9 0.7 %copy-start.7 = (f32[3,128]{1,0:T(4,128)S(1)}, f32[3,128]{1,0:T(4,128)}, u32[]{:S(2)}) copy-start(f32[3,128]{1,0:T(4,128)} %param.12) | copy-start | bytes 4612
  5.0 6.5 %copy-start.3 = (bf16[128,1024]{1,0:T(8,128)(2,1)S(1)}, bf16[128,1024]{1,0:T(8,128)(2,1)}, u32[]{:S(2)}) copy-start(bf16[128,1024]{1,0:T(8,128)(2,1)} %param.10) | copy-start | bytes 786436
  5.1 13.3 %collective-permute-start.5 = (bf16[64,1024]{1,0:T(8,128)(2,1)S(1)}, bf16[64,1024]{1,0:T(8,128)(2,1)S(1)}, u32[]{:S(2)}, u32[]{:S(2)}) collective-permute-start(bf16[64,1024]{1,0:T(8,128)(2,1)S(1)} %convolution_convert_fusion), channel_id=1, source_target_pairs={{0,2},{2,0},{4,6},{6,4},{8,10},{10,8},{12,14},{14,12},{1,3},{3,1},... | collective-permute-start | bytes 393224 | tf_op jit(solution)/shard_map/ppermute | solution.py:14
  9.3 5.2 %collective-permute-start.1 = (bf16[64,1024]{1,0:T(8,128)(2,1)S(1)}, bf16[64,1024]{1,0:T(8,128)(2,1)S(1)}, u32[]{:S(2)}, u32[]{:S(2)}) collective-permute-start(bf16[64,1024]{1,0:T(8,128)(2,1)S(1)} %fusion.4), channel_id=1, source_target_pairs={{0,4},{2,6},{4,0},{6,2},{8,12},{10,14},{12,8},{14,10},{1,5},{3,7},... | collective-permute-start | bytes 393224 | tf_op jit(solution)/shard_map/ppermute | solution.py:14
  14.6 8.2 %collective-permute-start.2 = (bf16[64,1024]{1,0:T(8,128)(2,1)S(1)}, bf16[64,1024]{1,0:T(8,128)(2,1)S(1)}, u32[]{:S(2)}, u32[]{:S(2)}) collective-permute-start(bf16[64,1024]{1,0:T(8,128)(2,1)S(1)} %fusion.6), channel_id=1, source_target_pairs={{0,8},{2,10},{4,12},{6,14},{8,0},{10,2},{12,4},{14,6},{1,9},{3,11}... | collective-permute-start | bytes 393224 | tf_op jit(solution)/shard_map/ppermute | solution.py:14
  18.5 5.6 %collective-permute-start.6 = (bf16[64,1024]{1,0:T(8,128)(2,1)S(1)}, bf16[64,1024]{1,0:T(8,128)(2,1)S(1)}, u32[]{:S(2)}, u32[]{:S(2)}) collective-permute-start(bf16[64,1024]{1,0:T(8,128)(2,1)S(1)} %fusion.12), channel_id=1, source_target_pairs={{0,4},{2,6},{4,0},{6,2},{8,12},{10,14},{12,8},{14,10},{1,5},{3,7},... | collective-permute-start | bytes 393224 | tf_op jit(solution)/shard_map/ppermute | solution.py:14
  23.1 1.8 %collective-permute-start.3 = (f32[64]{0:T(128)S(1)}, f32[64]{0:T(128)S(1)}, u32[]{:S(2)}, u32[]{:S(2)}) collective-permute-start(f32[64]{0:T(128)S(1)} %get-tuple-element.24), channel_id=1, source_target_pairs={{0,1},{1,0},{2,3},{3,2},{4,5},{5,4},{6,7},{7,6},{8,9},{9,8},{10,11... | collective-permute-start | bytes 776 | tf_op jit(solution)/shard_map/ppermute | solution.py:69
  24.1 0.8 %copy-start.4 = (f32[1024]{0:T(1024)S(1)}, f32[1024]{0:T(1024)}, u32[]{:S(2)}) copy-start(f32[1024]{0:T(1024)} %param.14) | copy-start | bytes 12292
  24.3 8.7 %collective-permute-start.7 = (bf16[64,1024]{1,0:T(8,128)(2,1)S(1)}, bf16[64,1024]{1,0:T(8,128)(2,1)S(1)}, u32[]{:S(2)}, u32[]{:S(2)}) collective-permute-start(bf16[64,1024]{1,0:T(8,128)(2,1)S(1)} %fusion.14), channel_id=1, source_target_pairs={{0,8},{2,10},{4,12},{6,14},{8,0},{10,2},{12,4},{14,6},{1,9},{3,11}... | collective-permute-start | bytes 393224 | tf_op jit(solution)/shard_map/ppermute | solution.py:14
  30.8 2.2 %copy-start.1 = (f32[64,1024]{1,0:T(8,128)S(1)}, f32[64,1024]{1,0:T(8,128)}, u32[]{:S(2)}) copy-start(f32[64,1024]{1,0:T(8,128)} %shard_map.120) | copy-start | bytes 786436
  30.9 2.2 %collective-permute-start.4 = (f32[64]{0:T(128)S(1)}, f32[64]{0:T(128)S(1)}, u32[]{:S(2)}, u32[]{:S(2)}) collective-permute-start(f32[64]{0:T(128)S(1)} %multiply_reduce_fusion.2), channel_id=1, source_target_pairs={{0,1},{1,0},{2,3},{3,2},{4,5},{5,4},{6,7},{7,6},{8,9},{9,8},{10,11... | collective-permute-start | bytes 776 | tf_op jit(solution)/shard_map/ppermute | solution.py:69
  33.6 1.6 %collective-permute-start.8 = (f32[64]{0:T(128)S(1)}, f32[64]{0:T(128)S(1)}, u32[]{:S(2)}, u32[]{:S(2)}) collective-permute-start(f32[64]{0:T(128)S(1)} %multiply_reduce_fusion.1), channel_id=1, source_target_pairs={{0,1},{1,0},{2,3},{3,2},{4,5},{5,4},{6,7},{7,6},{8,9},{9,8},{10,11... | collective-permute-start | bytes 776 | tf_op jit(solution)/shard_map/ppermute | solution.py:69
  33.7 12.0 %collective-permute-start.9 = (bf16[64,1024]{1,0:T(8,128)(2,1)S(1)}, bf16[64,1024]{1,0:T(8,128)(2,1)S(1)}, u32[]{:S(2)}, u32[]{:S(2)}) collective-permute-start(bf16[64,1024]{1,0:T(8,128)(2,1)S(1)} %fusion.18), channel_id=1, source_target_pairs={{0,8},{2,10},{4,12},{6,14},{8,0},{10,2},{12,4},{14,6},{1,9},{3,11}... | collective-permute-start | bytes 393224 | tf_op jit(solution)/shard_map/ppermute | solution.py:14
  40.0 3.7 %copy-start.2 = (f32[64,1024]{1,0:T(8,128)S(1)}, f32[64,1024]{1,0:T(8,128)}, u32[]{:S(2)}) copy-start(f32[64,1024]{1,0:T(8,128)} %shard_map.121) | copy-start | bytes 786436
  44.1 9.3 %collective-permute-start.12 = (bf16[64,1024]{1,0:T(8,128)(2,1)S(1)}, bf16[64,1024]{1,0:T(8,128)(2,1)S(1)}, u32[]{:S(2)}, u32[]{:S(2)}) collective-permute-start(bf16[64,1024]{1,0:T(8,128)(2,1)S(1)} %fusion.35), channel_id=1, source_target_pairs={{0,8},{2,10},{4,12},{6,14},{8,0},{10,2},{12,4},{14,6},{1,9},{3,11}... | collective-permute-start | bytes 393224 | tf_op jit(solution)/shard_map/ppermute | solution.py:14
  46.0 7.9 %collective-permute-start.10 = (bf16[64,1024]{1,0:T(8,128)(2,1)S(1)}, bf16[64,1024]{1,0:T(8,128)(2,1)S(1)}, u32[]{:S(2)}, u32[]{:S(2)}) collective-permute-start(bf16[64,1024]{1,0:T(8,128)(2,1)S(1)} %fusion.25), channel_id=1, source_target_pairs={{0,4},{2,6},{4,0},{6,2},{8,12},{10,14},{12,8},{14,10},{1,5},{3,7},... | collective-permute-start | bytes 393224 | tf_op jit(solution)/shard_map/ppermute | solution.py:14
  53.8 5.0 %collective-permute-start.13 = (bf16[64,1024]{1,0:T(8,128)(2,1)S(1)}, bf16[64,1024]{1,0:T(8,128)(2,1)S(1)}, u32[]{:S(2)}, u32[]{:S(2)}) collective-permute-start(bf16[64,1024]{1,0:T(8,128)(2,1)S(1)} %fusion.40), channel_id=1, source_target_pairs={{0,4},{2,6},{4,0},{6,2},{8,12},{10,14},{12,8},{14,10},{1,5},{3,7},... | collective-permute-start | bytes 393224 | tf_op jit(solution)/shard_map/ppermute | solution.py:14
  54.2 9.1 %collective-permute-start.11 = (bf16[64,1024]{1,0:T(8,128)(2,1)S(1)}, bf16[64,1024]{1,0:T(8,128)(2,1)S(1)}, u32[]{:S(2)}, u32[]{:S(2)}) collective-permute-start(bf16[64,1024]{1,0:T(8,128)(2,1)S(1)} %fusion.30), channel_id=1, source_target_pairs={{0,2},{2,0},{4,6},{6,4},{8,10},{10,8},{12,14},{14,12},{1,3},{3,1},... | collective-permute-start | bytes 393224 | tf_op jit(solution)/shard_map/ppermute | solution.py:14
  59.2 5.0 %collective-permute-start.14 = (bf16[64,1024]{1,0:T(8,128)(2,1)S(1)}, bf16[64,1024]{1,0:T(8,128)(2,1)S(1)}, u32[]{:S(2)}, u32[]{:S(2)}) collective-permute-start(bf16[64,1024]{1,0:T(8,128)(2,1)S(1)} %fusion.45), channel_id=1, source_target_pairs={{0,2},{2,0},{4,6},{6,4},{8,10},{10,8},{12,14},{14,12},{1,3},{3,1},... | collective-permute-start | bytes 393224 | tf_op jit(solution)/shard_map/ppermute | solution.py:14
  60.9 1.2 %collective-permute-start.16 = (f32[3,128]{1,0:T(4,128)S(1)}, f32[3,128]{1,0:T(4,128)S(1)}, u32[]{:S(2)}, u32[]{:S(2)}) collective-permute-start(f32[3,128]{1,0:T(4,128)S(1)} %maximum_maximum_fusion.1), channel_id=1, source_target_pairs={{0,1},{1,0},{2,3},{3,2},{4,5},{5,4},{6,7},{7,6},{8,9},{9,8},{10,11... | collective-permute-start | bytes 4616 | tf_op jit(solution)/shard_map/ppermute | solution.py:69
  61.0 1.7 %collective-permute-start.15 = (f32[3,128]{1,0:T(4,128)S(1)}, f32[3,128]{1,0:T(4,128)S(1)}, u32[]{:S(2)}, u32[]{:S(2)}) collective-permute-start(f32[3,128]{1,0:T(4,128)S(1)} %maximum_maximum_fusion), channel_id=1, source_target_pairs={{0,1},{1,0},{2,3},{3,2},{4,5},{5,4},{6,7},{7,6},{8,9},{9,8},{10,11... | collective-permute-start | bytes 4616 | tf_op jit(solution)/shard_map/ppermute | solution.py:69
  64.6 1.3 %collective-permute-start.17 = (f32[1,128,128]{2,1,0:T(8,128)S(1)}, f32[1,128,128]{2,1,0:T(8,128)S(1)}, u32[]{:S(2)}, u32[]{:S(2)}) collective-permute-start(f32[1,128,128]{2,1,0:T(8,128)S(1)} %convolution_bitcast_fusion.1), channel_id=1, source_target_pairs={{0,1},{1,0},{2,3},{3,2},{4,5},{5,4},{6,7},{7,6},{8,9},{9,8},{10,11... | collective-permute-start | bytes 196616 | tf_op jit(solution)/shard_map/ppermute | solution.py:69

commit v14 on v13

--- a/solution.py
+++ b/solution.py
@@ -82,16 +82,18 @@
     nblk = blocks.shape[0]
     blen = blocks.shape[1]
     tok_blocks = tokens.reshape(nblk, blen, width)
-    chunks = CHUNKS if tok % CHUNKS == 0 else 1
-    rows = tok // chunks
-    spans = [slice(chunk * rows, (chunk + 1) * rows) for chunk in range(chunks)]
+    first = (tok * 5 // 8) // 16 * 16
+    if CHUNKS == 2 and 0 < first < tok:
+        spans = [slice(0, first), slice(first, tok)]
+    else:
+        spans = [slice(0, tok)]
     states = [[None] * sections for _ in spans]
     mates = [[None] * sections for _ in spans]
     if nblk == 1:
         pieces = [
             jnp.einsum(
                 "kij,kjd->kid", blocks[:, rs], tok_blocks, preferred_element_type=jnp.float32
-            ).astype(jnp.bfloat16).reshape(rows, width)
+            ).astype(jnp.bfloat16).reshape(rs.stop - rs.start, width)
             for rs in spans
         ]
     else:

time: 66.8 us -> 76.9 us (1.15)
  waiting for transfers between devices: 22.1 us -> 33.9 us
  starting transfers between devices: 19.9 us -> 17.7 us
    ppermute x12, waiting for transfers between devices: 21.2 us -> 32.4 us  [from_partner(): return lax.ppermute(value, axis, pairs)]
    ppermute x12, starting transfers between devices: 19 us -> 16.5 us  [from_partner(): return lax.ppermute(value, axis, pairs)]
  transfers between devices with their start and end apart: 18 -> 18, of which waited for: 10 -> 15; matrix products, arithmetic and copies ran while one was open for 15% -> 10% of each run, Pallas kernels for 12% -> 6%
where the time goes in v14:
time: 76.9 us; the launch traced here: 76.7 us
  waiting for transfers between devices  33.9 us (44%)
  starting transfers between devices  17.7 us (23%)
  other arithmetic  9.36 us (12%)
  Pallas kernels  8.32 us (11%)
  matrix products  2.58 us (3%)
  blocking collectives  2.47 us (3%)
  local copies, waits for them, and re-layouts  1.49 us (2%)
  between operations  0.85 us (1%)
    ppermute x12, waiting for transfers between devices, from_partner(): return lax.ppermute(value, axis, pairs)  32.4 us
    ppermute x12, starting transfers between devices, from_partner(): return lax.ppermute(value, axis, pairs)  16.5 us
    pallas_call x2, Pallas kernels, ffn_grad(): pl.pallas_call(ffn_kernel, grid=(groups_here // per_step,), in_specs=[act...  8.32 us
    psum x1, blocking collectives, body(): reduce_hid = hid_sum if chunk == 0 else lambda v: lax.psum(v, 'hid')  2.47 us
    reduce_sum x2, other arithmetic, body(): inner = reduce_hid(jnp.sum(resid * scaled, axis=-1))  2.36 us
    add x3, other arithmetic, hid_sum(): total = total + lax.ppermute(value, 'hid', pairs)  1.95 us
    reduce_sum x6, other arithmetic, body(): jnp.sum(back_f * mates[chunk][section].astype(jnp.float32), axis=-1)  1.66 us
    ppermute x6, waiting for transfers between devices, hid_sum(): total = total + lax.ppermute(value, 'hid', pairs)  1.55 us
  transfers between devices with their start and end apart: 18, of which 15 were waited for; matrix products, arithmetic and copies ran while one was open for 10% of the time, Pallas kernels for 6%

profile of v14, /device:TPU:0, one launch (start us, length us, event | category | flops | bytes accessed | tf_op | source)
XLA Modules:
  0.0 76.7 jit_solution(14710447100849253552)
XLA Ops:
  0.7 1.2 %convolution_convert_fusion = bf16[80,1024]{1,0:T(8,128)(2,1)S(1)} fusion(bf16[128,1024]{1,0:T(8,128)(2,1)} %param.9, bf16[1,128,128]{2,1,0:T(8,128)(2,1)} %param.11), kind=kOutput, calls=%fused_computation.3 | convolution fusion | flops 21053440 | bytes 446464 | tf_op jit(solution)/shard_map/kij,kjd->kid/dot_general | solution.py:94
  1.9 3.0 %collective-permute-start = (bf16[80,1024]{1,0:T(8,128)(2,1)S(1)}, bf16[80,1024]{1,0:T(8,128)(2,1)S(1)}, u32[]{:S(2)}, u32[]{:S(2)}) collective-permute-start(bf16[80,1024]{1,0:T(8,128)(2,1)S(1)} %convolution_convert_fusion), channel_id=1, source_target_pairs={{0,2},{2,0},{4,6},{6,4},{8,10},{10,8},{12,14},{14,12},{1,3},{3,1},... | collective-permute-start | bytes 491528 | tf_op jit(solution)/shard_map/ppermute | solution.py:14
  5.2 0.7 slice.66.cot_ref
  5.9 4.0 %collective-permute-done = bf16[80,1024]{1,0:T(8,128)(2,1)S(1)} collective-permute-done((bf16[80,1024]{1,0:T(8,128)(2,1)S(1)}, bf16[80,1024]{1,0:T(8,128)(2,1)S(1)}, u32[]{:S(2)}, u32[]{:S(2)}) %collective-permute-start) | collective-permute-done | bytes 163872 | tf_op jit(solution)/shard_map/ppermute | solution.py:14
  10.0 2.1 %collective-permute-start.1 = (bf16[80,1024]{1,0:T(8,128)(2,1)S(1)}, bf16[80,1024]{1,0:T(8,128)(2,1)S(1)}, u32[]{:S(2)}, u32[]{:S(2)}) collective-permute-start(bf16[80,1024]{1,0:T(8,128)(2,1)S(1)} %fusion.4), channel_id=1, source_target_pairs={{0,4},{2,6},{4,0},{6,2},{8,12},{10,14},{12,8},{14,10},{1,5},{3,7},... | collective-permute-start | bytes 491528 | tf_op jit(solution)/shard_map/ppermute | solution.py:14
  12.2 3.2 %collective-permute-done.1 = bf16[80,1024]{1,0:T(8,128)(2,1)S(1)} collective-permute-done((bf16[80,1024]{1,0:T(8,128)(2,1)S(1)}, bf16[80,1024]{1,0:T(8,128)(2,1)S(1)}, u32[]{:S(2)}, u32[]{:S(2)}) %collective-permute-start.1) | collective-permute-done | bytes 163872 | tf_op jit(solution)/shard_map/ppermute | solution.py:14
  15.6 3.6 %collective-permute-start.2 = (bf16[80,1024]{1,0:T(8,128)(2,1)S(1)}, bf16[80,1024]{1,0:T(8,128)(2,1)S(1)}, u32[]{:S(2)}, u32[]{:S(2)}) collective-permute-start(bf16[80,1024]{1,0:T(8,128)(2,1)S(1)} %fusion.6), channel_id=1, source_target_pairs={{0,8},{2,10},{4,12},{6,14},{8,0},{10,2},{12,4},{14,6},{1,9},{3,11}... | collective-permute-start | bytes 491528 | tf_op jit(solution)/shard_map/ppermute | solution.py:14
  19.3 1.3 %collective-permute-start.6 = (bf16[48,1024]{1,0:T(8,128)(2,1)S(1)}, bf16[48,1024]{1,0:T(8,128)(2,1)S(1)}, u32[]{:S(2)}, u32[]{:S(2)}) collective-permute-start(bf16[48,1024]{1,0:T(8,128)(2,1)S(1)} %fusion.27), channel_id=1, source_target_pairs={{0,4},{2,6},{4,0},{6,2},{8,12},{10,14},{12,8},{14,10},{1,5},{3,7},... | collective-permute-start | bytes 294920 | tf_op jit(solution)/shard_map/ppermute | solution.py:14
  20.6 3.8 %collective-permute-done.2 = bf16[80,1024]{1,0:T(8,128)(2,1)S(1)} collective-permute-done((bf16[80,1024]{1,0:T(8,128)(2,1)S(1)}, bf16[80,1024]{1,0:T(8,128)(2,1)S(1)}, u32[]{:S(2)}, u32[]{:S(2)}) %collective-permute-start.2) | collective-permute-done | bytes 163872 | tf_op jit(solution)/shard_map/ppermute | solution.py:14
  25.0 1.1 %collective-permute-start.7 = (bf16[48,1024]{1,0:T(8,128)(2,1)S(1)}, bf16[48,1024]{1,0:T(8,128)(2,1)S(1)}, u32[]{:S(2)}, u32[]{:S(2)}) collective-permute-start(bf16[48,1024]{1,0:T(8,128)(2,1)S(1)} %fusion.29), channel_id=1, source_target_pairs={{0,8},{2,10},{4,12},{6,14},{8,0},{10,2},{12,4},{14,6},{1,9},{3,11}... | collective-permute-start | bytes 294920 | tf_op jit(solution)/shard_map/ppermute | solution.py:14
  26.1 0.8 multiply_convert_fusion.normed_ref
  26.9 4.4 %shard_map.120 = f32[80,1024]{1,0:T(8,128)} custom-call(bf16[80,1024]{1,0:T(8,128)(2,1)} %multiply_convert_fusion.normed_ref, bf16[80,1024]{1,0:T(8,128)(2,1)} %slice.66.cot_ref, bf16[8,128,512]{2,1,0:T(8,128)(2,1)} %wg_ref.3, bf16[8,128,512]{2,1,0:T(8,128)(2,1)} %wu_ref.3, bf16[8,512,128]{2,1,0:T(8,128)(2,1)} %wd_ref.3), custom_call_target="tpu_custom_call" | custom-call | flops 419430400 | bytes 3801088 | tf_op jit(solution)/shard_map/pallas_call | solution.py:44
  31.2 1.2 %multiply_reduce_fusion = f32[80]{0:T(128)S(1)} fusion(f32[80,1024]{1,0:T(8,128)} %shard_map.120, bf16[80,1024]{1,0:T(8,128)(2,1)S(1)} %get-tuple-element.25, f32[1024]{0:T(1024)S(1)} %copy-done.4, bf16[128,1024]{1,0:T(8,128)(2,1)S(1)} %copy-done), kind=kLoop, calls=%fused_computation.63 | loop fusion | flops 573360 | bytes 659776 | tf_op jit(solution)/shard_map/reduce_sum | solution.py:131
  34.5 0.6 slice.75.cot_ref
  35.5 0.7 multiply_convert_fusion.1.normed_ref
  36.2 3.9 %shard_map.121 = f32[48,1024]{1,0:T(8,128)} custom-call(bf16[48,1024]{1,0:T(8,128)(2,1)} %multiply_convert_fusion.1.normed_ref, bf16[48,1024]{1,0:T(8,128)(2,1)} %slice.75.cot_ref, bf16[8,128,512]{2,1,0:T(8,128)(2,1)} %wg_ref.3, bf16[8,128,512]{2,1,0:T(8,128)(2,1)} %wu_ref.3, bf16[8,512,128]{2,1,0:T(8,128)(2,1)} %wd_ref.3), custom_call_target="tpu_custom_call" | custom-call | flops 251658240 | bytes 3538944 | tf_op jit(solution)/shard_map/pallas_call | solution.py:44
  40.1 1.1 %multiply_reduce_fusion.2 = f32[48]{0:T(128)S(1)} fusion(f32[48,1024]{1,0:T(8,128)} %shard_map.121, bf16[48,1024]{1,0:T(8,128)(2,1)S(1)} %fusion.31, f32[1024]{0:T(1024)S(1)} %copy-done.4, bf16[128,1024]{1,0:T(8,128)(2,1)S(1)} %copy-done), kind=kLoop, calls=%fused_computation.100 | loop fusion | flops 344016 | bytes 397504 | tf_op jit(solution)/shard_map/reduce_sum | solution.py:131
  41.3 2.5 %psum.7 = f32[48]{0:T(128)S(1)} all-reduce(f32[48]{0:T(128)S(1)} %multiply_reduce_fusion.2), channel_id=1, replica_groups=mesh['groups'=2,'seq'=8,'hid'=2] {'hid'}, use_global_device_ids=true, to_apply=%region_4.0 | all-reduce | flops 48 | bytes 384 | tf_op jit(solution)/shard_map/psum | solution.py:125
  44.1 1.9 %collective-permute-start.12 = (bf16[48,1024]{1,0:T(8,128)(2,1)S(1)}, bf16[48,1024]{1,0:T(8,128)(2,1)S(1)}, u32[]{:S(2)}, u32[]{:S(2)}) collective-permute-start(bf16[48,1024]{1,0:T(8,128)(2,1)S(1)} %fusion.35), channel_id=1, source_target_pairs={{0,8},{2,10},{4,12},{6,14},{8,0},{10,2},{12,4},{14,6},{1,9},{3,11}... | collective-permute-start | bytes 294920 | tf_op jit(solution)/shard_map/ppermute | solution.py:14
  46.0 1.0 %collective-permute-start.9 = (bf16[80,1024]{1,0:T(8,128)(2,1)S(1)}, bf16[80,1024]{1,0:T(8,128)(2,1)S(1)}, u32[]{:S(2)}, u32[]{:S(2)}) collective-permute-start(bf16[80,1024]{1,0:T(8,128)(2,1)S(1)} %fusion.10), channel_id=1, source_target_pairs={{0,8},{2,10},{4,12},{6,14},{8,0},{10,2},{12,4},{14,6},{1,9},{3,11}... | collective-permute-start | bytes 491528 | tf_op jit(solution)/shard_map/ppermute | solution.py:14
  47.1 9.0 %collective-permute-done.12 = bf16[48,1024]{1,0:T(8,128)(2,1)S(1)} collective-permute-done((bf16[48,1024]{1,0:T(8,128)(2,1)S(1)}, bf16[48,1024]{1,0:T(8,128)(2,1)S(1)}, u32[]{:S(2)}, u32[]{:S(2)}) %collective-permute-start.12) | collective-permute-done | bytes 98336 | tf_op jit(solution)/shard_map/ppermute | solution.py:14
  56.5 2.7 %collective-permute-done.9 = bf16[80,1024]{1,0:T(8,128)(2,1)S(1)} collective-permute-done((bf16[80,1024]{1,0:T(8,128)(2,1)S(1)}, bf16[80,1024]{1,0:T(8,128)(2,1)S(1)}, u32[]{:S(2)}, u32[]{:S(2)}) %collective-permute-start.9) | collective-permute-done | bytes 163872 | tf_op jit(solution)/shard_map/ppermute | solution.py:14
  59.5 1.7 %collective-permute-done.13 = bf16[48,1024]{1,0:T(8,128)(2,1)S(1)} collective-permute-done((bf16[48,1024]{1,0:T(8,128)(2,1)S(1)}, bf16[48,1024]{1,0:T(8,128)(2,1)S(1)}, u32[]{:S(2)}, u32[]{:S(2)}) %collective-permute-start.13) | collective-permute-done | bytes 98336 | tf_op jit(solution)/shard_map/ppermute | solution.py:14
  61.6 1.6 %collective-permute-start.14 = (bf16[48,1024]{1,0:T(8,128)(2,1)S(1)}, bf16[48,1024]{1,0:T(8,128)(2,1)S(1)}, u32[]{:S(2)}, u32[]{:S(2)}) collective-permute-start(bf16[48,1024]{1,0:T(8,128)(2,1)S(1)} %fusion.45), channel_id=1, source_target_pairs={{0,2},{2,0},{4,6},{6,4},{8,10},{10,8},{12,14},{14,12},{1,3},{3,1},... | collective-permute-start | bytes 294920 | tf_op jit(solution)/shard_map/ppermute | solution.py:14
  63.3 2.9 %collective-permute-done.14 = bf16[48,1024]{1,0:T(8,128)(2,1)S(1)} collective-permute-done((bf16[48,1024]{1,0:T(8,128)(2,1)S(1)}, bf16[48,1024]{1,0:T(8,128)(2,1)S(1)}, u32[]{:S(2)}, u32[]{:S(2)}) %collective-permute-start.14) | collective-permute-done | bytes 98336 | tf_op jit(solution)/shard_map/ppermute | solution.py:14
  66.3 2.3 %collective-permute-done.10 = bf16[80,1024]{1,0:T(8,128)(2,1)S(1)} collective-permute-done((bf16[80,1024]{1,0:T(8,128)(2,1)S(1)}, bf16[80,1024]{1,0:T(8,128)(2,1)S(1)}, u32[]{:S(2)}, u32[]{:S(2)}) %collective-permute-start.10) | collective-permute-done | bytes 163872 | tf_op jit(solution)/shard_map/ppermute | solution.py:14
  69.0 0.6 collective-permute-start.11
  70.8 0.7 fusion.69
  71.5 0.7 fusion.70
  72.1 2.2 %collective-permute-done.11 = bf16[80,1024]{1,0:T(8,128)(2,1)S(1)} collective-permute-done((bf16[80,1024]{1,0:T(8,128)(2,1)S(1)}, bf16[80,1024]{1,0:T(8,128)(2,1)S(1)}, u32[]{:S(2)}, u32[]{:S(2)}) %collective-permute-start.11) | collective-permute-done | bytes 163872 | tf_op jit(solution)/shard_map/ppermute | solution.py:14
  74.8 1.0 %fusion.1 = bf16[128,1024]{1,0:T(8,128)(2,1)} fusion(f32[48,1024]{1,0:T(8,128)S(1)} %get-tuple-element.27, f32[80,1024]{1,0:T(8,128)S(1)} %get-tuple-element.26, bf16[48,1024]{1,0:T(8,128)(2,1)S(1)} %fusion.44, bf16[80,1024]{1,0:T(8,128)(2,1)S(1)} %fusion.21, bf16[1,128,128]{2,1,0:T(8,128)(2,1)S(1)} %copy-done.5), kind=kOutput, calls=%fused_computation.2 | convolution fusion | flops 34471936 | bytes 1081344 | tf_op jit(solution)/shard_map/kij,kid->kjd/dot_general | solution.py:169
  76.1 0.6 add.125
  (66 shorter events, 7.6 us)
Async XLA Ops:
  0.6 4.2 %copy-start.5 = (bf16[1,128,128]{2,1,0:T(8,128)(2,1)S(1)}, bf16[1,128,128]{2,1,0:T(8,128)(2,1)}, u32[]{:S(2)}) copy-start(bf16[1,128,128]{2,1,0:T(8,128)(2,1)} %param.11) | copy-start | bytes 98308
  0.6 4.2 %copy-start = (bf16[128,1024]{1,0:T(8,128)(2,1)S(1)}, bf16[128,1024]{1,0:T(8,128)(2,1)}, u32[]{:S(2)}) copy-start(bf16[128,1024]{1,0:T(8,128)(2,1)} %param.9) | copy-start | bytes 786436
  1.9 3.3 %copy-start.3 = (bf16[128,1024]{1,0:T(8,128)(2,1)S(1)}, bf16[128,1024]{1,0:T(8,128)(2,1)}, u32[]{:S(2)}) copy-start(bf16[128,1024]{1,0:T(8,128)(2,1)} %param.10) | copy-start | bytes 786436
  1.9 8.0 %collective-permute-start = (bf16[80,1024]{1,0:T(8,128)(2,1)S(1)}, bf16[80,1024]{1,0:T(8,128)(2,1)S(1)}, u32[]{:S(2)}, u32[]{:S(2)}) collective-permute-start(bf16[80,1024]{1,0:T(8,128)(2,1)S(1)} %convolution_convert_fusion), channel_id=1, source_target_pairs={{0,2},{2,0},{4,6},{6,4},{8,10},{10,8},{12,14},{14,12},{1,3},{3,1},... | collective-permute-start | bytes 491528 | tf_op jit(solution)/shard_map/ppermute | solution.py:14
  5.1 0.8 %copy-start.6 = (f32[3,128]{1,0:T(4,128)S(1)}, f32[3,128]{1,0:T(4,128)}, u32[]{:S(2)}) copy-start(f32[3,128]{1,0:T(4,128)} %param.12) | copy-start | bytes 4612
  5.1 0.8 %copy-start.7 = (f32[3,128]{1,0:T(4,128)S(1)}, f32[3,128]{1,0:T(4,128)}, u32[]{:S(2)}) copy-start(f32[3,128]{1,0:T(4,128)} %param.13) | copy-start | bytes 4612
  5.1 14.1 %collective-permute-start.5 = (bf16[48,1024]{1,0:T(8,128)(2,1)S(1)}, bf16[48,1024]{1,0:T(8,128)(2,1)S(1)}, u32[]{:S(2)}, u32[]{:S(2)}) collective-permute-start(bf16[48,1024]{1,0:T(8,128)(2,1)S(1)} %convolution_convert_fusion.1), channel_id=1, source_target_pairs={{0,2},{2,0},{4,6},{6,4},{8,10},{10,8},{12,14},{14,12},{1,3},{3,1},... | collective-permute-start | bytes 294920 | tf_op jit(solution)/shard_map/ppermute | solution.py:14
  10.0 5.4 %collective-permute-start.1 = (bf16[80,1024]{1,0:T(8,128)(2,1)S(1)}, bf16[80,1024]{1,0:T(8,128)(2,1)S(1)}, u32[]{:S(2)}, u32[]{:S(2)}) collective-permute-start(bf16[80,1024]{1,0:T(8,128)(2,1)S(1)} %fusion.4), channel_id=1, source_target_pairs={{0,4},{2,6},{4,0},{6,2},{8,12},{10,14},{12,8},{14,10},{1,5},{3,7},... | collective-permute-start | bytes 491528 | tf_op jit(solution)/shard_map/ppermute | solution.py:14
  15.6 8.8 %collective-permute-start.2 = (bf16[80,1024]{1,0:T(8,128)(2,1)S(1)}, bf16[80,1024]{1,0:T(8,128)(2,1)S(1)}, u32[]{:S(2)}, u32[]{:S(2)}) collective-permute-start(bf16[80,1024]{1,0:T(8,128)(2,1)S(1)} %fusion.6), channel_id=1, source_target_pairs={{0,8},{2,10},{4,12},{6,14},{8,0},{10,2},{12,4},{14,6},{1,9},{3,11}... | collective-permute-start | bytes 491528 | tf_op jit(solution)/shard_map/ppermute | solution.py:14
  19.3 5.5 %collective-permute-start.6 = (bf16[48,1024]{1,0:T(8,128)(2,1)S(1)}, bf16[48,1024]{1,0:T(8,128)(2,1)S(1)}, u32[]{:S(2)}, u32[]{:S(2)}) collective-permute-start(bf16[48,1024]{1,0:T(8,128)(2,1)S(1)} %fusion.27), channel_id=1, source_target_pairs={{0,4},{2,6},{4,0},{6,2},{8,12},{10,14},{12,8},{14,10},{1,5},{3,7},... | collective-permute-start | bytes 294920 | tf_op jit(solution)/shard_map/ppermute | solution.py:14
  24.7 1.4 %collective-permute-start.3 = (f32[80]{0:T(128)S(1)}, f32[80]{0:T(128)S(1)}, u32[]{:S(2)}, u32[]{:S(2)}) collective-permute-start(f32[80]{0:T(128)S(1)} %get-tuple-element.24), channel_id=1, source_target_pairs={{0,1},{1,0},{2,3},{3,2},{4,5},{5,4},{6,7},{7,6},{8,9},{9,8},{10,11... | collective-permute-start | bytes 968 | tf_op jit(solution)/shard_map/ppermute | solution.py:69
  24.9 1.2 %copy-start.4 = (f32[1024]{0:T(1024)S(1)}, f32[1024]{0:T(1024)}, u32[]{:S(2)}) copy-start(f32[1024]{0:T(1024)} %param.14) | copy-start | bytes 12292
  25.0 8.1 %collective-permute-start.7 = (bf16[48,1024]{1,0:T(8,128)(2,1)S(1)}, bf16[48,1024]{1,0:T(8,128)(2,1)S(1)}, u32[]{:S(2)}, u32[]{:S(2)}) collective-permute-start(bf16[48,1024]{1,0:T(8,128)(2,1)S(1)} %fusion.29), channel_id=1, source_target_pairs={{0,8},{2,10},{4,12},{6,14},{8,0},{10,2},{12,4},{14,6},{1,9},{3,11}... | collective-permute-start | bytes 294920 | tf_op jit(solution)/shard_map/ppermute | solution.py:14
  31.2 2.4 %copy-start.1 = (f32[80,1024]{1,0:T(8,128)S(1)}, f32[80,1024]{1,0:T(8,128)}, u32[]{:S(2)}) copy-start(f32[80,1024]{1,0:T(8,128)} %shard_map.120) | copy-start | bytes 983044
  32.5 1.2 %collective-permute-start.4 = (f32[80]{0:T(128)S(1)}, f32[80]{0:T(128)S(1)}, u32[]{:S(2)}, u32[]{:S(2)}) collective-permute-start(f32[80]{0:T(128)S(1)} %multiply_reduce_fusion), channel_id=1, source_target_pairs={{0,1},{1,0},{2,3},{3,2},{4,5},{5,4},{6,7},{7,6},{8,9},{9,8},{10,11... | collective-permute-start | bytes 968 | tf_op jit(solution)/shard_map/ppermute | solution.py:69
  34.3 1.2 %collective-permute-start.8 = (f32[48]{0:T(128)S(1)}, f32[48]{0:T(128)S(1)}, u32[]{:S(2)}, u32[]{:S(2)}) collective-permute-start(f32[48]{0:T(128)S(1)} %multiply_reduce_fusion.3), channel_id=1, source_target_pairs={{0,1},{1,0},{2,3},{3,2},{4,5},{5,4},{6,7},{7,6},{8,9},{9,8},{10,11... | collective-permute-start | bytes 584 | tf_op jit(solution)/shard_map/ppermute | solution.py:69
  40.1 3.6 %copy-start.2 = (f32[48,1024]{1,0:T(8,128)S(1)}, f32[48,1024]{1,0:T(8,128)}, u32[]{:S(2)}) copy-start(f32[48,1024]{1,0:T(8,128)} %shard_map.121) | copy-start | bytes 589828
  44.1 12.0 %collective-permute-start.12 = (bf16[48,1024]{1,0:T(8,128)(2,1)S(1)}, bf16[48,1024]{1,0:T(8,128)(2,1)S(1)}, u32[]{:S(2)}, u32[]{:S(2)}) collective-permute-start(bf16[48,1024]{1,0:T(8,128)(2,1)S(1)} %fusion.35), channel_id=1, source_target_pairs={{0,8},{2,10},{4,12},{6,14},{8,0},{10,2},{12,4},{14,6},{1,9},{3,11}... | collective-permute-start | bytes 294920 | tf_op jit(solution)/shard_map/ppermute | solution.py:14
  46.0 13.2 %collective-permute-start.9 = (bf16[80,1024]{1,0:T(8,128)(2,1)S(1)}, bf16[80,1024]{1,0:T(8,128)(2,1)S(1)}, u32[]{:S(2)}, u32[]{:S(2)}) collective-permute-start(bf16[80,1024]{1,0:T(8,128)(2,1)S(1)} %fusion.10), channel_id=1, source_target_pairs={{0,8},{2,10},{4,12},{6,14},{8,0},{10,2},{12,4},{14,6},{1,9},{3,11}... | collective-permute-start | bytes 491528 | tf_op jit(solution)/shard_map/ppermute | solution.py:14
  56.5 4.8 %collective-permute-start.13 = (bf16[48,1024]{1,0:T(8,128)(2,1)S(1)}, bf16[48,1024]{1,0:T(8,128)(2,1)S(1)}, u32[]{:S(2)}, u32[]{:S(2)}) collective-permute-start(bf16[48,1024]{1,0:T(8,128)(2,1)S(1)} %fusion.40), channel_id=1, source_target_pairs={{0,4},{2,6},{4,0},{6,2},{8,12},{10,14},{12,8},{14,10},{1,5},{3,7},... | collective-permute-start | bytes 294920 | tf_op jit(solution)/shard_map/ppermute | solution.py:14
  61.6 4.7 %collective-permute-start.14 = (bf16[48,1024]{1,0:T(8,128)(2,1)S(1)}, bf16[48,1024]{1,0:T(8,128)(2,1)S(1)}, u32[]{:S(2)}, u32[]{:S(2)}) collective-permute-start(bf16[48,1024]{1,0:T(8,128)(2,1)S(1)} %fusion.45), channel_id=1, source_target_pairs={{0,2},{2,0},{4,6},{6,4},{8,10},{10,8},{12,14},{14,12},{1,3},{3,1},... | collective-permute-start | bytes 294920 | tf_op jit(solution)/shard_map/ppermute | solution.py:14
  63.2 5.4 %collective-permute-start.10 = (bf16[80,1024]{1,0:T(8,128)(2,1)S(1)}, bf16[80,1024]{1,0:T(8,128)(2,1)S(1)}, u32[]{:S(2)}, u32[]{:S(2)}) collective-permute-start(bf16[80,1024]{1,0:T(8,128)(2,1)S(1)} %fusion.17), channel_id=1, source_target_pairs={{0,4},{2,6},{4,0},{6,2},{8,12},{10,14},{12,8},{14,10},{1,5},{3,7},... | collective-permute-start | bytes 491528 | tf_op jit(solution)/shard_map/ppermute | solution.py:14
  69.0 5.4 %collective-permute-start.11 = (bf16[80,1024]{1,0:T(8,128)(2,1)S(1)}, bf16[80,1024]{1,0:T(8,128)(2,1)S(1)}, u32[]{:S(2)}, u32[]{:S(2)}) collective-permute-start(bf16[80,1024]{1,0:T(8,128)(2,1)S(1)} %fusion.22), channel_id=1, source_target_pairs={{0,2},{2,0},{4,6},{6,4},{8,10},{10,8},{12,14},{14,12},{1,3},{3,1},... | collective-permute-start | bytes 491528 | tf_op jit(solution)/shard_map/ppermute | solution.py:14
  69.6 1.2 %collective-permute-start.16 = (f32[3,128]{1,0:T(4,128)S(1)}, f32[3,128]{1,0:T(4,128)S(1)}, u32[]{:S(2)}, u32[]{:S(2)}) collective-permute-start(f32[3,128]{1,0:T(4,128)S(1)} %maximum_maximum_fusion.1), channel_id=1, source_target_pairs={{0,1},{1,0},{2,3},{3,2},{4,5},{5,4},{6,7},{7,6},{8,9},{9,8},{10,11... | collective-permute-start | bytes 4616 | tf_op jit(solution)/shard_map/ppermute | solution.py:69
  69.7 1.7 %collective-permute-start.15 = (f32[3,128]{1,0:T(4,128)S(1)}, f32[3,128]{1,0:T(4,128)S(1)}, u32[]{:S(2)}, u32[]{:S(2)}) collective-permute-start(f32[3,128]{1,0:T(4,128)S(1)} %maximum_maximum_fusion), channel_id=1, source_target_pairs={{0,1},{1,0},{2,3},{3,2},{4,5},{5,4},{6,7},{7,6},{8,9},{9,8},{10,11... | collective-permute-start | bytes 4616 | tf_op jit(solution)/shard_map/ppermute | solution.py:69
  74.7 1.3 %collective-permute-start.17 = (f32[1,128,128]{2,1,0:T(8,128)S(1)}, f32[1,128,128]{2,1,0:T(8,128)S(1)}, u32[]{:S(2)}, u32[]{:S(2)}) collective-permute-start(f32[1,128,128]{2,1,0:T(8,128)S(1)} %convolution_bitcast_fusion.1), channel_id=1, source_target_pairs={{0,1},{1,0},{2,3},{3,2},{4,5},{5,4},{6,7},{7,6},{8,9},{9,8},{10,11... | collective-permute-start | bytes 196616 | tf_op jit(solution)/shard_map/ppermute | solution.py:69

commit v15 on v13

--- a/solution.py
+++ b/solution.py
@@ -14,30 +14,32 @@
     return lax.ppermute(value, axis, pairs)
 
 
-def ffn_kernel(normed_ref, cot_ref, wg_ref, wu_ref, wd_ref, out_ref):
-    cblock = wg_ref.shape[1]
+def ffn_kernel(normed_ref, cot_ref, wgu_ref, wd_ref, out_ref):
+    cblock = wgu_ref.shape[1]
+    hidden = wd_ref.shape[1]
     contract_last = (((1,), (1,)), ((), ()))
-    for group in range(wg_ref.shape[0]):
+    for group in range(wgu_ref.shape[0]):
         cols = slice(group * cblock, (group + 1) * cblock)
-        normed = normed_ref[:, cols]
-        w_gate = wg_ref[group]
-        w_up = wu_ref[group]
-        gate_pre = jnp.dot(normed, w_gate, preferred_element_type=jnp.float32)
-        up_val = jnp.dot(normed, w_up, preferred_element_type=jnp.float32)
+        w_both = wgu_ref[group]
+        both = jnp.dot(normed_ref[:, cols], w_both, preferred_element_type=jnp.float32)
+        gate_pre = both[:, :hidden]
+        up_val = both[:, hidden:]
         d_hidden = lax.dot_general(
             cot_ref[:, cols], wd_ref[group], contract_last, preferred_element_type=jnp.float32
         )
         sig = 1.0 / (1.0 + jnp.exp(-gate_pre))
         d_up = (d_hidden * gate_pre * sig).astype(jnp.bfloat16)
         d_gate = (d_hidden * up_val * sig * (1.0 + gate_pre * (1.0 - sig))).astype(jnp.bfloat16)
+        d_both = jnp.concatenate([d_gate, d_up], axis=1)
         out_ref[:, cols] = lax.dot_general(
-            d_gate, w_gate, contract_last, preferred_element_type=jnp.float32
-        ) + lax.dot_general(d_up, w_up, contract_last, preferred_element_type=jnp.float32)
+            d_both, w_both, contract_last, preferred_element_type=jnp.float32
+        )
 
 
-def ffn_grad(normed, cotangent, w_gate, w_up, w_down, per_step=4):
+def ffn_grad(normed, cotangent, w_both, w_down, per_step=4):
     tok, width = normed.shape
-    groups_here, cblock, hidden = w_gate.shape
+    groups_here, cblock, hidden2 = w_both.shape
+    hidden = w_down.shape[1]
     if groups_here % per_step:
         per_step = 1
     act = pl.BlockSpec((tok, cblock * per_step), lambda g: (0, g))
@@ -47,8 +49,7 @@
         in_specs=[
             act,
             act,
-            pl.BlockSpec((per_step, cblock, hidden), lambda g: (g, 0, 0)),
-            pl.BlockSpec((per_step, cblock, hidden), lambda g: (g, 0, 0)),
+            pl.BlockSpec((per_step, cblock, hidden2), lambda g: (g, 0, 0)),
             pl.BlockSpec((per_step, hidden, cblock), lambda g: (g, 0, 0)),
         ],
         out_specs=act,
@@ -58,7 +59,7 @@
             transcendentals=tok * hidden * groups_here,
             bytes_accessed=3 * groups_here * cblock * hidden * 2 + tok * width * 8,
         ),
-    )(normed, cotangent, w_gate, w_up, w_down)
+    )(normed, cotangent, w_both, w_down)
 
 
 def hid_sum(value):
@@ -82,6 +83,7 @@
     nblk = blocks.shape[0]
     blen = blocks.shape[1]
     tok_blocks = tokens.reshape(nblk, blen, width)
+    w_both = jnp.concatenate([w_gate, w_up], axis=-1)
     chunks = CHUNKS if tok % CHUNKS == 0 else 1
     rows = tok // chunks
     spans = [slice(chunk * rows, (chunk + 1) * rows) for chunk in range(chunks)]
@@ -124,7 +126,7 @@
         square = hid_sum(jnp.sum(resid * resid, axis=-1))
         inv = lax.rsqrt(square / D + 1e-06)
         normed = (resid * inv[:, None] * norm_gain).astype(jnp.bfloat16)
-        d_normed = ffn_grad(normed, cot, w_gate, w_up, w_down)
+        d_normed = ffn_grad(normed, cot, w_both, w_down)
         scaled = norm_gain * d_normed
         inner = reduce_hid(jnp.sum(resid * scaled, axis=-1))
         d_resid = (

time: 66.8 us -> 72.2 us (1.081)
  other arithmetic: 9.3 us -> 13.2 us
  local copies, waits for them, and re-layouts: 1.2 us -> 4.85 us
  waiting for transfers between devices: 22.1 us -> 19.7 us
  starting transfers between devices: 19.9 us -> 18.5 us
  matrix products: 2.57 us -> 3.57 us
    ppermute x12, waiting for transfers between devices: 21.2 us -> 17.9 us  [from_partner(): return lax.ppermute(value, axis, pairs)]
    reduce_sum x6, other arithmetic: 1.65 us -> 3.74 us  [body(): jnp.sum(back_f * mates[chunk][section].astype(jnp.float32), axis=-1)]
    mul x1, local copies, waits for them, and re-layouts: 0.07 us -> 1.53 us  [body(): coef_cross[section, rs][:, None] * mate.astype(jnp.float32)]
    ppermute x12, starting transfers between devices: 19 us -> 17.6 us  [from_partner(): return lax.ppermute(value, axis, pairs)]
    unnamed x16 -> x65, local copies, waits for them, and re-layouts: 0.42 us -> 1.49 us
    ppermute x6, waiting for transfers between devices: 0.84 us -> 1.86 us  [hid_sum(): total = total + lax.ppermute(value, 'hid', pairs)]
    dot_general x2, matrix products: 1.36 us -> 2.37 us  [body(): jnp.einsum('kij,kjd->kid', blocks[:, rs], tok_blocks, preferred_element_t...]
    slice x1, local copies, waits for them, and re-layouts: 0.71 us -> 1.69 us  [body(): cot = cotangent[rs]]
  transfers between devices with their start and end apart: 18 -> 18, of which waited for: 10 -> 9; matrix products, arithmetic and copies ran while one was open for 15% -> 25% of each run, Pallas kernels for 12% -> 11%
where the time goes in v15:
time: 72.2 us; the launch traced here: 71.8 us
  waiting for transfers between devices  19.7 us (27%)
  starting transfers between devices  18.5 us (26%)
  other arithmetic  13.2 us (18%)
  Pallas kernels  8.25 us (11%)
  local copies, waits for them, and re-layouts  4.85 us (7%)
  matrix products  3.57 us (5%)
  blocking collectives  2.47 us (3%)
  between operations  1.16 us (2%)
    ppermute x12, waiting for transfers between devices, from_partner(): return lax.ppermute(value, axis, pairs)  17.9 us
    ppermute x12, starting transfers between devices, from_partner(): return lax.ppermute(value, axis, pairs)  17.6 us
    pallas_call x2, Pallas kernels, ffn_grad(): pl.pallas_call(ffn_kernel, grid=(groups_here // per_step,), in_specs=[act...  8.25 us
    reduce_sum x6, other arithmetic, body(): jnp.sum(back_f * mates[chunk][section].astype(jnp.float32), axis=-1)  3.74 us
    psum x1, blocking collectives, body(): reduce_hid = hid_sum if chunk == 0 else lambda v: lax.psum(v, 'hid')  2.47 us
    dot_general x2, matrix products, body(): jnp.einsum('kij,kjd->kid', blocks[:, rs], tok_blocks, preferred_element_t...  2.37 us
    reduce_sum x2, other arithmetic, body(): inner = reduce_hid(jnp.sum(resid * scaled, axis=-1))  2.32 us
    add x3, other arithmetic, hid_sum(): total = total + lax.ppermute(value, 'hid', pairs)  1.95 us
  transfers between devices with their start and end apart: 18, of which 9 were waited for; matrix products, arithmetic and copies ran while one was open for 25% of the time, Pallas kernels for 11%

profile of v15, /device:TPU:0, one launch (start us, length us, event | category | flops | bytes accessed | tf_op | source)
XLA Modules:
  0.0 71.8 jit_solution(16899629246607448885)
XLA Ops:
  0.6 1.2 %convolution_convert_fusion.1 = bf16[64,1024]{1,0:T(8,128)(2,1)S(1)} fusion(bf16[128,1024]{1,0:T(8,128)(2,1)} %param.9, bf16[1,128,128]{2,1,0:T(8,128)(2,1)} %param.11), kind=kOutput, calls=%fused_computation.4 | convolution fusion | flops 16842752 | bytes 409600 | tf_op jit(solution)/shard_map/kij,kjd->kid/dot_general | solution.py:94
  1.9 3.0 %collective-permute-start = (bf16[64,1024]{1,0:T(8,128)(2,1)S(1)}, bf16[64,1024]{1,0:T(8,128)(2,1)S(1)}, u32[]{:S(2)}, u32[]{:S(2)}) collective-permute-start(bf16[64,1024]{1,0:T(8,128)(2,1)S(1)} %convolution_convert_fusion.1), channel_id=1, source_target_pairs={{0,2},{2,0},{4,6},{6,4},{8,10},{10,8},{12,14},{14,12},{1,3},{3,1},... | collective-permute-start | bytes 393224 | tf_op jit(solution)/shard_map/ppermute | solution.py:14
  4.9 1.1 %convolution_convert_fusion = bf16[64,1024]{1,0:T(8,128)(2,1)S(1)} fusion(bf16[128,1024]{1,0:T(8,128)(2,1)} %param.9, bf16[1,128,128]{2,1,0:T(8,128)(2,1)} %param.11), kind=kOutput, calls=%fused_computation.3 | convolution fusion | flops 16842752 | bytes 409600 | tf_op jit(solution)/shard_map/kij,kjd->kid/dot_general | solution.py:94
  6.1 1.7 %fusion.66 = (bf16[64,1024]{1,0:T(8,128)(2,1)}, bf16[64,1024]{1,0:T(8,128)(2,1)}) fusion(bf16[128,1024]{1,0:T(8,128)(2,1)} %param.10), kind=kLoop, calls=%fused_computation.134 | loop fusion | bytes 524288 | tf_op jit(solution)/shard_map/slice | solution.py:121
  7.8 1.5 %slice_bitcast_fusion.6 = (f32[64]{0:T(128)S(1)}, f32[64]{0:T(128)S(1)}, f32[64]{0:T(128)S(1)}, f32[64]{0:T(128)S(1)}, f32[64]{0:T(128)}, /*index=5*/f32[64]{0:T...) fusion(f32[3,128]{1,0:T(4,128)} %param.13, ...), kind=kLoop, calls=%fused_computation.124 | loop fusion | bytes 6144 | tf_op jit(solution)/shard_map/mul | solution.py:112
  9.4 1.4 %constant_dynamic-update-slice_fusion.1 = bf16[8,128,1024]{2,1,0:T(8,128)(2,1)S(1)} fusion(bf16[8,128,512]{2,1,0:T(8,128)(2,1)} %param.15), kind=kLoop, calls=%fused_computation.109 | loop fusion | bytes 2097152
  10.9 2.2 %collective-permute-start.1 = (bf16[64,1024]{1,0:T(8,128)(2,1)S(1)}, bf16[64,1024]{1,0:T(8,128)(2,1)S(1)}, u32[]{:S(2)}, u32[]{:S(2)}) collective-permute-start(bf16[64,1024]{1,0:T(8,128)(2,1)S(1)} %fusion.4), channel_id=1, source_target_pairs={{0,4},{2,6},{4,0},{6,2},{8,12},{10,14},{12,8},{14,10},{1,5},{3,7},... | collective-permute-start | bytes 393224 | tf_op jit(solution)/shard_map/ppermute | solution.py:14
  13.3 2.8 %collective-permute-done.1 = bf16[64,1024]{1,0:T(8,128)(2,1)S(1)} collective-permute-done((bf16[64,1024]{1,0:T(8,128)(2,1)S(1)}, bf16[64,1024]{1,0:T(8,128)(2,1)S(1)}, u32[]{:S(2)}, u32[]{:S(2)}) %collective-permute-start.1) | collective-permute-done | bytes 131104 | tf_op jit(solution)/shard_map/ppermute | solution.py:14
  16.2 3.1 %collective-permute-start.2 = (bf16[64,1024]{1,0:T(8,128)(2,1)S(1)}, bf16[64,1024]{1,0:T(8,128)(2,1)}, u32[]{:S(2)}, u32[]{:S(2)}) collective-permute-start(bf16[64,1024]{1,0:T(8,128)(2,1)S(1)} %fusion.6), channel_id=1, source_target_pairs={{0,8},{2,10},{4,12},{6,14},{8,0},{10,2},{12,4},{14,6},{1,9},{3,11}... | collective-permute-start | bytes 393224 | tf_op jit(solution)/shard_map/ppermute | solution.py:14
  19.4 1.6 %collective-permute-start.6 = (bf16[64,1024]{1,0:T(8,128)(2,1)S(1)}, bf16[64,1024]{1,0:T(8,128)(2,1)S(1)}, u32[]{:S(2)}, u32[]{:S(2)}) collective-permute-start(bf16[64,1024]{1,0:T(8,128)(2,1)S(1)} %fusion.12), channel_id=1, source_target_pairs={{0,4},{2,6},{4,0},{6,2},{8,12},{10,14},{12,8},{14,10},{1,5},{3,7},... | collective-permute-start | bytes 393224 | tf_op jit(solution)/shard_map/ppermute | solution.py:14
  21.1 3.1 %collective-permute-done.2 = bf16[64,1024]{1,0:T(8,128)(2,1)} collective-permute-done((bf16[64,1024]{1,0:T(8,128)(2,1)S(1)}, bf16[64,1024]{1,0:T(8,128)(2,1)}, u32[]{:S(2)}, u32[]{:S(2)}) %collective-permute-start.2) | collective-permute-done | bytes 131104 | tf_op jit(solution)/shard_map/ppermute | solution.py:14
  24.2 1.2 %multiply_reduce_fusion.3 = (f32[64]{0:T(128)S(1)}, bf16[64,1024]{1,0:T(8,128)(2,1)S(1)}) fusion(bf16[128,1024]{1,0:T(8,128)(2,1)S(1)} %copy-done.1, bf16[64,1024]{1,0:T(8,128)(2,1)} %collective-permute-done.2, f32[64]{0:T(128)S(1)} %get-tuple-element.36, bf16[64,1024]{1,0:T(8,128)(2,1)S(1)} %fusion.6, f32[64]{0:T(128)S(1)} %get-tuple-element.47), kind=kLoop, calls=%fused_computation.102 | loop fusion | flops 786368 | bytes 525056 | tf_op jit(solution)/shard_map/reduce_sum | solution.py:126
  25.6 1.3 %collective-permute-start.7 = (bf16[64,1024]{1,0:T(8,128)(2,1)S(1)}, bf16[64,1024]{1,0:T(8,128)(2,1)}, u32[]{:S(2)}, u32[]{:S(2)}) collective-permute-start(bf16[64,1024]{1,0:T(8,128)(2,1)S(1)} %fusion.14), channel_id=1, source_target_pairs={{0,8},{2,10},{4,12},{6,14},{8,0},{10,2},{12,4},{14,6},{1,9},{3,11}... | collective-permute-start | bytes 393224 | tf_op jit(solution)/shard_map/ppermute | solution.py:14
  27.7 4.1 %shard_map.120 = f32[64,1024]{1,0:T(8,128)} custom-call(bf16[64,1024]{1,0:T(8,128)(2,1)} %multiply_convert_fusion.1.normed_ref, bf16[64,1024]{1,0:T(8,128)(2,1)} %get-tuple-element.29.cot_ref, bf16[8,128,1024]{2,1,0:T(8,128)(2,1)} %copy-done, bf16[8,512,128]{2,1,0:T(8,128)(2,1)} %wd_ref.3), custom_call_target="tpu_custom_call" | custom-call | flops 335544320 | bytes 3670016 | tf_op jit(solution)/shard_map/pallas_call | solution.py:46
  31.8 1.1 %multiply_reduce_fusion.2 = f32[64]{0:T(128)S(1)} fusion(f32[64,1024]{1,0:T(8,128)} %shard_map.120, bf16[64,1024]{1,0:T(8,128)(2,1)S(1)} %get-tuple-element.25, f32[1024]{0:T(1024)S(1)} %copy-done.12, bf16[128,1024]{1,0:T(8,128)(2,1)S(1)} %copy-done.1), kind=kLoop, calls=%fused_computation.100 | loop fusion | flops 458688 | bytes 528640 | tf_op jit(solution)/shard_map/reduce_sum | solution.py:131
  33.2 2.1 %collective-permute-done.7 = bf16[64,1024]{1,0:T(8,128)(2,1)} collective-permute-done((bf16[64,1024]{1,0:T(8,128)(2,1)S(1)}, bf16[64,1024]{1,0:T(8,128)(2,1)}, u32[]{:S(2)}, u32[]{:S(2)}) %collective-permute-start.7) | collective-permute-done | bytes 131104 | tf_op jit(solution)/shard_map/ppermute | solution.py:14
  35.3 1.0 %fusion.16 = bf16[64,1024]{1,0:T(8,128)(2,1)S(1)} fusion(bf16[64,1024]{1,0:T(8,128)(2,1)S(1)} %fusion.14, bf16[64,1024]{1,0:T(8,128)(2,1)} %collective-permute-done.7, f32[64]{0:T(128)} %get-tuple-element.40, f32[64]{0:T(128)} %get-tuple-element.46), kind=kLoop, calls=%fused_computation.62 | loop fusion | flops 393216 | bytes 393728 | tf_op jit(solution)/shard_map/convert_element_type | solution.py:113
  36.4 1.3 %fusion.22 = (f32[64]{0:T(128)S(1)}, f32[64]{0:T(128)S(1)}, bf16[64,1024]{1,0:T(8,128)(2,1)S(1)}, f32[64,1024]{1,0:T(8,128)S(1)}) fusion(bf16[64,1024]{1,0:T(8,128)(2,1)} %collective-permute-done.2, bf16[64,1024]{1,0:T(8,128)(2,1)S(1)} %fusion.6, f32[64]{0:T(128)S(1)} %fusion.56, bf16[64,1024]{1,0:T(8,128)(2,1)S(1)} %get-tuple-element.25, ...), kind=kLoop, calls=%fused_computation.68 | loop fusion | flops 1376128 | bytes 1315840 | tf_op jit(solution)/shard_map/reduce_sum | solution.py:151
  38.2 1.0 %collective-permute-done.8 = f32[64]{0:T(128)S(1)} collective-permute-done((f32[64]{0:T(128)S(1)}, f32[64]{0:T(128)S(1)}, u32[]{:S(2)}, u32[]{:S(2)}) %collective-permute-start.8) | collective-permute-done | bytes 288 | tf_op jit(solution)/shard_map/ppermute | solution.py:70
  39.2 0.7 %multiply_convert_fusion.normed_ref = bf16[64,1024]{1,0:T(8,128)(2,1)} fusion(bf16[64,1024]{1,0:T(8,128)(2,1)S(1)} %fusion.16, f32[64]{0:T(128)S(1)} %add_rsqrt_fusion, f32[1024]{0:T(1024)S(1)} %copy-done.12, bf16[128,1024]{1,0:T(8,128)(2,1)S(1)} %copy-done.1), kind=kLoop, calls=%fused_computation.97 | loop fusion | flops 458752 | bytes 397568 | tf_op jit(solution)/shard_map/convert_element_type | solution.py:128
  39.9 4.1 %shard_map.121 = f32[64,1024]{1,0:T(8,128)} custom-call(bf16[64,1024]{1,0:T(8,128)(2,1)} %multiply_convert_fusion.normed_ref, bf16[64,1024]{1,0:T(8,128)(2,1)} %get-tuple-element.28.cot_ref, bf16[8,128,1024]{2,1,0:T(8,128)(2,1)} %copy-done, bf16[8,512,128]{2,1,0:T(8,128)(2,1)} %wd_ref.3), custom_call_target="tpu_custom_call" | custom-call | flops 335544320 | bytes 3670016 | tf_op jit(solution)/shard_map/pallas_call | solution.py:46
  44.1 1.2 %multiply_reduce_fusion = f32[64]{0:T(128)S(1)} fusion(f32[64,1024]{1,0:T(8,128)} %shard_map.121, bf16[64,1024]{1,0:T(8,128)(2,1)S(1)} %fusion.16, f32[1024]{0:T(1024)S(1)} %copy-done.12, bf16[128,1024]{1,0:T(8,128)(2,1)S(1)} %copy-done.1), kind=kLoop, calls=%fused_computation.96 | loop fusion | flops 458688 | bytes 528640 | tf_op jit(solution)/shard_map/reduce_sum | solution.py:131
  45.3 2.5 %psum.7 = f32[64]{0:T(128)S(1)} all-reduce(f32[64]{0:T(128)S(1)} %multiply_reduce_fusion), channel_id=1, replica_groups=mesh['groups'=2,'seq'=8,'hid'=2] {'hid'}, use_global_device_ids=true, to_apply=%region_4.0 | all-reduce | flops 64 | bytes 512 | tf_op jit(solution)/shard_map/psum | solution.py:125
  47.8 1.4 %fusion.37 = (f32[64]{0:T(128)S(1)}, f32[64]{0:T(128)S(1)}, bf16[64,1024]{1,0:T(8,128)(2,1)S(1)}, f32[64,1024]{1,0:T(8,128)S(1)}) fusion(bf16[64,1024]{1,0:T(8,128)(2,1)} %collective-permute-done.7, bf16[64,1024]{1,0:T(8,128)(2,1)S(1)} %fusion.14, f32[64]{0:T(128)S(1)} %fusion.55, bf16[64,1024]{1,0:T(8,128)(2,1)S(1)} %fusion.16, ...), kind=kLoop, calls=%fused_computation.83 | loop fusion | flops 1376128 | bytes 1315840 | tf_op jit(solution)/shard_map/reduce_sum | solution.py:151
  49.3 1.9 %collective-permute-start.12 = (bf16[64,1024]{1,0:T(8,128)(2,1)S(1)}, bf16[64,1024]{1,0:T(8,128)(2,1)S(1)}, u32[]{:S(2)}, u32[]{:S(2)}) collective-permute-start(bf16[64,1024]{1,0:T(8,128)(2,1)S(1)} %fusion.35), channel_id=1, source_target_pairs={{0,8},{2,10},{4,12},{6,14},{8,0},{10,2},{12,4},{14,6},{1,9},{3,11}... | collective-permute-start | bytes 393224 | tf_op jit(solution)/shard_map/ppermute | solution.py:14
  51.6 0.9 %collective-permute-start.10 = (bf16[64,1024]{1,0:T(8,128)(2,1)S(1)}, bf16[64,1024]{1,0:T(8,128)(2,1)S(1)}, u32[]{:S(2)}, u32[]{:S(2)}) collective-permute-start(bf16[64,1024]{1,0:T(8,128)(2,1)S(1)} %fusion.25), channel_id=1, source_target_pairs={{0,4},{2,6},{4,0},{6,2},{8,12},{10,14},{12,8},{14,10},{1,5},{3,7},... | collective-permute-start | bytes 393224 | tf_op jit(solution)/shard_map/ppermute | solution.py:14
  52.6 6.1 %collective-permute-done.12 = bf16[64,1024]{1,0:T(8,128)(2,1)S(1)} collective-permute-done((bf16[64,1024]{1,0:T(8,128)(2,1)S(1)}, bf16[64,1024]{1,0:T(8,128)(2,1)S(1)}, u32[]{:S(2)}, u32[]{:S(2)}) %collective-permute-start.12) | collective-permute-done | bytes 131104 | tf_op jit(solution)/shard_map/ppermute | solution.py:14
  59.5 1.6 %collective-permute-start.11 = (bf16[64,1024]{1,0:T(8,128)(2,1)S(1)}, bf16[64,1024]{1,0:T(8,128)(2,1)S(1)}, u32[]{:S(2)}, u32[]{:S(2)}) collective-permute-start(bf16[64,1024]{1,0:T(8,128)(2,1)S(1)} %fusion.30), channel_id=1, source_target_pairs={{0,2},{2,0},{4,6},{6,4},{8,10},{10,8},{12,14},{14,12},{1,3},{3,1},... | collective-permute-start | bytes 393224 | tf_op jit(solution)/shard_map/ppermute | solution.py:14
  61.1 3.0 %collective-permute-done.13 = bf16[64,1024]{1,0:T(8,128)(2,1)S(1)} collective-permute-done((bf16[64,1024]{1,0:T(8,128)(2,1)S(1)}, bf16[64,1024]{1,0:T(8,128)(2,1)S(1)}, u32[]{:S(2)}, u32[]{:S(2)}) %collective-permute-start.13) | collective-permute-done | bytes 131104 | tf_op jit(solution)/shard_map/ppermute | solution.py:14
  64.5 1.6 %collective-permute-start.14 = (bf16[64,1024]{1,0:T(8,128)(2,1)S(1)}, bf16[64,1024]{1,0:T(8,128)(2,1)S(1)}, u32[]{:S(2)}, u32[]{:S(2)}) collective-permute-start(bf16[64,1024]{1,0:T(8,128)(2,1)S(1)} %fusion.45), channel_id=1, source_target_pairs={{0,2},{2,0},{4,6},{6,4},{8,10},{10,8},{12,14},{14,12},{1,3},{3,1},... | collective-permute-start | bytes 393224 | tf_op jit(solution)/shard_map/ppermute | solution.py:14
  68.7 0.8 %collective-permute-done.14 = bf16[64,1024]{1,0:T(8,128)(2,1)S(1)} collective-permute-done((bf16[64,1024]{1,0:T(8,128)(2,1)S(1)}, bf16[64,1024]{1,0:T(8,128)(2,1)S(1)}, u32[]{:S(2)}, u32[]{:S(2)}) %collective-permute-start.14) | collective-permute-done | bytes 131104 | tf_op jit(solution)/shard_map/ppermute | solution.py:14
  69.9 1.0 %fusion.1 = bf16[128,1024]{1,0:T(8,128)(2,1)} fusion(f32[64,1024]{1,0:T(8,128)S(1)} %get-tuple-element.26, f32[64,1024]{1,0:T(8,128)S(1)} %get-tuple-element.27, bf16[64,1024]{1,0:T(8,128)(2,1)S(1)} %fusion.44, bf16[64,1024]{1,0:T(8,128)(2,1)S(1)} %fusion.29, bf16[1,128,128]{2,1,0:T(8,128)(2,1)S(1)} %copy-done.13), kind=kOutput, calls=%fused_computation.2 | convolution fusion | flops 34471936 | bytes 1081344 | tf_op jit(solution)/shard_map/kij,kid->kjd/dot_general | solution.py:169
  (113 shorter events, 7.8 us)
Async XLA Ops:
  1.9 8.9 %collective-permute-start = (bf16[64,1024]{1,0:T(8,128)(2,1)S(1)}, bf16[64,1024]{1,0:T(8,128)(2,1)S(1)}, u32[]{:S(2)}, u32[]{:S(2)}) collective-permute-start(bf16[64,1024]{1,0:T(8,128)(2,1)S(1)} %convolution_convert_fusion.1), channel_id=1, source_target_pairs={{0,2},{2,0},{4,6},{6,4},{8,10},{10,8},{12,14},{14,12},{1,3},{3,1},... | collective-permute-start | bytes 393224 | tf_op jit(solution)/shard_map/ppermute | solution.py:14
  6.0 13.3 %collective-permute-start.5 = (bf16[64,1024]{1,0:T(8,128)(2,1)S(1)}, bf16[64,1024]{1,0:T(8,128)(2,1)S(1)}, u32[]{:S(2)}, u32[]{:S(2)}) collective-permute-start(bf16[64,1024]{1,0:T(8,128)(2,1)S(1)} %convolution_convert_fusion), channel_id=1, source_target_pairs={{0,2},{2,0},{4,6},{6,4},{8,10},{10,8},{12,14},{14,12},{1,3},{3,1},... | collective-permute-start | bytes 393224 | tf_op jit(solution)/shard_map/ppermute | solution.py:14
  9.4 14.8 %copy-start.23 = (f32[64]{0:T(128)}, f32[64]{0:T(128)S(1)}, u32[]{:S(2)}) copy-start(f32[64]{0:T(128)S(1)} %get-tuple-element.36) | copy-start | bytes 772
  9.4 14.8 %copy-start.30 = (f32[64]{0:T(128)}, f32[64]{0:T(128)S(1)}, u32[]{:S(2)}) copy-start(f32[64]{0:T(128)S(1)} %get-tuple-element.47) | copy-start | bytes 772
  9.4 16.1 %copy-start.18 = (f32[64]{0:T(128)}, f32[64]{0:T(128)S(1)}, u32[]{:S(2)}) copy-start(f32[64]{0:T(128)S(1)} %get-tuple-element.41) | copy-start | bytes 772
  9.4 16.1 %copy-start.25 = (f32[64]{0:T(128)}, f32[64]{0:T(128)S(1)}, u32[]{:S(2)}) copy-start(f32[64]{0:T(128)S(1)} %get-tuple-element.42) | copy-start | bytes 772
  10.8 16.1 %copy-start.12 = (f32[1024]{0:T(1024)S(1)}, f32[1024]{0:T(1024)}, u32[]{:S(2)}) copy-start(f32[1024]{0:T(1024)} %param.14) | copy-start | bytes 12292
  10.9 5.1 %collective-permute-start.1 = (bf16[64,1024]{1,0:T(8,128)(2,1)S(1)}, bf16[64,1024]{1,0:T(8,128)(2,1)S(1)}, u32[]{:S(2)}, u32[]{:S(2)}) collective-permute-start(bf16[64,1024]{1,0:T(8,128)(2,1)S(1)} %fusion.4), channel_id=1, source_target_pairs={{0,4},{2,6},{4,0},{6,2},{8,12},{10,14},{12,8},{14,10},{1,5},{3,7},... | collective-permute-start | bytes 393224 | tf_op jit(solution)/shard_map/ppermute | solution.py:14
  16.2 8.0 %collective-permute-start.2 = (bf16[64,1024]{1,0:T(8,128)(2,1)S(1)}, bf16[64,1024]{1,0:T(8,128)(2,1)}, u32[]{:S(2)}, u32[]{:S(2)}) collective-permute-start(bf16[64,1024]{1,0:T(8,128)(2,1)S(1)} %fusion.6), channel_id=1, source_target_pairs={{0,8},{2,10},{4,12},{6,14},{8,0},{10,2},{12,4},{14,6},{1,9},{3,11}... | collective-permute-start | bytes 393224 | tf_op jit(solution)/shard_map/ppermute | solution.py:14
  19.4 6.0 %collective-permute-start.6 = (bf16[64,1024]{1,0:T(8,128)(2,1)S(1)}, bf16[64,1024]{1,0:T(8,128)(2,1)S(1)}, u32[]{:S(2)}, u32[]{:S(2)}) collective-permute-start(bf16[64,1024]{1,0:T(8,128)(2,1)S(1)} %fusion.12), channel_id=1, source_target_pairs={{0,4},{2,6},{4,0},{6,2},{8,12},{10,14},{12,8},{14,10},{1,5},{3,7},... | collective-permute-start | bytes 393224 | tf_op jit(solution)/shard_map/ppermute | solution.py:14
  25.3 1.6 %collective-permute-start.3 = (f32[64]{0:T(128)S(1)}, f32[64]{0:T(128)S(1)}, u32[]{:S(2)}, u32[]{:S(2)}) collective-permute-start(f32[64]{0:T(128)S(1)} %get-tuple-element.24), channel_id=1, source_target_pairs={{0,1},{1,0},{2,3},{3,2},{4,5},{5,4},{6,7},{7,6},{8,9},{9,8},{10,11... | collective-permute-start | bytes 776 | tf_op jit(solution)/shard_map/ppermute | solution.py:70
  25.6 9.8 %collective-permute-start.7 = (bf16[64,1024]{1,0:T(8,128)(2,1)S(1)}, bf16[64,1024]{1,0:T(8,128)(2,1)}, u32[]{:S(2)}, u32[]{:S(2)}) collective-permute-start(bf16[64,1024]{1,0:T(8,128)(2,1)S(1)} %fusion.14), channel_id=1, source_target_pairs={{0,8},{2,10},{4,12},{6,14},{8,0},{10,2},{12,4},{14,6},{1,9},{3,11}... | collective-permute-start | bytes 393224 | tf_op jit(solution)/shard_map/ppermute | solution.py:14
  32.9 3.4 %collective-permute-start.4 = (f32[64]{0:T(128)S(1)}, f32[64]{0:T(128)S(1)}, u32[]{:S(2)}, u32[]{:S(2)}) collective-permute-start(f32[64]{0:T(128)S(1)} %multiply_reduce_fusion.2), channel_id=1, source_target_pairs={{0,1},{1,0},{2,3},{3,2},{4,5},{5,4},{6,7},{7,6},{8,9},{9,8},{10,11... | collective-permute-start | bytes 776 | tf_op jit(solution)/shard_map/ppermute | solution.py:70
  38.0 1.2 %collective-permute-start.8 = (f32[64]{0:T(128)S(1)}, f32[64]{0:T(128)S(1)}, u32[]{:S(2)}, u32[]{:S(2)}) collective-permute-start(f32[64]{0:T(128)S(1)} %multiply_reduce_fusion.1), channel_id=1, source_target_pairs={{0,1},{1,0},{2,3},{3,2},{4,5},{5,4},{6,7},{7,6},{8,9},{9,8},{10,11... | collective-permute-start | bytes 776 | tf_op jit(solution)/shard_map/ppermute | solution.py:70
  38.1 13.2 %collective-permute-start.9 = (bf16[64,1024]{1,0:T(8,128)(2,1)S(1)}, bf16[64,1024]{1,0:T(8,128)(2,1)S(1)}, u32[]{:S(2)}, u32[]{:S(2)}) collective-permute-start(bf16[64,1024]{1,0:T(8,128)(2,1)S(1)} %fusion.18), channel_id=1, source_target_pairs={{0,8},{2,10},{4,12},{6,14},{8,0},{10,2},{12,4},{14,6},{1,9},{3,11}... | collective-permute-start | bytes 393224 | tf_op jit(solution)/shard_map/ppermute | solution.py:14
  44.1 14.6 %copy-start.9 = (bf16[64,1024]{1,0:T(8,128)(2,1)S(1)}, bf16[64,1024]{1,0:T(8,128)(2,1)}, u32[]{:S(2)}) copy-start(bf16[64,1024]{1,0:T(8,128)(2,1)} %copy-done.8) | copy-start | bytes 393220
  44.1 14.6 %copy-start.29 = (f32[64]{0:T(128)S(1)}, f32[64]{0:T(128)}, u32[]{:S(2)}) copy-start(f32[64]{0:T(128)} %get-tuple-element.46) | copy-start | bytes 772
  44.1 14.9 %copy-start.19 = (f32[64]{0:T(128)S(1)}, f32[64]{0:T(128)}, u32[]{:S(2)}) copy-start(f32[64]{0:T(128)} %copy-done.18) | copy-start | bytes 772
  44.1 15.1 %copy-start.7 = (bf16[64,1024]{1,0:T(8,128)(2,1)S(1)}, bf16[64,1024]{1,0:T(8,128)(2,1)}, u32[]{:S(2)}) copy-start(bf16[64,1024]{1,0:T(8,128)(2,1)} %copy-done.6) | copy-start | bytes 393220
  44.1 15.1 %copy-start.28 = (f32[64]{0:T(128)S(1)}, f32[64]{0:T(128)}, u32[]{:S(2)}) copy-start(f32[64]{0:T(128)} %copy-done.27) | copy-start | bytes 772
  47.8 16.3 %copy-start.5 = (bf16[64,1024]{1,0:T(8,128)(2,1)S(1)}, bf16[64,1024]{1,0:T(8,128)(2,1)}, u32[]{:S(2)}) copy-start(bf16[64,1024]{1,0:T(8,128)(2,1)} %copy-done.4) | copy-start | bytes 393220
  47.8 16.3 %copy-start.26 = (f32[64]{0:T(128)S(1)}, f32[64]{0:T(128)}, u32[]{:S(2)}) copy-start(f32[64]{0:T(128)} %copy-done.25) | copy-start | bytes 772
  49.2 15.2 %copy-start.15 = (f32[64]{0:T(128)S(1)}, f32[64]{0:T(128)}, u32[]{:S(2)}) copy-start(f32[64]{0:T(128)} %copy-done.14) | copy-start | bytes 772
  49.3 9.4 %collective-permute-start.12 = (bf16[64,1024]{1,0:T(8,128)(2,1)S(1)}, bf16[64,1024]{1,0:T(8,128)(2,1)S(1)}, u32[]{:S(2)}, u32[]{:S(2)}) collective-permute-start(bf16[64,1024]{1,0:T(8,128)(2,1)S(1)} %fusion.35), channel_id=1, source_target_pairs={{0,8},{2,10},{4,12},{6,14},{8,0},{10,2},{12,4},{14,6},{1,9},{3,11}... | collective-permute-start | bytes 393224 | tf_op jit(solution)/shard_map/ppermute | solution.py:14
  51.6 18.3 %copy-start.13 = (bf16[1,128,128]{2,1,0:T(8,128)(2,1)S(1)}, bf16[1,128,128]{2,1,0:T(8,128)(2,1)}, u32[]{:S(2)}) copy-start(bf16[1,128,128]{2,1,0:T(8,128)(2,1)} %param.11) | copy-start | bytes 98308
  51.6 7.5 %collective-permute-start.10 = (bf16[64,1024]{1,0:T(8,128)(2,1)S(1)}, bf16[64,1024]{1,0:T(8,128)(2,1)S(1)}, u32[]{:S(2)}, u32[]{:S(2)}) collective-permute-start(bf16[64,1024]{1,0:T(8,128)(2,1)S(1)} %fusion.25), channel_id=1, source_target_pairs={{0,4},{2,6},{4,0},{6,2},{8,12},{10,14},{12,8},{14,10},{1,5},{3,7},... | collective-permute-start | bytes 393224 | tf_op jit(solution)/shard_map/ppermute | solution.py:14
  59.1 5.0 %collective-permute-start.13 = (bf16[64,1024]{1,0:T(8,128)(2,1)S(1)}, bf16[64,1024]{1,0:T(8,128)(2,1)S(1)}, u32[]{:S(2)}, u32[]{:S(2)}) collective-permute-start(bf16[64,1024]{1,0:T(8,128)(2,1)S(1)} %fusion.40), channel_id=1, source_target_pairs={{0,4},{2,6},{4,0},{6,2},{8,12},{10,14},{12,8},{14,10},{1,5},{3,7},... | collective-permute-start | bytes 393224 | tf_op jit(solution)/shard_map/ppermute | solution.py:14
  59.5 9.1 %collective-permute-start.11 = (bf16[64,1024]{1,0:T(8,128)(2,1)S(1)}, bf16[64,1024]{1,0:T(8,128)(2,1)S(1)}, u32[]{:S(2)}, u32[]{:S(2)}) collective-permute-start(bf16[64,1024]{1,0:T(8,128)(2,1)S(1)} %fusion.30), channel_id=1, source_target_pairs={{0,2},{2,0},{4,6},{6,4},{8,10},{10,8},{12,14},{14,12},{1,3},{3,1},... | collective-permute-start | bytes 393224 | tf_op jit(solution)/shard_map/ppermute | solution.py:14
  64.5 5.0 %collective-permute-start.14 = (bf16[64,1024]{1,0:T(8,128)(2,1)S(1)}, bf16[64,1024]{1,0:T(8,128)(2,1)S(1)}, u32[]{:S(2)}, u32[]{:S(2)}) collective-permute-start(bf16[64,1024]{1,0:T(8,128)(2,1)S(1)} %fusion.45), channel_id=1, source_target_pairs={{0,2},{2,0},{4,6},{6,4},{8,10},{10,8},{12,14},{14,12},{1,3},{3,1},... | collective-permute-start | bytes 393224 | tf_op jit(solution)/shard_map/ppermute | solution.py:14
  66.1 1.2 %collective-permute-start.16 = (f32[3,128]{1,0:T(4,128)S(1)}, f32[3,128]{1,0:T(4,128)S(1)}, u32[]{:S(2)}, u32[]{:S(2)}) collective-permute-start(f32[3,128]{1,0:T(4,128)S(1)} %maximum_maximum_fusion.1), channel_id=1, source_target_pairs={{0,1},{1,0},{2,3},{3,2},{4,5},{5,4},{6,7},{7,6},{8,9},{9,8},{10,11... | collective-permute-start | bytes 4616 | tf_op jit(solution)/shard_map/ppermute | solution.py:70
  66.2 1.7 %collective-permute-start.15 = (f32[3,128]{1,0:T(4,128)S(1)}, f32[3,128]{1,0:T(4,128)S(1)}, u32[]{:S(2)}, u32[]{:S(2)}) collective-permute-start(f32[3,128]{1,0:T(4,128)S(1)} %maximum_maximum_fusion), channel_id=1, source_target_pairs={{0,1},{1,0},{2,3},{3,2},{4,5},{5,4},{6,7},{7,6},{8,9},{9,8},{10,11... | collective-permute-start | bytes 4616 | tf_op jit(solution)/shard_map/ppermute | solution.py:70
  69.9 1.3 %collective-permute-start.17 = (f32[1,128,128]{2,1,0:T(8,128)S(1)}, f32[1,128,128]{2,1,0:T(8,128)S(1)}, u32[]{:S(2)}, u32[]{:S(2)}) collective-permute-start(f32[1,128,128]{2,1,0:T(8,128)S(1)} %convolution_bitcast_fusion.1), channel_id=1, source_target_pairs={{0,1},{1,0},{2,3},{3,2},{4,5},{5,4},{6,7},{7,6},{8,9},{9,8},{10,11... | collective-permute-start | bytes 196616 | tf_op jit(solution)/shard_map/ppermute | solution.py:70
  (18 other events, 158.2 us)

commit v16 on v13

--- a/solution.py
+++ b/solution.py
@@ -3,6 +3,7 @@
 from jax import lax
 from jax.sharding import PartitionSpec as P
 from jax.experimental import pallas as pl
+from jax.experimental.pallas import tpu as pltpu
 
 D = 2048
 CHUNKS = 2
@@ -35,23 +36,14 @@
         ) + lax.dot_general(d_up, w_up, contract_last, preferred_element_type=jnp.float32)
 
 
-def ffn_grad(normed, cotangent, w_gate, w_up, w_down, per_step=4):
+def ffn_grad(normed, cotangent, w_gate, w_up, w_down):
     tok, width = normed.shape
     groups_here, cblock, hidden = w_gate.shape
-    if groups_here % per_step:
-        per_step = 1
-    act = pl.BlockSpec((tok, cblock * per_step), lambda g: (0, g))
+    whole = pl.BlockSpec(memory_space=pltpu.VMEM)
     return pl.pallas_call(
         ffn_kernel,
-        grid=(groups_here // per_step,),
-        in_specs=[
-            act,
-            act,
-            pl.BlockSpec((per_step, cblock, hidden), lambda g: (g, 0, 0)),
-            pl.BlockSpec((per_step, cblock, hidden), lambda g: (g, 0, 0)),
-            pl.BlockSpec((per_step, hidden, cblock), lambda g: (g, 0, 0)),
-        ],
-        out_specs=act,
+        in_specs=[whole] * 5,
+        out_specs=whole,
         out_shape=jax.ShapeDtypeStruct((tok, width), jnp.float32),
         cost_estimate=pl.CostEstimate(
             flops=10 * tok * cblock * hidden * groups_here,

time: 66.8 us -> 67.2 us (level)
  transfers between devices with their start and end apart: 18 -> 18, of which waited for: 10 -> 10; matrix products, arithmetic and copies ran while one was open for 15% -> 15% of each run, Pallas kernels for 12% -> 13%
where the time goes in v16:
time: 67.2 us; the launch traced here: 67 us
  waiting for transfers between devices  21.8 us (32%)
  starting transfers between devices  20.2 us (30%)
  other arithmetic  9.3 us (14%)
  Pallas kernels  8.56 us (13%)
  matrix products  2.57 us (4%)
  blocking collectives  2.47 us (4%)
  local copies, waits for them, and re-layouts  1.2 us (2%)
  between operations  0.89 us (1%)
    ppermute x12, waiting for transfers between devices, from_partner(): return lax.ppermute(value, axis, pairs)  21 us
    ppermute x12, starting transfers between devices, from_partner(): return lax.ppermute(value, axis, pairs)  19.2 us
    pallas_call x2, Pallas kernels, ffn_grad(): pl.pallas_call(ffn_kernel, in_specs=[whole] * 5, out_specs=whole, out_sha...  8.56 us
    psum x1, blocking collectives, body(): reduce_hid = hid_sum if chunk == 0 else lambda v: lax.psum(v, 'hid')  2.47 us
    reduce_sum x2, other arithmetic, body(): inner = reduce_hid(jnp.sum(resid * scaled, axis=-1))  2.29 us
    add x3, other arithmetic, hid_sum(): total = total + lax.ppermute(value, 'hid', pairs)  1.95 us
    reduce_sum x6, other arithmetic, body(): jnp.sum(back_f * mates[chunk][section].astype(jnp.float32), axis=-1)  1.65 us
    convert_element_type x2, other arithmetic, body(): normed = (resid * inv[:, None] * norm_gain).astype(jnp.bfloat16)  1.5 us
  transfers between devices with their start and end apart: 18, of which 10 were waited for; matrix products, arithmetic and copies ran while one was open for 15% of the time, Pallas kernels for 13%

profile of v16, /device:TPU:0, one launch (start us, length us, event | category | flops | bytes accessed | tf_op | source)
XLA Modules:
  0.0 67.0 jit_solution(17343706708798080209)
XLA Ops:
  0.7 1.2 %convolution_convert_fusion.1 = bf16[64,1024]{1,0:T(8,128)(2,1)S(1)} fusion(bf16[128,1024]{1,0:T(8,128)(2,1)} %param.9, bf16[1,128,128]{2,1,0:T(8,128)(2,1)} %param.11), kind=kOutput, calls=%fused_computation.4 | convolution fusion | flops 16842752 | bytes 409600 | tf_op jit(solution)/shard_map/kij,kjd->kid/dot_general | solution.py:84
  1.8 3.0 %collective-permute-start = (bf16[64,1024]{1,0:T(8,128)(2,1)S(1)}, bf16[64,1024]{1,0:T(8,128)(2,1)S(1)}, u32[]{:S(2)}, u32[]{:S(2)}) collective-permute-start(bf16[64,1024]{1,0:T(8,128)(2,1)S(1)} %convolution_convert_fusion.1), channel_id=1, source_target_pairs={{0,2},{2,0},{4,6},{6,4},{8,10},{10,8},{12,14},{14,12},{1,3},{3,1},... | collective-permute-start | bytes 393224 | tf_op jit(solution)/shard_map/ppermute | solution.py:15
  5.6 3.5 %collective-permute-done = bf16[64,1024]{1,0:T(8,128)(2,1)S(1)} collective-permute-done((bf16[64,1024]{1,0:T(8,128)(2,1)S(1)}, bf16[64,1024]{1,0:T(8,128)(2,1)S(1)}, u32[]{:S(2)}, u32[]{:S(2)}) %collective-permute-start) | collective-permute-done | bytes 131104 | tf_op jit(solution)/shard_map/ppermute | solution.py:15
  9.3 2.2 %collective-permute-start.1 = (bf16[64,1024]{1,0:T(8,128)(2,1)S(1)}, bf16[64,1024]{1,0:T(8,128)(2,1)S(1)}, u32[]{:S(2)}, u32[]{:S(2)}) collective-permute-start(bf16[64,1024]{1,0:T(8,128)(2,1)S(1)} %fusion.4), channel_id=1, source_target_pairs={{0,4},{2,6},{4,0},{6,2},{8,12},{10,14},{12,8},{14,10},{1,5},{3,7},... | collective-permute-start | bytes 393224 | tf_op jit(solution)/shard_map/ppermute | solution.py:15
  11.5 0.7 %fusion.66 = (bf16[64,1024]{1,0:T(8,128)(2,1)}, bf16[64,1024]{1,0:T(8,128)(2,1)}) fusion(bf16[128,1024]{1,0:T(8,128)(2,1)S(1)} %copy-done.3), kind=kLoop, calls=%fused_computation.132 | loop fusion | bytes 524288 | tf_op jit(solution)/shard_map/slice | solution.py:111
  12.2 2.2 %collective-permute-done.1 = bf16[64,1024]{1,0:T(8,128)(2,1)S(1)} collective-permute-done((bf16[64,1024]{1,0:T(8,128)(2,1)S(1)}, bf16[64,1024]{1,0:T(8,128)(2,1)S(1)}, u32[]{:S(2)}, u32[]{:S(2)}) %collective-permute-start.1) | collective-permute-done | bytes 131104 | tf_op jit(solution)/shard_map/ppermute | solution.py:15
  14.6 3.8 %collective-permute-start.2 = (bf16[64,1024]{1,0:T(8,128)(2,1)S(1)}, bf16[64,1024]{1,0:T(8,128)(2,1)S(1)}, u32[]{:S(2)}, u32[]{:S(2)}) collective-permute-start(bf16[64,1024]{1,0:T(8,128)(2,1)S(1)} %fusion.6), channel_id=1, source_target_pairs={{0,8},{2,10},{4,12},{6,14},{8,0},{10,2},{12,4},{14,6},{1,9},{3,11}... | collective-permute-start | bytes 393224 | tf_op jit(solution)/shard_map/ppermute | solution.py:15
  18.5 1.2 %collective-permute-start.6 = (bf16[64,1024]{1,0:T(8,128)(2,1)S(1)}, bf16[64,1024]{1,0:T(8,128)(2,1)S(1)}, u32[]{:S(2)}, u32[]{:S(2)}) collective-permute-start(bf16[64,1024]{1,0:T(8,128)(2,1)S(1)} %fusion.12), channel_id=1, source_target_pairs={{0,4},{2,6},{4,0},{6,2},{8,12},{10,14},{12,8},{14,10},{1,5},{3,7},... | collective-permute-start | bytes 393224 | tf_op jit(solution)/shard_map/ppermute | solution.py:15
  19.7 3.1 %collective-permute-done.2 = bf16[64,1024]{1,0:T(8,128)(2,1)S(1)} collective-permute-done((bf16[64,1024]{1,0:T(8,128)(2,1)S(1)}, bf16[64,1024]{1,0:T(8,128)(2,1)S(1)}, u32[]{:S(2)}, u32[]{:S(2)}) %collective-permute-start.2) | collective-permute-done | bytes 131104 | tf_op jit(solution)/shard_map/ppermute | solution.py:15
  23.1 1.0 %collective-permute-done.6 = bf16[64,1024]{1,0:T(8,128)(2,1)S(1)} collective-permute-done((bf16[64,1024]{1,0:T(8,128)(2,1)S(1)}, bf16[64,1024]{1,0:T(8,128)(2,1)S(1)}, u32[]{:S(2)}, u32[]{:S(2)}) %collective-permute-start.6) | collective-permute-done | bytes 131104 | tf_op jit(solution)/shard_map/ppermute | solution.py:15
  24.3 0.6 collective-permute-start.7
  24.9 0.8 %multiply_convert_fusion.1.normed_ref = bf16[64,1024]{1,0:T(8,128)(2,1)} fusion(bf16[64,1024]{1,0:T(8,128)(2,1)S(1)} %get-tuple-element.25, f32[1024]{0:T(1024)S(1)} %copy-done.4, f32[64]{0:T(128)S(1)} %add_rsqrt_fusion.1, bf16[128,1024]{1,0:T(8,128)(2,1)S(1)} %copy-done), kind=kLoop, calls=%fused_computation.101 | loop fusion | flops 458752 | bytes 397568 | tf_op jit(solution)/shard_map/convert_element_type | solution.py:118
  25.7 4.3 %shard_map.120 = f32[64,1024]{1,0:T(8,128)} custom-call(bf16[64,1024]{1,0:T(8,128)(2,1)} %multiply_convert_fusion.1.normed_ref, bf16[64,1024]{1,0:T(8,128)(2,1)} %get-tuple-element.29.cot_ref, bf16[8,128,512]{2,1,0:T(8,128)(2,1)} %wg_ref.3, bf16[8,128,512]{2,1,0:T(8,128)(2,1)} %wu_ref.3, bf16[8,512,128]{2,1,0:T(8,128)(2,1)} %wd_ref.3), custom_call_target="tpu_custom_call" | custom-call | flops 335544320 | bytes 3670016 | tf_op jit(solution)/shard_map/pallas_call | solution.py:43
  29.9 1.1 %multiply_reduce_fusion.2 = f32[64]{0:T(128)S(1)} fusion(f32[64,1024]{1,0:T(8,128)} %shard_map.120, bf16[64,1024]{1,0:T(8,128)(2,1)S(1)} %get-tuple-element.25, f32[1024]{0:T(1024)S(1)} %copy-done.4, bf16[128,1024]{1,0:T(8,128)(2,1)S(1)} %copy-done), kind=kLoop, calls=%fused_computation.100 | loop fusion | flops 458688 | bytes 528640 | tf_op jit(solution)/shard_map/reduce_sum | solution.py:121
  31.3 1.6 %collective-permute-done.7 = bf16[64,1024]{1,0:T(8,128)(2,1)S(1)} collective-permute-done((bf16[64,1024]{1,0:T(8,128)(2,1)S(1)}, bf16[64,1024]{1,0:T(8,128)(2,1)S(1)}, u32[]{:S(2)}, u32[]{:S(2)}) %collective-permute-start.7) | collective-permute-done | bytes 131104 | tf_op jit(solution)/shard_map/ppermute | solution.py:15
  33.7 1.7 %collective-permute-start.9 = (bf16[64,1024]{1,0:T(8,128)(2,1)S(1)}, bf16[64,1024]{1,0:T(8,128)(2,1)S(1)}, u32[]{:S(2)}, u32[]{:S(2)}) collective-permute-start(bf16[64,1024]{1,0:T(8,128)(2,1)S(1)} %fusion.18), channel_id=1, source_target_pairs={{0,8},{2,10},{4,12},{6,14},{8,0},{10,2},{12,4},{14,6},{1,9},{3,11}... | collective-permute-start | bytes 393224 | tf_op jit(solution)/shard_map/ppermute | solution.py:15
  35.5 0.8 %multiply_convert_fusion.normed_ref = bf16[64,1024]{1,0:T(8,128)(2,1)} fusion(bf16[64,1024]{1,0:T(8,128)(2,1)S(1)} %fusion.16, f32[64]{0:T(128)S(1)} %add_rsqrt_fusion, f32[1024]{0:T(1024)S(1)} %copy-done.4, bf16[128,1024]{1,0:T(8,128)(2,1)S(1)} %copy-done), kind=kLoop, calls=%fused_computation.97 | loop fusion | flops 458752 | bytes 397568 | tf_op jit(solution)/shard_map/convert_element_type | solution.py:118
  36.2 4.3 %shard_map.121 = f32[64,1024]{1,0:T(8,128)} custom-call(bf16[64,1024]{1,0:T(8,128)(2,1)} %multiply_convert_fusion.normed_ref, bf16[64,1024]{1,0:T(8,128)(2,1)} %get-tuple-element.28.cot_ref, bf16[8,128,512]{2,1,0:T(8,128)(2,1)} %wg_ref.3, bf16[8,128,512]{2,1,0:T(8,128)(2,1)} %wu_ref.3, bf16[8,512,128]{2,1,0:T(8,128)(2,1)} %wd_ref.3), custom_call_target="tpu_custom_call" | custom-call | flops 335544320 | bytes 3670016 | tf_op jit(solution)/shard_map/pallas_call | solution.py:43
  40.5 1.2 %multiply_reduce_fusion = f32[64]{0:T(128)S(1)} fusion(f32[64,1024]{1,0:T(8,128)} %shard_map.121, bf16[64,1024]{1,0:T(8,128)(2,1)S(1)} %fusion.16, f32[1024]{0:T(1024)S(1)} %copy-done.4, bf16[128,1024]{1,0:T(8,128)(2,1)S(1)} %copy-done), kind=kLoop, calls=%fused_computation.96 | loop fusion | flops 458688 | bytes 528640 | tf_op jit(solution)/shard_map/reduce_sum | solution.py:121
  41.7 2.5 %psum.7 = f32[64]{0:T(128)S(1)} all-reduce(f32[64]{0:T(128)S(1)} %multiply_reduce_fusion), channel_id=1, replica_groups=mesh['groups'=2,'seq'=8,'hid'=2] {'hid'}, use_global_device_ids=true, to_apply=%region_4.0 | all-reduce | flops 64 | bytes 512 | tf_op jit(solution)/shard_map/psum | solution.py:115
  44.6 1.3 %collective-permute-start.12 = (bf16[64,1024]{1,0:T(8,128)(2,1)S(1)}, bf16[64,1024]{1,0:T(8,128)(2,1)S(1)}, u32[]{:S(2)}, u32[]{:S(2)}) collective-permute-start(bf16[64,1024]{1,0:T(8,128)(2,1)S(1)} %fusion.35), channel_id=1, source_target_pairs={{0,8},{2,10},{4,12},{6,14},{8,0},{10,2},{12,4},{14,6},{1,9},{3,11}... | collective-permute-start | bytes 393224 | tf_op jit(solution)/shard_map/ppermute | solution.py:15
  46.2 1.9 %collective-permute-start.10 = (bf16[64,1024]{1,0:T(8,128)(2,1)S(1)}, bf16[64,1024]{1,0:T(8,128)(2,1)S(1)}, u32[]{:S(2)}, u32[]{:S(2)}) collective-permute-start(bf16[64,1024]{1,0:T(8,128)(2,1)S(1)} %fusion.25), channel_id=1, source_target_pairs={{0,4},{2,6},{4,0},{6,2},{8,12},{10,14},{12,8},{14,10},{1,5},{3,7},... | collective-permute-start | bytes 393224 | tf_op jit(solution)/shard_map/ppermute | solution.py:15
  48.1 5.8 %collective-permute-done.12 = bf16[64,1024]{1,0:T(8,128)(2,1)S(1)} collective-permute-done((bf16[64,1024]{1,0:T(8,128)(2,1)S(1)}, bf16[64,1024]{1,0:T(8,128)(2,1)S(1)}, u32[]{:S(2)}, u32[]{:S(2)}) %collective-permute-start.12) | collective-permute-done | bytes 131104 | tf_op jit(solution)/shard_map/ppermute | solution.py:15
  54.7 1.6 %collective-permute-start.11 = (bf16[64,1024]{1,0:T(8,128)(2,1)S(1)}, bf16[64,1024]{1,0:T(8,128)(2,1)S(1)}, u32[]{:S(2)}, u32[]{:S(2)}) collective-permute-start(bf16[64,1024]{1,0:T(8,128)(2,1)S(1)} %fusion.30), channel_id=1, source_target_pairs={{0,2},{2,0},{4,6},{6,4},{8,10},{10,8},{12,14},{14,12},{1,3},{3,1},... | collective-permute-start | bytes 393224 | tf_op jit(solution)/shard_map/ppermute | solution.py:15
  56.3 3.0 %collective-permute-done.13 = bf16[64,1024]{1,0:T(8,128)(2,1)S(1)} collective-permute-done((bf16[64,1024]{1,0:T(8,128)(2,1)S(1)}, bf16[64,1024]{1,0:T(8,128)(2,1)S(1)}, u32[]{:S(2)}, u32[]{:S(2)}) %collective-permute-start.13) | collective-permute-done | bytes 131104 | tf_op jit(solution)/shard_map/ppermute | solution.py:15
  59.6 1.6 %collective-permute-start.14 = (bf16[64,1024]{1,0:T(8,128)(2,1)S(1)}, bf16[64,1024]{1,0:T(8,128)(2,1)S(1)}, u32[]{:S(2)}, u32[]{:S(2)}) collective-permute-start(bf16[64,1024]{1,0:T(8,128)(2,1)S(1)} %fusion.45), channel_id=1, source_target_pairs={{0,2},{2,0},{4,6},{6,4},{8,10},{10,8},{12,14},{14,12},{1,3},{3,1},... | collective-permute-start | bytes 393224 | tf_op jit(solution)/shard_map/ppermute | solution.py:15
  61.9 0.6 collective-permute-done.16
  62.5 0.7 fusion.70
  63.1 0.7 fusion.71
  63.9 0.7 %collective-permute-done.14 = bf16[64,1024]{1,0:T(8,128)(2,1)S(1)} collective-permute-done((bf16[64,1024]{1,0:T(8,128)(2,1)S(1)}, bf16[64,1024]{1,0:T(8,128)(2,1)S(1)}, u32[]{:S(2)}, u32[]{:S(2)}) %collective-permute-start.14) | collective-permute-done | bytes 131104 | tf_op jit(solution)/shard_map/ppermute | solution.py:15
  65.1 1.0 %fusion.1 = bf16[128,1024]{1,0:T(8,128)(2,1)} fusion(f32[64,1024]{1,0:T(8,128)S(1)} %get-tuple-element.26, f32[64,1024]{1,0:T(8,128)S(1)} %get-tuple-element.27, bf16[64,1024]{1,0:T(8,128)(2,1)S(1)} %fusion.44, bf16[64,1024]{1,0:T(8,128)(2,1)S(1)} %fusion.29, bf16[1,128,128]{2,1,0:T(8,128)(2,1)S(1)} %copy-done.5), kind=kOutput, calls=%fused_computation.2 | convolution fusion | flops 34471936 | bytes 1081344 | tf_op jit(solution)/shard_map/kij,kid->kjd/dot_general | solution.py:159
  66.3 0.6 add.109
  (63 shorter events, 5.9 us)
Async XLA Ops:
  0.6 4.2 %copy-start.5 = (bf16[1,128,128]{2,1,0:T(8,128)(2,1)S(1)}, bf16[1,128,128]{2,1,0:T(8,128)(2,1)}, u32[]{:S(2)}) copy-start(bf16[1,128,128]{2,1,0:T(8,128)(2,1)} %param.11) | copy-start | bytes 98308
  0.6 4.2 %copy-start = (bf16[128,1024]{1,0:T(8,128)(2,1)S(1)}, bf16[128,1024]{1,0:T(8,128)(2,1)}, u32[]{:S(2)}) copy-start(bf16[128,1024]{1,0:T(8,128)(2,1)} %param.9) | copy-start | bytes 786436
  1.8 7.3 %collective-permute-start = (bf16[64,1024]{1,0:T(8,128)(2,1)S(1)}, bf16[64,1024]{1,0:T(8,128)(2,1)S(1)}, u32[]{:S(2)}, u32[]{:S(2)}) collective-permute-start(bf16[64,1024]{1,0:T(8,128)(2,1)S(1)} %convolution_convert_fusion.1), channel_id=1, source_target_pairs={{0,2},{2,0},{4,6},{6,4},{8,10},{10,8},{12,14},{14,12},{1,3},{3,1},... | collective-permute-start | bytes 393224 | tf_op jit(solution)/shard_map/ppermute | solution.py:15
  4.9 0.7 %copy-start.6 = (f32[3,128]{1,0:T(4,128)S(1)}, f32[3,128]{1,0:T(4,128)}, u32[]{:S(2)}) copy-start(f32[3,128]{1,0:T(4,128)} %param.13) | copy-start | bytes 4612
  4.9 0.7 %copy-start.7 = (f32[3,128]{1,0:T(4,128)S(1)}, f32[3,128]{1,0:T(4,128)}, u32[]{:S(2)}) copy-start(f32[3,128]{1,0:T(4,128)} %param.12) | copy-start | bytes 4612
  5.0 6.5 %copy-start.3 = (bf16[128,1024]{1,0:T(8,128)(2,1)S(1)}, bf16[128,1024]{1,0:T(8,128)(2,1)}, u32[]{:S(2)}) copy-start(bf16[128,1024]{1,0:T(8,128)(2,1)} %param.10) | copy-start | bytes 786436
  5.1 13.3 %collective-permute-start.5 = (bf16[64,1024]{1,0:T(8,128)(2,1)S(1)}, bf16[64,1024]{1,0:T(8,128)(2,1)S(1)}, u32[]{:S(2)}, u32[]{:S(2)}) collective-permute-start(bf16[64,1024]{1,0:T(8,128)(2,1)S(1)} %convolution_convert_fusion), channel_id=1, source_target_pairs={{0,2},{2,0},{4,6},{6,4},{8,10},{10,8},{12,14},{14,12},{1,3},{3,1},... | collective-permute-start | bytes 393224 | tf_op jit(solution)/shard_map/ppermute | solution.py:15
  9.3 5.2 %collective-permute-start.1 = (bf16[64,1024]{1,0:T(8,128)(2,1)S(1)}, bf16[64,1024]{1,0:T(8,128)(2,1)S(1)}, u32[]{:S(2)}, u32[]{:S(2)}) collective-permute-start(bf16[64,1024]{1,0:T(8,128)(2,1)S(1)} %fusion.4), channel_id=1, source_target_pairs={{0,4},{2,6},{4,0},{6,2},{8,12},{10,14},{12,8},{14,10},{1,5},{3,7},... | collective-permute-start | bytes 393224 | tf_op jit(solution)/shard_map/ppermute | solution.py:15
  14.6 8.2 %collective-permute-start.2 = (bf16[64,1024]{1,0:T(8,128)(2,1)S(1)}, bf16[64,1024]{1,0:T(8,128)(2,1)S(1)}, u32[]{:S(2)}, u32[]{:S(2)}) collective-permute-start(bf16[64,1024]{1,0:T(8,128)(2,1)S(1)} %fusion.6), channel_id=1, source_target_pairs={{0,8},{2,10},{4,12},{6,14},{8,0},{10,2},{12,4},{14,6},{1,9},{3,11}... | collective-permute-start | bytes 393224 | tf_op jit(solution)/shard_map/ppermute | solution.py:15
  18.5 5.6 %collective-permute-start.6 = (bf16[64,1024]{1,0:T(8,128)(2,1)S(1)}, bf16[64,1024]{1,0:T(8,128)(2,1)S(1)}, u32[]{:S(2)}, u32[]{:S(2)}) collective-permute-start(bf16[64,1024]{1,0:T(8,128)(2,1)S(1)} %fusion.12), channel_id=1, source_target_pairs={{0,4},{2,6},{4,0},{6,2},{8,12},{10,14},{12,8},{14,10},{1,5},{3,7},... | collective-permute-start | bytes 393224 | tf_op jit(solution)/shard_map/ppermute | solution.py:15
  23.1 1.8 %collective-permute-start.3 = (f32[64]{0:T(128)S(1)}, f32[64]{0:T(128)S(1)}, u32[]{:S(2)}, u32[]{:S(2)}) collective-permute-start(f32[64]{0:T(128)S(1)} %get-tuple-element.24), channel_id=1, source_target_pairs={{0,1},{1,0},{2,3},{3,2},{4,5},{5,4},{6,7},{7,6},{8,9},{9,8},{10,11... | collective-permute-start | bytes 776 | tf_op jit(solution)/shard_map/ppermute | solution.py:61
  24.1 0.8 %copy-start.4 = (f32[1024]{0:T(1024)S(1)}, f32[1024]{0:T(1024)}, u32[]{:S(2)}) copy-start(f32[1024]{0:T(1024)} %param.14) | copy-start | bytes 12292
  24.3 8.7 %collective-permute-start.7 = (bf16[64,1024]{1,0:T(8,128)(2,1)S(1)}, bf16[64,1024]{1,0:T(8,128)(2,1)S(1)}, u32[]{:S(2)}, u32[]{:S(2)}) collective-permute-start(bf16[64,1024]{1,0:T(8,128)(2,1)S(1)} %fusion.14), channel_id=1, source_target_pairs={{0,8},{2,10},{4,12},{6,14},{8,0},{10,2},{12,4},{14,6},{1,9},{3,11}... | collective-permute-start | bytes 393224 | tf_op jit(solution)/shard_map/ppermute | solution.py:15
  31.1 2.0 %copy-start.1 = (f32[64,1024]{1,0:T(8,128)S(1)}, f32[64,1024]{1,0:T(8,128)}, u32[]{:S(2)}) copy-start(f32[64,1024]{1,0:T(8,128)} %shard_map.120) | copy-start | bytes 786436
  31.1 2.0 %collective-permute-start.4 = (f32[64]{0:T(128)S(1)}, f32[64]{0:T(128)S(1)}, u32[]{:S(2)}, u32[]{:S(2)}) collective-permute-start(f32[64]{0:T(128)S(1)} %multiply_reduce_fusion.2), channel_id=1, source_target_pairs={{0,1},{1,0},{2,3},{3,2},{4,5},{5,4},{6,7},{7,6},{8,9},{9,8},{10,11... | collective-permute-start | bytes 776 | tf_op jit(solution)/shard_map/ppermute | solution.py:61
  33.6 1.8 %collective-permute-start.8 = (f32[64]{0:T(128)S(1)}, f32[64]{0:T(128)S(1)}, u32[]{:S(2)}, u32[]{:S(2)}) collective-permute-start(f32[64]{0:T(128)S(1)} %multiply_reduce_fusion.1), channel_id=1, source_target_pairs={{0,1},{1,0},{2,3},{3,2},{4,5},{5,4},{6,7},{7,6},{8,9},{9,8},{10,11... | collective-permute-start | bytes 776 | tf_op jit(solution)/shard_map/ppermute | solution.py:61
  33.7 12.2 %collective-permute-start.9 = (bf16[64,1024]{1,0:T(8,128)(2,1)S(1)}, bf16[64,1024]{1,0:T(8,128)(2,1)S(1)}, u32[]{:S(2)}, u32[]{:S(2)}) collective-permute-start(bf16[64,1024]{1,0:T(8,128)(2,1)S(1)} %fusion.18), channel_id=1, source_target_pairs={{0,8},{2,10},{4,12},{6,14},{8,0},{10,2},{12,4},{14,6},{1,9},{3,11}... | collective-permute-start | bytes 393224 | tf_op jit(solution)/shard_map/ppermute | solution.py:15
  40.5 3.7 %copy-start.2 = (f32[64,1024]{1,0:T(8,128)S(1)}, f32[64,1024]{1,0:T(8,128)}, u32[]{:S(2)}) copy-start(f32[64,1024]{1,0:T(8,128)} %shard_map.121) | copy-start | bytes 786436
  44.6 9.3 %collective-permute-start.12 = (bf16[64,1024]{1,0:T(8,128)(2,1)S(1)}, bf16[64,1024]{1,0:T(8,128)(2,1)S(1)}, u32[]{:S(2)}, u32[]{:S(2)}) collective-permute-start(bf16[64,1024]{1,0:T(8,128)(2,1)S(1)} %fusion.35), channel_id=1, source_target_pairs={{0,8},{2,10},{4,12},{6,14},{8,0},{10,2},{12,4},{14,6},{1,9},{3,11}... | collective-permute-start | bytes 393224 | tf_op jit(solution)/shard_map/ppermute | solution.py:15
  46.2 8.1 %collective-permute-start.10 = (bf16[64,1024]{1,0:T(8,128)(2,1)S(1)}, bf16[64,1024]{1,0:T(8,128)(2,1)S(1)}, u32[]{:S(2)}, u32[]{:S(2)}) collective-permute-start(bf16[64,1024]{1,0:T(8,128)(2,1)S(1)} %fusion.25), channel_id=1, source_target_pairs={{0,4},{2,6},{4,0},{6,2},{8,12},{10,14},{12,8},{14,10},{1,5},{3,7},... | collective-permute-start | bytes 393224 | tf_op jit(solution)/shard_map/ppermute | solution.py:15
  54.2 5.0 %collective-permute-start.13 = (bf16[64,1024]{1,0:T(8,128)(2,1)S(1)}, bf16[64,1024]{1,0:T(8,128)(2,1)S(1)}, u32[]{:S(2)}, u32[]{:S(2)}) collective-permute-start(bf16[64,1024]{1,0:T(8,128)(2,1)S(1)} %fusion.40), channel_id=1, source_target_pairs={{0,4},{2,6},{4,0},{6,2},{8,12},{10,14},{12,8},{14,10},{1,5},{3,7},... | collective-permute-start | bytes 393224 | tf_op jit(solution)/shard_map/ppermute | solution.py:15
  54.7 9.1 %collective-permute-start.11 = (bf16[64,1024]{1,0:T(8,128)(2,1)S(1)}, bf16[64,1024]{1,0:T(8,128)(2,1)S(1)}, u32[]{:S(2)}, u32[]{:S(2)}) collective-permute-start(bf16[64,1024]{1,0:T(8,128)(2,1)S(1)} %fusion.30), channel_id=1, source_target_pairs={{0,2},{2,0},{4,6},{6,4},{8,10},{10,8},{12,14},{14,12},{1,3},{3,1},... | collective-permute-start | bytes 393224 | tf_op jit(solution)/shard_map/ppermute | solution.py:15
  59.6 5.0 %collective-permute-start.14 = (bf16[64,1024]{1,0:T(8,128)(2,1)S(1)}, bf16[64,1024]{1,0:T(8,128)(2,1)S(1)}, u32[]{:S(2)}, u32[]{:S(2)}) collective-permute-start(bf16[64,1024]{1,0:T(8,128)(2,1)S(1)} %fusion.45), channel_id=1, source_target_pairs={{0,2},{2,0},{4,6},{6,4},{8,10},{10,8},{12,14},{14,12},{1,3},{3,1},... | collective-permute-start | bytes 393224 | tf_op jit(solution)/shard_map/ppermute | solution.py:15
  61.3 1.2 %collective-permute-start.16 = (f32[3,128]{1,0:T(4,128)S(1)}, f32[3,128]{1,0:T(4,128)S(1)}, u32[]{:S(2)}, u32[]{:S(2)}) collective-permute-start(f32[3,128]{1,0:T(4,128)S(1)} %maximum_maximum_fusion.1), channel_id=1, source_target_pairs={{0,1},{1,0},{2,3},{3,2},{4,5},{5,4},{6,7},{7,6},{8,9},{9,8},{10,11... | collective-permute-start | bytes 4616 | tf_op jit(solution)/shard_map/ppermute | solution.py:61
  61.4 1.7 %collective-permute-start.15 = (f32[3,128]{1,0:T(4,128)S(1)}, f32[3,128]{1,0:T(4,128)S(1)}, u32[]{:S(2)}, u32[]{:S(2)}) collective-permute-start(f32[3,128]{1,0:T(4,128)S(1)} %maximum_maximum_fusion), channel_id=1, source_target_pairs={{0,1},{1,0},{2,3},{3,2},{4,5},{5,4},{6,7},{7,6},{8,9},{9,8},{10,11... | collective-permute-start | bytes 4616 | tf_op jit(solution)/shard_map/ppermute | solution.py:61
  65.0 1.3 %collective-permute-start.17 = (f32[1,128,128]{2,1,0:T(8,128)S(1)}, f32[1,128,128]{2,1,0:T(8,128)S(1)}, u32[]{:S(2)}, u32[]{:S(2)}) collective-permute-start(f32[1,128,128]{2,1,0:T(8,128)S(1)} %convolution_bitcast_fusion.1), channel_id=1, source_target_pairs={{0,1},{1,0},{2,3},{3,2},{4,5},{5,4},{6,7},{7,6},{8,9},{9,8},{10,11... | collective-permute-start | bytes 196616 | tf_op jit(solution)/shard_map/ppermute | solution.py:61

commit v17 on v13

--- a/solution.py
+++ b/solution.py
@@ -59,6 +59,15 @@
             bytes_accessed=3 * groups_here * cblock * hidden * 2 + tok * width * 8,
         ),
     )(normed, cotangent, w_gate, w_up, w_down)
+
+
+def hid_sum_sync(value):
+    size = lax.axis_size("hid")
+    parts = lax.all_to_all(jnp.stack([value] * size), "hid", 0, 0)
+    total = parts[0]
+    for index in range(1, size):
+        total = total + parts[index]
+    return total
 
 
 def hid_sum(value):
@@ -120,7 +129,7 @@
         tok_f = tokens[rs].astype(jnp.float32)
         mixed_f = mixed.astype(jnp.float32)
         resid = tok_f + tok_f * mixed_f
-        reduce_hid = hid_sum if chunk == 0 else (lambda v: lax.psum(v, "hid"))
+        reduce_hid = hid_sum if chunk == 0 else hid_sum_sync
         square = hid_sum(jnp.sum(resid * resid, axis=-1))
         inv = lax.rsqrt(square / D + 1e-06)
         normed = (resid * inv[:, None] * norm_gain).astype(jnp.bfloat16)

time: 66.8 us -> 68 us (1.018)
  blocking collectives: 2.47 us -> 3.66 us
    all_to_all x0 -> x1, blocking collectives: none -> 3.66 us  [hid_sum_sync(): parts = lax.all_to_all(jnp.stack([value] * size), 'hid', 0, 0)]
    psum x1 -> x0, blocking collectives: 2.47 us -> none  [body(): reduce_hid = hid_sum if chunk == 0 else lambda v: lax.psum(v, 'hid')]
where the time goes in v17:
time: 68 us; the launch traced here: 67.8 us
  waiting for transfers between devices  22.1 us (32%)
  starting transfers between devices  20 us (29%)
  other arithmetic  9.31 us (14%)
  Pallas kernels  8.11 us (12%)
  blocking collectives  3.66 us (5%)
  matrix products  2.57 us (4%)
  local copies, waits for them, and re-layouts  1.2 us (2%)
  between operations  0.89 us (1%)
    ppermute x12, waiting for transfers between devices, from_partner(): return lax.ppermute(value, axis, pairs)  21.2 us
    ppermute x12, starting transfers between devices, from_partner(): return lax.ppermute(value, axis, pairs)  19 us
    pallas_call x2, Pallas kernels, ffn_grad(): pl.pallas_call(ffn_kernel, grid=(groups_here // per_step,), in_specs=[act...  8.11 us
    all_to_all x1, blocking collectives, hid_sum_sync(): parts = lax.all_to_all(jnp.stack([value] * size), 'hid', 0, 0)  3.66 us
    reduce_sum x2, other arithmetic, body(): inner = reduce_hid(jnp.sum(resid * scaled, axis=-1))  2.29 us
    add x3, other arithmetic, hid_sum(): total = total + lax.ppermute(value, 'hid', pairs)  1.95 us
    reduce_sum x6, other arithmetic, body(): jnp.sum(back_f * mates[chunk][section].astype(jnp.float32), axis=-1)  1.64 us
    convert_element_type x2, other arithmetic, body(): normed = (resid * inv[:, None] * norm_gain).astype(jnp.bfloat16)  1.5 us
  transfers between devices with their start and end apart: 18, of which 10 were waited for; matrix products, arithmetic and copies ran while one was open for 15% of the time, Pallas kernels for 12%

profile of v17, /device:TPU:0, one launch (start us, length us, event | category | flops | bytes accessed | tf_op | source)
XLA Modules:
  0.0 67.8 jit_solution(1492822385899970693)
XLA Ops:
  0.7 1.2 %convolution_convert_fusion.1 = bf16[64,1024]{1,0:T(8,128)(2,1)S(1)} fusion(bf16[128,1024]{1,0:T(8,128)(2,1)} %param.9, bf16[1,128,128]{2,1,0:T(8,128)(2,1)} %param.11), kind=kOutput, calls=%fused_computation.4 | convolution fusion | flops 16842752 | bytes 409600 | tf_op jit(solution)/shard_map/kij,kjd->kid/dot_general | solution.py:101
  1.8 3.0 %collective-permute-start = (bf16[64,1024]{1,0:T(8,128)(2,1)S(1)}, bf16[64,1024]{1,0:T(8,128)(2,1)S(1)}, u32[]{:S(2)}, u32[]{:S(2)}) collective-permute-start(bf16[64,1024]{1,0:T(8,128)(2,1)S(1)} %convolution_convert_fusion.1), channel_id=1, source_target_pairs={{0,2},{2,0},{4,6},{6,4},{8,10},{10,8},{12,14},{14,12},{1,3},{3,1},... | collective-permute-start | bytes 393224 | tf_op jit(solution)/shard_map/ppermute | solution.py:14
  5.6 3.5 %collective-permute-done = bf16[64,1024]{1,0:T(8,128)(2,1)S(1)} collective-permute-done((bf16[64,1024]{1,0:T(8,128)(2,1)S(1)}, bf16[64,1024]{1,0:T(8,128)(2,1)S(1)}, u32[]{:S(2)}, u32[]{:S(2)}) %collective-permute-start) | collective-permute-done | bytes 131104 | tf_op jit(solution)/shard_map/ppermute | solution.py:14
  9.3 2.2 %collective-permute-start.1 = (bf16[64,1024]{1,0:T(8,128)(2,1)S(1)}, bf16[64,1024]{1,0:T(8,128)(2,1)S(1)}, u32[]{:S(2)}, u32[]{:S(2)}) collective-permute-start(bf16[64,1024]{1,0:T(8,128)(2,1)S(1)} %fusion.4), channel_id=1, source_target_pairs={{0,4},{2,6},{4,0},{6,2},{8,12},{10,14},{12,8},{14,10},{1,5},{3,7},... | collective-permute-start | bytes 393224 | tf_op jit(solution)/shard_map/ppermute | solution.py:14
  11.5 0.7 %fusion.67 = (bf16[64,1024]{1,0:T(8,128)(2,1)}, bf16[64,1024]{1,0:T(8,128)(2,1)}) fusion(bf16[128,1024]{1,0:T(8,128)(2,1)S(1)} %copy-done.3), kind=kLoop, calls=%fused_computation.135 | loop fusion | bytes 524288 | tf_op jit(solution)/shard_map/slice | solution.py:128
  12.2 2.2 %collective-permute-done.1 = bf16[64,1024]{1,0:T(8,128)(2,1)S(1)} collective-permute-done((bf16[64,1024]{1,0:T(8,128)(2,1)S(1)}, bf16[64,1024]{1,0:T(8,128)(2,1)S(1)}, u32[]{:S(2)}, u32[]{:S(2)}) %collective-permute-start.1) | collective-permute-done | bytes 131104 | tf_op jit(solution)/shard_map/ppermute | solution.py:14
  14.6 3.8 %collective-permute-start.2 = (bf16[64,1024]{1,0:T(8,128)(2,1)S(1)}, bf16[64,1024]{1,0:T(8,128)(2,1)S(1)}, u32[]{:S(2)}, u32[]{:S(2)}) collective-permute-start(bf16[64,1024]{1,0:T(8,128)(2,1)S(1)} %fusion.6), channel_id=1, source_target_pairs={{0,8},{2,10},{4,12},{6,14},{8,0},{10,2},{12,4},{14,6},{1,9},{3,11}... | collective-permute-start | bytes 393224 | tf_op jit(solution)/shard_map/ppermute | solution.py:14
  18.5 1.2 %collective-permute-start.6 = (bf16[64,1024]{1,0:T(8,128)(2,1)S(1)}, bf16[64,1024]{1,0:T(8,128)(2,1)S(1)}, u32[]{:S(2)}, u32[]{:S(2)}) collective-permute-start(bf16[64,1024]{1,0:T(8,128)(2,1)S(1)} %fusion.12), channel_id=1, source_target_pairs={{0,4},{2,6},{4,0},{6,2},{8,12},{10,14},{12,8},{14,10},{1,5},{3,7},... | collective-permute-start | bytes 393224 | tf_op jit(solution)/shard_map/ppermute | solution.py:14
  19.7 3.1 %collective-permute-done.2 = bf16[64,1024]{1,0:T(8,128)(2,1)S(1)} collective-permute-done((bf16[64,1024]{1,0:T(8,128)(2,1)S(1)}, bf16[64,1024]{1,0:T(8,128)(2,1)S(1)}, u32[]{:S(2)}, u32[]{:S(2)}) %collective-permute-start.2) | collective-permute-done | bytes 131104 | tf_op jit(solution)/shard_map/ppermute | solution.py:14
  23.1 1.0 %collective-permute-done.6 = bf16[64,1024]{1,0:T(8,128)(2,1)S(1)} collective-permute-done((bf16[64,1024]{1,0:T(8,128)(2,1)S(1)}, bf16[64,1024]{1,0:T(8,128)(2,1)S(1)}, u32[]{:S(2)}, u32[]{:S(2)}) %collective-permute-start.6) | collective-permute-done | bytes 131104 | tf_op jit(solution)/shard_map/ppermute | solution.py:14
  24.2 0.6 collective-permute-start.7
  24.9 0.8 %multiply_convert_fusion.1.normed_ref = bf16[64,1024]{1,0:T(8,128)(2,1)} fusion(bf16[64,1024]{1,0:T(8,128)(2,1)S(1)} %get-tuple-element.25, f32[1024]{0:T(1024)S(1)} %copy-done.4, f32[64]{0:T(128)S(1)} %add_rsqrt_fusion.1, bf16[128,1024]{1,0:T(8,128)(2,1)S(1)} %copy-done), kind=kLoop, calls=%fused_computation.101 | loop fusion | flops 458752 | bytes 397568 | tf_op jit(solution)/shard_map/convert_element_type | solution.py:135
  25.7 4.1 %shard_map.120 = f32[64,1024]{1,0:T(8,128)} custom-call(bf16[64,1024]{1,0:T(8,128)(2,1)} %multiply_convert_fusion.1.normed_ref, bf16[64,1024]{1,0:T(8,128)(2,1)} %get-tuple-element.29.cot_ref, bf16[8,128,512]{2,1,0:T(8,128)(2,1)} %wg_ref.3, bf16[8,128,512]{2,1,0:T(8,128)(2,1)} %wu_ref.3, bf16[8,512,128]{2,1,0:T(8,128)(2,1)} %wd_ref.3), custom_call_target="tpu_custom_call" | custom-call | flops 335544320 | bytes 3670016 | tf_op jit(solution)/shard_map/pallas_call | solution.py:44
  29.7 1.1 %multiply_reduce_fusion.2 = f32[64]{0:T(128)S(1)} fusion(f32[64,1024]{1,0:T(8,128)} %shard_map.120, bf16[64,1024]{1,0:T(8,128)(2,1)S(1)} %get-tuple-element.25, f32[1024]{0:T(1024)S(1)} %copy-done.4, bf16[128,1024]{1,0:T(8,128)(2,1)S(1)} %copy-done), kind=kLoop, calls=%fused_computation.100 | loop fusion | flops 458688 | bytes 528640 | tf_op jit(solution)/shard_map/reduce_sum | solution.py:138
  31.1 1.8 %collective-permute-done.7 = bf16[64,1024]{1,0:T(8,128)(2,1)S(1)} collective-permute-done((bf16[64,1024]{1,0:T(8,128)(2,1)S(1)}, bf16[64,1024]{1,0:T(8,128)(2,1)S(1)}, u32[]{:S(2)}, u32[]{:S(2)}) %collective-permute-start.7) | collective-permute-done | bytes 131104 | tf_op jit(solution)/shard_map/ppermute | solution.py:14
  33.7 1.5 %collective-permute-start.9 = (bf16[64,1024]{1,0:T(8,128)(2,1)S(1)}, bf16[64,1024]{1,0:T(8,128)(2,1)S(1)}, u32[]{:S(2)}, u32[]{:S(2)}) collective-permute-start(bf16[64,1024]{1,0:T(8,128)(2,1)S(1)} %fusion.18), channel_id=1, source_target_pairs={{0,8},{2,10},{4,12},{6,14},{8,0},{10,2},{12,4},{14,6},{1,9},{3,11}... | collective-permute-start | bytes 393224 | tf_op jit(solution)/shard_map/ppermute | solution.py:14
  35.2 0.8 %multiply_convert_fusion.normed_ref = bf16[64,1024]{1,0:T(8,128)(2,1)} fusion(bf16[64,1024]{1,0:T(8,128)(2,1)S(1)} %fusion.16, f32[64]{0:T(128)S(1)} %add_rsqrt_fusion, f32[1024]{0:T(1024)S(1)} %copy-done.4, bf16[128,1024]{1,0:T(8,128)(2,1)S(1)} %copy-done), kind=kLoop, calls=%fused_computation.97 | loop fusion | flops 458752 | bytes 397568 | tf_op jit(solution)/shard_map/convert_element_type | solution.py:135
  36.0 4.1 %shard_map.121 = f32[64,1024]{1,0:T(8,128)} custom-call(bf16[64,1024]{1,0:T(8,128)(2,1)} %multiply_convert_fusion.normed_ref, bf16[64,1024]{1,0:T(8,128)(2,1)} %get-tuple-element.28.cot_ref, bf16[8,128,512]{2,1,0:T(8,128)(2,1)} %wg_ref.3, bf16[8,128,512]{2,1,0:T(8,128)(2,1)} %wu_ref.3, bf16[8,512,128]{2,1,0:T(8,128)(2,1)} %wd_ref.3), custom_call_target="tpu_custom_call" | custom-call | flops 335544320 | bytes 3670016 | tf_op jit(solution)/shard_map/pallas_call | solution.py:44
  40.0 1.2 %multiply_reduce_fusion = f32[64]{0:T(128)S(1)} fusion(f32[64,1024]{1,0:T(8,128)} %shard_map.121, bf16[64,1024]{1,0:T(8,128)(2,1)S(1)} %fusion.16, f32[1024]{0:T(1024)S(1)} %copy-done.4, bf16[128,1024]{1,0:T(8,128)(2,1)S(1)} %copy-done), kind=kLoop, calls=%fused_computation.96 | loop fusion | flops 458688 | bytes 528640 | tf_op jit(solution)/shard_map/reduce_sum | solution.py:138
  41.2 3.7 %all_to_all.9 = f32[2,1,64]{2,1,0:T(1,128)S(1)} all-to-all(f32[2,1,64]{2,1,0:T(1,128)S(1)} %bitcast.90), channel_id=1, replica_groups=mesh['groups'=2,'seq'=8,'hid'=2] {'hid'}, dimensions={0} | all-to-all | bytes 1024 | tf_op jit(solution)/shard_map/all_to_all | solution.py:66
  45.3 1.5 %collective-permute-start.12 = (bf16[64,1024]{1,0:T(8,128)(2,1)S(1)}, bf16[64,1024]{1,0:T(8,128)(2,1)S(1)}, u32[]{:S(2)}, u32[]{:S(2)}) collective-permute-start(bf16[64,1024]{1,0:T(8,128)(2,1)S(1)} %fusion.35), channel_id=1, source_target_pairs={{0,8},{2,10},{4,12},{6,14},{8,0},{10,2},{12,4},{14,6},{1,9},{3,11}... | collective-permute-start | bytes 393224 | tf_op jit(solution)/shard_map/ppermute | solution.py:14
  47.2 1.6 %collective-permute-start.10 = (bf16[64,1024]{1,0:T(8,128)(2,1)S(1)}, bf16[64,1024]{1,0:T(8,128)(2,1)S(1)}, u32[]{:S(2)}, u32[]{:S(2)}) collective-permute-start(bf16[64,1024]{1,0:T(8,128)(2,1)S(1)} %fusion.25), channel_id=1, source_target_pairs={{0,4},{2,6},{4,0},{6,2},{8,12},{10,14},{12,8},{14,10},{1,5},{3,7},... | collective-permute-start | bytes 393224 | tf_op jit(solution)/shard_map/ppermute | solution.py:14
  48.8 5.8 %collective-permute-done.12 = bf16[64,1024]{1,0:T(8,128)(2,1)S(1)} collective-permute-done((bf16[64,1024]{1,0:T(8,128)(2,1)S(1)}, bf16[64,1024]{1,0:T(8,128)(2,1)S(1)}, u32[]{:S(2)}, u32[]{:S(2)}) %collective-permute-start.12) | collective-permute-done | bytes 131104 | tf_op jit(solution)/shard_map/ppermute | solution.py:14
  55.5 1.6 %collective-permute-start.11 = (bf16[64,1024]{1,0:T(8,128)(2,1)S(1)}, bf16[64,1024]{1,0:T(8,128)(2,1)S(1)}, u32[]{:S(2)}, u32[]{:S(2)}) collective-permute-start(bf16[64,1024]{1,0:T(8,128)(2,1)S(1)} %fusion.30), channel_id=1, source_target_pairs={{0,2},{2,0},{4,6},{6,4},{8,10},{10,8},{12,14},{14,12},{1,3},{3,1},... | collective-permute-start | bytes 393224 | tf_op jit(solution)/shard_map/ppermute | solution.py:14
  57.1 3.0 %collective-permute-done.13 = bf16[64,1024]{1,0:T(8,128)(2,1)S(1)} collective-permute-done((bf16[64,1024]{1,0:T(8,128)(2,1)S(1)}, bf16[64,1024]{1,0:T(8,128)(2,1)S(1)}, u32[]{:S(2)}, u32[]{:S(2)}) %collective-permute-start.13) | collective-permute-done | bytes 131104 | tf_op jit(solution)/shard_map/ppermute | solution.py:14
  60.4 1.6 %collective-permute-start.14 = (bf16[64,1024]{1,0:T(8,128)(2,1)S(1)}, bf16[64,1024]{1,0:T(8,128)(2,1)S(1)}, u32[]{:S(2)}, u32[]{:S(2)}) collective-permute-start(bf16[64,1024]{1,0:T(8,128)(2,1)S(1)} %fusion.45), channel_id=1, source_target_pairs={{0,2},{2,0},{4,6},{6,4},{8,10},{10,8},{12,14},{14,12},{1,3},{3,1},... | collective-permute-start | bytes 393224 | tf_op jit(solution)/shard_map/ppermute | solution.py:14
  62.7 0.6 collective-permute-done.16
  63.3 0.7 fusion.71
  63.9 0.7 fusion.72
  64.7 0.7 %collective-permute-done.14 = bf16[64,1024]{1,0:T(8,128)(2,1)S(1)} collective-permute-done((bf16[64,1024]{1,0:T(8,128)(2,1)S(1)}, bf16[64,1024]{1,0:T(8,128)(2,1)S(1)}, u32[]{:S(2)}, u32[]{:S(2)}) %collective-permute-start.14) | collective-permute-done | bytes 131104 | tf_op jit(solution)/shard_map/ppermute | solution.py:14
  65.9 1.0 %fusion.1 = bf16[128,1024]{1,0:T(8,128)(2,1)} fusion(f32[64,1024]{1,0:T(8,128)S(1)} %get-tuple-element.26, f32[64,1024]{1,0:T(8,128)S(1)} %get-tuple-element.27, bf16[64,1024]{1,0:T(8,128)(2,1)S(1)} %fusion.44, bf16[64,1024]{1,0:T(8,128)(2,1)S(1)} %fusion.29, bf16[1,128,128]{2,1,0:T(8,128)(2,1)S(1)} %copy-done.5), kind=kOutput, calls=%fused_computation.2 | convolution fusion | flops 34471936 | bytes 1081344 | tf_op jit(solution)/shard_map/kij,kid->kjd/dot_general | solution.py:176
  67.1 0.6 add.115
  (64 shorter events, 5.9 us)
Async XLA Ops:
  0.6 4.2 %copy-start.5 = (bf16[1,128,128]{2,1,0:T(8,128)(2,1)S(1)}, bf16[1,128,128]{2,1,0:T(8,128)(2,1)}, u32[]{:S(2)}) copy-start(bf16[1,128,128]{2,1,0:T(8,128)(2,1)} %param.11) | copy-start | bytes 98308
  0.6 4.2 %copy-start = (bf16[128,1024]{1,0:T(8,128)(2,1)S(1)}, bf16[128,1024]{1,0:T(8,128)(2,1)}, u32[]{:S(2)}) copy-start(bf16[128,1024]{1,0:T(8,128)(2,1)} %param.9) | copy-start | bytes 786436
  1.8 7.3 %collective-permute-start = (bf16[64,1024]{1,0:T(8,128)(2,1)S(1)}, bf16[64,1024]{1,0:T(8,128)(2,1)S(1)}, u32[]{:S(2)}, u32[]{:S(2)}) collective-permute-start(bf16[64,1024]{1,0:T(8,128)(2,1)S(1)} %convolution_convert_fusion.1), channel_id=1, source_target_pairs={{0,2},{2,0},{4,6},{6,4},{8,10},{10,8},{12,14},{14,12},{1,3},{3,1},... | collective-permute-start | bytes 393224 | tf_op jit(solution)/shard_map/ppermute | solution.py:14
  4.9 0.7 %copy-start.6 = (f32[3,128]{1,0:T(4,128)S(1)}, f32[3,128]{1,0:T(4,128)}, u32[]{:S(2)}) copy-start(f32[3,128]{1,0:T(4,128)} %param.13) | copy-start | bytes 4612
  4.9 0.7 %copy-start.7 = (f32[3,128]{1,0:T(4,128)S(1)}, f32[3,128]{1,0:T(4,128)}, u32[]{:S(2)}) copy-start(f32[3,128]{1,0:T(4,128)} %param.12) | copy-start | bytes 4612
  5.0 6.5 %copy-start.3 = (bf16[128,1024]{1,0:T(8,128)(2,1)S(1)}, bf16[128,1024]{1,0:T(8,128)(2,1)}, u32[]{:S(2)}) copy-start(bf16[128,1024]{1,0:T(8,128)(2,1)} %param.10) | copy-start | bytes 786436
  5.1 13.3 %collective-permute-start.5 = (bf16[64,1024]{1,0:T(8,128)(2,1)S(1)}, bf16[64,1024]{1,0:T(8,128)(2,1)S(1)}, u32[]{:S(2)}, u32[]{:S(2)}) collective-permute-start(bf16[64,1024]{1,0:T(8,128)(2,1)S(1)} %convolution_convert_fusion), channel_id=1, source_target_pairs={{0,2},{2,0},{4,6},{6,4},{8,10},{10,8},{12,14},{14,12},{1,3},{3,1},... | collective-permute-start | bytes 393224 | tf_op jit(solution)/shard_map/ppermute | solution.py:14
  9.3 5.2 %collective-permute-start.1 = (bf16[64,1024]{1,0:T(8,128)(2,1)S(1)}, bf16[64,1024]{1,0:T(8,128)(2,1)S(1)}, u32[]{:S(2)}, u32[]{:S(2)}) collective-permute-start(bf16[64,1024]{1,0:T(8,128)(2,1)S(1)} %fusion.4), channel_id=1, source_target_pairs={{0,4},{2,6},{4,0},{6,2},{8,12},{10,14},{12,8},{14,10},{1,5},{3,7},... | collective-permute-start | bytes 393224 | tf_op jit(solution)/shard_map/ppermute | solution.py:14
  14.6 8.2 %collective-permute-start.2 = (bf16[64,1024]{1,0:T(8,128)(2,1)S(1)}, bf16[64,1024]{1,0:T(8,128)(2,1)S(1)}, u32[]{:S(2)}, u32[]{:S(2)}) collective-permute-start(bf16[64,1024]{1,0:T(8,128)(2,1)S(1)} %fusion.6), channel_id=1, source_target_pairs={{0,8},{2,10},{4,12},{6,14},{8,0},{10,2},{12,4},{14,6},{1,9},{3,11}... | collective-permute-start | bytes 393224 | tf_op jit(solution)/shard_map/ppermute | solution.py:14
  18.5 5.6 %collective-permute-start.6 = (bf16[64,1024]{1,0:T(8,128)(2,1)S(1)}, bf16[64,1024]{1,0:T(8,128)(2,1)S(1)}, u32[]{:S(2)}, u32[]{:S(2)}) collective-permute-start(bf16[64,1024]{1,0:T(8,128)(2,1)S(1)} %fusion.12), channel_id=1, source_target_pairs={{0,4},{2,6},{4,0},{6,2},{8,12},{10,14},{12,8},{14,10},{1,5},{3,7},... | collective-permute-start | bytes 393224 | tf_op jit(solution)/shard_map/ppermute | solution.py:14
  23.1 1.8 %collective-permute-start.3 = (f32[64]{0:T(128)S(1)}, f32[64]{0:T(128)S(1)}, u32[]{:S(2)}, u32[]{:S(2)}) collective-permute-start(f32[64]{0:T(128)S(1)} %get-tuple-element.24), channel_id=1, source_target_pairs={{0,1},{1,0},{2,3},{3,2},{4,5},{5,4},{6,7},{7,6},{8,9},{9,8},{10,11... | collective-permute-start | bytes 776 | tf_op jit(solution)/shard_map/ppermute | solution.py:78
  24.1 0.8 %copy-start.4 = (f32[1024]{0:T(1024)S(1)}, f32[1024]{0:T(1024)}, u32[]{:S(2)}) copy-start(f32[1024]{0:T(1024)} %param.14) | copy-start | bytes 12292
  24.2 8.7 %collective-permute-start.7 = (bf16[64,1024]{1,0:T(8,128)(2,1)S(1)}, bf16[64,1024]{1,0:T(8,128)(2,1)S(1)}, u32[]{:S(2)}, u32[]{:S(2)}) collective-permute-start(bf16[64,1024]{1,0:T(8,128)(2,1)S(1)} %fusion.14), channel_id=1, source_target_pairs={{0,8},{2,10},{4,12},{6,14},{8,0},{10,2},{12,4},{14,6},{1,9},{3,11}... | collective-permute-start | bytes 393224 | tf_op jit(solution)/shard_map/ppermute | solution.py:14
  30.8 2.2 %copy-start.1 = (f32[64,1024]{1,0:T(8,128)S(1)}, f32[64,1024]{1,0:T(8,128)}, u32[]{:S(2)}) copy-start(f32[64,1024]{1,0:T(8,128)} %shard_map.120) | copy-start | bytes 786436
  30.8 2.2 %collective-permute-start.4 = (f32[64]{0:T(128)S(1)}, f32[64]{0:T(128)S(1)}, u32[]{:S(2)}, u32[]{:S(2)}) collective-permute-start(f32[64]{0:T(128)S(1)} %multiply_reduce_fusion.2), channel_id=1, source_target_pairs={{0,1},{1,0},{2,3},{3,2},{4,5},{5,4},{6,7},{7,6},{8,9},{9,8},{10,11... | collective-permute-start | bytes 776 | tf_op jit(solution)/shard_map/ppermute | solution.py:78
  33.6 1.6 %collective-permute-start.8 = (f32[64]{0:T(128)S(1)}, f32[64]{0:T(128)S(1)}, u32[]{:S(2)}, u32[]{:S(2)}) collective-permute-start(f32[64]{0:T(128)S(1)} %multiply_reduce_fusion.1), channel_id=1, source_target_pairs={{0,1},{1,0},{2,3},{3,2},{4,5},{5,4},{6,7},{7,6},{8,9},{9,8},{10,11... | collective-permute-start | bytes 776 | tf_op jit(solution)/shard_map/ppermute | solution.py:78
  33.7 13.2 %collective-permute-start.9 = (bf16[64,1024]{1,0:T(8,128)(2,1)S(1)}, bf16[64,1024]{1,0:T(8,128)(2,1)S(1)}, u32[]{:S(2)}, u32[]{:S(2)}) collective-permute-start(bf16[64,1024]{1,0:T(8,128)(2,1)S(1)} %fusion.18), channel_id=1, source_target_pairs={{0,8},{2,10},{4,12},{6,14},{8,0},{10,2},{12,4},{14,6},{1,9},{3,11}... | collective-permute-start | bytes 393224 | tf_op jit(solution)/shard_map/ppermute | solution.py:14
  40.0 4.9 %copy-start.2 = (f32[64,1024]{1,0:T(8,128)S(1)}, f32[64,1024]{1,0:T(8,128)}, u32[]{:S(2)}) copy-start(f32[64,1024]{1,0:T(8,128)} %shard_map.121) | copy-start | bytes 786436
  45.3 9.4 %collective-permute-start.12 = (bf16[64,1024]{1,0:T(8,128)(2,1)S(1)}, bf16[64,1024]{1,0:T(8,128)(2,1)S(1)}, u32[]{:S(2)}, u32[]{:S(2)}) collective-permute-start(bf16[64,1024]{1,0:T(8,128)(2,1)S(1)} %fusion.35), channel_id=1, source_target_pairs={{0,8},{2,10},{4,12},{6,14},{8,0},{10,2},{12,4},{14,6},{1,9},{3,11}... | collective-permute-start | bytes 393224 | tf_op jit(solution)/shard_map/ppermute | solution.py:14
  47.2 7.9 %collective-permute-start.10 = (bf16[64,1024]{1,0:T(8,128)(2,1)S(1)}, bf16[64,1024]{1,0:T(8,128)(2,1)S(1)}, u32[]{:S(2)}, u32[]{:S(2)}) collective-permute-start(bf16[64,1024]{1,0:T(8,128)(2,1)S(1)} %fusion.25), channel_id=1, source_target_pairs={{0,4},{2,6},{4,0},{6,2},{8,12},{10,14},{12,8},{14,10},{1,5},{3,7},... | collective-permute-start | bytes 393224 | tf_op jit(solution)/shard_map/ppermute | solution.py:14
  55.0 5.0 %collective-permute-start.13 = (bf16[64,1024]{1,0:T(8,128)(2,1)S(1)}, bf16[64,1024]{1,0:T(8,128)(2,1)S(1)}, u32[]{:S(2)}, u32[]{:S(2)}) collective-permute-start(bf16[64,1024]{1,0:T(8,128)(2,1)S(1)} %fusion.40), channel_id=1, source_target_pairs={{0,4},{2,6},{4,0},{6,2},{8,12},{10,14},{12,8},{14,10},{1,5},{3,7},... | collective-permute-start | bytes 393224 | tf_op jit(solution)/shard_map/ppermute | solution.py:14
  55.5 9.1 %collective-permute-start.11 = (bf16[64,1024]{1,0:T(8,128)(2,1)S(1)}, bf16[64,1024]{1,0:T(8,128)(2,1)S(1)}, u32[]{:S(2)}, u32[]{:S(2)}) collective-permute-start(bf16[64,1024]{1,0:T(8,128)(2,1)S(1)} %fusion.30), channel_id=1, source_target_pairs={{0,2},{2,0},{4,6},{6,4},{8,10},{10,8},{12,14},{14,12},{1,3},{3,1},... | collective-permute-start | bytes 393224 | tf_op jit(solution)/shard_map/ppermute | solution.py:14
  60.4 5.0 %collective-permute-start.14 = (bf16[64,1024]{1,0:T(8,128)(2,1)S(1)}, bf16[64,1024]{1,0:T(8,128)(2,1)S(1)}, u32[]{:S(2)}, u32[]{:S(2)}) collective-permute-start(bf16[64,1024]{1,0:T(8,128)(2,1)S(1)} %fusion.45), channel_id=1, source_target_pairs={{0,2},{2,0},{4,6},{6,4},{8,10},{10,8},{12,14},{14,12},{1,3},{3,1},... | collective-permute-start | bytes 393224 | tf_op jit(solution)/shard_map/ppermute | solution.py:14
  62.1 1.2 %collective-permute-start.16 = (f32[3,128]{1,0:T(4,128)S(1)}, f32[3,128]{1,0:T(4,128)S(1)}, u32[]{:S(2)}, u32[]{:S(2)}) collective-permute-start(f32[3,128]{1,0:T(4,128)S(1)} %maximum_maximum_fusion.1), channel_id=1, source_target_pairs={{0,1},{1,0},{2,3},{3,2},{4,5},{5,4},{6,7},{7,6},{8,9},{9,8},{10,11... | collective-permute-start | bytes 4616 | tf_op jit(solution)/shard_map/ppermute | solution.py:78
  62.2 1.7 %collective-permute-start.15 = (f32[3,128]{1,0:T(4,128)S(1)}, f32[3,128]{1,0:T(4,128)S(1)}, u32[]{:S(2)}, u32[]{:S(2)}) collective-permute-start(f32[3,128]{1,0:T(4,128)S(1)} %maximum_maximum_fusion), channel_id=1, source_target_pairs={{0,1},{1,0},{2,3},{3,2},{4,5},{5,4},{6,7},{7,6},{8,9},{9,8},{10,11... | collective-permute-start | bytes 4616 | tf_op jit(solution)/shard_map/ppermute | solution.py:78
  65.8 1.3 %collective-permute-start.17 = (f32[1,128,128]{2,1,0:T(8,128)S(1)}, f32[1,128,128]{2,1,0:T(8,128)S(1)}, u32[]{:S(2)}, u32[]{:S(2)}) collective-permute-start(f32[1,128,128]{2,1,0:T(8,128)S(1)} %convolution_bitcast_fusion.1), channel_id=1, source_target_pairs={{0,1},{1,0},{2,3},{3,2},{4,5},{5,4},{6,7},{7,6},{8,9},{9,8},{10,11... | collective-permute-start | bytes 196616 | tf_op jit(solution)/shard_map/ppermute | solution.py:78

commit v18 on v13

--- a/solution.py
+++ b/solution.py
@@ -6,6 +6,7 @@
 
 D = 2048
 CHUNKS = 2
+LANES = 128
 
 
 def from_partner(value, axis, distance):
@@ -126,7 +127,8 @@
         normed = (resid * inv[:, None] * norm_gain).astype(jnp.bfloat16)
         d_normed = ffn_grad(normed, cot, w_gate, w_up, w_down)
         scaled = norm_gain * d_normed
-        inner = reduce_hid(jnp.sum(resid * scaled, axis=-1))
+        lanes = jnp.sum((resid * scaled).reshape(resid.shape[0], -1, LANES), axis=1)
+        inner = reduce_hid(jnp.sum(lax.optimization_barrier(lanes), axis=-1))
         d_resid = (
             cot.astype(jnp.float32)
             + inv[:, None] * scaled

time: 66.8 us -> 67 us (level)
    unnamed x0 -> x2, other arithmetic: none -> 2.01 us
    reduce_sum x2 -> x4, other arithmetic: 2.29 us -> 0.35 us  [the longest x2 0.21 us: body(): inner = reduce_hid(jnp.sum(lax.optimization_barrier(lanes), axis=-1))]
where the time goes in v18:
time: 67 us; the launch traced here: 66.7 us
  waiting for transfers between devices  21.9 us (33%)
  starting transfers between devices  20.1 us (30%)
  other arithmetic  9.37 us (14%)
  Pallas kernels  8.11 us (12%)
  matrix products  2.57 us (4%)
  blocking collectives  2.47 us (4%)
  local copies, waits for them, and re-layouts  1.3 us (2%)
  between operations  0.92 us (1%)
    ppermute x12, waiting for transfers between devices, from_partner(): return lax.ppermute(value, axis, pairs)  21.1 us
    ppermute x12, starting transfers between devices, from_partner(): return lax.ppermute(value, axis, pairs)  19.1 us
    pallas_call x2, Pallas kernels, ffn_grad(): pl.pallas_call(ffn_kernel, grid=(groups_here // per_step,), in_specs=[act...  8.11 us
    psum x1, blocking collectives, body(): reduce_hid = hid_sum if chunk == 0 else lambda v: lax.psum(v, 'hid')  2.47 us
    unnamed x2, other arithmetic  2.01 us
    add x3, other arithmetic, hid_sum(): total = total + lax.ppermute(value, 'hid', pairs)  1.95 us
    reduce_sum x6, other arithmetic, body(): jnp.sum(back_f * mates[chunk][section].astype(jnp.float32), axis=-1)  1.64 us
    convert_element_type x2, other arithmetic, body(): normed = (resid * inv[:, None] * norm_gain).astype(jnp.bfloat16)  1.5 us
  transfers between devices with their start and end apart: 18, of which 10 were waited for; matrix products, arithmetic and copies ran while one was open for 15% of the time, Pallas kernels for 12%

profile of v18, /device:TPU:0, one launch (start us, length us, event | category | flops | bytes accessed | tf_op | source)
XLA Modules:
  0.0 66.7 jit_solution(5721853697374404288)
XLA Ops:
  0.7 1.2 %convolution_convert_fusion.1 = bf16[64,1024]{1,0:T(8,128)(2,1)S(1)} fusion(bf16[128,1024]{1,0:T(8,128)(2,1)} %param.9, bf16[1,128,128]{2,1,0:T(8,128)(2,1)} %param.11), kind=kOutput, calls=%fused_computation.4 | convolution fusion | flops 16842752 | bytes 409600 | tf_op jit(solution)/shard_map/kij,kjd->kid/dot_general | solution.py:93
  1.8 3.0 %collective-permute-start = (bf16[64,1024]{1,0:T(8,128)(2,1)S(1)}, bf16[64,1024]{1,0:T(8,128)(2,1)S(1)}, u32[]{:S(2)}, u32[]{:S(2)}) collective-permute-start(bf16[64,1024]{1,0:T(8,128)(2,1)S(1)} %convolution_convert_fusion.1), channel_id=1, source_target_pairs={{0,2},{2,0},{4,6},{6,4},{8,10},{10,8},{12,14},{14,12},{1,3},{3,1},... | collective-permute-start | bytes 393224 | tf_op jit(solution)/shard_map/ppermute | solution.py:15
  5.6 3.5 %collective-permute-done = bf16[64,1024]{1,0:T(8,128)(2,1)S(1)} collective-permute-done((bf16[64,1024]{1,0:T(8,128)(2,1)S(1)}, bf16[64,1024]{1,0:T(8,128)(2,1)S(1)}, u32[]{:S(2)}, u32[]{:S(2)}) %collective-permute-start) | collective-permute-done | bytes 131104 | tf_op jit(solution)/shard_map/ppermute | solution.py:15
  9.3 2.2 %collective-permute-start.1 = (bf16[64,1024]{1,0:T(8,128)(2,1)S(1)}, bf16[64,1024]{1,0:T(8,128)(2,1)S(1)}, u32[]{:S(2)}, u32[]{:S(2)}) collective-permute-start(bf16[64,1024]{1,0:T(8,128)(2,1)S(1)} %fusion.4), channel_id=1, source_target_pairs={{0,4},{2,6},{4,0},{6,2},{8,12},{10,14},{12,8},{14,10},{1,5},{3,7},... | collective-permute-start | bytes 393224 | tf_op jit(solution)/shard_map/ppermute | solution.py:15
  11.5 0.7 %fusion.66 = (bf16[64,1024]{1,0:T(8,128)(2,1)}, bf16[64,1024]{1,0:T(8,128)(2,1)}) fusion(bf16[128,1024]{1,0:T(8,128)(2,1)S(1)} %copy-done.3), kind=kLoop, calls=%fused_computation.134 | loop fusion | bytes 524288 | tf_op jit(solution)/shard_map/slice | solution.py:120
  12.2 2.2 %collective-permute-done.1 = bf16[64,1024]{1,0:T(8,128)(2,1)S(1)} collective-permute-done((bf16[64,1024]{1,0:T(8,128)(2,1)S(1)}, bf16[64,1024]{1,0:T(8,128)(2,1)S(1)}, u32[]{:S(2)}, u32[]{:S(2)}) %collective-permute-start.1) | collective-permute-done | bytes 131104 | tf_op jit(solution)/shard_map/ppermute | solution.py:15
  14.6 3.8 %collective-permute-start.2 = (bf16[64,1024]{1,0:T(8,128)(2,1)S(1)}, bf16[64,1024]{1,0:T(8,128)(2,1)S(1)}, u32[]{:S(2)}, u32[]{:S(2)}) collective-permute-start(bf16[64,1024]{1,0:T(8,128)(2,1)S(1)} %fusion.6), channel_id=1, source_target_pairs={{0,8},{2,10},{4,12},{6,14},{8,0},{10,2},{12,4},{14,6},{1,9},{3,11}... | collective-permute-start | bytes 393224 | tf_op jit(solution)/shard_map/ppermute | solution.py:15
  18.5 1.2 %collective-permute-start.6 = (bf16[64,1024]{1,0:T(8,128)(2,1)S(1)}, bf16[64,1024]{1,0:T(8,128)(2,1)S(1)}, u32[]{:S(2)}, u32[]{:S(2)}) collective-permute-start(bf16[64,1024]{1,0:T(8,128)(2,1)S(1)} %fusion.12), channel_id=1, source_target_pairs={{0,4},{2,6},{4,0},{6,2},{8,12},{10,14},{12,8},{14,10},{1,5},{3,7},... | collective-permute-start | bytes 393224 | tf_op jit(solution)/shard_map/ppermute | solution.py:15
  19.7 3.1 %collective-permute-done.2 = bf16[64,1024]{1,0:T(8,128)(2,1)S(1)} collective-permute-done((bf16[64,1024]{1,0:T(8,128)(2,1)S(1)}, bf16[64,1024]{1,0:T(8,128)(2,1)S(1)}, u32[]{:S(2)}, u32[]{:S(2)}) %collective-permute-start.2) | collective-permute-done | bytes 131104 | tf_op jit(solution)/shard_map/ppermute | solution.py:15
  23.1 1.0 %collective-permute-done.6 = bf16[64,1024]{1,0:T(8,128)(2,1)S(1)} collective-permute-done((bf16[64,1024]{1,0:T(8,128)(2,1)S(1)}, bf16[64,1024]{1,0:T(8,128)(2,1)S(1)}, u32[]{:S(2)}, u32[]{:S(2)}) %collective-permute-start.6) | collective-permute-done | bytes 131104 | tf_op jit(solution)/shard_map/ppermute | solution.py:15
  24.2 0.6 collective-permute-start.7
  24.9 0.8 %multiply_convert_fusion.1.normed_ref = bf16[64,1024]{1,0:T(8,128)(2,1)} fusion(bf16[64,1024]{1,0:T(8,128)(2,1)S(1)} %get-tuple-element.25, f32[1024]{0:T(1024)S(1)} %copy-done.4, f32[64]{0:T(128)S(1)} %add_rsqrt_fusion.1, bf16[128,1024]{1,0:T(8,128)(2,1)S(1)} %copy-done), kind=kLoop, calls=%fused_computation.103 | loop fusion | flops 458752 | bytes 397568 | tf_op jit(solution)/shard_map/convert_element_type | solution.py:127
  25.7 4.1 %shard_map.120 = f32[64,1024]{1,0:T(8,128)} custom-call(bf16[64,1024]{1,0:T(8,128)(2,1)} %multiply_convert_fusion.1.normed_ref, bf16[64,1024]{1,0:T(8,128)(2,1)} %get-tuple-element.29.cot_ref, bf16[8,128,512]{2,1,0:T(8,128)(2,1)} %wg_ref.3, bf16[8,128,512]{2,1,0:T(8,128)(2,1)} %wu_ref.3, bf16[8,512,128]{2,1,0:T(8,128)(2,1)} %wd_ref.3), custom_call_target="tpu_custom_call" | custom-call | flops 335544320 | bytes 3670016 | tf_op jit(solution)/shard_map/pallas_call | solution.py:45
  29.7 1.0 %multiply_bitcast_fusion.1 = f32[8,8,8,128]{3,1,2,0:T(8,128)S(1)} fusion(f32[64,1024]{1,0:T(8,128)} %shard_map.120, bf16[64,1024]{1,0:T(8,128)(2,1)S(1)} %get-tuple-element.25, f32[1024]{0:T(1024)S(1)} %copy-done.4, bf16[128,1024]{1,0:T(8,128)(2,1)S(1)} %copy-done), kind=kLoop, calls=%fused_computation.102 | loop fusion | flops 393216 | bytes 790528
  31.2 1.7 %collective-permute-done.7 = bf16[64,1024]{1,0:T(8,128)(2,1)S(1)} collective-permute-done((bf16[64,1024]{1,0:T(8,128)(2,1)S(1)}, bf16[64,1024]{1,0:T(8,128)(2,1)S(1)}, u32[]{:S(2)}, u32[]{:S(2)}) %collective-permute-start.7) | collective-permute-done | bytes 131104 | tf_op jit(solution)/shard_map/ppermute | solution.py:15
  33.7 1.6 %collective-permute-start.9 = (bf16[64,1024]{1,0:T(8,128)(2,1)S(1)}, bf16[64,1024]{1,0:T(8,128)(2,1)S(1)}, u32[]{:S(2)}, u32[]{:S(2)}) collective-permute-start(bf16[64,1024]{1,0:T(8,128)(2,1)S(1)} %fusion.18), channel_id=1, source_target_pairs={{0,8},{2,10},{4,12},{6,14},{8,0},{10,2},{12,4},{14,6},{1,9},{3,11}... | collective-permute-start | bytes 393224 | tf_op jit(solution)/shard_map/ppermute | solution.py:15
  35.4 0.8 %multiply_convert_fusion.normed_ref = bf16[64,1024]{1,0:T(8,128)(2,1)} fusion(bf16[64,1024]{1,0:T(8,128)(2,1)S(1)} %fusion.16, f32[64]{0:T(128)S(1)} %add_rsqrt_fusion, f32[1024]{0:T(1024)S(1)} %copy-done.4, bf16[128,1024]{1,0:T(8,128)(2,1)S(1)} %copy-done), kind=kLoop, calls=%fused_computation.99 | loop fusion | flops 458752 | bytes 397568 | tf_op jit(solution)/shard_map/convert_element_type | solution.py:127
  36.1 4.1 %shard_map.121 = f32[64,1024]{1,0:T(8,128)} custom-call(bf16[64,1024]{1,0:T(8,128)(2,1)} %multiply_convert_fusion.normed_ref, bf16[64,1024]{1,0:T(8,128)(2,1)} %get-tuple-element.28.cot_ref, bf16[8,128,512]{2,1,0:T(8,128)(2,1)} %wg_ref.3, bf16[8,128,512]{2,1,0:T(8,128)(2,1)} %wu_ref.3, bf16[8,512,128]{2,1,0:T(8,128)(2,1)} %wd_ref.3), custom_call_target="tpu_custom_call" | custom-call | flops 335544320 | bytes 3670016 | tf_op jit(solution)/shard_map/pallas_call | solution.py:45
  40.2 1.0 %multiply_bitcast_fusion = f32[8,8,8,128]{3,1,2,0:T(8,128)S(1)} fusion(f32[64,1024]{1,0:T(8,128)} %shard_map.121, bf16[64,1024]{1,0:T(8,128)(2,1)S(1)} %fusion.16, f32[1024]{0:T(1024)S(1)} %copy-done.4, bf16[128,1024]{1,0:T(8,128)(2,1)S(1)} %copy-done), kind=kLoop, calls=%fused_computation.98 | loop fusion | flops 393216 | bytes 790528
  41.4 2.5 %psum.7 = f32[64]{0:T(128)S(1)} all-reduce(f32[64]{0:T(128)S(1)} %reduce_sum.167), channel_id=1, replica_groups=mesh['groups'=2,'seq'=8,'hid'=2] {'hid'}, use_global_device_ids=true, to_apply=%region_6.0 | all-reduce | flops 64 | bytes 512 | tf_op jit(solution)/shard_map/psum | solution.py:124
  44.3 1.4 %collective-permute-start.12 = (bf16[64,1024]{1,0:T(8,128)(2,1)S(1)}, bf16[64,1024]{1,0:T(8,128)(2,1)S(1)}, u32[]{:S(2)}, u32[]{:S(2)}) collective-permute-start(bf16[64,1024]{1,0:T(8,128)(2,1)S(1)} %fusion.35), channel_id=1, source_target_pairs={{0,8},{2,10},{4,12},{6,14},{8,0},{10,2},{12,4},{14,6},{1,9},{3,11}... | collective-permute-start | bytes 393224 | tf_op jit(solution)/shard_map/ppermute | solution.py:15
  46.1 1.8 %collective-permute-start.10 = (bf16[64,1024]{1,0:T(8,128)(2,1)S(1)}, bf16[64,1024]{1,0:T(8,128)(2,1)S(1)}, u32[]{:S(2)}, u32[]{:S(2)}) collective-permute-start(bf16[64,1024]{1,0:T(8,128)(2,1)S(1)} %fusion.25), channel_id=1, source_target_pairs={{0,4},{2,6},{4,0},{6,2},{8,12},{10,14},{12,8},{14,10},{1,5},{3,7},... | collective-permute-start | bytes 393224 | tf_op jit(solution)/shard_map/ppermute | solution.py:15
  47.8 5.8 %collective-permute-done.12 = bf16[64,1024]{1,0:T(8,128)(2,1)S(1)} collective-permute-done((bf16[64,1024]{1,0:T(8,128)(2,1)S(1)}, bf16[64,1024]{1,0:T(8,128)(2,1)S(1)}, u32[]{:S(2)}, u32[]{:S(2)}) %collective-permute-start.12) | collective-permute-done | bytes 131104 | tf_op jit(solution)/shard_map/ppermute | solution.py:15
  54.4 1.6 %collective-permute-start.11 = (bf16[64,1024]{1,0:T(8,128)(2,1)S(1)}, bf16[64,1024]{1,0:T(8,128)(2,1)S(1)}, u32[]{:S(2)}, u32[]{:S(2)}) collective-permute-start(bf16[64,1024]{1,0:T(8,128)(2,1)S(1)} %fusion.30), channel_id=1, source_target_pairs={{0,2},{2,0},{4,6},{6,4},{8,10},{10,8},{12,14},{14,12},{1,3},{3,1},... | collective-permute-start | bytes 393224 | tf_op jit(solution)/shard_map/ppermute | solution.py:15
  56.1 3.0 %collective-permute-done.13 = bf16[64,1024]{1,0:T(8,128)(2,1)S(1)} collective-permute-done((bf16[64,1024]{1,0:T(8,128)(2,1)S(1)}, bf16[64,1024]{1,0:T(8,128)(2,1)S(1)}, u32[]{:S(2)}, u32[]{:S(2)}) %collective-permute-start.13) | collective-permute-done | bytes 131104 | tf_op jit(solution)/shard_map/ppermute | solution.py:15
  59.4 1.6 %collective-permute-start.14 = (bf16[64,1024]{1,0:T(8,128)(2,1)S(1)}, bf16[64,1024]{1,0:T(8,128)(2,1)S(1)}, u32[]{:S(2)}, u32[]{:S(2)}) collective-permute-start(bf16[64,1024]{1,0:T(8,128)(2,1)S(1)} %fusion.45), channel_id=1, source_target_pairs={{0,2},{2,0},{4,6},{6,4},{8,10},{10,8},{12,14},{14,12},{1,3},{3,1},... | collective-permute-start | bytes 393224 | tf_op jit(solution)/shard_map/ppermute | solution.py:15
  61.7 0.6 collective-permute-done.16
  62.2 0.7 fusion.70
  62.9 0.7 fusion.71
  63.7 0.8 %collective-permute-done.14 = bf16[64,1024]{1,0:T(8,128)(2,1)S(1)} collective-permute-done((bf16[64,1024]{1,0:T(8,128)(2,1)S(1)}, bf16[64,1024]{1,0:T(8,128)(2,1)S(1)}, u32[]{:S(2)}, u32[]{:S(2)}) %collective-permute-start.14) | collective-permute-done | bytes 131104 | tf_op jit(solution)/shard_map/ppermute | solution.py:15
  64.9 1.0 %fusion.1 = bf16[128,1024]{1,0:T(8,128)(2,1)} fusion(f32[64,1024]{1,0:T(8,128)S(1)} %get-tuple-element.26, f32[64,1024]{1,0:T(8,128)S(1)} %get-tuple-element.27, bf16[64,1024]{1,0:T(8,128)(2,1)S(1)} %fusion.44, bf16[64,1024]{1,0:T(8,128)(2,1)S(1)} %fusion.29, bf16[1,128,128]{2,1,0:T(8,128)(2,1)S(1)} %copy-done.5), kind=kOutput, calls=%fused_computation.2 | convolution fusion | flops 34471936 | bytes 1081344 | tf_op jit(solution)/shard_map/kij,kid->kjd/dot_general | solution.py:169
  66.1 0.6 add.109
  (69 shorter events, 6.3 us)
Async XLA Ops:
  0.6 4.2 %copy-start.5 = (bf16[1,128,128]{2,1,0:T(8,128)(2,1)S(1)}, bf16[1,128,128]{2,1,0:T(8,128)(2,1)}, u32[]{:S(2)}) copy-start(bf16[1,128,128]{2,1,0:T(8,128)(2,1)} %param.11) | copy-start | bytes 98308
  0.6 4.2 %copy-start = (bf16[128,1024]{1,0:T(8,128)(2,1)S(1)}, bf16[128,1024]{1,0:T(8,128)(2,1)}, u32[]{:S(2)}) copy-start(bf16[128,1024]{1,0:T(8,128)(2,1)} %param.9) | copy-start | bytes 786436
  1.8 7.3 %collective-permute-start = (bf16[64,1024]{1,0:T(8,128)(2,1)S(1)}, bf16[64,1024]{1,0:T(8,128)(2,1)S(1)}, u32[]{:S(2)}, u32[]{:S(2)}) collective-permute-start(bf16[64,1024]{1,0:T(8,128)(2,1)S(1)} %convolution_convert_fusion.1), channel_id=1, source_target_pairs={{0,2},{2,0},{4,6},{6,4},{8,10},{10,8},{12,14},{14,12},{1,3},{3,1},... | collective-permute-start | bytes 393224 | tf_op jit(solution)/shard_map/ppermute | solution.py:15
  4.9 0.7 %copy-start.6 = (f32[3,128]{1,0:T(4,128)S(1)}, f32[3,128]{1,0:T(4,128)}, u32[]{:S(2)}) copy-start(f32[3,128]{1,0:T(4,128)} %param.13) | copy-start | bytes 4612
  4.9 0.7 %copy-start.7 = (f32[3,128]{1,0:T(4,128)S(1)}, f32[3,128]{1,0:T(4,128)}, u32[]{:S(2)}) copy-start(f32[3,128]{1,0:T(4,128)} %param.12) | copy-start | bytes 4612
  5.0 6.5 %copy-start.3 = (bf16[128,1024]{1,0:T(8,128)(2,1)S(1)}, bf16[128,1024]{1,0:T(8,128)(2,1)}, u32[]{:S(2)}) copy-start(bf16[128,1024]{1,0:T(8,128)(2,1)} %param.10) | copy-start | bytes 786436
  5.1 13.3 %collective-permute-start.5 = (bf16[64,1024]{1,0:T(8,128)(2,1)S(1)}, bf16[64,1024]{1,0:T(8,128)(2,1)S(1)}, u32[]{:S(2)}, u32[]{:S(2)}) collective-permute-start(bf16[64,1024]{1,0:T(8,128)(2,1)S(1)} %convolution_convert_fusion), channel_id=1, source_target_pairs={{0,2},{2,0},{4,6},{6,4},{8,10},{10,8},{12,14},{14,12},{1,3},{3,1},... | collective-permute-start | bytes 393224 | tf_op jit(solution)/shard_map/ppermute | solution.py:15
  9.3 5.2 %collective-permute-start.1 = (bf16[64,1024]{1,0:T(8,128)(2,1)S(1)}, bf16[64,1024]{1,0:T(8,128)(2,1)S(1)}, u32[]{:S(2)}, u32[]{:S(2)}) collective-permute-start(bf16[64,1024]{1,0:T(8,128)(2,1)S(1)} %fusion.4), channel_id=1, source_target_pairs={{0,4},{2,6},{4,0},{6,2},{8,12},{10,14},{12,8},{14,10},{1,5},{3,7},... | collective-permute-start | bytes 393224 | tf_op jit(solution)/shard_map/ppermute | solution.py:15
  14.6 8.2 %collective-permute-start.2 = (bf16[64,1024]{1,0:T(8,128)(2,1)S(1)}, bf16[64,1024]{1,0:T(8,128)(2,1)S(1)}, u32[]{:S(2)}, u32[]{:S(2)}) collective-permute-start(bf16[64,1024]{1,0:T(8,128)(2,1)S(1)} %fusion.6), channel_id=1, source_target_pairs={{0,8},{2,10},{4,12},{6,14},{8,0},{10,2},{12,4},{14,6},{1,9},{3,11}... | collective-permute-start | bytes 393224 | tf_op jit(solution)/shard_map/ppermute | solution.py:15
  18.5 5.6 %collective-permute-start.6 = (bf16[64,1024]{1,0:T(8,128)(2,1)S(1)}, bf16[64,1024]{1,0:T(8,128)(2,1)S(1)}, u32[]{:S(2)}, u32[]{:S(2)}) collective-permute-start(bf16[64,1024]{1,0:T(8,128)(2,1)S(1)} %fusion.12), channel_id=1, source_target_pairs={{0,4},{2,6},{4,0},{6,2},{8,12},{10,14},{12,8},{14,10},{1,5},{3,7},... | collective-permute-start | bytes 393224 | tf_op jit(solution)/shard_map/ppermute | solution.py:15
  23.1 1.8 %collective-permute-start.3 = (f32[64]{0:T(128)S(1)}, f32[64]{0:T(128)S(1)}, u32[]{:S(2)}, u32[]{:S(2)}) collective-permute-start(f32[64]{0:T(128)S(1)} %get-tuple-element.24), channel_id=1, source_target_pairs={{0,1},{1,0},{2,3},{3,2},{4,5},{5,4},{6,7},{7,6},{8,9},{9,8},{10,11... | collective-permute-start | bytes 776 | tf_op jit(solution)/shard_map/ppermute | solution.py:70
  24.1 0.8 %copy-start.4 = (f32[1024]{0:T(1024)S(1)}, f32[1024]{0:T(1024)}, u32[]{:S(2)}) copy-start(f32[1024]{0:T(1024)} %param.14) | copy-start | bytes 12292
  24.2 8.7 %collective-permute-start.7 = (bf16[64,1024]{1,0:T(8,128)(2,1)S(1)}, bf16[64,1024]{1,0:T(8,128)(2,1)S(1)}, u32[]{:S(2)}, u32[]{:S(2)}) collective-permute-start(bf16[64,1024]{1,0:T(8,128)(2,1)S(1)} %fusion.14), channel_id=1, source_target_pairs={{0,8},{2,10},{4,12},{6,14},{8,0},{10,2},{12,4},{14,6},{1,9},{3,11}... | collective-permute-start | bytes 393224 | tf_op jit(solution)/shard_map/ppermute | solution.py:15
  30.9 2.2 %copy-start.1 = (f32[64,1024]{1,0:T(8,128)S(1)}, f32[64,1024]{1,0:T(8,128)}, u32[]{:S(2)}) copy-start(f32[64,1024]{1,0:T(8,128)} %shard_map.120) | copy-start | bytes 786436
  31.0 2.1 %collective-permute-start.4 = (f32[64]{0:T(128)S(1)}, f32[64]{0:T(128)S(1)}, u32[]{:S(2)}, u32[]{:S(2)}) collective-permute-start(f32[64]{0:T(128)S(1)} %reduce_sum.164), channel_id=1, source_target_pairs={{0,1},{1,0},{2,3},{3,2},{4,5},{5,4},{6,7},{7,6},{8,9},{9,8},{10,11... | collective-permute-start | bytes 776 | tf_op jit(solution)/shard_map/ppermute | solution.py:70
  33.6 1.7 %collective-permute-start.8 = (f32[64]{0:T(128)S(1)}, f32[64]{0:T(128)S(1)}, u32[]{:S(2)}, u32[]{:S(2)}) collective-permute-start(f32[64]{0:T(128)S(1)} %multiply_reduce_fusion), channel_id=1, source_target_pairs={{0,1},{1,0},{2,3},{3,2},{4,5},{5,4},{6,7},{7,6},{8,9},{9,8},{10,11... | collective-permute-start | bytes 776 | tf_op jit(solution)/shard_map/ppermute | solution.py:70
  33.7 12.0 %collective-permute-start.9 = (bf16[64,1024]{1,0:T(8,128)(2,1)S(1)}, bf16[64,1024]{1,0:T(8,128)(2,1)S(1)}, u32[]{:S(2)}, u32[]{:S(2)}) collective-permute-start(bf16[64,1024]{1,0:T(8,128)(2,1)S(1)} %fusion.18), channel_id=1, source_target_pairs={{0,8},{2,10},{4,12},{6,14},{8,0},{10,2},{12,4},{14,6},{1,9},{3,11}... | collective-permute-start | bytes 393224 | tf_op jit(solution)/shard_map/ppermute | solution.py:15
  41.2 2.7 %copy-start.2 = (f32[64,1024]{1,0:T(8,128)S(1)}, f32[64,1024]{1,0:T(8,128)}, u32[]{:S(2)}) copy-start(f32[64,1024]{1,0:T(8,128)} %shard_map.121) | copy-start | bytes 786436
  44.3 9.3 %collective-permute-start.12 = (bf16[64,1024]{1,0:T(8,128)(2,1)S(1)}, bf16[64,1024]{1,0:T(8,128)(2,1)S(1)}, u32[]{:S(2)}, u32[]{:S(2)}) collective-permute-start(bf16[64,1024]{1,0:T(8,128)(2,1)S(1)} %fusion.35), channel_id=1, source_target_pairs={{0,8},{2,10},{4,12},{6,14},{8,0},{10,2},{12,4},{14,6},{1,9},{3,11}... | collective-permute-start | bytes 393224 | tf_op jit(solution)/shard_map/ppermute | solution.py:15
  46.1 8.0 %collective-permute-start.10 = (bf16[64,1024]{1,0:T(8,128)(2,1)S(1)}, bf16[64,1024]{1,0:T(8,128)(2,1)S(1)}, u32[]{:S(2)}, u32[]{:S(2)}) collective-permute-start(bf16[64,1024]{1,0:T(8,128)(2,1)S(1)} %fusion.25), channel_id=1, source_target_pairs={{0,4},{2,6},{4,0},{6,2},{8,12},{10,14},{12,8},{14,10},{1,5},{3,7},... | collective-permute-start | bytes 393224 | tf_op jit(solution)/shard_map/ppermute | solution.py:15
  54.0 5.0 %collective-permute-start.13 = (bf16[64,1024]{1,0:T(8,128)(2,1)S(1)}, bf16[64,1024]{1,0:T(8,128)(2,1)S(1)}, u32[]{:S(2)}, u32[]{:S(2)}) collective-permute-start(bf16[64,1024]{1,0:T(8,128)(2,1)S(1)} %fusion.40), channel_id=1, source_target_pairs={{0,4},{2,6},{4,0},{6,2},{8,12},{10,14},{12,8},{14,10},{1,5},{3,7},... | collective-permute-start | bytes 393224 | tf_op jit(solution)/shard_map/ppermute | solution.py:15
  54.4 9.1 %collective-permute-start.11 = (bf16[64,1024]{1,0:T(8,128)(2,1)S(1)}, bf16[64,1024]{1,0:T(8,128)(2,1)S(1)}, u32[]{:S(2)}, u32[]{:S(2)}) collective-permute-start(bf16[64,1024]{1,0:T(8,128)(2,1)S(1)} %fusion.30), channel_id=1, source_target_pairs={{0,2},{2,0},{4,6},{6,4},{8,10},{10,8},{12,14},{14,12},{1,3},{3,1},... | collective-permute-start | bytes 393224 | tf_op jit(solution)/shard_map/ppermute | solution.py:15
  59.4 5.0 %collective-permute-start.14 = (bf16[64,1024]{1,0:T(8,128)(2,1)S(1)}, bf16[64,1024]{1,0:T(8,128)(2,1)S(1)}, u32[]{:S(2)}, u32[]{:S(2)}) collective-permute-start(bf16[64,1024]{1,0:T(8,128)(2,1)S(1)} %fusion.45), channel_id=1, source_target_pairs={{0,2},{2,0},{4,6},{6,4},{8,10},{10,8},{12,14},{14,12},{1,3},{3,1},... | collective-permute-start | bytes 393224 | tf_op jit(solution)/shard_map/ppermute | solution.py:15
  61.1 1.2 %collective-permute-start.16 = (f32[3,128]{1,0:T(4,128)S(1)}, f32[3,128]{1,0:T(4,128)S(1)}, u32[]{:S(2)}, u32[]{:S(2)}) collective-permute-start(f32[3,128]{1,0:T(4,128)S(1)} %maximum_maximum_fusion.1), channel_id=1, source_target_pairs={{0,1},{1,0},{2,3},{3,2},{4,5},{5,4},{6,7},{7,6},{8,9},{9,8},{10,11... | collective-permute-start | bytes 4616 | tf_op jit(solution)/shard_map/ppermute | solution.py:70
  61.2 1.7 %collective-permute-start.15 = (f32[3,128]{1,0:T(4,128)S(1)}, f32[3,128]{1,0:T(4,128)S(1)}, u32[]{:S(2)}, u32[]{:S(2)}) collective-permute-start(f32[3,128]{1,0:T(4,128)S(1)} %maximum_maximum_fusion), channel_id=1, source_target_pairs={{0,1},{1,0},{2,3},{3,2},{4,5},{5,4},{6,7},{7,6},{8,9},{9,8},{10,11... | collective-permute-start | bytes 4616 | tf_op jit(solution)/shard_map/ppermute | solution.py:70
  64.8 1.3 %collective-permute-start.17 = (f32[1,128,128]{2,1,0:T(8,128)S(1)}, f32[1,128,128]{2,1,0:T(8,128)S(1)}, u32[]{:S(2)}, u32[]{:S(2)}) collective-permute-start(f32[1,128,128]{2,1,0:T(8,128)S(1)} %convolution_bitcast_fusion.1), channel_id=1, source_target_pairs={{0,1},{1,0},{2,3},{3,2},{4,5},{5,4},{6,7},{7,6},{8,9},{9,8},{10,11... | collective-permute-start | bytes 196616 | tf_op jit(solution)/shard_map/ppermute | solution.py:70

commit v19 on v13

--- a/solution.py
+++ b/solution.py
@@ -14,9 +14,11 @@
     return lax.ppermute(value, axis, pairs)
 
 
-def ffn_kernel(normed_ref, cot_ref, wg_ref, wu_ref, wd_ref, out_ref):
+def ffn_kernel(normed_ref, cot_ref, tok_ref, mix_ref, gain_ref, wg_ref, wu_ref, wd_ref,
+               out_ref, acc_ref):
     cblock = wg_ref.shape[1]
     contract_last = (((1,), (1,)), ((), ()))
+    acc = jnp.zeros(acc_ref.shape, jnp.float32)
     for group in range(wg_ref.shape[0]):
         cols = slice(group * cblock, (group + 1) * cblock)
         normed = normed_ref[:, cols]
@@ -30,12 +32,24 @@
         sig = 1.0 / (1.0 + jnp.exp(-gate_pre))
         d_up = (d_hidden * gate_pre * sig).astype(jnp.bfloat16)
         d_gate = (d_hidden * up_val * sig * (1.0 + gate_pre * (1.0 - sig))).astype(jnp.bfloat16)
-        out_ref[:, cols] = lax.dot_general(
+        d_normed = lax.dot_general(
             d_gate, w_gate, contract_last, preferred_element_type=jnp.float32
         ) + lax.dot_general(d_up, w_up, contract_last, preferred_element_type=jnp.float32)
-
-
-def ffn_grad(normed, cotangent, w_gate, w_up, w_down, per_step=4):
+        out_ref[:, cols] = d_normed
+        tok = tok_ref[:, cols].astype(jnp.float32)
+        resid = tok + tok * mix_ref[:, cols].astype(jnp.float32)
+        acc = acc + resid * (gain_ref[:, cols] * d_normed)
+
+    @pl.when(pl.program_id(0) == 0)
+    def _():
+        acc_ref[...] = acc
+
+    @pl.when(pl.program_id(0) > 0)
+    def _():
+        acc_ref[...] += acc
+
+
+def ffn_grad(normed, cotangent, tokens, mixed, norm_gain, w_gate, w_up, w_down, per_step=4):
     tok, width = normed.shape
     groups_here, cblock, hidden = w_gate.shape
     if groups_here % per_step:
@@ -47,18 +61,24 @@
         in_specs=[
             act,
             act,
+            act,
+            act,
+            pl.BlockSpec((1, cblock * per_step), lambda g: (0, g)),
             pl.BlockSpec((per_step, cblock, hidden), lambda g: (g, 0, 0)),
             pl.BlockSpec((per_step, cblock, hidden), lambda g: (g, 0, 0)),
             pl.BlockSpec((per_step, hidden, cblock), lambda g: (g, 0, 0)),
         ],
-        out_specs=act,
-        out_shape=jax.ShapeDtypeStruct((tok, width), jnp.float32),
+        out_specs=[act, pl.BlockSpec((tok, cblock), lambda g: (0, 0))],
+        out_shape=[
+            jax.ShapeDtypeStruct((tok, width), jnp.float32),
+            jax.ShapeDtypeStruct((tok, cblock), jnp.float32),
+        ],
         cost_estimate=pl.CostEstimate(
             flops=10 * tok * cblock * hidden * groups_here,
             transcendentals=tok * hidden * groups_here,
-            bytes_accessed=3 * groups_here * cblock * hidden * 2 + tok * width * 8,
+            bytes_accessed=3 * groups_here * cblock * hidden * 2 + tok * width * 12,
         ),
-    )(normed, cotangent, w_gate, w_up, w_down)
+    )(normed, cotangent, tokens, mixed, norm_gain[None, :], w_gate, w_up, w_down)
 
 
 def hid_sum(value):
@@ -124,9 +144,11 @@
         square = hid_sum(jnp.sum(resid * resid, axis=-1))
         inv = lax.rsqrt(square / D + 1e-06)
         normed = (resid * inv[:, None] * norm_gain).astype(jnp.bfloat16)
-        d_normed = ffn_grad(normed, cot, w_gate, w_up, w_down)
+        d_normed, lanes = ffn_grad(
+            normed, cot, tokens[rs], mixed, norm_gain, w_gate, w_up, w_down
+        )
         scaled = norm_gain * d_normed
-        inner = reduce_hid(jnp.sum(resid * scaled, axis=-1))
+        inner = reduce_hid(jnp.sum(lanes, axis=-1))
         d_resid = (
             cot.astype(jnp.float32)
             + inv[:, None] * scaled

time: 66.8 us -> 68.1 us (1.019)
  local copies, waits for them, and re-layouts: 1.2 us -> 2.31 us
  starting transfers between devices: 19.9 us -> 19.1 us
    reduce_sum x6, other arithmetic: 1.65 us -> 2.6 us  [body(): jnp.sum(back_f * mates[chunk][section].astype(jnp.float32), axis=-1)]
    ppermute x12, starting transfers between devices: 19 us -> 18.1 us  [from_partner(): return lax.ppermute(value, axis, pairs)]
    slice x0 -> x1, local copies, waits for them, and re-layouts: none -> 0.72 us  [body(): tok_f = tokens[rs].astype(jnp.float32)]
  transfers between devices with their start and end apart: 18 -> 18, of which waited for: 10 -> 11; matrix products, arithmetic and copies ran while one was open for 15% -> 16% of each run, Pallas kernels for 12% -> 13%
where the time goes in v19:
time: 68.1 us; the launch traced here: 67.8 us
  waiting for transfers between devices  22.2 us (33%)
  starting transfers between devices  19.1 us (28%)
  other arithmetic  9.72 us (14%)
  Pallas kernels  8.48 us (12%)
  matrix products  2.57 us (4%)
  blocking collectives  2.47 us (4%)
  local copies, waits for them, and re-layouts  2.31 us (3%)
  between operations  0.91 us (1%)
    ppermute x12, waiting for transfers between devices, from_partner(): return lax.ppermute(value, axis, pairs)  21.1 us
    ppermute x12, starting transfers between devices, from_partner(): return lax.ppermute(value, axis, pairs)  18.1 us
    pallas_call x2, Pallas kernels, ffn_grad(): pl.pallas_call(ffn_kernel, grid=(groups_here // per_step,), in_specs=[act...  8.48 us
    reduce_sum x6, other arithmetic, body(): jnp.sum(back_f * mates[chunk][section].astype(jnp.float32), axis=-1)  2.6 us
    psum x1, blocking collectives, body(): reduce_hid = hid_sum if chunk == 0 else lambda v: lax.psum(v, 'hid')  2.47 us
    add x3, other arithmetic, hid_sum(): total = total + lax.ppermute(value, 'hid', pairs)  1.95 us
    reduce_sum x2, other arithmetic, body(): inner = reduce_hid(jnp.sum(lanes, axis=-1))  1.77 us
    convert_element_type x2, other arithmetic, body(): normed = (resid * inv[:, None] * norm_gain).astype(jnp.bfloat16)  1.48 us
  transfers between devices with their start and end apart: 18, of which 11 were waited for; matrix products, arithmetic and copies ran while one was open for 16% of the time, Pallas kernels for 13%

profile of v19, /device:TPU:0, one launch (start us, length us, event | category | flops | bytes accessed | tf_op | source)
XLA Modules:
  0.0 67.8 jit_solution(17700521213190187251)
XLA Ops:
  0.7 1.2 %convolution_convert_fusion.1 = bf16[64,1024]{1,0:T(8,128)(2,1)S(1)} fusion(bf16[128,1024]{1,0:T(8,128)(2,1)} %param.9, bf16[1,128,128]{2,1,0:T(8,128)(2,1)} %param.11), kind=kOutput, calls=%fused_computation.4 | convolution fusion | flops 16842752 | bytes 409600 | tf_op jit(solution)/shard_map/kij,kjd->kid/dot_general | solution.py:112
  1.8 3.0 %collective-permute-start = (bf16[64,1024]{1,0:T(8,128)(2,1)S(1)}, bf16[64,1024]{1,0:T(8,128)(2,1)S(1)}, u32[]{:S(2)}, u32[]{:S(2)}) collective-permute-start(bf16[64,1024]{1,0:T(8,128)(2,1)S(1)} %convolution_convert_fusion.1), channel_id=1, source_target_pairs={{0,2},{2,0},{4,6},{6,4},{8,10},{10,8},{12,14},{14,12},{1,3},{3,1},... | collective-permute-start | bytes 393224 | tf_op jit(solution)/shard_map/ppermute | solution.py:14
  5.1 0.7 %fusion.66 = (bf16[64,1024]{1,0:T(8,128)(2,1)}, bf16[64,1024]{1,0:T(8,128)(2,1)}) fusion(bf16[128,1024]{1,0:T(8,128)(2,1)S(1)} %copy-done), kind=kLoop, calls=%fused_computation.130 | loop fusion | bytes 524288 | tf_op jit(solution)/shard_map/slice | solution.py:140
  5.9 3.2 %collective-permute-done = bf16[64,1024]{1,0:T(8,128)(2,1)S(1)} collective-permute-done((bf16[64,1024]{1,0:T(8,128)(2,1)S(1)}, bf16[64,1024]{1,0:T(8,128)(2,1)S(1)}, u32[]{:S(2)}, u32[]{:S(2)}) %collective-permute-start) | collective-permute-done | bytes 131104 | tf_op jit(solution)/shard_map/ppermute | solution.py:14
  9.3 2.2 %collective-permute-start.1 = (bf16[64,1024]{1,0:T(8,128)(2,1)S(1)}, bf16[64,1024]{1,0:T(8,128)(2,1)S(1)}, u32[]{:S(2)}, u32[]{:S(2)}) collective-permute-start(bf16[64,1024]{1,0:T(8,128)(2,1)S(1)} %fusion.4), channel_id=1, source_target_pairs={{0,4},{2,6},{4,0},{6,2},{8,12},{10,14},{12,8},{14,10},{1,5},{3,7},... | collective-permute-start | bytes 393224 | tf_op jit(solution)/shard_map/ppermute | solution.py:14
  11.5 0.7 %fusion.67 = (bf16[64,1024]{1,0:T(8,128)(2,1)}, bf16[64,1024]{1,0:T(8,128)(2,1)}) fusion(bf16[128,1024]{1,0:T(8,128)(2,1)S(1)} %copy-done.5), kind=kLoop, calls=%fused_computation.131 | loop fusion | bytes 524288 | tf_op jit(solution)/shard_map/slice | solution.py:139
  12.2 2.2 %collective-permute-done.1 = bf16[64,1024]{1,0:T(8,128)(2,1)S(1)} collective-permute-done((bf16[64,1024]{1,0:T(8,128)(2,1)S(1)}, bf16[64,1024]{1,0:T(8,128)(2,1)S(1)}, u32[]{:S(2)}, u32[]{:S(2)}) %collective-permute-start.1) | collective-permute-done | bytes 131104 | tf_op jit(solution)/shard_map/ppermute | solution.py:14
  14.6 3.8 %collective-permute-start.2 = (bf16[64,1024]{1,0:T(8,128)(2,1)S(1)}, bf16[64,1024]{1,0:T(8,128)(2,1)S(1)}, u32[]{:S(2)}, u32[]{:S(2)}) collective-permute-start(bf16[64,1024]{1,0:T(8,128)(2,1)S(1)} %fusion.6), channel_id=1, source_target_pairs={{0,8},{2,10},{4,12},{6,14},{8,0},{10,2},{12,4},{14,6},{1,9},{3,11}... | collective-permute-start | bytes 393224 | tf_op jit(solution)/shard_map/ppermute | solution.py:14
  18.5 1.2 %collective-permute-start.6 = (bf16[64,1024]{1,0:T(8,128)(2,1)S(1)}, bf16[64,1024]{1,0:T(8,128)(2,1)S(1)}, u32[]{:S(2)}, u32[]{:S(2)}) collective-permute-start(bf16[64,1024]{1,0:T(8,128)(2,1)S(1)} %fusion.12), channel_id=1, source_target_pairs={{0,4},{2,6},{4,0},{6,2},{8,12},{10,14},{12,8},{14,10},{1,5},{3,7},... | collective-permute-start | bytes 393224 | tf_op jit(solution)/shard_map/ppermute | solution.py:14
  19.7 3.1 %collective-permute-done.2 = bf16[64,1024]{1,0:T(8,128)(2,1)S(1)} collective-permute-done((bf16[64,1024]{1,0:T(8,128)(2,1)S(1)}, bf16[64,1024]{1,0:T(8,128)(2,1)S(1)}, u32[]{:S(2)}, u32[]{:S(2)}) %collective-permute-start.2) | collective-permute-done | bytes 131104 | tf_op jit(solution)/shard_map/ppermute | solution.py:14
  23.1 1.0 %collective-permute-done.6 = bf16[64,1024]{1,0:T(8,128)(2,1)S(1)} collective-permute-done((bf16[64,1024]{1,0:T(8,128)(2,1)S(1)}, bf16[64,1024]{1,0:T(8,128)(2,1)S(1)}, u32[]{:S(2)}, u32[]{:S(2)}) %collective-permute-start.6) | collective-permute-done | bytes 131104 | tf_op jit(solution)/shard_map/ppermute | solution.py:14
  24.9 0.7 %multiply_convert_fusion.1.normed_ref = bf16[64,1024]{1,0:T(8,128)(2,1)} fusion(bf16[64,1024]{1,0:T(8,128)(2,1)S(1)} %get-tuple-element.33.mix_ref, f32[1024]{0:T(1024)S(1)} %copy-done.7, f32[64]{0:T(128)S(1)} %add_rsqrt_fusion.1, bf16[128,1024]{1,0:T(8,128)(2,1)S(1)} %copy-done), kind=kLoop, calls=%fused_computation.99 | loop fusion | flops 458752 | bytes 397568 | tf_op jit(solution)/shard_map/convert_element_type | solution.py:146
  25.7 4.2 %shard_map.120 = (f32[64,1024]{1,0:T(8,128)}, f32[64,128]{1,0:T(8,128)}) custom-call(bf16[64,1024]{1,0:T(8,128)(2,1)} %multiply_convert_fusion.1.normed_ref, bf16[64,1024]{1,0:T(8,128)(2,1)} %get-tuple-element.39.cot_ref, bf16[64,1024]{1,0:T(8,128)(2,1)} %get-tuple-element.37.tok_ref, bf16[64,1024]{1,0:T(8,128)(2,1)} %copy-done.3, f32[1,1024]{1,0:T(1,128)} %bitcast.57, ...), custom_call_target="tpu_custom_call" | custom-call | flops 335544320 | bytes 3932160 | tf_op jit(solution)/shard_map/pallas_call | solution.py:58
  29.9 0.9 %reduce_sum.145 = f32[64]{0:T(128)S(1)} reduce(f32[64,128]{1,0:T(8,128)} %get-tuple-element.10, f32[]{:T(128)} %constant.8.clone.1), dimensions={1}, to_apply=%region_1.0 | reduce | flops 8128 | bytes 33028 | tf_op jit(solution)/shard_map/reduce_sum | solution.py:151
  31.1 1.9 %collective-permute-done.7 = bf16[64,1024]{1,0:T(8,128)(2,1)S(1)} collective-permute-done((bf16[64,1024]{1,0:T(8,128)(2,1)S(1)}, bf16[64,1024]{1,0:T(8,128)(2,1)S(1)}, u32[]{:S(2)}, u32[]{:S(2)}) %collective-permute-start.7) | collective-permute-done | bytes 131104 | tf_op jit(solution)/shard_map/ppermute | solution.py:14
  33.1 0.7 %copy-done.4 = bf16[64,1024]{1,0:T(8,128)(2,1)S(1)} copy-done((bf16[64,1024]{1,0:T(8,128)(2,1)S(1)}, bf16[64,1024]{1,0:T(8,128)(2,1)}, u32[]{:S(2)}) %copy-start.4) | copy-done | bytes 131096
  34.5 0.8 %collective-permute-start.9 = (bf16[64,1024]{1,0:T(8,128)(2,1)S(1)}, bf16[64,1024]{1,0:T(8,128)(2,1)S(1)}, u32[]{:S(2)}, u32[]{:S(2)}) collective-permute-start(bf16[64,1024]{1,0:T(8,128)(2,1)S(1)} %fusion.18), channel_id=1, source_target_pairs={{0,8},{2,10},{4,12},{6,14},{8,0},{10,2},{12,4},{14,6},{1,9},{3,11}... | collective-permute-start | bytes 393224 | tf_op jit(solution)/shard_map/ppermute | solution.py:14
  35.6 0.7 %multiply_convert_fusion.normed_ref = bf16[64,1024]{1,0:T(8,128)(2,1)} fusion(bf16[64,1024]{1,0:T(8,128)(2,1)S(1)} %fusion.16.mix_ref, f32[64]{0:T(128)S(1)} %add_rsqrt_fusion, f32[1024]{0:T(1024)S(1)} %copy-done.8, bf16[128,1024]{1,0:T(8,128)(2,1)S(1)} %copy-done), kind=kLoop, calls=%fused_computation.96 | loop fusion | flops 458752 | bytes 397568 | tf_op jit(solution)/shard_map/convert_element_type | solution.py:146
  36.3 4.3 %shard_map.121 = (f32[64,1024]{1,0:T(8,128)}, f32[64,128]{1,0:T(8,128)}) custom-call(bf16[64,1024]{1,0:T(8,128)(2,1)} %multiply_convert_fusion.normed_ref, bf16[64,1024]{1,0:T(8,128)(2,1)} %get-tuple-element.38.cot_ref, bf16[64,1024]{1,0:T(8,128)(2,1)} %get-tuple-element.36.tok_ref, bf16[64,1024]{1,0:T(8,128)(2,1)} %copy-done.1, f32[1,1024]{1,0:T(1,128)} %bitcast.58, ...), custom_call_target="tpu_custom_call" | custom-call | flops 335544320 | bytes 3932160 | tf_op jit(solution)/shard_map/pallas_call | solution.py:58
  40.6 0.9 %reduce_sum.147 = f32[64]{0:T(128)S(1)} reduce(f32[64,128]{1,0:T(8,128)} %get-tuple-element.13, f32[]{:T(128)} %constant.8.clone.1), dimensions={1}, to_apply=%region_3.0 | reduce | flops 8128 | bytes 33028 | tf_op jit(solution)/shard_map/reduce_sum | solution.py:151
  41.5 2.5 %psum.7 = f32[64]{0:T(128)S(1)} all-reduce(f32[64]{0:T(128)S(1)} %reduce_sum.147), channel_id=1, replica_groups=mesh['groups'=2,'seq'=8,'hid'=2] {'hid'}, use_global_device_ids=true, to_apply=%region_4.0 | all-reduce | flops 64 | bytes 512 | tf_op jit(solution)/shard_map/psum | solution.py:143
  44.0 1.3 %fusion.37 = (f32[64]{0:T(128)S(1)}, f32[64]{0:T(128)S(1)}, bf16[64,1024]{1,0:T(8,128)(2,1)S(1)}, f32[64,1024]{1,0:T(8,128)S(1)}) fusion(bf16[64,1024]{1,0:T(8,128)(2,1)S(1)} %collective-permute-done.7, bf16[64,1024]{1,0:T(8,128)(2,1)S(1)} %fusion.14, f32[64]{0:T(128)S(1)} %fusion.55, bf16[64,1024]{1,0:T(8,128)(2,1)S(1)} %copy-done.2, ...), kind=kLoop, calls=%fused_computation.83 | loop fusion | flops 1376128 | bytes 1315840 | tf_op jit(solution)/shard_map/reduce_sum | solution.py:171
  45.3 2.0 %collective-permute-start.12 = (bf16[64,1024]{1,0:T(8,128)(2,1)S(1)}, bf16[64,1024]{1,0:T(8,128)(2,1)S(1)}, u32[]{:S(2)}, u32[]{:S(2)}) collective-permute-start(bf16[64,1024]{1,0:T(8,128)(2,1)S(1)} %fusion.35), channel_id=1, source_target_pairs={{0,8},{2,10},{4,12},{6,14},{8,0},{10,2},{12,4},{14,6},{1,9},{3,11}... | collective-permute-start | bytes 393224 | tf_op jit(solution)/shard_map/ppermute | solution.py:14
  47.6 1.2 %collective-permute-start.10 = (bf16[64,1024]{1,0:T(8,128)(2,1)S(1)}, bf16[64,1024]{1,0:T(8,128)(2,1)S(1)}, u32[]{:S(2)}, u32[]{:S(2)}) collective-permute-start(bf16[64,1024]{1,0:T(8,128)(2,1)S(1)} %fusion.25), channel_id=1, source_target_pairs={{0,4},{2,6},{4,0},{6,2},{8,12},{10,14},{12,8},{14,10},{1,5},{3,7},... | collective-permute-start | bytes 393224 | tf_op jit(solution)/shard_map/ppermute | solution.py:14
  48.8 5.9 %collective-permute-done.12 = bf16[64,1024]{1,0:T(8,128)(2,1)S(1)} collective-permute-done((bf16[64,1024]{1,0:T(8,128)(2,1)S(1)}, bf16[64,1024]{1,0:T(8,128)(2,1)S(1)}, u32[]{:S(2)}, u32[]{:S(2)}) %collective-permute-start.12) | collective-permute-done | bytes 131104 | tf_op jit(solution)/shard_map/ppermute | solution.py:14
  55.5 1.6 %collective-permute-start.11 = (bf16[64,1024]{1,0:T(8,128)(2,1)S(1)}, bf16[64,1024]{1,0:T(8,128)(2,1)S(1)}, u32[]{:S(2)}, u32[]{:S(2)}) collective-permute-start(bf16[64,1024]{1,0:T(8,128)(2,1)S(1)} %fusion.30), channel_id=1, source_target_pairs={{0,2},{2,0},{4,6},{6,4},{8,10},{10,8},{12,14},{14,12},{1,3},{3,1},... | collective-permute-start | bytes 393224 | tf_op jit(solution)/shard_map/ppermute | solution.py:14
  57.1 3.0 %collective-permute-done.13 = bf16[64,1024]{1,0:T(8,128)(2,1)S(1)} collective-permute-done((bf16[64,1024]{1,0:T(8,128)(2,1)S(1)}, bf16[64,1024]{1,0:T(8,128)(2,1)S(1)}, u32[]{:S(2)}, u32[]{:S(2)}) %collective-permute-start.13) | collective-permute-done | bytes 131104 | tf_op jit(solution)/shard_map/ppermute | solution.py:14
  60.5 1.6 %collective-permute-start.14 = (bf16[64,1024]{1,0:T(8,128)(2,1)S(1)}, bf16[64,1024]{1,0:T(8,128)(2,1)S(1)}, u32[]{:S(2)}, u32[]{:S(2)}) collective-permute-start(bf16[64,1024]{1,0:T(8,128)(2,1)S(1)} %fusion.45), channel_id=1, source_target_pairs={{0,2},{2,0},{4,6},{6,4},{8,10},{10,8},{12,14},{14,12},{1,3},{3,1},... | collective-permute-start | bytes 393224 | tf_op jit(solution)/shard_map/ppermute | solution.py:14
  63.3 0.7 fusion.71
  63.9 0.7 fusion.72
  64.7 0.8 %collective-permute-done.14 = bf16[64,1024]{1,0:T(8,128)(2,1)S(1)} collective-permute-done((bf16[64,1024]{1,0:T(8,128)(2,1)S(1)}, bf16[64,1024]{1,0:T(8,128)(2,1)S(1)}, u32[]{:S(2)}, u32[]{:S(2)}) %collective-permute-start.14) | collective-permute-done | bytes 131104 | tf_op jit(solution)/shard_map/ppermute | solution.py:14
  65.9 1.0 %fusion.1 = bf16[128,1024]{1,0:T(8,128)(2,1)} fusion(f32[64,1024]{1,0:T(8,128)S(1)} %get-tuple-element.34, f32[64,1024]{1,0:T(8,128)S(1)} %get-tuple-element.35, bf16[64,1024]{1,0:T(8,128)(2,1)S(1)} %fusion.44, bf16[64,1024]{1,0:T(8,128)(2,1)S(1)} %fusion.29, bf16[1,128,128]{2,1,0:T(8,128)(2,1)S(1)} %copy-done.10), kind=kOutput, calls=%fused_computation.2 | convolution fusion | flops 34471936 | bytes 1081344 | tf_op jit(solution)/shard_map/kij,kid->kjd/dot_general | solution.py:189
  (74 shorter events, 7.4 us)
Async XLA Ops:
  0.6 4.2 %copy-start.10 = (bf16[1,128,128]{2,1,0:T(8,128)(2,1)S(1)}, bf16[1,128,128]{2,1,0:T(8,128)(2,1)}, u32[]{:S(2)}) copy-start(bf16[1,128,128]{2,1,0:T(8,128)(2,1)} %param.11) | copy-start | bytes 98308
  0.6 4.2 %copy-start = (bf16[128,1024]{1,0:T(8,128)(2,1)S(1)}, bf16[128,1024]{1,0:T(8,128)(2,1)}, u32[]{:S(2)}) copy-start(bf16[128,1024]{1,0:T(8,128)(2,1)} %param.9) | copy-start | bytes 786436
  1.8 7.3 %collective-permute-start = (bf16[64,1024]{1,0:T(8,128)(2,1)S(1)}, bf16[64,1024]{1,0:T(8,128)(2,1)S(1)}, u32[]{:S(2)}, u32[]{:S(2)}) collective-permute-start(bf16[64,1024]{1,0:T(8,128)(2,1)S(1)} %convolution_convert_fusion.1), channel_id=1, source_target_pairs={{0,2},{2,0},{4,6},{6,4},{8,10},{10,8},{12,14},{14,12},{1,3},{3,1},... | collective-permute-start | bytes 393224 | tf_op jit(solution)/shard_map/ppermute | solution.py:14
  5.0 13.3 %collective-permute-start.5 = (bf16[64,1024]{1,0:T(8,128)(2,1)S(1)}, bf16[64,1024]{1,0:T(8,128)(2,1)S(1)}, u32[]{:S(2)}, u32[]{:S(2)}) collective-permute-start(bf16[64,1024]{1,0:T(8,128)(2,1)S(1)} %convolution_convert_fusion), channel_id=1, source_target_pairs={{0,2},{2,0},{4,6},{6,4},{8,10},{10,8},{12,14},{14,12},{1,3},{3,1},... | collective-permute-start | bytes 393224 | tf_op jit(solution)/shard_map/ppermute | solution.py:14
  5.1 0.7 %copy-start.11 = (f32[3,128]{1,0:T(4,128)S(1)}, f32[3,128]{1,0:T(4,128)}, u32[]{:S(2)}) copy-start(f32[3,128]{1,0:T(4,128)} %param.13) | copy-start | bytes 4612
  5.1 0.7 %copy-start.12 = (f32[3,128]{1,0:T(4,128)S(1)}, f32[3,128]{1,0:T(4,128)}, u32[]{:S(2)}) copy-start(f32[3,128]{1,0:T(4,128)} %param.12) | copy-start | bytes 4612
  5.9 5.6 %copy-start.5 = (bf16[128,1024]{1,0:T(8,128)(2,1)S(1)}, bf16[128,1024]{1,0:T(8,128)(2,1)}, u32[]{:S(2)}) copy-start(bf16[128,1024]{1,0:T(8,128)(2,1)} %param.10) | copy-start | bytes 786436
  9.3 5.2 %collective-permute-start.1 = (bf16[64,1024]{1,0:T(8,128)(2,1)S(1)}, bf16[64,1024]{1,0:T(8,128)(2,1)S(1)}, u32[]{:S(2)}, u32[]{:S(2)}) collective-permute-start(bf16[64,1024]{1,0:T(8,128)(2,1)S(1)} %fusion.4), channel_id=1, source_target_pairs={{0,4},{2,6},{4,0},{6,2},{8,12},{10,14},{12,8},{14,10},{1,5},{3,7},... | collective-permute-start | bytes 393224 | tf_op jit(solution)/shard_map/ppermute | solution.py:14
  14.6 8.2 %collective-permute-start.2 = (bf16[64,1024]{1,0:T(8,128)(2,1)S(1)}, bf16[64,1024]{1,0:T(8,128)(2,1)S(1)}, u32[]{:S(2)}, u32[]{:S(2)}) collective-permute-start(bf16[64,1024]{1,0:T(8,128)(2,1)S(1)} %fusion.6), channel_id=1, source_target_pairs={{0,8},{2,10},{4,12},{6,14},{8,0},{10,2},{12,4},{14,6},{1,9},{3,11}... | collective-permute-start | bytes 393224 | tf_op jit(solution)/shard_map/ppermute | solution.py:14
  18.5 5.6 %collective-permute-start.6 = (bf16[64,1024]{1,0:T(8,128)(2,1)S(1)}, bf16[64,1024]{1,0:T(8,128)(2,1)S(1)}, u32[]{:S(2)}, u32[]{:S(2)}) collective-permute-start(bf16[64,1024]{1,0:T(8,128)(2,1)S(1)} %fusion.12), channel_id=1, source_target_pairs={{0,4},{2,6},{4,0},{6,2},{8,12},{10,14},{12,8},{14,10},{1,5},{3,7},... | collective-permute-start | bytes 393224 | tf_op jit(solution)/shard_map/ppermute | solution.py:14
  23.1 1.9 %copy-start.3 = (bf16[64,1024]{1,0:T(8,128)(2,1)}, bf16[64,1024]{1,0:T(8,128)(2,1)S(1)}, u32[]{:S(2)}) copy-start(bf16[64,1024]{1,0:T(8,128)(2,1)S(1)} %get-tuple-element.33.mix_ref) | copy-start | bytes 393220
  23.1 1.8 %collective-permute-start.3 = (f32[64]{0:T(128)S(1)}, f32[64]{0:T(128)S(1)}, u32[]{:S(2)}, u32[]{:S(2)}) collective-permute-start(f32[64]{0:T(128)S(1)} %get-tuple-element.32), channel_id=1, source_target_pairs={{0,1},{1,0},{2,3},{3,2},{4,5},{5,4},{6,7},{7,6},{8,9},{9,8},{10,11... | collective-permute-start | bytes 776 | tf_op jit(solution)/shard_map/ppermute | solution.py:89
  24.1 0.8 %copy-start.7 = (f32[1024]{0:T(1024)S(1)}, f32[1024]{0:T(1024)}, u32[]{:S(2)}) copy-start(f32[1024]{0:T(1024)} %param.14) | copy-start | bytes 12292
  24.2 8.7 %collective-permute-start.7 = (bf16[64,1024]{1,0:T(8,128)(2,1)S(1)}, bf16[64,1024]{1,0:T(8,128)(2,1)S(1)}, u32[]{:S(2)}, u32[]{:S(2)}) collective-permute-start(bf16[64,1024]{1,0:T(8,128)(2,1)S(1)} %fusion.14), channel_id=1, source_target_pairs={{0,8},{2,10},{4,12},{6,14},{8,0},{10,2},{12,4},{14,6},{1,9},{3,11}... | collective-permute-start | bytes 393224 | tf_op jit(solution)/shard_map/ppermute | solution.py:14
  29.9 3.2 %copy-start.6 = (f32[64,1024]{1,0:T(8,128)S(1)}, f32[64,1024]{1,0:T(8,128)}, u32[]{:S(2)}) copy-start(f32[64,1024]{1,0:T(8,128)} %get-tuple-element.9) | copy-start | bytes 786436
  30.8 2.3 %collective-permute-start.4 = (f32[64]{0:T(128)S(1)}, f32[64]{0:T(128)S(1)}, u32[]{:S(2)}, u32[]{:S(2)}) collective-permute-start(f32[64]{0:T(128)S(1)} %reduce_sum.145), channel_id=1, source_target_pairs={{0,1},{1,0},{2,3},{3,2},{4,5},{5,4},{6,7},{7,6},{8,9},{9,8},{10,11... | collective-permute-start | bytes 776 | tf_op jit(solution)/shard_map/ppermute | solution.py:89
  32.9 0.9 %copy-start.4 = (bf16[64,1024]{1,0:T(8,128)(2,1)S(1)}, bf16[64,1024]{1,0:T(8,128)(2,1)}, u32[]{:S(2)}) copy-start(bf16[64,1024]{1,0:T(8,128)(2,1)} %copy-done.3) | copy-start | bytes 393220
  32.9 0.9 %copy-start.8 = (f32[1024]{0:T(1024)S(1)}, f32[1024]{0:T(1024)}, u32[]{:S(2)}) copy-start(f32[1024]{0:T(1024)} %param.14) | copy-start | bytes 12292
  33.1 2.5 %copy-start.1 = (bf16[64,1024]{1,0:T(8,128)(2,1)}, bf16[64,1024]{1,0:T(8,128)(2,1)S(1)}, u32[]{:S(2)}) copy-start(bf16[64,1024]{1,0:T(8,128)(2,1)S(1)} %fusion.16.mix_ref) | copy-start | bytes 393220
  34.4 1.2 %collective-permute-start.8 = (f32[64]{0:T(128)S(1)}, f32[64]{0:T(128)S(1)}, u32[]{:S(2)}, u32[]{:S(2)}) collective-permute-start(f32[64]{0:T(128)S(1)} %multiply_reduce_fusion), channel_id=1, source_target_pairs={{0,1},{1,0},{2,3},{3,2},{4,5},{5,4},{6,7},{7,6},{8,9},{9,8},{10,11... | collective-permute-start | bytes 776 | tf_op jit(solution)/shard_map/ppermute | solution.py:89
  34.5 12.8 %collective-permute-start.9 = (bf16[64,1024]{1,0:T(8,128)(2,1)S(1)}, bf16[64,1024]{1,0:T(8,128)(2,1)S(1)}, u32[]{:S(2)}, u32[]{:S(2)}) collective-permute-start(bf16[64,1024]{1,0:T(8,128)(2,1)S(1)} %fusion.18), channel_id=1, source_target_pairs={{0,8},{2,10},{4,12},{6,14},{8,0},{10,2},{12,4},{14,6},{1,9},{3,11}... | collective-permute-start | bytes 393224 | tf_op jit(solution)/shard_map/ppermute | solution.py:14
  36.3 7.6 %copy-start.2 = (bf16[64,1024]{1,0:T(8,128)(2,1)S(1)}, bf16[64,1024]{1,0:T(8,128)(2,1)}, u32[]{:S(2)}) copy-start(bf16[64,1024]{1,0:T(8,128)(2,1)} %copy-done.1) | copy-start | bytes 393220
  41.5 2.5 %copy-start.9 = (f32[1024]{0:T(1024)S(1)}, f32[1024]{0:T(1024)}, u32[]{:S(2)}) copy-start(f32[1024]{0:T(1024)} %param.14) | copy-start | bytes 12292
  45.3 9.4 %collective-permute-start.12 = (bf16[64,1024]{1,0:T(8,128)(2,1)S(1)}, bf16[64,1024]{1,0:T(8,128)(2,1)S(1)}, u32[]{:S(2)}, u32[]{:S(2)}) collective-permute-start(bf16[64,1024]{1,0:T(8,128)(2,1)S(1)} %fusion.35), channel_id=1, source_target_pairs={{0,8},{2,10},{4,12},{6,14},{8,0},{10,2},{12,4},{14,6},{1,9},{3,11}... | collective-permute-start | bytes 393224 | tf_op jit(solution)/shard_map/ppermute | solution.py:14
  47.6 7.5 %collective-permute-start.10 = (bf16[64,1024]{1,0:T(8,128)(2,1)S(1)}, bf16[64,1024]{1,0:T(8,128)(2,1)S(1)}, u32[]{:S(2)}, u32[]{:S(2)}) collective-permute-start(bf16[64,1024]{1,0:T(8,128)(2,1)S(1)} %fusion.25), channel_id=1, source_target_pairs={{0,4},{2,6},{4,0},{6,2},{8,12},{10,14},{12,8},{14,10},{1,5},{3,7},... | collective-permute-start | bytes 393224 | tf_op jit(solution)/shard_map/ppermute | solution.py:14
  55.1 5.0 %collective-permute-start.13 = (bf16[64,1024]{1,0:T(8,128)(2,1)S(1)}, bf16[64,1024]{1,0:T(8,128)(2,1)S(1)}, u32[]{:S(2)}, u32[]{:S(2)}) collective-permute-start(bf16[64,1024]{1,0:T(8,128)(2,1)S(1)} %fusion.40), channel_id=1, source_target_pairs={{0,4},{2,6},{4,0},{6,2},{8,12},{10,14},{12,8},{14,10},{1,5},{3,7},... | collective-permute-start | bytes 393224 | tf_op jit(solution)/shard_map/ppermute | solution.py:14
  55.5 9.1 %collective-permute-start.11 = (bf16[64,1024]{1,0:T(8,128)(2,1)S(1)}, bf16[64,1024]{1,0:T(8,128)(2,1)S(1)}, u32[]{:S(2)}, u32[]{:S(2)}) collective-permute-start(bf16[64,1024]{1,0:T(8,128)(2,1)S(1)} %fusion.30), channel_id=1, source_target_pairs={{0,2},{2,0},{4,6},{6,4},{8,10},{10,8},{12,14},{14,12},{1,3},{3,1},... | collective-permute-start | bytes 393224 | tf_op jit(solution)/shard_map/ppermute | solution.py:14
  60.5 5.0 %collective-permute-start.14 = (bf16[64,1024]{1,0:T(8,128)(2,1)S(1)}, bf16[64,1024]{1,0:T(8,128)(2,1)S(1)}, u32[]{:S(2)}, u32[]{:S(2)}) collective-permute-start(bf16[64,1024]{1,0:T(8,128)(2,1)S(1)} %fusion.45), channel_id=1, source_target_pairs={{0,2},{2,0},{4,6},{6,4},{8,10},{10,8},{12,14},{14,12},{1,3},{3,1},... | collective-permute-start | bytes 393224 | tf_op jit(solution)/shard_map/ppermute | solution.py:14
  62.1 1.2 %collective-permute-start.16 = (f32[3,128]{1,0:T(4,128)S(1)}, f32[3,128]{1,0:T(4,128)S(1)}, u32[]{:S(2)}, u32[]{:S(2)}) collective-permute-start(f32[3,128]{1,0:T(4,128)S(1)} %maximum_maximum_fusion.1), channel_id=1, source_target_pairs={{0,1},{1,0},{2,3},{3,2},{4,5},{5,4},{6,7},{7,6},{8,9},{9,8},{10,11... | collective-permute-start | bytes 4616 | tf_op jit(solution)/shard_map/ppermute | solution.py:89
  62.2 1.7 %collective-permute-start.15 = (f32[3,128]{1,0:T(4,128)S(1)}, f32[3,128]{1,0:T(4,128)S(1)}, u32[]{:S(2)}, u32[]{:S(2)}) collective-permute-start(f32[3,128]{1,0:T(4,128)S(1)} %maximum_maximum_fusion), channel_id=1, source_target_pairs={{0,1},{1,0},{2,3},{3,2},{4,5},{5,4},{6,7},{7,6},{8,9},{9,8},{10,11... | collective-permute-start | bytes 4616 | tf_op jit(solution)/shard_map/ppermute | solution.py:89
  65.8 1.3 %collective-permute-start.17 = (f32[1,128,128]{2,1,0:T(8,128)S(1)}, f32[1,128,128]{2,1,0:T(8,128)S(1)}, u32[]{:S(2)}, u32[]{:S(2)}) collective-permute-start(f32[1,128,128]{2,1,0:T(8,128)S(1)} %convolution_bitcast_fusion.1), channel_id=1, source_target_pairs={{0,1},{1,0},{2,3},{3,2},{4,5},{5,4},{6,7},{7,6},{8,9},{9,8},{10,11... | collective-permute-start | bytes 196616 | tf_op jit(solution)/shard_map/ppermute | solution.py:89

commit v20 on v13

--- a/solution.py
+++ b/solution.py
@@ -30,9 +30,10 @@
         sig = 1.0 / (1.0 + jnp.exp(-gate_pre))
         d_up = (d_hidden * gate_pre * sig).astype(jnp.bfloat16)
         d_gate = (d_hidden * up_val * sig * (1.0 + gate_pre * (1.0 - sig))).astype(jnp.bfloat16)
-        out_ref[:, cols] = lax.dot_general(
-            d_gate, w_gate, contract_last, preferred_element_type=jnp.float32
-        ) + lax.dot_general(d_up, w_up, contract_last, preferred_element_type=jnp.float32)
+        out_ref[:, cols] = (
+            lax.dot_general(d_gate, w_gate, contract_last, preferred_element_type=jnp.float32)
+            + lax.dot_general(d_up, w_up, contract_last, preferred_element_type=jnp.float32)
+        ).astype(out_ref.dtype)
 
 
 def ffn_grad(normed, cotangent, w_gate, w_up, w_down, per_step=4):
@@ -52,7 +53,7 @@
             pl.BlockSpec((per_step, hidden, cblock), lambda g: (g, 0, 0)),
         ],
         out_specs=act,
-        out_shape=jax.ShapeDtypeStruct((tok, width), jnp.float32),
+        out_shape=jax.ShapeDtypeStruct((tok, width), jnp.bfloat16),
         cost_estimate=pl.CostEstimate(
             flops=10 * tok * cblock * hidden * groups_here,
             transcendentals=tok * hidden * groups_here,

time: 66.8 us -> 67.2 us (level)
  local copies, waits for them, and re-layouts: 1.2 us -> 1.96 us
  starting transfers between devices: 19.9 us -> 19.2 us
    unnamed x16, local copies, waits for them, and re-layouts: 0.42 us -> 1.17 us
    ppermute x12, starting transfers between devices: 19 us -> 18.3 us  [from_partner(): return lax.ppermute(value, axis, pairs)]
  transfers between devices with their start and end apart: 18 -> 18, of which waited for: 10 -> 11; matrix products, arithmetic and copies ran while one was open for 15% -> 15% of each run, Pallas kernels for 12% -> 12%
where the time goes in v20:
time: 67.2 us; the launch traced here: 66.9 us
  waiting for transfers between devices  22.4 us (33%)
  starting transfers between devices  19.2 us (29%)
  other arithmetic  9.22 us (14%)
  Pallas kernels  8.16 us (12%)
  matrix products  2.57 us (4%)
  blocking collectives  2.47 us (4%)
  local copies, waits for them, and re-layouts  1.96 us (3%)
  between operations  0.87 us (1%)
    ppermute x12, waiting for transfers between devices, from_partner(): return lax.ppermute(value, axis, pairs)  21.3 us
    ppermute x12, starting transfers between devices, from_partner(): return lax.ppermute(value, axis, pairs)  18.3 us
    pallas_call x2, Pallas kernels, ffn_grad(): pl.pallas_call(ffn_kernel, grid=(groups_here // per_step,), in_specs=[act...  8.16 us
    psum x1, blocking collectives, body(): reduce_hid = hid_sum if chunk == 0 else lambda v: lax.psum(v, 'hid')  2.47 us
    reduce_sum x2, other arithmetic, body(): inner = reduce_hid(jnp.sum(resid * scaled, axis=-1))  2.22 us
    add x3, other arithmetic, hid_sum(): total = total + lax.ppermute(value, 'hid', pairs)  1.95 us
    reduce_sum x6, other arithmetic, body(): jnp.sum(back_f * mates[chunk][section].astype(jnp.float32), axis=-1)  1.64 us
    convert_element_type x2, other arithmetic, body(): normed = (resid * inv[:, None] * norm_gain).astype(jnp.bfloat16)  1.5 us
  transfers between devices with their start and end apart: 18, of which 11 were waited for; matrix products, arithmetic and copies ran while one was open for 15% of the time, Pallas kernels for 12%

profile of v20, /device:TPU:0, one launch (start us, length us, event | category | flops | bytes accessed | tf_op | source)
XLA Modules:
  0.0 66.9 jit_solution(6544374040570424632)
XLA Ops:
  0.7 1.2 %convolution_convert_fusion.1 = bf16[64,1024]{1,0:T(8,128)(2,1)S(1)} fusion(bf16[128,1024]{1,0:T(8,128)(2,1)} %param.9, bf16[1,128,128]{2,1,0:T(8,128)(2,1)} %param.11), kind=kOutput, calls=%fused_computation.4 | convolution fusion | flops 16842752 | bytes 409600 | tf_op jit(solution)/shard_map/kij,kjd->kid/dot_general | solution.py:93
  1.8 3.0 %collective-permute-start = (bf16[64,1024]{1,0:T(8,128)(2,1)S(1)}, bf16[64,1024]{1,0:T(8,128)(2,1)S(1)}, u32[]{:S(2)}, u32[]{:S(2)}) collective-permute-start(bf16[64,1024]{1,0:T(8,128)(2,1)S(1)} %convolution_convert_fusion.1), channel_id=1, source_target_pairs={{0,2},{2,0},{4,6},{6,4},{8,10},{10,8},{12,14},{14,12},{1,3},{3,1},... | collective-permute-start | bytes 393224 | tf_op jit(solution)/shard_map/ppermute | solution.py:14
  5.6 3.5 %collective-permute-done = bf16[64,1024]{1,0:T(8,128)(2,1)S(1)} collective-permute-done((bf16[64,1024]{1,0:T(8,128)(2,1)S(1)}, bf16[64,1024]{1,0:T(8,128)(2,1)S(1)}, u32[]{:S(2)}, u32[]{:S(2)}) %collective-permute-start) | collective-permute-done | bytes 131104 | tf_op jit(solution)/shard_map/ppermute | solution.py:14
  9.3 2.2 %collective-permute-start.1 = (bf16[64,1024]{1,0:T(8,128)(2,1)S(1)}, bf16[64,1024]{1,0:T(8,128)(2,1)S(1)}, u32[]{:S(2)}, u32[]{:S(2)}) collective-permute-start(bf16[64,1024]{1,0:T(8,128)(2,1)S(1)} %fusion.4), channel_id=1, source_target_pairs={{0,4},{2,6},{4,0},{6,2},{8,12},{10,14},{12,8},{14,10},{1,5},{3,7},... | collective-permute-start | bytes 393224 | tf_op jit(solution)/shard_map/ppermute | solution.py:14
  11.5 0.7 %fusion.66 = (bf16[64,1024]{1,0:T(8,128)(2,1)}, bf16[64,1024]{1,0:T(8,128)(2,1)}) fusion(bf16[128,1024]{1,0:T(8,128)(2,1)S(1)} %copy-done.3), kind=kLoop, calls=%fused_computation.134 | loop fusion | bytes 524288 | tf_op jit(solution)/shard_map/slice | solution.py:120
  12.2 2.2 %collective-permute-done.1 = bf16[64,1024]{1,0:T(8,128)(2,1)S(1)} collective-permute-done((bf16[64,1024]{1,0:T(8,128)(2,1)S(1)}, bf16[64,1024]{1,0:T(8,128)(2,1)S(1)}, u32[]{:S(2)}, u32[]{:S(2)}) %collective-permute-start.1) | collective-permute-done | bytes 131104 | tf_op jit(solution)/shard_map/ppermute | solution.py:14
  14.6 3.8 %collective-permute-start.2 = (bf16[64,1024]{1,0:T(8,128)(2,1)S(1)}, bf16[64,1024]{1,0:T(8,128)(2,1)S(1)}, u32[]{:S(2)}, u32[]{:S(2)}) collective-permute-start(bf16[64,1024]{1,0:T(8,128)(2,1)S(1)} %fusion.6), channel_id=1, source_target_pairs={{0,8},{2,10},{4,12},{6,14},{8,0},{10,2},{12,4},{14,6},{1,9},{3,11}... | collective-permute-start | bytes 393224 | tf_op jit(solution)/shard_map/ppermute | solution.py:14
  18.5 1.2 %collective-permute-start.6 = (bf16[64,1024]{1,0:T(8,128)(2,1)S(1)}, bf16[64,1024]{1,0:T(8,128)(2,1)S(1)}, u32[]{:S(2)}, u32[]{:S(2)}) collective-permute-start(bf16[64,1024]{1,0:T(8,128)(2,1)S(1)} %fusion.12), channel_id=1, source_target_pairs={{0,4},{2,6},{4,0},{6,2},{8,12},{10,14},{12,8},{14,10},{1,5},{3,7},... | collective-permute-start | bytes 393224 | tf_op jit(solution)/shard_map/ppermute | solution.py:14
  19.7 3.1 %collective-permute-done.2 = bf16[64,1024]{1,0:T(8,128)(2,1)S(1)} collective-permute-done((bf16[64,1024]{1,0:T(8,128)(2,1)S(1)}, bf16[64,1024]{1,0:T(8,128)(2,1)S(1)}, u32[]{:S(2)}, u32[]{:S(2)}) %collective-permute-start.2) | collective-permute-done | bytes 131104 | tf_op jit(solution)/shard_map/ppermute | solution.py:14
  23.1 1.0 %collective-permute-done.6 = bf16[64,1024]{1,0:T(8,128)(2,1)S(1)} collective-permute-done((bf16[64,1024]{1,0:T(8,128)(2,1)S(1)}, bf16[64,1024]{1,0:T(8,128)(2,1)S(1)}, u32[]{:S(2)}, u32[]{:S(2)}) %collective-permute-start.6) | collective-permute-done | bytes 131104 | tf_op jit(solution)/shard_map/ppermute | solution.py:14
  24.3 0.6 collective-permute-start.7
  24.9 0.7 %multiply_convert_fusion.1.normed_ref = bf16[64,1024]{1,0:T(8,128)(2,1)} fusion(bf16[64,1024]{1,0:T(8,128)(2,1)S(1)} %get-tuple-element.25, f32[1024]{0:T(1024)S(1)} %copy-done.4, f32[64]{0:T(128)S(1)} %add_rsqrt_fusion.1, bf16[128,1024]{1,0:T(8,128)(2,1)S(1)} %copy-done), kind=kLoop, calls=%fused_computation.103 | loop fusion | flops 458752 | bytes 397568 | tf_op jit(solution)/shard_map/convert_element_type | solution.py:127
  25.7 4.1 %shard_map.120 = bf16[64,1024]{1,0:T(8,128)(2,1)} custom-call(bf16[64,1024]{1,0:T(8,128)(2,1)} %multiply_convert_fusion.1.normed_ref, bf16[64,1024]{1,0:T(8,128)(2,1)} %get-tuple-element.29.cot_ref, bf16[8,128,512]{2,1,0:T(8,128)(2,1)} %wg_ref.3, bf16[8,128,512]{2,1,0:T(8,128)(2,1)} %wu_ref.3, bf16[8,512,128]{2,1,0:T(8,128)(2,1)} %wd_ref.3), custom_call_target="tpu_custom_call" | custom-call | flops 335544320 | bytes 3670016 | tf_op jit(solution)/shard_map/pallas_call | solution.py:45
  29.7 1.1 %multiply_reduce_fusion.2 = f32[64]{0:T(128)S(1)} fusion(bf16[64,1024]{1,0:T(8,128)(2,1)} %shard_map.120, bf16[64,1024]{1,0:T(8,128)(2,1)S(1)} %get-tuple-element.25, f32[1024]{0:T(1024)S(1)} %copy-done.4, bf16[128,1024]{1,0:T(8,128)(2,1)S(1)} %copy-done), kind=kLoop, calls=%fused_computation.101 | loop fusion | flops 524224 | bytes 397568 | tf_op jit(solution)/shard_map/reduce_sum | solution.py:130
  31.1 1.8 %collective-permute-done.7 = bf16[64,1024]{1,0:T(8,128)(2,1)S(1)} collective-permute-done((bf16[64,1024]{1,0:T(8,128)(2,1)S(1)}, bf16[64,1024]{1,0:T(8,128)(2,1)S(1)}, u32[]{:S(2)}, u32[]{:S(2)}) %collective-permute-start.7) | collective-permute-done | bytes 131104 | tf_op jit(solution)/shard_map/ppermute | solution.py:14
  33.1 0.8 %copy-done.1 = bf16[64,1024]{1,0:T(8,128)(2,1)S(1)} copy-done((bf16[64,1024]{1,0:T(8,128)(2,1)S(1)}, bf16[64,1024]{1,0:T(8,128)(2,1)}, u32[]{:S(2)}) %copy-start.1) | copy-done | bytes 131096
  34.5 0.8 %collective-permute-start.9 = (bf16[64,1024]{1,0:T(8,128)(2,1)S(1)}, bf16[64,1024]{1,0:T(8,128)(2,1)S(1)}, u32[]{:S(2)}, u32[]{:S(2)}) collective-permute-start(bf16[64,1024]{1,0:T(8,128)(2,1)S(1)} %fusion.18), channel_id=1, source_target_pairs={{0,8},{2,10},{4,12},{6,14},{8,0},{10,2},{12,4},{14,6},{1,9},{3,11}... | collective-permute-start | bytes 393224 | tf_op jit(solution)/shard_map/ppermute | solution.py:14
  35.6 0.8 %multiply_convert_fusion.normed_ref = bf16[64,1024]{1,0:T(8,128)(2,1)} fusion(bf16[64,1024]{1,0:T(8,128)(2,1)S(1)} %fusion.16, f32[64]{0:T(128)S(1)} %add_rsqrt_fusion, f32[1024]{0:T(1024)S(1)} %copy-done.4, bf16[128,1024]{1,0:T(8,128)(2,1)S(1)} %copy-done), kind=kLoop, calls=%fused_computation.98 | loop fusion | flops 458752 | bytes 397568 | tf_op jit(solution)/shard_map/convert_element_type | solution.py:127
  36.3 4.1 %shard_map.121 = bf16[64,1024]{1,0:T(8,128)(2,1)} custom-call(bf16[64,1024]{1,0:T(8,128)(2,1)} %multiply_convert_fusion.normed_ref, bf16[64,1024]{1,0:T(8,128)(2,1)} %get-tuple-element.28.cot_ref, bf16[8,128,512]{2,1,0:T(8,128)(2,1)} %wg_ref.3, bf16[8,128,512]{2,1,0:T(8,128)(2,1)} %wu_ref.3, bf16[8,512,128]{2,1,0:T(8,128)(2,1)} %wd_ref.3), custom_call_target="tpu_custom_call" | custom-call | flops 335544320 | bytes 3670016 | tf_op jit(solution)/shard_map/pallas_call | solution.py:45
  40.4 1.1 %multiply_reduce_fusion = f32[64]{0:T(128)S(1)} fusion(bf16[64,1024]{1,0:T(8,128)(2,1)} %shard_map.121, bf16[64,1024]{1,0:T(8,128)(2,1)S(1)} %fusion.16, f32[1024]{0:T(1024)S(1)} %copy-done.4, bf16[128,1024]{1,0:T(8,128)(2,1)S(1)} %copy-done), kind=kLoop, calls=%fused_computation.96 | loop fusion | flops 524224 | bytes 397568 | tf_op jit(solution)/shard_map/reduce_sum | solution.py:130
  41.6 2.5 %psum.7 = f32[64]{0:T(128)S(1)} all-reduce(f32[64]{0:T(128)S(1)} %multiply_reduce_fusion), channel_id=1, replica_groups=mesh['groups'=2,'seq'=8,'hid'=2] {'hid'}, use_global_device_ids=true, to_apply=%region_4.0 | all-reduce | flops 64 | bytes 512 | tf_op jit(solution)/shard_map/psum | solution.py:124
  44.4 1.9 %collective-permute-start.12 = (bf16[64,1024]{1,0:T(8,128)(2,1)S(1)}, bf16[64,1024]{1,0:T(8,128)(2,1)S(1)}, u32[]{:S(2)}, u32[]{:S(2)}) collective-permute-start(bf16[64,1024]{1,0:T(8,128)(2,1)S(1)} %fusion.35), channel_id=1, source_target_pairs={{0,8},{2,10},{4,12},{6,14},{8,0},{10,2},{12,4},{14,6},{1,9},{3,11}... | collective-permute-start | bytes 393224 | tf_op jit(solution)/shard_map/ppermute | solution.py:14
  46.7 1.2 %collective-permute-start.10 = (bf16[64,1024]{1,0:T(8,128)(2,1)S(1)}, bf16[64,1024]{1,0:T(8,128)(2,1)S(1)}, u32[]{:S(2)}, u32[]{:S(2)}) collective-permute-start(bf16[64,1024]{1,0:T(8,128)(2,1)S(1)} %fusion.25), channel_id=1, source_target_pairs={{0,4},{2,6},{4,0},{6,2},{8,12},{10,14},{12,8},{14,10},{1,5},{3,7},... | collective-permute-start | bytes 393224 | tf_op jit(solution)/shard_map/ppermute | solution.py:14
  47.9 5.9 %collective-permute-done.12 = bf16[64,1024]{1,0:T(8,128)(2,1)S(1)} collective-permute-done((bf16[64,1024]{1,0:T(8,128)(2,1)S(1)}, bf16[64,1024]{1,0:T(8,128)(2,1)S(1)}, u32[]{:S(2)}, u32[]{:S(2)}) %collective-permute-start.12) | collective-permute-done | bytes 131104 | tf_op jit(solution)/shard_map/ppermute | solution.py:14
  54.6 1.6 %collective-permute-start.11 = (bf16[64,1024]{1,0:T(8,128)(2,1)S(1)}, bf16[64,1024]{1,0:T(8,128)(2,1)S(1)}, u32[]{:S(2)}, u32[]{:S(2)}) collective-permute-start(bf16[64,1024]{1,0:T(8,128)(2,1)S(1)} %fusion.30), channel_id=1, source_target_pairs={{0,2},{2,0},{4,6},{6,4},{8,10},{10,8},{12,14},{14,12},{1,3},{3,1},... | collective-permute-start | bytes 393224 | tf_op jit(solution)/shard_map/ppermute | solution.py:14
  56.2 3.0 %collective-permute-done.13 = bf16[64,1024]{1,0:T(8,128)(2,1)S(1)} collective-permute-done((bf16[64,1024]{1,0:T(8,128)(2,1)S(1)}, bf16[64,1024]{1,0:T(8,128)(2,1)S(1)}, u32[]{:S(2)}, u32[]{:S(2)}) %collective-permute-start.13) | collective-permute-done | bytes 131104 | tf_op jit(solution)/shard_map/ppermute | solution.py:14
  59.6 1.6 %collective-permute-start.14 = (bf16[64,1024]{1,0:T(8,128)(2,1)S(1)}, bf16[64,1024]{1,0:T(8,128)(2,1)S(1)}, u32[]{:S(2)}, u32[]{:S(2)}) collective-permute-start(bf16[64,1024]{1,0:T(8,128)(2,1)S(1)} %fusion.45), channel_id=1, source_target_pairs={{0,2},{2,0},{4,6},{6,4},{8,10},{10,8},{12,14},{14,12},{1,3},{3,1},... | collective-permute-start | bytes 393224 | tf_op jit(solution)/shard_map/ppermute | solution.py:14
  62.4 0.7 fusion.70
  63.1 0.7 fusion.71
  63.9 0.7 %collective-permute-done.14 = bf16[64,1024]{1,0:T(8,128)(2,1)S(1)} collective-permute-done((bf16[64,1024]{1,0:T(8,128)(2,1)S(1)}, bf16[64,1024]{1,0:T(8,128)(2,1)S(1)}, u32[]{:S(2)}, u32[]{:S(2)}) %collective-permute-start.14) | collective-permute-done | bytes 131104 | tf_op jit(solution)/shard_map/ppermute | solution.py:14
  65.0 1.0 %fusion.1 = bf16[128,1024]{1,0:T(8,128)(2,1)} fusion(f32[64,1024]{1,0:T(8,128)S(1)} %get-tuple-element.26, f32[64,1024]{1,0:T(8,128)S(1)} %get-tuple-element.27, bf16[64,1024]{1,0:T(8,128)(2,1)S(1)} %fusion.44, bf16[64,1024]{1,0:T(8,128)(2,1)S(1)} %fusion.29, bf16[1,128,128]{2,1,0:T(8,128)(2,1)S(1)} %copy-done.5), kind=kOutput, calls=%fused_computation.2 | convolution fusion | flops 34471936 | bytes 1081344 | tf_op jit(solution)/shard_map/kij,kid->kjd/dot_general | solution.py:168
  66.3 0.6 add.109
  (63 shorter events, 6.7 us)
Async XLA Ops:
  0.6 4.2 %copy-start.5 = (bf16[1,128,128]{2,1,0:T(8,128)(2,1)S(1)}, bf16[1,128,128]{2,1,0:T(8,128)(2,1)}, u32[]{:S(2)}) copy-start(bf16[1,128,128]{2,1,0:T(8,128)(2,1)} %param.11) | copy-start | bytes 98308
  0.6 4.2 %copy-start = (bf16[128,1024]{1,0:T(8,128)(2,1)S(1)}, bf16[128,1024]{1,0:T(8,128)(2,1)}, u32[]{:S(2)}) copy-start(bf16[128,1024]{1,0:T(8,128)(2,1)} %param.9) | copy-start | bytes 786436
  1.8 7.3 %collective-permute-start = (bf16[64,1024]{1,0:T(8,128)(2,1)S(1)}, bf16[64,1024]{1,0:T(8,128)(2,1)S(1)}, u32[]{:S(2)}, u32[]{:S(2)}) collective-permute-start(bf16[64,1024]{1,0:T(8,128)(2,1)S(1)} %convolution_convert_fusion.1), channel_id=1, source_target_pairs={{0,2},{2,0},{4,6},{6,4},{8,10},{10,8},{12,14},{14,12},{1,3},{3,1},... | collective-permute-start | bytes 393224 | tf_op jit(solution)/shard_map/ppermute | solution.py:14
  4.9 0.7 %copy-start.6 = (f32[3,128]{1,0:T(4,128)S(1)}, f32[3,128]{1,0:T(4,128)}, u32[]{:S(2)}) copy-start(f32[3,128]{1,0:T(4,128)} %param.13) | copy-start | bytes 4612
  4.9 0.7 %copy-start.7 = (f32[3,128]{1,0:T(4,128)S(1)}, f32[3,128]{1,0:T(4,128)}, u32[]{:S(2)}) copy-start(f32[3,128]{1,0:T(4,128)} %param.12) | copy-start | bytes 4612
  5.0 6.5 %copy-start.3 = (bf16[128,1024]{1,0:T(8,128)(2,1)S(1)}, bf16[128,1024]{1,0:T(8,128)(2,1)}, u32[]{:S(2)}) copy-start(bf16[128,1024]{1,0:T(8,128)(2,1)} %param.10) | copy-start | bytes 786436
  5.1 13.3 %collective-permute-start.5 = (bf16[64,1024]{1,0:T(8,128)(2,1)S(1)}, bf16[64,1024]{1,0:T(8,128)(2,1)S(1)}, u32[]{:S(2)}, u32[]{:S(2)}) collective-permute-start(bf16[64,1024]{1,0:T(8,128)(2,1)S(1)} %convolution_convert_fusion), channel_id=1, source_target_pairs={{0,2},{2,0},{4,6},{6,4},{8,10},{10,8},{12,14},{14,12},{1,3},{3,1},... | collective-permute-start | bytes 393224 | tf_op jit(solution)/shard_map/ppermute | solution.py:14
  9.3 5.2 %collective-permute-start.1 = (bf16[64,1024]{1,0:T(8,128)(2,1)S(1)}, bf16[64,1024]{1,0:T(8,128)(2,1)S(1)}, u32[]{:S(2)}, u32[]{:S(2)}) collective-permute-start(bf16[64,1024]{1,0:T(8,128)(2,1)S(1)} %fusion.4), channel_id=1, source_target_pairs={{0,4},{2,6},{4,0},{6,2},{8,12},{10,14},{12,8},{14,10},{1,5},{3,7},... | collective-permute-start | bytes 393224 | tf_op jit(solution)/shard_map/ppermute | solution.py:14
  14.6 8.2 %collective-permute-start.2 = (bf16[64,1024]{1,0:T(8,128)(2,1)S(1)}, bf16[64,1024]{1,0:T(8,128)(2,1)S(1)}, u32[]{:S(2)}, u32[]{:S(2)}) collective-permute-start(bf16[64,1024]{1,0:T(8,128)(2,1)S(1)} %fusion.6), channel_id=1, source_target_pairs={{0,8},{2,10},{4,12},{6,14},{8,0},{10,2},{12,4},{14,6},{1,9},{3,11}... | collective-permute-start | bytes 393224 | tf_op jit(solution)/shard_map/ppermute | solution.py:14
  18.5 5.6 %collective-permute-start.6 = (bf16[64,1024]{1,0:T(8,128)(2,1)S(1)}, bf16[64,1024]{1,0:T(8,128)(2,1)S(1)}, u32[]{:S(2)}, u32[]{:S(2)}) collective-permute-start(bf16[64,1024]{1,0:T(8,128)(2,1)S(1)} %fusion.12), channel_id=1, source_target_pairs={{0,4},{2,6},{4,0},{6,2},{8,12},{10,14},{12,8},{14,10},{1,5},{3,7},... | collective-permute-start | bytes 393224 | tf_op jit(solution)/shard_map/ppermute | solution.py:14
  23.1 1.8 %collective-permute-start.3 = (f32[64]{0:T(128)S(1)}, f32[64]{0:T(128)S(1)}, u32[]{:S(2)}, u32[]{:S(2)}) collective-permute-start(f32[64]{0:T(128)S(1)} %get-tuple-element.24), channel_id=1, source_target_pairs={{0,1},{1,0},{2,3},{3,2},{4,5},{5,4},{6,7},{7,6},{8,9},{9,8},{10,11... | collective-permute-start | bytes 776 | tf_op jit(solution)/shard_map/ppermute | solution.py:70
  24.1 0.8 %copy-start.4 = (f32[1024]{0:T(1024)S(1)}, f32[1024]{0:T(1024)}, u32[]{:S(2)}) copy-start(f32[1024]{0:T(1024)} %param.14) | copy-start | bytes 12292
  24.3 8.7 %collective-permute-start.7 = (bf16[64,1024]{1,0:T(8,128)(2,1)S(1)}, bf16[64,1024]{1,0:T(8,128)(2,1)S(1)}, u32[]{:S(2)}, u32[]{:S(2)}) collective-permute-start(bf16[64,1024]{1,0:T(8,128)(2,1)S(1)} %fusion.14), channel_id=1, source_target_pairs={{0,8},{2,10},{4,12},{6,14},{8,0},{10,2},{12,4},{14,6},{1,9},{3,11}... | collective-permute-start | bytes 393224 | tf_op jit(solution)/shard_map/ppermute | solution.py:14
  30.8 2.2 %collective-permute-start.4 = (f32[64]{0:T(128)S(1)}, f32[64]{0:T(128)S(1)}, u32[]{:S(2)}, u32[]{:S(2)}) collective-permute-start(f32[64]{0:T(128)S(1)} %multiply_reduce_fusion.2), channel_id=1, source_target_pairs={{0,1},{1,0},{2,3},{3,2},{4,5},{5,4},{6,7},{7,6},{8,9},{9,8},{10,11... | collective-permute-start | bytes 776 | tf_op jit(solution)/shard_map/ppermute | solution.py:70
  32.9 0.9 %copy-start.1 = (bf16[64,1024]{1,0:T(8,128)(2,1)S(1)}, bf16[64,1024]{1,0:T(8,128)(2,1)}, u32[]{:S(2)}) copy-start(bf16[64,1024]{1,0:T(8,128)(2,1)} %shard_map.120) | copy-start | bytes 393220
  34.4 1.2 %collective-permute-start.8 = (f32[64]{0:T(128)S(1)}, f32[64]{0:T(128)S(1)}, u32[]{:S(2)}, u32[]{:S(2)}) collective-permute-start(f32[64]{0:T(128)S(1)} %multiply_reduce_fusion.1), channel_id=1, source_target_pairs={{0,1},{1,0},{2,3},{3,2},{4,5},{5,4},{6,7},{7,6},{8,9},{9,8},{10,11... | collective-permute-start | bytes 776 | tf_op jit(solution)/shard_map/ppermute | solution.py:70
  34.5 11.9 %collective-permute-start.9 = (bf16[64,1024]{1,0:T(8,128)(2,1)S(1)}, bf16[64,1024]{1,0:T(8,128)(2,1)S(1)}, u32[]{:S(2)}, u32[]{:S(2)}) collective-permute-start(bf16[64,1024]{1,0:T(8,128)(2,1)S(1)} %fusion.18), channel_id=1, source_target_pairs={{0,8},{2,10},{4,12},{6,14},{8,0},{10,2},{12,4},{14,6},{1,9},{3,11}... | collective-permute-start | bytes 393224 | tf_op jit(solution)/shard_map/ppermute | solution.py:14
  40.4 3.6 %copy-start.2 = (bf16[64,1024]{1,0:T(8,128)(2,1)S(1)}, bf16[64,1024]{1,0:T(8,128)(2,1)}, u32[]{:S(2)}) copy-start(bf16[64,1024]{1,0:T(8,128)(2,1)} %shard_map.121) | copy-start | bytes 393220
  44.4 9.4 %collective-permute-start.12 = (bf16[64,1024]{1,0:T(8,128)(2,1)S(1)}, bf16[64,1024]{1,0:T(8,128)(2,1)S(1)}, u32[]{:S(2)}, u32[]{:S(2)}) collective-permute-start(bf16[64,1024]{1,0:T(8,128)(2,1)S(1)} %fusion.35), channel_id=1, source_target_pairs={{0,8},{2,10},{4,12},{6,14},{8,0},{10,2},{12,4},{14,6},{1,9},{3,11}... | collective-permute-start | bytes 393224 | tf_op jit(solution)/shard_map/ppermute | solution.py:14
  46.7 7.5 %collective-permute-start.10 = (bf16[64,1024]{1,0:T(8,128)(2,1)S(1)}, bf16[64,1024]{1,0:T(8,128)(2,1)S(1)}, u32[]{:S(2)}, u32[]{:S(2)}) collective-permute-start(bf16[64,1024]{1,0:T(8,128)(2,1)S(1)} %fusion.25), channel_id=1, source_target_pairs={{0,4},{2,6},{4,0},{6,2},{8,12},{10,14},{12,8},{14,10},{1,5},{3,7},... | collective-permute-start | bytes 393224 | tf_op jit(solution)/shard_map/ppermute | solution.py:14
  54.2 5.0 %collective-permute-start.13 = (bf16[64,1024]{1,0:T(8,128)(2,1)S(1)}, bf16[64,1024]{1,0:T(8,128)(2,1)S(1)}, u32[]{:S(2)}, u32[]{:S(2)}) collective-permute-start(bf16[64,1024]{1,0:T(8,128)(2,1)S(1)} %fusion.40), channel_id=1, source_target_pairs={{0,4},{2,6},{4,0},{6,2},{8,12},{10,14},{12,8},{14,10},{1,5},{3,7},... | collective-permute-start | bytes 393224 | tf_op jit(solution)/shard_map/ppermute | solution.py:14
  54.6 9.1 %collective-permute-start.11 = (bf16[64,1024]{1,0:T(8,128)(2,1)S(1)}, bf16[64,1024]{1,0:T(8,128)(2,1)S(1)}, u32[]{:S(2)}, u32[]{:S(2)}) collective-permute-start(bf16[64,1024]{1,0:T(8,128)(2,1)S(1)} %fusion.30), channel_id=1, source_target_pairs={{0,2},{2,0},{4,6},{6,4},{8,10},{10,8},{12,14},{14,12},{1,3},{3,1},... | collective-permute-start | bytes 393224 | tf_op jit(solution)/shard_map/ppermute | solution.py:14
  59.6 5.0 %collective-permute-start.14 = (bf16[64,1024]{1,0:T(8,128)(2,1)S(1)}, bf16[64,1024]{1,0:T(8,128)(2,1)S(1)}, u32[]{:S(2)}, u32[]{:S(2)}) collective-permute-start(bf16[64,1024]{1,0:T(8,128)(2,1)S(1)} %fusion.45), channel_id=1, source_target_pairs={{0,2},{2,0},{4,6},{6,4},{8,10},{10,8},{12,14},{14,12},{1,3},{3,1},... | collective-permute-start | bytes 393224 | tf_op jit(solution)/shard_map/ppermute | solution.py:14
  61.3 1.2 %collective-permute-start.16 = (f32[3,128]{1,0:T(4,128)S(1)}, f32[3,128]{1,0:T(4,128)S(1)}, u32[]{:S(2)}, u32[]{:S(2)}) collective-permute-start(f32[3,128]{1,0:T(4,128)S(1)} %maximum_maximum_fusion.1), channel_id=1, source_target_pairs={{0,1},{1,0},{2,3},{3,2},{4,5},{5,4},{6,7},{7,6},{8,9},{9,8},{10,11... | collective-permute-start | bytes 4616 | tf_op jit(solution)/shard_map/ppermute | solution.py:70
  61.4 1.7 %collective-permute-start.15 = (f32[3,128]{1,0:T(4,128)S(1)}, f32[3,128]{1,0:T(4,128)S(1)}, u32[]{:S(2)}, u32[]{:S(2)}) collective-permute-start(f32[3,128]{1,0:T(4,128)S(1)} %maximum_maximum_fusion), channel_id=1, source_target_pairs={{0,1},{1,0},{2,3},{3,2},{4,5},{5,4},{6,7},{7,6},{8,9},{9,8},{10,11... | collective-permute-start | bytes 4616 | tf_op jit(solution)/shard_map/ppermute | solution.py:70
  65.0 1.3 %collective-permute-start.17 = (f32[1,128,128]{2,1,0:T(8,128)S(1)}, f32[1,128,128]{2,1,0:T(8,128)S(1)}, u32[]{:S(2)}, u32[]{:S(2)}) collective-permute-start(f32[1,128,128]{2,1,0:T(8,128)S(1)} %convolution_bitcast_fusion.1), channel_id=1, source_target_pairs={{0,1},{1,0},{2,3},{3,2},{4,5},{5,4},{6,7},{7,6},{8,9},{9,8},{10,11... | collective-permute-start | bytes 196616 | tf_op jit(solution)/shard_map/ppermute | solution.py:70

commit v21 on v13

--- a/solution.py
+++ b/solution.py
@@ -114,19 +114,26 @@
     sents = []
     directs = []
     previous = None
+    held = None
     for chunk, rs in enumerate(spans):
         mixed = tie(pieces[chunk], previous)
         cot = cotangent[rs]
         tok_f = tokens[rs].astype(jnp.float32)
         mixed_f = mixed.astype(jnp.float32)
         resid = tok_f + tok_f * mixed_f
-        reduce_hid = hid_sum if chunk == 0 else (lambda v: lax.psum(v, "hid"))
         square = hid_sum(jnp.sum(resid * resid, axis=-1))
         inv = lax.rsqrt(square / D + 1e-06)
         normed = (resid * inv[:, None] * norm_gain).astype(jnp.bfloat16)
         d_normed = ffn_grad(normed, cot, w_gate, w_up, w_down)
         scaled = norm_gain * d_normed
-        inner = reduce_hid(jnp.sum(resid * scaled, axis=-1))
+        partial = jnp.sum(resid * scaled, axis=-1)
+        if held is not None:
+            partial = tie(partial, held[0])
+        inner = hid_sum(partial)
+        if held is not None:
+            rest = from_partner(tie(held[1], inner), "seq", top)
+            sents[-1] = jnp.concatenate([held[0], rest], axis=1)
+            held = None
         d_resid = (
             cot.astype(jnp.float32)
             + inv[:, None] * scaled
@@ -136,7 +143,13 @@
         sent = (coef_cross[top, rs][:, None] * d_mixed.astype(jnp.float32)).astype(jnp.bfloat16)
         previous = sent
         backs.append(d_mixed)
-        sents.append(from_partner(sent, "seq", top))
+        half = width // 2
+        if chunk + 1 < len(spans) and half % 128 == 0:
+            first_half = from_partner(sent[:, :half], "seq", top)
+            held = (first_half, sent[:, half:])
+            sents.append(None)
+        else:
+            sents.append(from_partner(sent, "seq", top))
         directs.append(d_resid * (1.0 + mixed_f))
     grads_self = [[None] * sections for _ in spans]
     grads_cross = [[None] * sections for _ in spans]

time: 66.8 us -> 73.6 us (1.10)
  waiting for transfers between devices: 22.1 us -> 30.6 us
  blocking collectives: 2.47 us -> 0 us
  starting transfers between devices: 19.9 us -> 20.8 us
    ppermute x12 -> x13, waiting for transfers between devices: 21.2 us -> 29.2 us  [from_partner(): return lax.ppermute(value, axis, pairs)]
    psum x1 -> x0, blocking collectives: 2.47 us -> none  [body(): reduce_hid = hid_sum if chunk == 0 else lambda v: lax.psum(v, 'hid')]
    ppermute x12 -> x13, starting transfers between devices: 19 us -> 19.6 us  [from_partner(): return lax.ppermute(value, axis, pairs)]
    reduce_sum x6 -> x5, other arithmetic: 1.65 us -> 1.47 us  [body(): jnp.sum(back_f * mates[chunk][section].astype(jnp.float32), axis=-1)]
  transfers between devices with their start and end apart: 18 -> 20, of which waited for: 10 -> 11; matrix products, arithmetic and copies ran while one was open for 15% -> 12% of each run, Pallas kernels for 12% -> 11%
where the time goes in v21:
time: 73.6 us; the launch traced here: 73.4 us
  waiting for transfers between devices  30.6 us (42%)
  starting transfers between devices  20.8 us (28%)
  other arithmetic  9.13 us (12%)
  Pallas kernels  8.11 us (11%)
  matrix products  2.56 us (3%)
  local copies, waits for them, and re-layouts  1.27 us (2%)
  between operations  0.89 us (1%)
    ppermute x13, waiting for transfers between devices, from_partner(): return lax.ppermute(value, axis, pairs)  29.2 us
    ppermute x13, starting transfers between devices, from_partner(): return lax.ppermute(value, axis, pairs)  19.6 us
    pallas_call x2, Pallas kernels, ffn_grad(): pl.pallas_call(ffn_kernel, grid=(groups_here // per_step,), in_specs=[act...  8.11 us
    reduce_sum x2, other arithmetic, body(): partial = jnp.sum(resid * scaled, axis=-1)  2.29 us
    add x3, other arithmetic, hid_sum(): total = total + lax.ppermute(value, 'hid', pairs)  1.95 us
    convert_element_type x2, other arithmetic, body(): normed = (resid * inv[:, None] * norm_gain).astype(jnp.bfloat16)  1.5 us
    reduce_sum x5, other arithmetic, body(): jnp.sum(back_f * mates[chunk][section].astype(jnp.float32), axis=-1)  1.47 us
  transfers between devices with their start and end apart: 20, of which 11 were waited for; matrix products, arithmetic and copies ran while one was open for 12% of the time, Pallas kernels for 11%

profile of v21, /device:TPU:0, one launch (start us, length us, event | category | flops | bytes accessed | tf_op | source)
XLA Modules:
  0.0 73.4 jit_solution(14747796379956441007)
XLA Ops:
  0.7 1.2 %convolution_convert_fusion = bf16[64,1024]{1,0:T(8,128)(2,1)S(1)} fusion(bf16[128,1024]{1,0:T(8,128)(2,1)} %param.9, bf16[1,128,128]{2,1,0:T(8,128)(2,1)} %param.11), kind=kOutput, calls=%fused_computation.3 | convolution fusion | flops 16842752 | bytes 409600 | tf_op jit(solution)/shard_map/kij,kjd->kid/dot_general | solution.py:92
  1.8 3.0 %collective-permute-start.5 = (bf16[64,1024]{1,0:T(8,128)(2,1)S(1)}, bf16[64,1024]{1,0:T(8,128)(2,1)S(1)}, u32[]{:S(2)}, u32[]{:S(2)}) collective-permute-start(bf16[64,1024]{1,0:T(8,128)(2,1)S(1)} %convolution_convert_fusion), channel_id=1, source_target_pairs={{0,2},{2,0},{4,6},{6,4},{8,10},{10,8},{12,14},{14,12},{1,3},{3,1},... | collective-permute-start | bytes 393224 | tf_op jit(solution)/shard_map/ppermute | solution.py:14
  5.7 5.5 %collective-permute-done = bf16[64,1024]{1,0:T(8,128)(2,1)S(1)} collective-permute-done((bf16[64,1024]{1,0:T(8,128)(2,1)S(1)}, bf16[64,1024]{1,0:T(8,128)(2,1)S(1)}, u32[]{:S(2)}, u32[]{:S(2)}) %collective-permute-start) | collective-permute-done | bytes 131104 | tf_op jit(solution)/shard_map/ppermute | solution.py:14
  11.3 1.9 %collective-permute-start.1 = (bf16[64,1024]{1,0:T(8,128)(2,1)S(1)}, bf16[64,1024]{1,0:T(8,128)(2,1)S(1)}, u32[]{:S(2)}, u32[]{:S(2)}) collective-permute-start(bf16[64,1024]{1,0:T(8,128)(2,1)S(1)} %fusion.4), channel_id=1, source_target_pairs={{0,4},{2,6},{4,0},{6,2},{8,12},{10,14},{12,8},{14,10},{1,5},{3,7},... | collective-permute-start | bytes 393224 | tf_op jit(solution)/shard_map/ppermute | solution.py:14
  13.2 0.7 fusion.66
  13.9 2.4 %collective-permute-done.1 = bf16[64,1024]{1,0:T(8,128)(2,1)S(1)} collective-permute-done((bf16[64,1024]{1,0:T(8,128)(2,1)S(1)}, bf16[64,1024]{1,0:T(8,128)(2,1)S(1)}, u32[]{:S(2)}, u32[]{:S(2)}) %collective-permute-start.1) | collective-permute-done | bytes 131104 | tf_op jit(solution)/shard_map/ppermute | solution.py:14
  16.4 2.9 %collective-permute-start.2 = (bf16[64,1024]{1,0:T(8,128)(2,1)S(1)}, bf16[64,1024]{1,0:T(8,128)(2,1)S(1)}, u32[]{:S(2)}, u32[]{:S(2)}) collective-permute-start(bf16[64,1024]{1,0:T(8,128)(2,1)S(1)} %fusion.6), channel_id=1, source_target_pairs={{0,8},{2,10},{4,12},{6,14},{8,0},{10,2},{12,4},{14,6},{1,9},{3,11}... | collective-permute-start | bytes 393224 | tf_op jit(solution)/shard_map/ppermute | solution.py:14
  19.4 1.6 %collective-permute-start.6 = (bf16[64,1024]{1,0:T(8,128)(2,1)S(1)}, bf16[64,1024]{1,0:T(8,128)(2,1)S(1)}, u32[]{:S(2)}, u32[]{:S(2)}) collective-permute-start(bf16[64,1024]{1,0:T(8,128)(2,1)S(1)} %fusion.12), channel_id=1, source_target_pairs={{0,4},{2,6},{4,0},{6,2},{8,12},{10,14},{12,8},{14,10},{1,5},{3,7},... | collective-permute-start | bytes 393224 | tf_op jit(solution)/shard_map/ppermute | solution.py:14
  21.1 2.8 %collective-permute-done.2 = bf16[64,1024]{1,0:T(8,128)(2,1)S(1)} collective-permute-done((bf16[64,1024]{1,0:T(8,128)(2,1)S(1)}, bf16[64,1024]{1,0:T(8,128)(2,1)S(1)}, u32[]{:S(2)}, u32[]{:S(2)}) %collective-permute-start.2) | collective-permute-done | bytes 131104 | tf_op jit(solution)/shard_map/ppermute | solution.py:14
  24.7 1.2 %collective-permute-start.7 = (bf16[64,1024]{1,0:T(8,128)(2,1)S(1)}, bf16[64,1024]{1,0:T(8,128)(2,1)S(1)}, u32[]{:S(2)}, u32[]{:S(2)}) collective-permute-start(bf16[64,1024]{1,0:T(8,128)(2,1)S(1)} %fusion.14), channel_id=1, source_target_pairs={{0,8},{2,10},{4,12},{6,14},{8,0},{10,2},{12,4},{14,6},{1,9},{3,11}... | collective-permute-start | bytes 393224 | tf_op jit(solution)/shard_map/ppermute | solution.py:14
  25.9 0.8 %multiply_convert_fusion.1.normed_ref = bf16[64,1024]{1,0:T(8,128)(2,1)} fusion(bf16[64,1024]{1,0:T(8,128)(2,1)S(1)} %get-tuple-element.31, f32[1024]{0:T(1024)S(1)} %copy-done.4, f32[64]{0:T(128)S(1)} %add_rsqrt_fusion.1, bf16[128,1024]{1,0:T(8,128)(2,1)S(1)} %copy-done), kind=kLoop, calls=%fused_computation.101 | loop fusion | flops 458752 | bytes 397568 | tf_op jit(solution)/shard_map/convert_element_type | solution.py:126
  26.6 4.1 %shard_map.120 = f32[64,1024]{1,0:T(8,128)} custom-call(bf16[64,1024]{1,0:T(8,128)(2,1)} %multiply_convert_fusion.1.normed_ref, bf16[64,1024]{1,0:T(8,128)(2,1)} %get-tuple-element.35.cot_ref, bf16[8,128,512]{2,1,0:T(8,128)(2,1)} %wg_ref.3, bf16[8,128,512]{2,1,0:T(8,128)(2,1)} %wu_ref.3, bf16[8,512,128]{2,1,0:T(8,128)(2,1)} %wd_ref.3), custom_call_target="tpu_custom_call" | custom-call | flops 335544320 | bytes 3670016 | tf_op jit(solution)/shard_map/pallas_call | solution.py:44
  30.7 1.1 %multiply_reduce_fusion.2 = f32[64]{0:T(128)S(1)} fusion(f32[64,1024]{1,0:T(8,128)} %shard_map.120, bf16[64,1024]{1,0:T(8,128)(2,1)S(1)} %get-tuple-element.31, f32[1024]{0:T(1024)S(1)} %copy-done.4, bf16[128,1024]{1,0:T(8,128)(2,1)S(1)} %copy-done), kind=kLoop, calls=%fused_computation.100 | loop fusion | flops 458688 | bytes 528640 | tf_op jit(solution)/shard_map/reduce_sum | solution.py:129
  32.1 2.0 %collective-permute-done.7 = bf16[64,1024]{1,0:T(8,128)(2,1)S(1)} collective-permute-done((bf16[64,1024]{1,0:T(8,128)(2,1)S(1)}, bf16[64,1024]{1,0:T(8,128)(2,1)S(1)}, u32[]{:S(2)}, u32[]{:S(2)}) %collective-permute-start.7) | collective-permute-done | bytes 131104 | tf_op jit(solution)/shard_map/ppermute | solution.py:14
  34.8 0.9 %collective-permute-start.9 = (bf16[64,512]{1,0:T(8,128)(2,1)S(1)}, bf16[64,512]{1,0:T(8,128)(2,1)S(1)}, u32[]{:S(2)}, u32[]{:S(2)}) collective-permute-start(bf16[64,512]{1,0:T(8,128)(2,1)S(1)} %get-tuple-element.37), channel_id=1, source_target_pairs={{0,8},{2,10},{4,12},{6,14},{8,0},{10,2},{12,4},{14,6},{1,9},{3,11}... | collective-permute-start | bytes 196616 | tf_op jit(solution)/shard_map/ppermute | solution.py:14
  35.9 0.8 %multiply_convert_fusion.normed_ref = bf16[64,1024]{1,0:T(8,128)(2,1)} fusion(bf16[64,1024]{1,0:T(8,128)(2,1)S(1)} %fusion.16, f32[64]{0:T(128)S(1)} %add_rsqrt_fusion, f32[1024]{0:T(1024)S(1)} %copy-done.4, bf16[128,1024]{1,0:T(8,128)(2,1)S(1)} %copy-done), kind=kLoop, calls=%fused_computation.97 | loop fusion | flops 458752 | bytes 397568 | tf_op jit(solution)/shard_map/convert_element_type | solution.py:126
  36.7 4.1 %shard_map.121 = f32[64,1024]{1,0:T(8,128)} custom-call(bf16[64,1024]{1,0:T(8,128)(2,1)} %multiply_convert_fusion.normed_ref, bf16[64,1024]{1,0:T(8,128)(2,1)} %get-tuple-element.34.cot_ref, bf16[8,128,512]{2,1,0:T(8,128)(2,1)} %wg_ref.3, bf16[8,128,512]{2,1,0:T(8,128)(2,1)} %wu_ref.3, bf16[8,512,128]{2,1,0:T(8,128)(2,1)} %wd_ref.3), custom_call_target="tpu_custom_call" | custom-call | flops 335544320 | bytes 3670016 | tf_op jit(solution)/shard_map/pallas_call | solution.py:44
  40.7 1.2 %multiply_reduce_fusion = f32[64]{0:T(128)S(1)} fusion(f32[64,1024]{1,0:T(8,128)} %shard_map.121, bf16[64,1024]{1,0:T(8,128)(2,1)S(1)} %fusion.16, f32[1024]{0:T(1024)S(1)} %copy-done.4, bf16[128,1024]{1,0:T(8,128)(2,1)S(1)} %copy-done), kind=kLoop, calls=%fused_computation.96 | loop fusion | flops 458688 | bytes 528640 | tf_op jit(solution)/shard_map/reduce_sum | solution.py:129
  42.2 0.9 %collective-permute-done.10 = f32[64]{0:T(128)S(1)} collective-permute-done((f32[64]{0:T(128)S(1)}, f32[64]{0:T(128)S(1)}, u32[]{:S(2)}, u32[]{:S(2)}) %collective-permute-start.10) | collective-permute-done | bytes 288 | tf_op jit(solution)/shard_map/ppermute | solution.py:69
  43.5 2.0 %collective-permute-start.14 = (bf16[64,1024]{1,0:T(8,128)(2,1)S(1)}, bf16[64,1024]{1,0:T(8,128)(2,1)S(1)}, u32[]{:S(2)}, u32[]{:S(2)}) collective-permute-start(bf16[64,1024]{1,0:T(8,128)(2,1)S(1)} %fusion.35), channel_id=1, source_target_pairs={{0,8},{2,10},{4,12},{6,14},{8,0},{10,2},{12,4},{14,6},{1,9},{3,11}... | collective-permute-start | bytes 393224 | tf_op jit(solution)/shard_map/ppermute | solution.py:14
  45.5 1.0 %collective-permute-start.11 = (bf16[64,512]{1,0:T(8,128)(2,1)S(1)}, bf16[64,512]{1,0:T(8,128)(2,1)S(1)}, u32[]{:S(2)}, u32[]{:S(2)}) collective-permute-start(bf16[64,512]{1,0:T(8,128)(2,1)S(1)} %get-tuple-element.9), channel_id=1, source_target_pairs={{0,8},{2,10},{4,12},{6,14},{8,0},{10,2},{12,4},{14,6},{1,9},{3,11}... | collective-permute-start | bytes 196616 | tf_op jit(solution)/shard_map/ppermute | solution.py:14
  46.5 9.2 %collective-permute-done.11 = bf16[64,512]{1,0:T(8,128)(2,1)S(1)} collective-permute-done((bf16[64,512]{1,0:T(8,128)(2,1)S(1)}, bf16[64,512]{1,0:T(8,128)(2,1)S(1)}, u32[]{:S(2)}, u32[]{:S(2)}) %collective-permute-start.11) | collective-permute-done | bytes 65568 | tf_op jit(solution)/shard_map/ppermute | solution.py:14
  56.3 2.1 %collective-permute-start.12 = (bf16[64,1024]{1,0:T(8,128)(2,1)S(1)}, bf16[64,1024]{1,0:T(8,128)(2,1)S(1)}, u32[]{:S(2)}, u32[]{:S(2)}) collective-permute-start(bf16[64,1024]{1,0:T(8,128)(2,1)S(1)} %fusion.25), channel_id=1, source_target_pairs={{0,4},{2,6},{4,0},{6,2},{8,12},{10,14},{12,8},{14,10},{1,5},{3,7},... | collective-permute-start | bytes 393224 | tf_op jit(solution)/shard_map/ppermute | solution.py:14
  58.4 4.0 %collective-permute-done.15 = bf16[64,1024]{1,0:T(8,128)(2,1)S(1)} collective-permute-done((bf16[64,1024]{1,0:T(8,128)(2,1)S(1)}, bf16[64,1024]{1,0:T(8,128)(2,1)S(1)}, u32[]{:S(2)}, u32[]{:S(2)}) %collective-permute-start.15) | collective-permute-done | bytes 131104 | tf_op jit(solution)/shard_map/ppermute | solution.py:14
  62.8 1.8 %collective-permute-start.16 = (bf16[64,1024]{1,0:T(8,128)(2,1)S(1)}, bf16[64,1024]{1,0:T(8,128)(2,1)S(1)}, u32[]{:S(2)}, u32[]{:S(2)}) collective-permute-start(bf16[64,1024]{1,0:T(8,128)(2,1)S(1)} %fusion.45), channel_id=1, source_target_pairs={{0,2},{2,0},{4,6},{6,4},{8,10},{10,8},{12,14},{14,12},{1,3},{3,1},... | collective-permute-start | bytes 393224 | tf_op jit(solution)/shard_map/ppermute | solution.py:14
  65.0 0.5 collective-permute-start.17
  65.6 1.1 %collective-permute-start.13 = (bf16[64,1024]{1,0:T(8,128)(2,1)S(1)}, bf16[64,1024]{1,0:T(8,128)(2,1)S(1)}, u32[]{:S(2)}, u32[]{:S(2)}) collective-permute-start(bf16[64,1024]{1,0:T(8,128)(2,1)S(1)} %fusion.30), channel_id=1, source_target_pairs={{0,2},{2,0},{4,6},{6,4},{8,10},{10,8},{12,14},{14,12},{1,3},{3,1},... | collective-permute-start | bytes 393224 | tf_op jit(solution)/shard_map/ppermute | solution.py:14
  66.6 0.7 fusion.71
  67.3 0.7 fusion.72
  68.1 3.0 %collective-permute-done.13 = bf16[64,1024]{1,0:T(8,128)(2,1)S(1)} collective-permute-done((bf16[64,1024]{1,0:T(8,128)(2,1)S(1)}, bf16[64,1024]{1,0:T(8,128)(2,1)S(1)}, u32[]{:S(2)}, u32[]{:S(2)}) %collective-permute-start.13) | collective-permute-done | bytes 131104 | tf_op jit(solution)/shard_map/ppermute | solution.py:14
  71.5 1.0 %fusion.1 = bf16[128,1024]{1,0:T(8,128)(2,1)} fusion(f32[64,1024]{1,0:T(8,128)S(1)} %get-tuple-element.32, f32[64,1024]{1,0:T(8,128)S(1)} %get-tuple-element.33, bf16[64,1024]{1,0:T(8,128)(2,1)S(1)} %fusion.44, bf16[64,1024]{1,0:T(8,128)(2,1)S(1)} %fusion.29, bf16[1,128,128]{2,1,0:T(8,128)(2,1)S(1)} %copy-done.5), kind=kOutput, calls=%fused_computation.2 | convolution fusion | flops 34471936 | bytes 1081344 | tf_op jit(solution)/shard_map/kij,kid->kjd/dot_general | solution.py:180
  72.7 0.6 add.111
  (67 shorter events, 6.1 us)
Async XLA Ops:
  0.6 4.2 %copy-start = (bf16[128,1024]{1,0:T(8,128)(2,1)S(1)}, bf16[128,1024]{1,0:T(8,128)(2,1)}, u32[]{:S(2)}) copy-start(bf16[128,1024]{1,0:T(8,128)(2,1)} %param.9) | copy-start | bytes 786436
  0.6 4.2 %copy-start.5 = (bf16[1,128,128]{2,1,0:T(8,128)(2,1)S(1)}, bf16[1,128,128]{2,1,0:T(8,128)(2,1)}, u32[]{:S(2)}) copy-start(bf16[1,128,128]{2,1,0:T(8,128)(2,1)} %param.11) | copy-start | bytes 98308
  1.8 17.5 %collective-permute-start.5 = (bf16[64,1024]{1,0:T(8,128)(2,1)S(1)}, bf16[64,1024]{1,0:T(8,128)(2,1)S(1)}, u32[]{:S(2)}, u32[]{:S(2)}) collective-permute-start(bf16[64,1024]{1,0:T(8,128)(2,1)S(1)} %convolution_convert_fusion), channel_id=1, source_target_pairs={{0,2},{2,0},{4,6},{6,4},{8,10},{10,8},{12,14},{14,12},{1,3},{3,1},... | collective-permute-start | bytes 393224 | tf_op jit(solution)/shard_map/ppermute | solution.py:14
  4.8 0.7 copy-start.6
  4.9 0.8 %copy-start.7 = (f32[3,128]{1,0:T(4,128)S(1)}, f32[3,128]{1,0:T(4,128)}, u32[]{:S(2)}) copy-start(f32[3,128]{1,0:T(4,128)} %param.13) | copy-start | bytes 4612
  5.0 8.1 %copy-start.3 = (bf16[128,1024]{1,0:T(8,128)(2,1)S(1)}, bf16[128,1024]{1,0:T(8,128)(2,1)}, u32[]{:S(2)}) copy-start(bf16[128,1024]{1,0:T(8,128)(2,1)} %param.10) | copy-start | bytes 786436
  5.1 6.1 %collective-permute-start = (bf16[64,1024]{1,0:T(8,128)(2,1)S(1)}, bf16[64,1024]{1,0:T(8,128)(2,1)S(1)}, u32[]{:S(2)}, u32[]{:S(2)}) collective-permute-start(bf16[64,1024]{1,0:T(8,128)(2,1)S(1)} %convolution_convert_fusion.1), channel_id=1, source_target_pairs={{0,2},{2,0},{4,6},{6,4},{8,10},{10,8},{12,14},{14,12},{1,3},{3,1},... | collective-permute-start | bytes 393224 | tf_op jit(solution)/shard_map/ppermute | solution.py:14
  11.3 5.0 %collective-permute-start.1 = (bf16[64,1024]{1,0:T(8,128)(2,1)S(1)}, bf16[64,1024]{1,0:T(8,128)(2,1)S(1)}, u32[]{:S(2)}, u32[]{:S(2)}) collective-permute-start(bf16[64,1024]{1,0:T(8,128)(2,1)S(1)} %fusion.4), channel_id=1, source_target_pairs={{0,4},{2,6},{4,0},{6,2},{8,12},{10,14},{12,8},{14,10},{1,5},{3,7},... | collective-permute-start | bytes 393224 | tf_op jit(solution)/shard_map/ppermute | solution.py:14
  16.4 7.5 %collective-permute-start.2 = (bf16[64,1024]{1,0:T(8,128)(2,1)S(1)}, bf16[64,1024]{1,0:T(8,128)(2,1)S(1)}, u32[]{:S(2)}, u32[]{:S(2)}) collective-permute-start(bf16[64,1024]{1,0:T(8,128)(2,1)S(1)} %fusion.6), channel_id=1, source_target_pairs={{0,8},{2,10},{4,12},{6,14},{8,0},{10,2},{12,4},{14,6},{1,9},{3,11}... | collective-permute-start | bytes 393224 | tf_op jit(solution)/shard_map/ppermute | solution.py:14
  19.4 5.1 %collective-permute-start.6 = (bf16[64,1024]{1,0:T(8,128)(2,1)S(1)}, bf16[64,1024]{1,0:T(8,128)(2,1)S(1)}, u32[]{:S(2)}, u32[]{:S(2)}) collective-permute-start(bf16[64,1024]{1,0:T(8,128)(2,1)S(1)} %fusion.12), channel_id=1, source_target_pairs={{0,4},{2,6},{4,0},{6,2},{8,12},{10,14},{12,8},{14,10},{1,5},{3,7},... | collective-permute-start | bytes 393224 | tf_op jit(solution)/shard_map/ppermute | solution.py:14
  24.1 1.7 %collective-permute-start.3 = (f32[64]{0:T(128)S(1)}, f32[64]{0:T(128)S(1)}, u32[]{:S(2)}, u32[]{:S(2)}) collective-permute-start(f32[64]{0:T(128)S(1)} %get-tuple-element.30), channel_id=1, source_target_pairs={{0,1},{1,0},{2,3},{3,2},{4,5},{5,4},{6,7},{7,6},{8,9},{9,8},{10,11... | collective-permute-start | bytes 776 | tf_op jit(solution)/shard_map/ppermute | solution.py:69
  24.5 1.3 %copy-start.4 = (f32[1024]{0:T(1024)S(1)}, f32[1024]{0:T(1024)}, u32[]{:S(2)}) copy-start(f32[1024]{0:T(1024)} %param.14) | copy-start | bytes 12292
  24.7 9.4 %collective-permute-start.7 = (bf16[64,1024]{1,0:T(8,128)(2,1)S(1)}, bf16[64,1024]{1,0:T(8,128)(2,1)S(1)}, u32[]{:S(2)}, u32[]{:S(2)}) collective-permute-start(bf16[64,1024]{1,0:T(8,128)(2,1)S(1)} %fusion.14), channel_id=1, source_target_pairs={{0,8},{2,10},{4,12},{6,14},{8,0},{10,2},{12,4},{14,6},{1,9},{3,11}... | collective-permute-start | bytes 393224 | tf_op jit(solution)/shard_map/ppermute | solution.py:14
  31.8 2.4 %copy-start.1 = (f32[64,1024]{1,0:T(8,128)S(1)}, f32[64,1024]{1,0:T(8,128)}, u32[]{:S(2)}) copy-start(f32[64,1024]{1,0:T(8,128)} %shard_map.120) | copy-start | bytes 786436
  31.8 2.3 %collective-permute-start.4 = (f32[64]{0:T(128)S(1)}, f32[64]{0:T(128)S(1)}, u32[]{:S(2)}, u32[]{:S(2)}) collective-permute-start(f32[64]{0:T(128)S(1)} %multiply_reduce_fusion.2), channel_id=1, source_target_pairs={{0,1},{1,0},{2,3},{3,2},{4,5},{5,4},{6,7},{7,6},{8,9},{9,8},{10,11... | collective-permute-start | bytes 776 | tf_op jit(solution)/shard_map/ppermute | solution.py:69
  34.7 1.2 %collective-permute-start.8 = (f32[64]{0:T(128)S(1)}, f32[64]{0:T(128)S(1)}, u32[]{:S(2)}, u32[]{:S(2)}) collective-permute-start(f32[64]{0:T(128)S(1)} %multiply_reduce_fusion.1), channel_id=1, source_target_pairs={{0,1},{1,0},{2,3},{3,2},{4,5},{5,4},{6,7},{7,6},{8,9},{9,8},{10,11... | collective-permute-start | bytes 776 | tf_op jit(solution)/shard_map/ppermute | solution.py:69
  34.8 7.1 %collective-permute-start.9 = (bf16[64,512]{1,0:T(8,128)(2,1)S(1)}, bf16[64,512]{1,0:T(8,128)(2,1)S(1)}, u32[]{:S(2)}, u32[]{:S(2)}) collective-permute-start(bf16[64,512]{1,0:T(8,128)(2,1)S(1)} %get-tuple-element.37), channel_id=1, source_target_pairs={{0,8},{2,10},{4,12},{6,14},{8,0},{10,2},{12,4},{14,6},{1,9},{3,11}... | collective-permute-start | bytes 196616 | tf_op jit(solution)/shard_map/ppermute | solution.py:14
  40.7 2.4 %copy-start.2 = (f32[64,1024]{1,0:T(8,128)S(1)}, f32[64,1024]{1,0:T(8,128)}, u32[]{:S(2)}) copy-start(f32[64,1024]{1,0:T(8,128)} %shard_map.121) | copy-start | bytes 786436
  41.9 1.2 %collective-permute-start.10 = (f32[64]{0:T(128)S(1)}, f32[64]{0:T(128)S(1)}, u32[]{:S(2)}, u32[]{:S(2)}) collective-permute-start(f32[64]{0:T(128)S(1)} %multiply_reduce_fusion), channel_id=1, source_target_pairs={{0,1},{1,0},{2,3},{3,2},{4,5},{5,4},{6,7},{7,6},{8,9},{9,8},{10,11... | collective-permute-start | bytes 776 | tf_op jit(solution)/shard_map/ppermute | solution.py:69
  43.5 12.2 %collective-permute-start.14 = (bf16[64,1024]{1,0:T(8,128)(2,1)S(1)}, bf16[64,1024]{1,0:T(8,128)(2,1)S(1)}, u32[]{:S(2)}, u32[]{:S(2)}) collective-permute-start(bf16[64,1024]{1,0:T(8,128)(2,1)S(1)} %fusion.35), channel_id=1, source_target_pairs={{0,8},{2,10},{4,12},{6,14},{8,0},{10,2},{12,4},{14,6},{1,9},{3,11}... | collective-permute-start | bytes 393224 | tf_op jit(solution)/shard_map/ppermute | solution.py:14
  45.5 10.2 %collective-permute-start.11 = (bf16[64,512]{1,0:T(8,128)(2,1)S(1)}, bf16[64,512]{1,0:T(8,128)(2,1)S(1)}, u32[]{:S(2)}, u32[]{:S(2)}) collective-permute-start(bf16[64,512]{1,0:T(8,128)(2,1)S(1)} %get-tuple-element.9), channel_id=1, source_target_pairs={{0,8},{2,10},{4,12},{6,14},{8,0},{10,2},{12,4},{14,6},{1,9},{3,11}... | collective-permute-start | bytes 196616 | tf_op jit(solution)/shard_map/ppermute | solution.py:14
  56.2 6.3 %collective-permute-start.15 = (bf16[64,1024]{1,0:T(8,128)(2,1)S(1)}, bf16[64,1024]{1,0:T(8,128)(2,1)S(1)}, u32[]{:S(2)}, u32[]{:S(2)}) collective-permute-start(bf16[64,1024]{1,0:T(8,128)(2,1)S(1)} %fusion.40), channel_id=1, source_target_pairs={{0,4},{2,6},{4,0},{6,2},{8,12},{10,14},{12,8},{14,10},{1,5},{3,7},... | collective-permute-start | bytes 393224 | tf_op jit(solution)/shard_map/ppermute | solution.py:14
  56.3 8.2 %collective-permute-start.12 = (bf16[64,1024]{1,0:T(8,128)(2,1)S(1)}, bf16[64,1024]{1,0:T(8,128)(2,1)S(1)}, u32[]{:S(2)}, u32[]{:S(2)}) collective-permute-start(bf16[64,1024]{1,0:T(8,128)(2,1)S(1)} %fusion.25), channel_id=1, source_target_pairs={{0,4},{2,6},{4,0},{6,2},{8,12},{10,14},{12,8},{14,10},{1,5},{3,7},... | collective-permute-start | bytes 393224 | tf_op jit(solution)/shard_map/ppermute | solution.py:14
  62.8 5.2 %collective-permute-start.16 = (bf16[64,1024]{1,0:T(8,128)(2,1)S(1)}, bf16[64,1024]{1,0:T(8,128)(2,1)S(1)}, u32[]{:S(2)}, u32[]{:S(2)}) collective-permute-start(bf16[64,1024]{1,0:T(8,128)(2,1)S(1)} %fusion.45), channel_id=1, source_target_pairs={{0,2},{2,0},{4,6},{6,4},{8,10},{10,8},{12,14},{14,12},{1,3},{3,1},... | collective-permute-start | bytes 393224 | tf_op jit(solution)/shard_map/ppermute | solution.py:14
  64.9 1.7 %collective-permute-start.18 = (f32[3,128]{1,0:T(4,128)S(1)}, f32[3,128]{1,0:T(4,128)S(1)}, u32[]{:S(2)}, u32[]{:S(2)}) collective-permute-start(f32[3,128]{1,0:T(4,128)S(1)} %maximum_maximum_fusion.1), channel_id=1, source_target_pairs={{0,1},{1,0},{2,3},{3,2},{4,5},{5,4},{6,7},{7,6},{8,9},{9,8},{10,11... | collective-permute-start | bytes 4616 | tf_op jit(solution)/shard_map/ppermute | solution.py:69
  65.0 2.3 %collective-permute-start.17 = (f32[3,128]{1,0:T(4,128)S(1)}, f32[3,128]{1,0:T(4,128)S(1)}, u32[]{:S(2)}, u32[]{:S(2)}) collective-permute-start(f32[3,128]{1,0:T(4,128)S(1)} %maximum_maximum_fusion), channel_id=1, source_target_pairs={{0,1},{1,0},{2,3},{3,2},{4,5},{5,4},{6,7},{7,6},{8,9},{9,8},{10,11... | collective-permute-start | bytes 4616 | tf_op jit(solution)/shard_map/ppermute | solution.py:69
  65.6 5.5 %collective-permute-start.13 = (bf16[64,1024]{1,0:T(8,128)(2,1)S(1)}, bf16[64,1024]{1,0:T(8,128)(2,1)S(1)}, u32[]{:S(2)}, u32[]{:S(2)}) collective-permute-start(bf16[64,1024]{1,0:T(8,128)(2,1)S(1)} %fusion.30), channel_id=1, source_target_pairs={{0,2},{2,0},{4,6},{6,4},{8,10},{10,8},{12,14},{14,12},{1,3},{3,1},... | collective-permute-start | bytes 393224 | tf_op jit(solution)/shard_map/ppermute | solution.py:14
  71.4 1.3 %collective-permute-start.19 = (f32[1,128,128]{2,1,0:T(8,128)S(1)}, f32[1,128,128]{2,1,0:T(8,128)S(1)}, u32[]{:S(2)}, u32[]{:S(2)}) collective-permute-start(f32[1,128,128]{2,1,0:T(8,128)S(1)} %convolution_bitcast_fusion.1), channel_id=1, source_target_pairs={{0,1},{1,0},{2,3},{3,2},{4,5},{5,4},{6,7},{7,6},{8,9},{9,8},{10,11... | collective-permute-start | bytes 196616 | tf_op jit(solution)/shard_map/ppermute | solution.py:69
